TPU v7x, 512 devices: a whole 4x4x16 slice. The times are simulated.
512 devices in a mesh: grp: 4 (over y), seq: 32 (over z, core), head: 4 (over x).
Axes of the slice: x: 4, y: 4, z: 16, core: 2. Of those that a mesh axis runs over, the one named last changes fastest.
Arguments:
- light_q: bfloat16 [16384, 4096], P(('grp', 'seq'), 'head'), may hold values from -6 to 6
- light_k: bfloat16 [16384, 4096], P(('grp', 'seq'), 'head'), may hold values from -6 to 6
- light_v: bfloat16 [16384, 4096], P(('grp', 'seq'), 'head'), may hold values from -6 to 6
- log_decay: float32 [32, 16384], P('head', ('grp', 'seq')), may hold values from -1 to 0
- light_gain: float32 [4096], P('head'), may hold values from 0.1 to 1.9
- soft_q: bfloat16 [16384, 8192], P(('grp', 'seq'), 'head'), may hold values from -5 to 5
- soft_k: bfloat16 [16384, 1024], P(('grp', 'seq'), 'head'), may hold values from -5 to 5
- soft_v: bfloat16 [16384, 1024], P(('grp', 'seq'), 'head'), may hold values from -6 to 6
- segment_ids: int32 [128], replicated, may hold values from 0 to 32, never falling along the last dimension, each value on 1 to 8 neighbouring positions
Outputs:
- light_out: bfloat16 [16384, 4096], P(('grp', 'seq'), 'head')
- soft_out: bfloat16 [16384, 8192], P(('grp', 'seq'), 'head')
Inputs may be any that keep to these rules, and one draw needn't show every extreme that they name: `segment_ids`: segment numbers never fall along the sequence; each document covers 1 to 8 blocks, and one covers exactly 8.
All inputs are finite; a program needn't handle non-finite values.
Results may differ from a plain program's by a relative error of at most 0.0054.
Values may be sent and summed in bfloat16 or wider, within the bound.
No kernel may reach another device: no remote copies, remote signals or barrier semaphores. Data moves between devices by JAX's collectives and lax.ppermute only.
A program may use at most 192 MiB of HBM per device.

v0:
```python
from functools import partial

import jax
import jax.numpy as jnp
from jax import lax
from jax.sharding import PartitionSpec as P

LIGHTNING_HEADS = 32
HEAD_DIM = 128
BLOCK = 128
WINDOW_DEV = 8


NEG_FLOOR = -10000.0
MASK_FILL = -1e30


def prefix(x, axis, combine, identity):
    count, here = (lax.axis_size(axis), lax.axis_index(axis))
    everything = jax.tree.map(lambda part: lax.all_gather(part, axis), x)
    start = jax.tree.map(
        lambda part, zero: jnp.broadcast_to(jnp.asarray(zero, part.dtype), part.shape), x, identity
    )

    def lap(k, before):
        reached = k < here
        new = combine(before, jax.tree.map(lambda part: part[k], everything))
        return jax.tree.map(lambda a, b: jnp.where(reached, a, b), new, before)

    return lax.fori_loop(0, count, lap, start)


def from_behind(x, axis, by):
    count = lax.axis_size(axis)
    pairs = [(i, i + by) for i in range(count) if 0 <= i + by < count]
    return lax.ppermute(x, axis, pairs)


def join_states(earlier, later):
    return (earlier[0] * later[0], earlier[1] * later[0][:, None, None] + later[1])


def token_segments(segment_ids, row_start, tok_rows):
    blocks = lax.dynamic_slice_in_dim(segment_ids, row_start // BLOCK, tok_rows // BLOCK)
    return jnp.repeat(blocks, BLOCK)


def lightning_local(light_q, light_k, light_v, log_decay, seg_tok, prev_last):
    tok_rows, feat_width = light_q.shape
    head_count = feat_width // HEAD_DIM
    queries = light_q.reshape(tok_rows, head_count, HEAD_DIM)
    key_rows = light_k.reshape(tok_rows, head_count, HEAD_DIM)
    value_rows = light_v.reshape(tok_rows, head_count, HEAD_DIM)
    levels = jnp.cumsum(log_decay, axis=1)
    offsets = jnp.arange(tok_rows, dtype=jnp.int32)
    allowed = (offsets[:, None] >= offsets[None, :]) & (seg_tok[:, None] == seg_tok[None, :])
    decays = jnp.exp(jnp.where(allowed[None], levels[:, :, None] - levels[:, None, :], NEG_FLOOR))
    scores = jnp.einsum("thd,shd->hts", queries, key_rows, preferred_element_type=jnp.float32)
    weights = (scores * decays).astype(jnp.bfloat16)
    intra_part = jnp.einsum("hts,shd->thd", weights, value_rows, preferred_element_type=jnp.float32)
    last_seg = seg_tok[tok_rows - 1]
    tail_gain = jnp.exp(
        jnp.where(
            (seg_tok == last_seg)[None, :], levels[:, tok_rows - 1 : tok_rows] - levels, NEG_FLOOR
        )
    )
    keyed = (key_rows * tail_gain.T[:, :, None]).astype(jnp.bfloat16)
    local_state = jnp.einsum("shd,she->hde", keyed, value_rows, preferred_element_type=jnp.float32)
    first_seg = seg_tok[0]
    joined = (first_seg == prev_last) & jnp.all(seg_tok == first_seg)
    carry_gain = jnp.where(joined, jnp.exp(levels[:, tok_rows - 1]), 0.0)
    reach_gain = jnp.where(
        ((seg_tok == first_seg) & (first_seg == prev_last))[None, :], jnp.exp(levels), 0.0
    )
    return (intra_part, (carry_gain, local_state), reach_gain, queries)


def absorb(running, queries, key_rows, value_rows, allowed):
    row_max, row_mass, weighted = running
    scores = jnp.einsum(
        "tkgd,skd->tkgs", queries, key_rows, preferred_element_type=jnp.float32
    ) * HEAD_DIM ** (-0.5)
    scores = jnp.where(allowed[:, None, None, :], scores, MASK_FILL)
    new_max = jnp.maximum(row_max, jnp.max(scores, axis=-1))
    exponent = jnp.exp(scores - new_max[..., None])
    shrink = jnp.exp(row_max - new_max)
    row_mass = row_mass * shrink + jnp.sum(exponent, axis=-1)
    update = jnp.einsum(
        "tkgs,skd->tkgd",
        exponent.astype(jnp.bfloat16),
        value_rows,
        preferred_element_type=jnp.float32,
    )
    weighted = weighted * shrink[..., None] + update
    return (new_max, row_mass, weighted)


def body(light_q, light_k, light_v, log_decay, light_gain, soft_q, soft_k, soft_v, segment_ids):
    tok_rows = light_q.shape[0]
    position = lax.axis_index(("grp", "seq"))
    row_start = position * tok_rows
    seg_tok = token_segments(segment_ids, row_start, tok_rows)
    prev_index = jnp.maximum(position * (tok_rows // BLOCK) - 1, 0)
    prev_last = jnp.where(
        position > 0, lax.dynamic_index_in_dim(segment_ids, prev_index, keepdims=False), -1
    )
    intra_part, element, reach_gain, queries = lightning_local(
        light_q, light_k, light_v, log_decay, seg_tok, prev_last
    )
    identity = (jnp.ones_like(element[0]), jnp.zeros_like(element[1]))
    entering = prefix(element, ("grp", "seq"), join_states, identity)
    state_rounded = entering[1].astype(jnp.bfloat16)
    inter_part = (
        jnp.einsum("thd,hde->the", queries, state_rounded, preferred_element_type=jnp.float32)
        * reach_gain.T[:, :, None]
    )
    mixed = (intra_part + inter_part).reshape(tok_rows, -1)
    square_sum = lax.psum(jnp.sum(mixed * mixed, axis=1), "head")
    inv_norm = lax.rsqrt(square_sum / (LIGHTNING_HEADS * HEAD_DIM) + 1e-06)
    light_out = (mixed * inv_norm[:, None] * light_gain).astype(jnp.bfloat16)
    kv_pair = jnp.stack([soft_k, soft_v])
    window_len = min(WINDOW_DEV, lax.axis_size(("grp", "seq")))

    def pass_on(stride, running):
        in_flight, gathered = running
        in_flight = from_behind(in_flight, ("grp", "seq"), 1)
        gathered = lax.dynamic_update_index_in_dim(gathered, in_flight, stride, 0)
        return (in_flight, gathered)

    gathered = jnp.zeros((window_len,) + kv_pair.shape, kv_pair.dtype).at[0].set(kv_pair)
    window = lax.fori_loop(1, window_len, pass_on, (kv_pair, gathered))[1]
    kv_heads = soft_k.shape[1] // HEAD_DIM
    group_size = soft_q.shape[1] // soft_k.shape[1]
    soft_queries = soft_q.reshape(tok_rows, kv_heads, group_size, HEAD_DIM)
    query_pos = row_start + jnp.arange(tok_rows, dtype=jnp.int32)
    slots_per = max(1, 512 // tok_rows)
    running = (
        jnp.full((tok_rows, kv_heads, group_size), MASK_FILL, jnp.float32),
        jnp.zeros((tok_rows, kv_heads, group_size), jnp.float32),
        jnp.zeros((tok_rows, kv_heads, group_size, HEAD_DIM), jnp.float32),
    )
    for first_slot in range(0, window_len, slots_per):
        slot_list = list(range(first_slot, min(first_slot + slots_per, window_len)))
        chosen = window[first_slot : first_slot + len(slot_list)]
        key_rows = chosen[:, 0].reshape(-1, kv_heads, HEAD_DIM)
        value_rows = chosen[:, 1].reshape(-1, kv_heads, HEAD_DIM)
        key_pos = jnp.concatenate(
            [
                (position - source) * tok_rows + jnp.arange(tok_rows, dtype=jnp.int32)
                for source in slot_list
            ]
        )
        key_seg = jnp.concatenate(
            [
                token_segments(segment_ids, jnp.maximum(position - source, 0) * tok_rows, tok_rows)
                for source in slot_list
            ]
        )
        allowed = (
            (key_pos[None, :] <= query_pos[:, None])
            & (key_pos >= 0)[None, :]
            & (key_seg[None, :] == seg_tok[:, None])
        )
        step_fn = partial(
            absorb, queries=soft_queries, key_rows=key_rows, value_rows=value_rows, allowed=allowed
        )
        running = step_fn(running)
    row_max, row_mass, weighted = running
    soft_out = (weighted / row_mass[..., None]).reshape(tok_rows, -1).astype(jnp.bfloat16)
    return (light_out, soft_out)


def solution(mesh):
    placed = (
        P(("grp", "seq"), "head"),
        P(("grp", "seq"), "head"),
        P(("grp", "seq"), "head"),
        P("head", ("grp", "seq")),
        P("head"),
        P(("grp", "seq"), "head"),
        P(("grp", "seq"), "head"),
        P(("grp", "seq"), "head"),
        P(),
    )
    return jax.shard_map(
        body,
        mesh=mesh,
        in_specs=placed,
        out_specs=(P(("grp", "seq"), "head"), P(("grp", "seq"), "head")),
        check_vma=False,
    )
```

profile of v0, /device:TPU:32, one launch (start us, length us, event | category | flops | bytes accessed | tf_op | source)
XLA Modules:
  0.0 523.1 jit_solution(7139498409304828782)
XLA Ops:
  8.4 1.7 fusion.75
  13.8 1.3 dynamic-slice.7
  15.9 260.6 %all-reduce.1 = f32[1024]{0:T(1024)S(1)} all-reduce(f32[1024]{0:T(1024)S(1)} %dynamic-update-slice.3), channel_id=2, replica_groups=mesh['grp'=4,'seq'=32,'head'=4] {'grp','seq'}, use_global_device_ids=true, to_apply=%add.1 | all-reduce | flops 1024 | bytes 8192
  278.8 53.9 %while.30 = (s32[]{:T(128)}, bf16[2,128,256]{2,1,0:T(8,128)(2,1)S(1)}, bf16[8,2,128,256]{3,2,1,0:T(8,128)(2,1)S(1)}, s32[]{:T(128)}, s32[]{:T(128)}, /*index=5*/s32[]{:T(128)}) while((s32[]{:T(128)}, bf16[2,128,256]{2,1,0:T(8,128)(2,1)S(1)}, bf16[8,2,128,256]{3,2,1,0:T(8,128)(2,1)S(1)}, s32[]{:T(128)}, s32[]{:T(128)}, ...), condition=%wide.region_6.7_spmd, body=%wide.region_5.6_spmd.sunk | while | flops 5 | bytes 1048731 | solution.py:131
  278.8 1.9 collective-permute-start
  280.7 6.9 %collective-permute-done = bf16[2,128,256]{2,1,0:T(8,128)(2,1)S(1)} collective-permute-done((bf16[2,128,256]{2,1,0:T(8,128)(2,1)S(1)}, bf16[2,128,256]{2,1,0:T(8,128)(2,1)S(1)}, u32[]{:S(2)}, u32[]{:S(2)}) %collective-permute-start) | collective-permute-done | bytes 131104 | tf_op jit(solution)/shard_map/while/body/eval_jaxpr/ppermute | solution.py:36
  287.7 1.9 collective-permute-start
  289.6 6.8 %collective-permute-done = bf16[2,128,256]{2,1,0:T(8,128)(2,1)S(1)} collective-permute-done((bf16[2,128,256]{2,1,0:T(8,128)(2,1)S(1)}, bf16[2,128,256]{2,1,0:T(8,128)(2,1)S(1)}, u32[]{:S(2)}, u32[]{:S(2)}) %collective-permute-start) | collective-permute-done | bytes 131104 | tf_op jit(solution)/shard_map/while/body/eval_jaxpr/ppermute | solution.py:36
  296.5 1.9 collective-permute-start
  298.4 6.7 %collective-permute-done = bf16[2,128,256]{2,1,0:T(8,128)(2,1)S(1)} collective-permute-done((bf16[2,128,256]{2,1,0:T(8,128)(2,1)S(1)}, bf16[2,128,256]{2,1,0:T(8,128)(2,1)S(1)}, u32[]{:S(2)}, u32[]{:S(2)}) %collective-permute-start) | collective-permute-done | bytes 131104 | tf_op jit(solution)/shard_map/while/body/eval_jaxpr/ppermute | solution.py:36
  305.2 1.9 collective-permute-start
  307.1 6.5 %collective-permute-done = bf16[2,128,256]{2,1,0:T(8,128)(2,1)S(1)} collective-permute-done((bf16[2,128,256]{2,1,0:T(8,128)(2,1)S(1)}, bf16[2,128,256]{2,1,0:T(8,128)(2,1)S(1)}, u32[]{:S(2)}, u32[]{:S(2)}) %collective-permute-start) | collective-permute-done | bytes 131104 | tf_op jit(solution)/shard_map/while/body/eval_jaxpr/ppermute | solution.py:36
  313.7 1.9 collective-permute-start
  315.6 4.4 collective-permute-done
  320.0 1.9 collective-permute-start
  322.0 4.4 collective-permute-done
  326.4 1.9 collective-permute-start
  328.3 4.4 collective-permute-done
  348.0 155.8 %while.31 = (s32[]{:T(128)}, f32[8,128,128]{2,1,0:T(8,128)S(1)}, s32[]{:T(128)}, f32[128,8]{1,0:T(8,128)S(1)}, f32[128,8,128,128]{3,2,1,0:T(8,128)}, /*index=5*/s32[]{:T(128)}, s32[]{:T(128)}) while((s32[]{:T(128)}, f32[8,128,128]{2,1,0:T(8,128)S(1)}, s32[]{:T(128)}, f32[128,8]{1,0:T(8,128)S(1)}, f32[128,8,128,128]{3,2,1,0:T(8,128)}, ...), condition=%wide.region_2.3_spmd.clone, body=%wide.region_1.2_spmd.clone.sunk | while | flops 524292 | bytes 1573073 | solution.py:30
  351.7 1.2 fusion.84
  352.9 1.2 fusion.84
  354.1 1.2 fusion.84
  355.3 1.2 fusion.84
  356.6 1.2 fusion.84
  362.6 1.2 fusion.84
  363.9 1.2 fusion.84
  365.1 1.2 fusion.84
  366.3 1.2 fusion.84
  367.5 1.2 fusion.84
  368.7 1.2 fusion.84
  374.8 1.2 fusion.84
  504.8 10.6 %psum.7 = f32[128]{0:T(128)S(1)} all-reduce(f32[128]{0:T(128)S(1)} %get-tuple-element.245), channel_id=1, replica_groups=mesh['grp'=4,'seq'=32,'head'=4] {'head'}, use_global_device_ids=true, to_apply=%region_4.5 | all-reduce | flops 128 | bytes 1024 | tf_op jit(solution)/shard_map/psum | solution.py:118
  (315 shorter events, 160.3 us)
Async XLA Ops:
  7.2 5.5 %copy-start = (bf16[128,1024]{1,0:T(8,128)(2,1)S(1)}, bf16[128,1024]{1,0:T(8,128)(2,1)}, u32[]{:S(2)}) copy-start(bf16[128,1024]{1,0:T(8,128)(2,1)} %param.17) | copy-start | bytes 786436
  7.2 340.8 %all-gather.4.cloned.1.call-start = ((), (), s32[]{:S(2)}) async-start(), calls=%async_computation | async-start | bytes 67633152 | tf_op jit(solution)/shard_map/all_gather | solution.py:20
  278.8 8.8 %collective-permute-start = (bf16[2,128,256]{2,1,0:T(8,128)(2,1)S(1)}, bf16[2,128,256]{2,1,0:T(8,128)(2,1)S(1)}, u32[]{:S(2)}, u32[]{:S(2)}) collective-permute-start(bf16[2,128,256]{2,1,0:T(8,128)(2,1)S(1)} %get-tuple-element.339), channel_id=1, source_target_pairs={{0,4},{4,8},{8,12},{12,16},{16,20},{20,24},{24,28},{28,32},{32,36}... | collective-permute-start | bytes 393224 | tf_op jit(solution)/shard_map/while/body/eval_jaxpr/ppermute | solution.py:36
  287.7 8.8 %collective-permute-start = (bf16[2,128,256]{2,1,0:T(8,128)(2,1)S(1)}, bf16[2,128,256]{2,1,0:T(8,128)(2,1)S(1)}, u32[]{:S(2)}, u32[]{:S(2)}) collective-permute-start(bf16[2,128,256]{2,1,0:T(8,128)(2,1)S(1)} %get-tuple-element.339), channel_id=1, source_target_pairs={{0,4},{4,8},{8,12},{12,16},{16,20},{20,24},{24,28},{28,32},{32,36}... | collective-permute-start | bytes 393224 | tf_op jit(solution)/shard_map/while/body/eval_jaxpr/ppermute | solution.py:36
  296.5 8.6 %collective-permute-start = (bf16[2,128,256]{2,1,0:T(8,128)(2,1)S(1)}, bf16[2,128,256]{2,1,0:T(8,128)(2,1)S(1)}, u32[]{:S(2)}, u32[]{:S(2)}) collective-permute-start(bf16[2,128,256]{2,1,0:T(8,128)(2,1)S(1)} %get-tuple-element.339), channel_id=1, source_target_pairs={{0,4},{4,8},{8,12},{12,16},{16,20},{20,24},{24,28},{28,32},{32,36}... | collective-permute-start | bytes 393224 | tf_op jit(solution)/shard_map/while/body/eval_jaxpr/ppermute | solution.py:36
  305.2 8.5 %collective-permute-start = (bf16[2,128,256]{2,1,0:T(8,128)(2,1)S(1)}, bf16[2,128,256]{2,1,0:T(8,128)(2,1)S(1)}, u32[]{:S(2)}, u32[]{:S(2)}) collective-permute-start(bf16[2,128,256]{2,1,0:T(8,128)(2,1)S(1)} %get-tuple-element.339), channel_id=1, source_target_pairs={{0,4},{4,8},{8,12},{12,16},{16,20},{20,24},{24,28},{28,32},{32,36}... | collective-permute-start | bytes 393224 | tf_op jit(solution)/shard_map/while/body/eval_jaxpr/ppermute | solution.py:36
  313.7 6.3 %collective-permute-start = (bf16[2,128,256]{2,1,0:T(8,128)(2,1)S(1)}, bf16[2,128,256]{2,1,0:T(8,128)(2,1)S(1)}, u32[]{:S(2)}, u32[]{:S(2)}) collective-permute-start(bf16[2,128,256]{2,1,0:T(8,128)(2,1)S(1)} %get-tuple-element.339), channel_id=1, source_target_pairs={{0,4},{4,8},{8,12},{12,16},{16,20},{20,24},{24,28},{28,32},{32,36}... | collective-permute-start | bytes 393224 | tf_op jit(solution)/shard_map/while/body/eval_jaxpr/ppermute | solution.py:36
  320.0 6.3 %collective-permute-start = (bf16[2,128,256]{2,1,0:T(8,128)(2,1)S(1)}, bf16[2,128,256]{2,1,0:T(8,128)(2,1)S(1)}, u32[]{:S(2)}, u32[]{:S(2)}) collective-permute-start(bf16[2,128,256]{2,1,0:T(8,128)(2,1)S(1)} %get-tuple-element.339), channel_id=1, source_target_pairs={{0,4},{4,8},{8,12},{12,16},{16,20},{20,24},{24,28},{28,32},{32,36}... | collective-permute-start | bytes 393224 | tf_op jit(solution)/shard_map/while/body/eval_jaxpr/ppermute | solution.py:36
  326.4 6.3 %collective-permute-start = (bf16[2,128,256]{2,1,0:T(8,128)(2,1)S(1)}, bf16[2,128,256]{2,1,0:T(8,128)(2,1)S(1)}, u32[]{:S(2)}, u32[]{:S(2)}) collective-permute-start(bf16[2,128,256]{2,1,0:T(8,128)(2,1)S(1)} %get-tuple-element.339), channel_id=1, source_target_pairs={{0,4},{4,8},{8,12},{12,16},{16,20},{20,24},{24,28},{28,32},{32,36}... | collective-permute-start | bytes 393224 | tf_op jit(solution)/shard_map/while/body/eval_jaxpr/ppermute | solution.py:36
  347.9 155.8 %copy-start.1 = (bf16[128,1024]{1,0:T(8,128)(2,1)S(1)}, bf16[128,1024]{1,0:T(8,128)(2,1)}, u32[]{:S(2)}) copy-start(bf16[128,1024]{1,0:T(8,128)(2,1)} %param.15) | copy-start | bytes 786436
  348.0 167.4 %copy-start.2 = (f32[1024]{0:T(1024)S(1)}, f32[1024]{0:T(1024)}, u32[]{:S(2)}) copy-start(f32[1024]{0:T(1024)} %param.19) | copy-start | bytes 12292
Sparse Core Ops, SparseCore 0:
  13.9 303.6 all-gather.3
where the time goes:
time: 530 us; the launch traced here: 523 us
  blocking collectives  271 us (51%)
  other arithmetic  156 us (29%)
  waiting for transfers between devices  40 us (8%)
  between operations  16.4 us (3%)
  local copies, waits for them, and re-layouts  15.5 us (3%)
  starting transfers between devices  13.5 us (3%)
  matrix products  5.76 us (1%)
    unnamed x1, blocking collectives  261 us
    select_n x128, other arithmetic, lap(): return jax.tree.map(lambda a, b: jnp.where(reached, a, b), new, before)  150 us
    ppermute x7, waiting for transfers between devices, from_behind(): return lax.ppermute(x, axis, pairs)  40 us
    ppermute x7, starting transfers between devices, from_behind(): return lax.ppermute(x, axis, pairs)  13.4 us
  transfers between devices with their start and end apart: 8, of which 7 were waited for; matrix products, arithmetic and copies ran while one was open for 4% of the time, Pallas kernels for 0%

commit v1 on v0

--- a/solution.py
+++ b/solution.py
@@ -34,6 +34,14 @@
     count = lax.axis_size(axis)
     pairs = [(i, i + by) for i in range(count) if 0 <= i + by < count]
     return lax.ppermute(x, axis, pairs)
+
+
+def window_scan(x, axis, width):
+    reach = 1
+    while reach < min(width, lax.axis_size(axis)):
+        x = join_states(jax.tree.map(lambda part: from_behind(part, axis, reach), x), x)
+        reach *= 2
+    return x
 
 
 def join_states(earlier, later):
@@ -107,9 +115,9 @@
     intra_part, element, reach_gain, queries = lightning_local(
         light_q, light_k, light_v, log_decay, seg_tok, prev_last
     )
-    identity = (jnp.ones_like(element[0]), jnp.zeros_like(element[1]))
-    entering = prefix(element, ("grp", "seq"), join_states, identity)
-    state_rounded = entering[1].astype(jnp.bfloat16)
+    reach = window_scan(element, ("grp", "seq"), WINDOW_DEV)
+    entering = from_behind(reach[1], ("grp", "seq"), 1)
+    state_rounded = entering.astype(jnp.bfloat16)
     inter_part = (
         jnp.einsum("thd,hde->the", queries, state_rounded, preferred_element_type=jnp.float32)
         * reach_gain.T[:, :, None]
@@ -121,14 +129,11 @@
     kv_pair = jnp.stack([soft_k, soft_v])
     window_len = min(WINDOW_DEV, lax.axis_size(("grp", "seq")))
 
-    def pass_on(stride, running):
-        in_flight, gathered = running
-        in_flight = from_behind(in_flight, ("grp", "seq"), 1)
-        gathered = lax.dynamic_update_index_in_dim(gathered, in_flight, stride, 0)
-        return (in_flight, gathered)
-
-    gathered = jnp.zeros((window_len,) + kv_pair.shape, kv_pair.dtype).at[0].set(kv_pair)
-    window = lax.fori_loop(1, window_len, pass_on, (kv_pair, gathered))[1]
+    window = kv_pair[None]
+    while window.shape[0] < window_len:
+        window = jnp.concatenate(
+            [window, from_behind(window, ("grp", "seq"), window.shape[0])]
+        )[:window_len]
     kv_heads = soft_k.shape[1] // HEAD_DIM
     group_size = soft_q.shape[1] // soft_k.shape[1]
     soft_queries = soft_q.reshape(tok_rows, kv_heads, group_size, HEAD_DIM)

time: 530 us -> 131 us (0.25)
  the two profiles are of different devices: /device:TPU:32 before, /device:TPU:24 now
where the time goes in v1:
time: 131 us; the launch traced here: 130 us
  waiting for transfers between devices  59.8 us (46%)
  starting transfers between devices  24.5 us (19%)
  local copies, waits for them, and re-layouts  11.3 us (9%)
  other arithmetic  10.8 us (8%)
  matrix products  10.8 us (8%)
  blocking collectives  10.5 us (8%)
  between operations  2.52 us (2%)
    ppermute x9, waiting for transfers between devices, from_behind(): return lax.ppermute(x, axis, pairs)  59.8 us
    ppermute x9, starting transfers between devices, from_behind(): return lax.ppermute(x, axis, pairs)  24.5 us
    psum x1, blocking collectives, body(): square_sum = lax.psum(jnp.sum(mixed * mixed, axis=1), 'head')  10.5 us
    dot_general x2, matrix products, absorb(): jnp.einsum('tkgd,skd->tkgs', queries, key_rows, preferred_element_type=jn...  5.48 us
    reshape x8, local copies, waits for them, and re-layouts, token_segments(): return jnp.repeat(blocks, BLOCK)  5.06 us
    reduce_sum x2, other arithmetic, absorb(): row_mass = row_mass * shrink + jnp.sum(exponent, axis=-1)  4.09 us
  transfers between devices with their start and end apart: 9, of which 5 were waited for; matrix products, arithmetic and copies ran while one was open for 22% of the time, Pallas kernels for 0%

profile of v1, /device:TPU:24, one launch (start us, length us, event | category | flops | bytes accessed | tf_op | source)
XLA Modules:
  0.0 130.2 jit_solution(15332785769938622828)
XLA Ops:
  0.7 1.0 maximum_bitcast_fusion
  1.6 1.9 %collective-permute-start.6 = (bf16[1,2,128,256]{3,2,1,0:T(8,128)(2,1)S(1)}, bf16[1,2,128,256]{3,2,1,0:T(8,128)(2,1)S(1)}, u32[]{:S(2)}, u32[]{:S(2)}) collective-permute-start(bf16[1,2,128,256]{3,2,1,0:T(8,128)(2,1)S(1)} %maximum_bitcast_fusion), channel_id=1, source_target_pairs={{0,4},{4,8},{8,12},{12,16},{16,20},{20,24},{24,28},{28,32},{32,36}... | collective-permute-start | bytes 393224 | tf_op jit(solution)/shard_map/ppermute | solution.py:36
  3.7 1.0 reduce_window_sum.11
  4.9 1.1 copy.46
  6.0 1.7 %fusion.74 = (s32[1]{0:T(128)}, s32[1]{0:T(128)}, s32[1]{0:T(128)}, s32[1]{0:T(128)}, s32[1]{0:T(128)}, /*index=5*/s32[1]{0:T(128)}, s32[1]{0:T(128)}, s32[1]{0:T(128)}, s32[1]{0:T(128)}, s32[1]{0:T(128)}) fusion(s32[128]{0:T(128)} %param.17, s32[]{:T(128)S(6)} %select_n.113, s32[]{:T(128)S(6)} %select_n.115, s32[]{:T(128)S(6)} %select_n.110, ...), kind=kLoop, calls=%fused_computation.101 | loop fusion | bytes 120 | tf_op jit(solution)/shard_map/dynamic_slice | solution.py:52
  9.1 1.2 fusion.45
  10.3 3.9 %collective-permute-start = (f32[8,128,128]{2,1,0:T(8,128)S(1)}, f32[8,128,128]{2,1,0:T(8,128)}, u32[]{:S(2)}, u32[]{:S(2)}) collective-permute-start(f32[8,128,128]{2,1,0:T(8,128)S(1)} %fusion.45), channel_id=1, source_target_pairs={{0,4},{4,8},{8,12},{12,16},{16,20},{20,24},{24,28},{28,32},{32,36}... | collective-permute-start | bytes 1572872 | tf_op jit(solution)/shard_map/ppermute | solution.py:36
  14.2 1.9 %collective-permute-start.2 = (f32[8]{0:T(128)S(1)}, f32[8]{0:T(128)S(1)}, u32[]{:S(2)}, u32[]{:S(2)}) collective-permute-start(f32[8]{0:T(128)S(1)} %broadcast_select_fusion), channel_id=1, source_target_pairs={{0,4},{4,8},{8,12},{12,16},{16,20},{20,24},{24,28},{28,32},{32,36}... | collective-permute-start | bytes 104 | tf_op jit(solution)/shard_map/ppermute | solution.py:36
  16.2 1.4 %convolution_bitcast_fusion.1 = f32[128,8,128]{0,2,1:T(8,128)S(1)} fusion(bf16[128,8,128]{0,2,1:T(8,128)(2,1)S(1)} %bitcast.122, f32[8,128]{1,0:T(8,128)S(1)} %reduce_window_sum.11, pred[128,128]{1,0:T(8,128)(4,1)S(1)} %iota_compare_fusion, bf16[128,1024]{1,0:T(8,128)(2,1)} %param.11, bf16[128,1024]{1,0:T(8,128)(2,1)S(1)} %copy-done), kind=kOutput, calls=%fused_computation.26 | convolution fusion | flops 67633152 | bytes 1331200 | tf_op jit(solution)/shard_map/hts,shd->thd/dot_general | solution.py:68
  19.6 0.7 reshape.275
  23.5 3.8 %collective-permute-start.7 = (bf16[2,2,128,256]{3,2,1,0:T(8,128)(2,1)S(1)}, bf16[2,2,128,256]{3,2,1,0:T(8,128)(2,1)S(1)}, u32[]{:S(2)}, u32[]{:S(2)}) collective-permute-start(bf16[2,2,128,256]{3,2,1,0:T(8,128)(2,1)S(1)} %pad_maximum_fusion.1), channel_id=1, source_target_pairs={{0,8},{4,12},{8,16},{12,20},{16,24},{20,28},{24,32},{28,36},{32,40... | collective-permute-start | bytes 786440 | tf_op jit(solution)/shard_map/ppermute | solution.py:36
  28.2 3.7 %collective-permute-start.4 = (f32[8]{0:T(128)S(1)}, f32[8]{0:T(128)S(1)}, u32[]{:S(2)}, u32[]{:S(2)}) collective-permute-start(f32[8]{0:T(128)S(1)} %fusion.77), channel_id=1, source_target_pairs={{0,8},{4,12},{8,16},{12,20},{16,24},{20,28},{24,32},{28,36},{32,40... | collective-permute-start | bytes 104 | tf_op jit(solution)/shard_map/ppermute | solution.py:36
  32.0 7.5 %collective-permute-done.4 = f32[8]{0:T(128)S(1)} collective-permute-done((f32[8]{0:T(128)S(1)}, f32[8]{0:T(128)S(1)}, u32[]{:S(2)}, u32[]{:S(2)}) %collective-permute-start.4) | collective-permute-done | bytes 64 | tf_op jit(solution)/shard_map/ppermute | solution.py:36
  39.5 1.9 %collective-permute-start.8 = (bf16[4,2,128,256]{3,2,1,0:T(8,128)(2,1)S(1)}, bf16[4,2,128,256]{3,2,1,0:T(8,128)(2,1)}, u32[]{:S(2)}, u32[]{:S(2)}) collective-permute-start(bf16[4,2,128,256]{3,2,1,0:T(8,128)(2,1)S(1)} %pad_maximum_fusion), channel_id=1, source_target_pairs={{0,16},{4,20},{8,24},{12,28},{16,32},{20,36},{24,40},{28,44},{32,4... | collective-permute-start | bytes 1572872 | tf_op jit(solution)/shard_map/ppermute | solution.py:36
  41.7 2.7 %fusion.4 = (f32[128,2,8]{0,2,1:T(8,128)S(1)}, f32[2,512,128,8]{2,1,3,0:T(8,128)}) fusion(pred[128,512]{0,1:T(8,128)(4,1)S(1)} %get-tuple-element.22, bf16[128,2,8,128]{3,2,1,0:T(8,128)(2,1)S(1)} %bitcast.116, bf16[512,2,128,1]{2,1,0,3:T(2,128)(2,1)S(1)} %bitcast.119), kind=kOutput, calls=%fused_computation.8 | convolution fusion | flops 271579136 | bytes 5054464 | tf_op jit(solution)/shard_map/tkgd,skd->tkgs/dot_general | solution.py:88
  44.4 1.2 multiply_add_fusion.2
  45.5 2.5 %collective-permute-start.1 = (f32[8,128,128]{2,1,0:T(8,128)S(1)}, f32[8,128,128]{2,1,0:T(8,128)}, u32[]{:S(2)}, u32[]{:S(2)}) collective-permute-start(f32[8,128,128]{2,1,0:T(8,128)S(1)} %multiply_add_fusion.2), channel_id=1, source_target_pairs={{0,8},{4,12},{8,16},{12,20},{16,24},{20,28},{24,32},{28,36},{32,40... | collective-permute-start | bytes 1572872 | tf_op jit(solution)/shard_map/ppermute | solution.py:36
  48.1 21.9 %collective-permute-done.8 = bf16[4,2,128,256]{3,2,1,0:T(8,128)(2,1)} collective-permute-done((bf16[4,2,128,256]{3,2,1,0:T(8,128)(2,1)S(1)}, bf16[4,2,128,256]{3,2,1,0:T(8,128)(2,1)}, u32[]{:S(2)}, u32[]{:S(2)}) %collective-permute-start.8) | collective-permute-done | bytes 524320 | tf_op jit(solution)/shard_map/ppermute | solution.py:36
  69.9 1.1 fusion.72
  71.1 2.8 %fusion.5 = (f32[128,2,8]{0,2,1:T(8,128)S(1)}, f32[2,512,128,8]{2,1,3,0:T(8,128)}) fusion(pred[128,512]{0,1:T(8,128)(4,1)S(1)} %get-tuple-element.21, bf16[128,2,8,128]{3,2,1,0:T(8,128)(2,1)S(1)} %bitcast.117, bf16[512,2,128,1]{2,1,0,3:T(2,128)(2,1)S(1)} %bitcast.120), kind=kOutput, calls=%fused_computation.9 | convolution fusion | flops 271579136 | bytes 5054464 | tf_op jit(solution)/shard_map/tkgd,skd->tkgs/dot_general | solution.py:88
  74.4 0.9 fusion
  75.4 3.2 %fusion.2 = f32[128,2,8]{0,2,1:T(8,128)S(1)} fusion(f32[2,512,128,8]{2,1,3,0:T(8,128)} %get-tuple-element.38, f32[128,2,8]{0,2,1:T(8,128)S(1)} %get-tuple-element.17, pred[128,512]{0,1:T(8,128)(4,1)S(1)} %get-tuple-element.21), kind=kLoop, calls=%fused_computation.6 | loop fusion | flops 4192256 | bytes 4276224 | tf_op jit(solution)/shard_map/reduce_sum | solution.py:95
  78.6 1.2 multiply_add_fusion.1
  79.8 2.8 %collective-permute-start.3 = (f32[8,128,128]{2,1,0:T(8,128)S(1)}, f32[8,128,128]{2,1,0:T(8,128)S(1)}, u32[]{:S(2)}, u32[]{:S(2)}) collective-permute-start(f32[8,128,128]{2,1,0:T(8,128)S(1)} %multiply_add_fusion.1), channel_id=1, source_target_pairs={{0,16},{4,20},{8,24},{12,28},{16,32},{20,36},{24,40},{28,44},{32,4... | collective-permute-start | bytes 1572872 | tf_op jit(solution)/shard_map/ppermute | solution.py:36
  82.6 1.1 fusion.30
  83.8 24.6 %collective-permute-done.3 = f32[8,128,128]{2,1,0:T(8,128)S(1)} collective-permute-done((f32[8,128,128]{2,1,0:T(8,128)S(1)}, f32[8,128,128]{2,1,0:T(8,128)S(1)}, u32[]{:S(2)}, u32[]{:S(2)}) %collective-permute-start.3) | collective-permute-done | bytes 524320 | tf_op jit(solution)/shard_map/ppermute | solution.py:36
  108.5 1.9 %collective-permute-start.5 = (bf16[8,128,128]{2,1,0:T(8,128)(2,1)S(1)}, bf16[8,128,128]{2,1,0:T(8,128)(2,1)S(1)}, u32[]{:S(2)}, u32[]{:S(2)}) collective-permute-start(bf16[8,128,128]{2,1,0:T(8,128)(2,1)S(1)} %multiply_add_fusion), channel_id=1, source_target_pairs={{0,4},{4,8},{8,12},{12,16},{16,20},{20,24},{24,28},{28,32},{32,36}... | collective-permute-start | bytes 786440 | tf_op jit(solution)/shard_map/ppermute | solution.py:36
  110.4 1.2 divide_convert_fusion
  111.6 1.0 copy.38
  112.6 5.7 %collective-permute-done.5 = bf16[8,128,128]{2,1,0:T(8,128)(2,1)S(1)} collective-permute-done((bf16[8,128,128]{2,1,0:T(8,128)(2,1)S(1)}, bf16[8,128,128]{2,1,0:T(8,128)(2,1)S(1)}, u32[]{:S(2)}, u32[]{:S(2)}) %collective-permute-start.5) | collective-permute-done | bytes 262176 | tf_op jit(solution)/shard_map/ppermute | solution.py:36
  118.9 10.5 %psum.7 = f32[128]{0:T(128)S(1)} all-reduce(f32[128]{0:T(128)S(1)} %get-tuple-element.33), channel_id=1, replica_groups=mesh['grp'=4,'seq'=32,'head'=4] {'head'}, use_global_device_ids=true, to_apply=%region_2.3 | all-reduce | flops 128 | bytes 1024 | tf_op jit(solution)/shard_map/psum | solution.py:126
  129.4 0.8 multiply_convert_fusion
  (52 shorter events, 7.9 us)
Async XLA Ops:
  0.6 15.6 %copy-start = (bf16[128,1024]{1,0:T(8,128)(2,1)S(1)}, bf16[128,1024]{1,0:T(8,128)(2,1)}, u32[]{:S(2)}) copy-start(bf16[128,1024]{1,0:T(8,128)(2,1)} %param.9) | copy-start | bytes 786436
  0.6 27.4 %copy-start.4 = (bf16[128,2048]{1,0:T(8,128)(2,1)S(1)}, bf16[128,2048]{1,0:T(8,128)(2,1)}, u32[]{:S(2)}) copy-start(bf16[128,2048]{1,0:T(8,128)(2,1)} %param.14) | copy-start | bytes 1572868
  1.6 21.9 %collective-permute-start.6 = (bf16[1,2,128,256]{3,2,1,0:T(8,128)(2,1)S(1)}, bf16[1,2,128,256]{3,2,1,0:T(8,128)(2,1)S(1)}, u32[]{:S(2)}, u32[]{:S(2)}) collective-permute-start(bf16[1,2,128,256]{3,2,1,0:T(8,128)(2,1)S(1)} %maximum_bitcast_fusion), channel_id=1, source_target_pairs={{0,4},{4,8},{8,12},{12,16},{16,20},{20,24},{24,28},{28,32},{32,36}... | collective-permute-start | bytes 393224 | tf_op jit(solution)/shard_map/ppermute | solution.py:36
  10.3 34.1 %collective-permute-start = (f32[8,128,128]{2,1,0:T(8,128)S(1)}, f32[8,128,128]{2,1,0:T(8,128)}, u32[]{:S(2)}, u32[]{:S(2)}) collective-permute-start(f32[8,128,128]{2,1,0:T(8,128)S(1)} %fusion.45), channel_id=1, source_target_pairs={{0,4},{4,8},{8,12},{12,16},{16,20},{20,24},{24,28},{28,32},{32,36}... | collective-permute-start | bytes 1572872 | tf_op jit(solution)/shard_map/ppermute | solution.py:36
  14.2 14.0 %collective-permute-start.2 = (f32[8]{0:T(128)S(1)}, f32[8]{0:T(128)S(1)}, u32[]{:S(2)}, u32[]{:S(2)}) collective-permute-start(f32[8]{0:T(128)S(1)} %broadcast_select_fusion), channel_id=1, source_target_pairs={{0,4},{4,8},{8,12},{12,16},{16,20},{20,24},{24,28},{28,32},{32,36}... | collective-permute-start | bytes 104 | tf_op jit(solution)/shard_map/ppermute | solution.py:36
  23.5 16.0 %collective-permute-start.7 = (bf16[2,2,128,256]{3,2,1,0:T(8,128)(2,1)S(1)}, bf16[2,2,128,256]{3,2,1,0:T(8,128)(2,1)S(1)}, u32[]{:S(2)}, u32[]{:S(2)}) collective-permute-start(bf16[2,2,128,256]{3,2,1,0:T(8,128)(2,1)S(1)} %pad_maximum_fusion.1), channel_id=1, source_target_pairs={{0,8},{4,12},{8,16},{12,20},{16,24},{20,28},{24,32},{28,36},{32,40... | collective-permute-start | bytes 786440 | tf_op jit(solution)/shard_map/ppermute | solution.py:36
  28.2 11.2 %collective-permute-start.4 = (f32[8]{0:T(128)S(1)}, f32[8]{0:T(128)S(1)}, u32[]{:S(2)}, u32[]{:S(2)}) collective-permute-start(f32[8]{0:T(128)S(1)} %fusion.77), channel_id=1, source_target_pairs={{0,8},{4,12},{8,16},{12,20},{16,24},{20,28},{24,32},{28,36},{32,40... | collective-permute-start | bytes 104 | tf_op jit(solution)/shard_map/ppermute | solution.py:36
  39.5 30.4 %collective-permute-start.8 = (bf16[4,2,128,256]{3,2,1,0:T(8,128)(2,1)S(1)}, bf16[4,2,128,256]{3,2,1,0:T(8,128)(2,1)}, u32[]{:S(2)}, u32[]{:S(2)}) collective-permute-start(bf16[4,2,128,256]{3,2,1,0:T(8,128)(2,1)S(1)} %pad_maximum_fusion), channel_id=1, source_target_pairs={{0,16},{4,20},{8,24},{12,28},{16,32},{20,36},{24,40},{28,44},{32,4... | collective-permute-start | bytes 1572872 | tf_op jit(solution)/shard_map/ppermute | solution.py:36
  45.5 33.0 %collective-permute-start.1 = (f32[8,128,128]{2,1,0:T(8,128)S(1)}, f32[8,128,128]{2,1,0:T(8,128)}, u32[]{:S(2)}, u32[]{:S(2)}) collective-permute-start(f32[8,128,128]{2,1,0:T(8,128)S(1)} %multiply_add_fusion.2), channel_id=1, source_target_pairs={{0,8},{4,12},{8,16},{12,20},{16,24},{20,28},{24,32},{28,36},{32,40... | collective-permute-start | bytes 1572872 | tf_op jit(solution)/shard_map/ppermute | solution.py:36
  71.1 3.3 %copy-start.1 = (f32[2,512,128,8]{2,1,3,0:T(8,128)S(1)}, f32[2,512,128,8]{2,1,3,0:T(8,128)}, u32[]{:S(2)}) copy-start(f32[2,512,128,8]{2,1,3,0:T(8,128)} %get-tuple-element.36) | copy-start | bytes 12582916
  75.4 7.2 %copy-start.2 = (f32[2,512,128,8]{2,1,3,0:T(8,128)S(1)}, f32[2,512,128,8]{2,1,3,0:T(8,128)}, u32[]{:S(2)}) copy-start(f32[2,512,128,8]{2,1,3,0:T(8,128)} %get-tuple-element.36) | copy-start | bytes 12582916
  79.8 30.7 %copy-start.3 = (f32[2,512,128,8]{2,1,3,0:T(8,128)S(1)}, f32[2,512,128,8]{2,1,3,0:T(8,128)}, u32[]{:S(2)}) copy-start(f32[2,512,128,8]{2,1,3,0:T(8,128)} %get-tuple-element.38) | copy-start | bytes 12582916
  79.8 28.6 %collective-permute-start.3 = (f32[8,128,128]{2,1,0:T(8,128)S(1)}, f32[8,128,128]{2,1,0:T(8,128)S(1)}, u32[]{:S(2)}, u32[]{:S(2)}) collective-permute-start(f32[8,128,128]{2,1,0:T(8,128)S(1)} %multiply_add_fusion.1), channel_id=1, source_target_pairs={{0,16},{4,20},{8,24},{12,28},{16,32},{20,36},{24,40},{28,44},{32,4... | collective-permute-start | bytes 1572872 | tf_op jit(solution)/shard_map/ppermute | solution.py:36
  108.5 9.8 %collective-permute-start.5 = (bf16[8,128,128]{2,1,0:T(8,128)(2,1)S(1)}, bf16[8,128,128]{2,1,0:T(8,128)(2,1)S(1)}, u32[]{:S(2)}, u32[]{:S(2)}) collective-permute-start(bf16[8,128,128]{2,1,0:T(8,128)(2,1)S(1)} %multiply_add_fusion), channel_id=1, source_target_pairs={{0,4},{4,8},{8,12},{12,16},{16,20},{20,24},{24,28},{28,32},{32,36}... | collective-permute-start | bytes 786440 | tf_op jit(solution)/shard_map/ppermute | solution.py:36
  110.4 19.0 %copy-start.5 = (f32[1024]{0:T(1024)S(1)}, f32[1024]{0:T(1024)}, u32[]{:S(2)}) copy-start(f32[1024]{0:T(1024)} %param.13) | copy-start | bytes 12292

commit v2 on v0

--- a/solution.py
+++ b/solution.py
@@ -15,25 +15,48 @@
 MASK_FILL = -1e30
 
 
-def prefix(x, axis, combine, identity):
-    count, here = (lax.axis_size(axis), lax.axis_index(axis))
-    everything = jax.tree.map(lambda part: lax.all_gather(part, axis), x)
-    start = jax.tree.map(
-        lambda part, zero: jnp.broadcast_to(jnp.asarray(zero, part.dtype), part.shape), x, identity
-    )
-
-    def lap(k, before):
-        reached = k < here
-        new = combine(before, jax.tree.map(lambda part: part[k], everything))
-        return jax.tree.map(lambda a, b: jnp.where(reached, a, b), new, before)
-
-    return lax.fori_loop(0, count, lap, start)
-
-
 def from_behind(x, axis, by):
     count = lax.axis_size(axis)
     pairs = [(i, i + by) for i in range(count) if 0 <= i + by < count]
     return lax.ppermute(x, axis, pairs)
+
+
+def shift_pairs(count, by, parity=None):
+    return [
+        (i, i + by)
+        for i in range(count)
+        if 0 <= i + by < count and (parity is None or i % 2 == parity)
+    ]
+
+
+def move(x, axis, pairs):
+    return jax.tree.map(lambda part: lax.ppermute(part, axis, pairs), x)
+
+
+def state_entering(element, axis, core):
+    count = lax.axis_size(axis)
+    pair = join_states(move(element, axis, shift_pairs(count, 1, 0)), element)
+    wide = pair
+    for chips in (1, 2):
+        wide = join_states(move(wide, axis, shift_pairs(count, 2 * chips, 1)), wide)
+    before = move(wide[1], axis, shift_pairs(count, 1, 1))
+    after = (before * element[0][:, None, None] + element[1]).astype(jnp.bfloat16)
+    after = lax.ppermute(after, axis, shift_pairs(count, 1, 0))
+    return jnp.where(core == 0, before.astype(jnp.bfloat16), after)
+
+
+def kv_window(kv_pair, axis, core, width):
+    count = lax.axis_size(axis)
+    ring = [kv_pair]
+    for step in range(1, width // 2 + 1):
+        parity = 1 if step == width // 2 else None
+        ring.append(lax.ppermute(ring[-1], axis, shift_pairs(count, 2, parity)))
+    half = width // 2
+    mine = jnp.stack(ring[:half])
+    sent = jnp.where(core == 1, jnp.stack(ring[1 : half + 1]), mine)
+    swap = [(i, i ^ 1) for i in range(count)]
+    theirs = lax.ppermute(sent, axis, swap)
+    return jnp.stack([mine, theirs], axis=1).reshape((width,) + kv_pair.shape)
 
 
 def join_states(earlier, later):
@@ -107,9 +130,8 @@
     intra_part, element, reach_gain, queries = lightning_local(
         light_q, light_k, light_v, log_decay, seg_tok, prev_last
     )
-    identity = (jnp.ones_like(element[0]), jnp.zeros_like(element[1]))
-    entering = prefix(element, ("grp", "seq"), join_states, identity)
-    state_rounded = entering[1].astype(jnp.bfloat16)
+    core = position % 2
+    state_rounded = state_entering(element, ("grp", "seq"), core)
     inter_part = (
         jnp.einsum("thd,hde->the", queries, state_rounded, preferred_element_type=jnp.float32)
         * reach_gain.T[:, :, None]
@@ -121,14 +143,7 @@
     kv_pair = jnp.stack([soft_k, soft_v])
     window_len = min(WINDOW_DEV, lax.axis_size(("grp", "seq")))
 
-    def pass_on(stride, running):
-        in_flight, gathered = running
-        in_flight = from_behind(in_flight, ("grp", "seq"), 1)
-        gathered = lax.dynamic_update_index_in_dim(gathered, in_flight, stride, 0)
-        return (in_flight, gathered)
-
-    gathered = jnp.zeros((window_len,) + kv_pair.shape, kv_pair.dtype).at[0].set(kv_pair)
-    window = lax.fori_loop(1, window_len, pass_on, (kv_pair, gathered))[1]
+    window = kv_window(kv_pair, ("grp", "seq"), core, window_len)
     kv_heads = soft_k.shape[1] // HEAD_DIM
     group_size = soft_q.shape[1] // soft_k.shape[1]
     soft_queries = soft_q.reshape(tok_rows, kv_heads, group_size, HEAD_DIM)

time: 530 us -> 115 us (0.22)
  the two profiles are of different devices: /device:TPU:32 before, /device:TPU:24 now
where the time goes in v2:
time: 115 us
  waiting for transfers between devices  37.5 us (33%)
  starting transfers between devices  25.6 us (22%)
  other arithmetic  16.4 us (14%)
  local copies, waits for them, and re-layouts  12.4 us (11%)
  blocking collectives  10.5 us (9%)
  matrix products  9.63 us (8%)
  between operations  2.56 us (2%)
    ppermute x6, waiting for transfers between devices, move(): return jax.tree.map(lambda part: lax.ppermute(part, axis, pairs), x)  22.1 us
    ppermute x4, waiting for transfers between devices, kv_window(): ring.append(lax.ppermute(ring[-1], axis, shift_pairs(count, 2, parity)))  15.5 us
    psum x1, blocking collectives, body(): square_sum = lax.psum(jnp.sum(mixed * mixed, axis=1), 'head')  10.5 us
    ppermute x4, starting transfers between devices, kv_window(): ring.append(lax.ppermute(ring[-1], axis, shift_pairs(count, 2, parity)))  10.2 us
    ppermute x6, starting transfers between devices, move(): return jax.tree.map(lambda part: lax.ppermute(part, axis, pairs), x)  8.45 us
    ppermute x1, starting transfers between devices, state_entering(): after = lax.ppermute(after, axis, shift_pairs(count, 1, 0))  5.07 us
    reshape x8, local copies, waits for them, and re-layouts, token_segments(): return jnp.repeat(blocks, BLOCK)  4.98 us
    reduce_sum x2, other arithmetic, absorb(): row_mass = row_mass * shrink + jnp.sum(exponent, axis=-1)  4.09 us
  transfers between devices with their start and end apart: 12, of which 3 were waited for; matrix products, arithmetic and copies ran while one was open for 27% of the time, Pallas kernels for 0%

profile of v2, /device:TPU:24, one launch (start us, length us, event | category | flops | bytes accessed | tf_op | source)
XLA Modules:
  0.0 114.7 jit_solution(7217823393311539083)
XLA Ops:
  0.7 1.0 fusion.76
  1.6 3.8 %collective-permute-start.7 = (bf16[2,128,256]{2,1,0:T(8,128)(2,1)S(1)}, bf16[2,128,256]{2,1,0:T(8,128)(2,1)S(1)}, u32[]{:S(2)}, u32[]{:S(2)}) collective-permute-start(bf16[2,128,256]{2,1,0:T(8,128)(2,1)S(1)} %get-tuple-element.21), channel_id=1, source_target_pairs={{0,8},{4,12},{8,16},{12,20},{16,24},{20,28},{24,32},{28,36},{32,40... | collective-permute-start | bytes 393224 | tf_op jit(solution)/shard_map/ppermute | solution.py:53
  5.6 1.0 reduce_window_sum.11
  6.8 1.1 copy.45
  7.9 1.7 %fusion.79 = (s32[1]{0:T(128)}, s32[1]{0:T(128)}, s32[1]{0:T(128)}, s32[1]{0:T(128)}, s32[1]{0:T(128)}, /*index=5*/s32[1]{0:T(128)}, s32[1]{0:T(128)}, s32[1]{0:T(128)}, s32[1]{0:T(128)}, s32[1]{0:T(128)}) fusion(s32[128]{0:T(128)} %param.17, s32[]{:T(128)S(6)} %select_n.140, s32[]{:T(128)S(6)} %select_n.142, s32[]{:T(128)S(6)} %select_n.135, ...), kind=kLoop, calls=%fused_computation.110 | loop fusion | bytes 120 | tf_op jit(solution)/shard_map/dynamic_slice | solution.py:67
  11.0 1.2 %fusion.46 = f32[8,128,128]{2,1,0:T(8,128)S(1)} fusion(bf16[128,8,128]{0,2,1:T(8,128)(2,1)S(1)} %bitcast.133, f32[128,8]{0,1:T(8,128)S(1)} %get-tuple-element.25, bf16[128,1024]{1,0:T(8,128)(2,1)} %param.11), kind=kOutput, calls=%fused_computation.52 | convolution fusion | flops 33947648 | bytes 1052672 | tf_op jit(solution)/shard_map/shd,she->hde/dot_general | solution.py:91
  12.2 1.5 %collective-permute-start = (f32[8,128,128]{2,1,0:T(8,128)S(1)}, f32[8,128,128]{2,1,0:T(8,128)S(1)}, u32[]{:S(2)}, u32[]{:S(2)}) collective-permute-start(f32[8,128,128]{2,1,0:T(8,128)S(1)} %fusion.46), channel_id=1, source_target_pairs={{0,4},{8,12},{16,20},{24,28},{32,36},{40,44},{48,52},{56,60},{64,6... | collective-permute-start | bytes 1572872 | tf_op jit(solution)/shard_map/ppermute | solution.py:33
  14.2 1.8 %collective-permute-start.2 = (f32[8]{0:T(128)}, f32[8]{0:T(128)}, u32[]{:S(2)}, u32[]{:S(2)}) collective-permute-start(f32[8]{0:T(128)} %broadcast_select_fusion), channel_id=1, source_target_pairs={{0,4},{8,12},{16,20},{24,28},{32,36},{40,44},{48,52},{56,60},{64,6... | collective-permute-start | bytes 104 | tf_op jit(solution)/shard_map/ppermute | solution.py:33
  16.0 2.3 %convolution_bitcast_fusion.1 = f32[128,8,128]{0,2,1:T(8,128)} fusion(bf16[128,8,128]{0,2,1:T(8,128)(2,1)S(1)} %bitcast.134, f32[8,128]{1,0:T(8,128)S(1)} %reduce_window_sum.11, pred[128,128]{1,0:T(8,128)(4,1)S(1)} %iota_compare_fusion, bf16[128,1024]{1,0:T(8,128)(2,1)} %param.11, bf16[128,1024]{1,0:T(8,128)(2,1)S(1)} %copy-done), kind=kOutput, calls=%fused_computation.26 | convolution fusion | flops 67633152 | bytes 1331200 | tf_op jit(solution)/shard_map/hts,shd->thd/dot_general | solution.py:83
  18.3 3.8 %collective-permute-start.8 = (bf16[2,128,256]{2,1,0:T(8,128)(2,1)S(1)}, bf16[2,128,256]{2,1,0:T(8,128)(2,1)S(1)}, u32[]{:S(2)}, u32[]{:S(2)}) collective-permute-start(bf16[2,128,256]{2,1,0:T(8,128)(2,1)S(1)} %collective-permute-done.7), channel_id=1, source_target_pairs={{0,8},{4,12},{8,16},{12,20},{16,24},{20,28},{24,32},{28,36},{32,40... | collective-permute-start | bytes 393224 | tf_op jit(solution)/shard_map/ppermute | solution.py:53
  22.1 9.0 %collective-permute-done.8 = bf16[2,128,256]{2,1,0:T(8,128)(2,1)S(1)} collective-permute-done((bf16[2,128,256]{2,1,0:T(8,128)(2,1)S(1)}, bf16[2,128,256]{2,1,0:T(8,128)(2,1)S(1)}, u32[]{:S(2)}, u32[]{:S(2)}) %collective-permute-start.8) | collective-permute-done | bytes 131104 | tf_op jit(solution)/shard_map/ppermute | solution.py:53
  31.2 1.9 %collective-permute-start.9 = (bf16[2,128,256]{2,1,0:T(8,128)(2,1)S(1)}, bf16[2,128,256]{2,1,0:T(8,128)(2,1)S(1)}, u32[]{:S(2)}, u32[]{:S(2)}) collective-permute-start(bf16[2,128,256]{2,1,0:T(8,128)(2,1)S(1)} %collective-permute-done.8), channel_id=1, source_target_pairs={{0,8},{4,12},{8,16},{12,20},{16,24},{20,28},{24,32},{28,36},{32,40... | collective-permute-start | bytes 393224 | tf_op jit(solution)/shard_map/ppermute | solution.py:53
  33.7 6.4 %collective-permute-done.9 = bf16[2,128,256]{2,1,0:T(8,128)(2,1)S(1)} collective-permute-done((bf16[2,128,256]{2,1,0:T(8,128)(2,1)S(1)}, bf16[2,128,256]{2,1,0:T(8,128)(2,1)S(1)}, u32[]{:S(2)}, u32[]{:S(2)}) %collective-permute-start.9) | collective-permute-done | bytes 131104 | tf_op jit(solution)/shard_map/ppermute | solution.py:53
  45.8 1.2 %add_compare_fusion = (pred[512]{0:T(512)(128)(4,1)}, pred[512]{0:T(512)(128)(4,1)}) fusion(s32[128]{0:T(128)S(1)} %reshape.278, s32[128]{0:T(128)S(1)} %reshape.277, s32[128]{0:T(128)S(1)} %reshape.276, s32[128]{0:T(128)S(1)} %reshape.275, s32[]{:T(128)} %bitcast.3, s32[128]{0:T(128)S(1)} %reshape.283, s32[128]{0:T(128)S(1)} %reshape.282, ...), kind=kLoop, calls=%fused_computation.86 | loop fusion | flops 4096 | bytes 5124 | tf_op jit(solution)/shard_map/eq | solution.py:177
  47.2 1.9 %collective-permute-start.11 = (bf16[4,2,128,256]{3,2,1,0:T(8,128)(2,1)S(1)}, bf16[4,2,128,256]{3,2,1,0:T(8,128)(2,1)}, u32[]{:S(2)}, u32[]{:S(2)}) collective-permute-start(bf16[4,2,128,256]{3,2,1,0:T(8,128)(2,1)S(1)} %get-tuple-element.18), channel_id=1, source_target_pairs={{0,4},{4,0},{8,12},{12,8},{16,20},{20,16},{24,28},{28,24},{32,36},... | collective-permute-start | bytes 1572872 | tf_op jit(solution)/shard_map/ppermute | solution.py:58
  49.1 1.5 %and_and_fusion = (pred[128,512]{0,1:T(8,128)(4,1)S(1)}, pred[128,512]{0,1:T(8,128)(4,1)S(1)}) fusion(s32[128]{0:T(128)S(1)} %get-tuple-element.54, s32[512]{0:T(512)S(1)} %get-tuple-element.9, pred[512]{0:T(512)(128)(4,1)} %get-tuple-element.46, pred[512]{0:T(512)(128)(4,1)S(1)} %get-tuple-element.8, pred[512]{0:T(512)(128)(4,1)} %get-tuple-element.45, ...), kind=kLoop, calls=%fused_computation.67 | loop fusion | flops 393216 | bytes 137728 | tf_op jit(solution)/shard_map/and | solution.py:175
  52.9 1.5 %collective-permute-start.1 = (f32[8,128,128]{2,1,0:T(8,128)S(1)}, f32[8,128,128]{2,1,0:T(8,128)}, u32[]{:S(2)}, u32[]{:S(2)}) collective-permute-start(f32[8,128,128]{2,1,0:T(8,128)S(1)} %multiply_add_fusion.2), channel_id=1, source_target_pairs={{4,12},{12,20},{20,28},{28,36},{36,44},{44,52},{52,60},{60,68},{68... | collective-permute-start | bytes 1572872 | tf_op jit(solution)/shard_map/ppermute | solution.py:33
  54.4 1.1 pad_maximum_fusion
  56.4 1.2 %multiply_add_fusion.1 = f32[8,128,128]{2,1,0:T(8,128)S(1)} fusion(f32[8,128,128]{2,1,0:T(8,128)S(1)} %multiply_add_fusion.2, f32[8,128,128]{2,1,0:T(8,128)} %collective-permute-done.1, f32[8]{0:T(128)S(1)} %fusion.81), kind=kLoop, calls=%fused_computation.42 | loop fusion | flops 262144 | bytes 1572896 | tf_op jit(solution)/shard_map/add | solution.py:63
  57.6 1.5 %collective-permute-start.3 = (f32[8,128,128]{2,1,0:T(8,128)S(1)}, f32[8,128,128]{2,1,0:T(8,128)}, u32[]{:S(2)}, u32[]{:S(2)}) collective-permute-start(f32[8,128,128]{2,1,0:T(8,128)S(1)} %multiply_add_fusion.1), channel_id=1, source_target_pairs={{4,20},{12,28},{20,36},{28,44},{36,52},{44,60},{52,68},{60,76},{68... | collective-permute-start | bytes 1572872 | tf_op jit(solution)/shard_map/ppermute | solution.py:33
  59.1 2.7 %fusion.5 = (f32[128,2,8]{0,2,1:T(8,128)S(1)}, f32[2,512,128,8]{2,1,3,0:T(8,128)}) fusion(pred[128,512]{0,1:T(8,128)(4,1)S(1)} %get-tuple-element.27, bf16[128,2,8,128]{3,2,1,0:T(8,128)(2,1)S(1)} %bitcast.126, bf16[512,2,128,1]{2,1,0,3:T(2,128)(2,1)S(1)} %bitcast.131), kind=kOutput, calls=%fused_computation.9 | convolution fusion | flops 271579136 | bytes 5054464 | tf_op jit(solution)/shard_map/tkgd,skd->tkgs/dot_general | solution.py:103
  62.6 2.0 %copy-done.2 = f32[2,512,128,8]{2,1,3,0:T(8,128)} copy-done((f32[2,512,128,8]{2,1,3,0:T(8,128)}, f32[2,512,128,8]{2,1,3,0:T(8,128)S(1)}, u32[]{:S(2)}) %copy-start.2) | copy-done | bytes 4194328
  64.6 0.9 fusion
  65.6 3.2 %fusion.2 = f32[128,2,8]{0,2,1:T(8,128)S(1)} fusion(f32[2,512,128,8]{2,1,3,0:T(8,128)} %get-tuple-element.44, f32[128,2,8]{0,2,1:T(8,128)S(1)} %get-tuple-element.23, pred[128,512]{0,1:T(8,128)(4,1)S(1)} %get-tuple-element.27), kind=kLoop, calls=%fused_computation.6 | loop fusion | flops 4192256 | bytes 4276224 | tf_op jit(solution)/shard_map/reduce_sum | solution.py:110
  68.8 1.2 %multiply_add_fusion = f32[8,128,128]{2,1,0:T(8,128)S(1)} fusion(f32[8,128,128]{2,1,0:T(8,128)S(1)} %multiply_add_fusion.1, f32[8,128,128]{2,1,0:T(8,128)} %collective-permute-done.3, f32[8]{0:T(128)S(1)} %mul.169), kind=kLoop, calls=%fused_computation.41 | loop fusion | flops 262144 | bytes 1572896 | tf_op jit(solution)/shard_map/add | solution.py:63
  70.0 1.6 %collective-permute-start.5 = (f32[8,128,128]{2,1,0:T(8,128)S(1)}, f32[8,128,128]{2,1,0:T(8,128)S(1)}, u32[]{:S(2)}, u32[]{:S(2)}) collective-permute-start(f32[8,128,128]{2,1,0:T(8,128)S(1)} %multiply_add_fusion), channel_id=1, source_target_pairs={{4,8},{12,16},{20,24},{28,32},{36,40},{44,48},{52,56},{60,64},{68,... | collective-permute-start | bytes 1572872 | tf_op jit(solution)/shard_map/ppermute | solution.py:33
  71.6 1.1 fusion.30
  72.8 22.1 %collective-permute-done.5 = f32[8,128,128]{2,1,0:T(8,128)S(1)} collective-permute-done((f32[8,128,128]{2,1,0:T(8,128)S(1)}, f32[8,128,128]{2,1,0:T(8,128)S(1)}, u32[]{:S(2)}, u32[]{:S(2)}) %collective-permute-start.5) | collective-permute-done | bytes 524320 | tf_op jit(solution)/shard_map/ppermute | solution.py:33
  95.5 5.1 %collective-permute-start.6 = (bf16[8,128,128]{2,1,0:T(8,128)(2,1)S(1)}, bf16[8,128,128]{2,1,0:T(8,128)(2,1)S(1)}, u32[]{:S(2)}, u32[]{:S(2)}) collective-permute-start(bf16[8,128,128]{2,1,0:T(8,128)(2,1)S(1)} %add_convert_fusion), channel_id=1, source_target_pairs={{0,4},{8,12},{16,20},{24,28},{32,36},{40,44},{48,52},{56,60},{64,6... | collective-permute-start | bytes 786440 | tf_op jit(solution)/shard_map/ppermute | solution.py:44
  100.6 1.1 %divide_convert_fusion = bf16[128,2,8,128]{0,3,2,1:T(8,128)(2,1)S(1)} fusion(f32[128,2,8,128]{0,3,2,1:T(8,128)S(1)} %fusion.30, f32[2,512,128,8]{2,1,3,0:T(8,128)S(1)} %copy-done.1, f32[128,2,8]{0,2,1:T(8,128)S(1)} %get-tuple-element.23, pred[128,512]{0,1:T(8,128)(4,1)S(1)} %get-tuple-element.27, f32[128,2,8]{0,2,1:T(8,128)S(1)} %get-tuple-element.6, ...), kind=kOutput, calls=%fused_computation.33 | convolution fusion | flops 273416192 | bytes 6111232 | tf_op jit(solution)/shard_map/tkgs,skd->tkgd/dot_general | solution.py:111
  101.8 1.0 copy.37
  103.4 10.5 %psum.7 = f32[128]{0:T(128)S(1)} all-reduce(f32[128]{0:T(128)S(1)} %get-tuple-element.39), channel_id=1, replica_groups=mesh['grp'=4,'seq'=32,'head'=4] {'head'}, use_global_device_ids=true, to_apply=%region_2.3 | all-reduce | flops 128 | bytes 1024 | tf_op jit(solution)/shard_map/psum | solution.py:140
  (65 shorter events, 13.3 us)
Async XLA Ops:
  0.6 15.4 %copy-start = (bf16[128,1024]{1,0:T(8,128)(2,1)S(1)}, bf16[128,1024]{1,0:T(8,128)(2,1)}, u32[]{:S(2)}) copy-start(bf16[128,1024]{1,0:T(8,128)(2,1)} %param.9) | copy-start | bytes 786436
  0.6 50.0 %copy-start.5 = (bf16[128,2048]{1,0:T(8,128)(2,1)S(1)}, bf16[128,2048]{1,0:T(8,128)(2,1)}, u32[]{:S(2)}) copy-start(bf16[128,2048]{1,0:T(8,128)(2,1)} %param.14) | copy-start | bytes 1572868
  1.6 16.7 %collective-permute-start.7 = (bf16[2,128,256]{2,1,0:T(8,128)(2,1)S(1)}, bf16[2,128,256]{2,1,0:T(8,128)(2,1)S(1)}, u32[]{:S(2)}, u32[]{:S(2)}) collective-permute-start(bf16[2,128,256]{2,1,0:T(8,128)(2,1)S(1)} %get-tuple-element.21), channel_id=1, source_target_pairs={{0,8},{4,12},{8,16},{12,20},{16,24},{20,28},{24,32},{28,36},{32,40... | collective-permute-start | bytes 393224 | tf_op jit(solution)/shard_map/ppermute | solution.py:53
  6.8 7.4 %copy-start.7 = (f32[8]{0:T(128)}, f32[8]{0:T(128)S(1)}, u32[]{:S(2)}) copy-start(f32[8]{0:T(128)S(1)} %slice_reduce_fusion) | copy-start | bytes 100
  12.2 40.0 %collective-permute-start = (f32[8,128,128]{2,1,0:T(8,128)S(1)}, f32[8,128,128]{2,1,0:T(8,128)S(1)}, u32[]{:S(2)}, u32[]{:S(2)}) collective-permute-start(f32[8,128,128]{2,1,0:T(8,128)S(1)} %fusion.46), channel_id=1, source_target_pairs={{0,4},{8,12},{16,20},{24,28},{32,36},{40,44},{48,52},{56,60},{64,6... | collective-permute-start | bytes 1572872 | tf_op jit(solution)/shard_map/ppermute | solution.py:33
  14.2 36.6 %collective-permute-start.2 = (f32[8]{0:T(128)}, f32[8]{0:T(128)}, u32[]{:S(2)}, u32[]{:S(2)}) collective-permute-start(f32[8]{0:T(128)} %broadcast_select_fusion), channel_id=1, source_target_pairs={{0,4},{8,12},{16,20},{24,28},{32,36},{40,44},{48,52},{56,60},{64,6... | collective-permute-start | bytes 104 | tf_op jit(solution)/shard_map/ppermute | solution.py:33
  18.3 12.9 %collective-permute-start.8 = (bf16[2,128,256]{2,1,0:T(8,128)(2,1)S(1)}, bf16[2,128,256]{2,1,0:T(8,128)(2,1)S(1)}, u32[]{:S(2)}, u32[]{:S(2)}) collective-permute-start(bf16[2,128,256]{2,1,0:T(8,128)(2,1)S(1)} %collective-permute-done.7), channel_id=1, source_target_pairs={{0,8},{4,12},{8,16},{12,20},{16,24},{20,28},{24,32},{28,36},{32,40... | collective-permute-start | bytes 393224 | tf_op jit(solution)/shard_map/ppermute | solution.py:53
  31.2 9.0 %collective-permute-start.9 = (bf16[2,128,256]{2,1,0:T(8,128)(2,1)S(1)}, bf16[2,128,256]{2,1,0:T(8,128)(2,1)S(1)}, u32[]{:S(2)}, u32[]{:S(2)}) collective-permute-start(bf16[2,128,256]{2,1,0:T(8,128)(2,1)S(1)} %collective-permute-done.8), channel_id=1, source_target_pairs={{0,8},{4,12},{8,16},{12,20},{16,24},{20,28},{24,32},{28,36},{32,40... | collective-permute-start | bytes 393224 | tf_op jit(solution)/shard_map/ppermute | solution.py:53
  40.1 6.9 %collective-permute-start.10 = (bf16[2,128,256]{2,1,0:T(8,128)(2,1)S(1)}, bf16[2,128,256]{2,1,0:T(8,128)(2,1)S(1)}, u32[]{:S(2)}, u32[]{:S(2)}) collective-permute-start(bf16[2,128,256]{2,1,0:T(8,128)(2,1)S(1)} %collective-permute-done.9), channel_id=1, source_target_pairs={{4,12},{12,20},{20,28},{28,36},{36,44},{44,52},{52,60},{60,68},{68... | collective-permute-start | bytes 393224 | tf_op jit(solution)/shard_map/ppermute | solution.py:53
  47.2 7.2 %collective-permute-start.11 = (bf16[4,2,128,256]{3,2,1,0:T(8,128)(2,1)S(1)}, bf16[4,2,128,256]{3,2,1,0:T(8,128)(2,1)}, u32[]{:S(2)}, u32[]{:S(2)}) collective-permute-start(bf16[4,2,128,256]{3,2,1,0:T(8,128)(2,1)S(1)} %get-tuple-element.18), channel_id=1, source_target_pairs={{0,4},{4,0},{8,12},{12,8},{16,20},{20,16},{24,28},{28,24},{32,36},... | collective-permute-start | bytes 1572872 | tf_op jit(solution)/shard_map/ppermute | solution.py:58
  51.5 0.7 collective-permute-start.4
  52.9 3.5 %collective-permute-start.1 = (f32[8,128,128]{2,1,0:T(8,128)S(1)}, f32[8,128,128]{2,1,0:T(8,128)}, u32[]{:S(2)}, u32[]{:S(2)}) collective-permute-start(f32[8,128,128]{2,1,0:T(8,128)S(1)} %multiply_add_fusion.2), channel_id=1, source_target_pairs={{4,12},{12,20},{20,28},{28,36},{36,44},{44,52},{52,60},{60,68},{68... | collective-permute-start | bytes 1572872 | tf_op jit(solution)/shard_map/ppermute | solution.py:33
  57.6 11.3 %collective-permute-start.3 = (f32[8,128,128]{2,1,0:T(8,128)S(1)}, f32[8,128,128]{2,1,0:T(8,128)}, u32[]{:S(2)}, u32[]{:S(2)}) collective-permute-start(f32[8,128,128]{2,1,0:T(8,128)S(1)} %multiply_add_fusion.1), channel_id=1, source_target_pairs={{4,20},{12,28},{20,36},{28,44},{36,52},{44,60},{52,68},{60,76},{68... | collective-permute-start | bytes 1572872 | tf_op jit(solution)/shard_map/ppermute | solution.py:33
  61.8 3.7 %copy-start.4 = (bf16[4,1,128,256]{3,2,1,0:T(8,128)(2,1)S(1)}, bf16[4,1,128,256]{3,2,1,0:T(8,128)(2,1)}, u32[]{:S(2)}) copy-start(bf16[4,1,128,256]{3,2,1,0:T(8,128)(2,1)} %get-tuple-element.16) | copy-start | bytes 786436
  62.6 2.0 %copy-start.2 = (f32[2,512,128,8]{2,1,3,0:T(8,128)}, f32[2,512,128,8]{2,1,3,0:T(8,128)S(1)}, u32[]{:S(2)}) copy-start(f32[2,512,128,8]{2,1,3,0:T(8,128)S(1)} %get-tuple-element.42) | copy-start | bytes 12582916
  65.6 6.0 %copy-start.3 = (f32[2,512,128,8]{2,1,3,0:T(8,128)S(1)}, f32[2,512,128,8]{2,1,3,0:T(8,128)}, u32[]{:S(2)}) copy-start(f32[2,512,128,8]{2,1,3,0:T(8,128)} %copy-done.2) | copy-start | bytes 12582916
  70.0 30.6 %copy-start.1 = (f32[2,512,128,8]{2,1,3,0:T(8,128)S(1)}, f32[2,512,128,8]{2,1,3,0:T(8,128)}, u32[]{:S(2)}) copy-start(f32[2,512,128,8]{2,1,3,0:T(8,128)} %get-tuple-element.44) | copy-start | bytes 12582916
  70.0 24.8 %collective-permute-start.5 = (f32[8,128,128]{2,1,0:T(8,128)S(1)}, f32[8,128,128]{2,1,0:T(8,128)S(1)}, u32[]{:S(2)}, u32[]{:S(2)}) collective-permute-start(f32[8,128,128]{2,1,0:T(8,128)S(1)} %multiply_add_fusion), channel_id=1, source_target_pairs={{4,8},{12,16},{20,24},{28,32},{36,40},{44,48},{52,56},{60,64},{68,... | collective-permute-start | bytes 1572872 | tf_op jit(solution)/shard_map/ppermute | solution.py:33
  95.5 7.3 %collective-permute-start.6 = (bf16[8,128,128]{2,1,0:T(8,128)(2,1)S(1)}, bf16[8,128,128]{2,1,0:T(8,128)(2,1)S(1)}, u32[]{:S(2)}, u32[]{:S(2)}) collective-permute-start(bf16[8,128,128]{2,1,0:T(8,128)(2,1)S(1)} %add_convert_fusion), channel_id=1, source_target_pairs={{0,4},{8,12},{16,20},{24,28},{32,36},{40,44},{48,52},{56,60},{64,6... | collective-permute-start | bytes 786440 | tf_op jit(solution)/shard_map/ppermute | solution.py:44
  100.6 2.2 %copy-start.6 = (f32[128,8,128]{0,2,1:T(8,128)S(1)}, f32[128,8,128]{0,2,1:T(8,128)}, u32[]{:S(2)}) copy-start(f32[128,8,128]{0,2,1:T(8,128)} %convolution_bitcast_fusion.1) | copy-start | bytes 1572868
  101.8 12.1 %copy-start.8 = (f32[1024]{0:T(1024)S(1)}, f32[1024]{0:T(1024)}, u32[]{:S(2)}) copy-start(f32[1024]{0:T(1024)} %param.13) | copy-start | bytes 12292

commit v3 on v2

--- a/solution.py
+++ b/solution.py
@@ -13,12 +13,6 @@
 
 NEG_FLOOR = -10000.0
 MASK_FILL = -1e30
-
-
-def from_behind(x, axis, by):
-    count = lax.axis_size(axis)
-    pairs = [(i, i + by) for i in range(count) if 0 <= i + by < count]
-    return lax.ppermute(x, axis, pairs)
 
 
 def shift_pairs(count, by, parity=None):
@@ -33,30 +27,36 @@
     return jax.tree.map(lambda part: lax.ppermute(part, axis, pairs), x)
 
 
-def state_entering(element, axis, core):
+def exchange(element, kv_pair, axis, core, width):
     count = lax.axis_size(axis)
-    pair = join_states(move(element, axis, shift_pairs(count, 1, 0)), element)
-    wide = pair
-    for chips in (1, 2):
-        wide = join_states(move(wide, axis, shift_pairs(count, 2 * chips, 1)), wide)
-    before = move(wide[1], axis, shift_pairs(count, 1, 1))
+    half = width // 2
+    ring = [kv_pair]
+
+    def ring_step(parity=None):
+        return lax.ppermute(ring[-1], axis, shift_pairs(count, 2, parity))
+
+    got = move(element, axis, shift_pairs(count, 1, 0))
+    got, kv_next = lax.optimization_barrier((got, ring_step()))
+    ring.append(kv_next)
+    wide = join_states(got, element)
+    got = move(wide, axis, shift_pairs(count, 2, 1))
+    got, kv_next = lax.optimization_barrier((got, ring_step()))
+    ring.append(kv_next)
+    wide = join_states(got, wide)
+    got = lax.ppermute(wide[1], axis, shift_pairs(count, 4, 1))
+    got, kv_next = lax.optimization_barrier((got, ring_step()))
+    ring.append(kv_next)
+    wide_state = got * wide[0][:, None, None] + wide[1]
+    before = lax.ppermute(wide_state, axis, shift_pairs(count, 1, 1))
+    before, kv_next = lax.optimization_barrier((before, ring_step(1)))
+    ring.append(kv_next)
     after = (before * element[0][:, None, None] + element[1]).astype(jnp.bfloat16)
     after = lax.ppermute(after, axis, shift_pairs(count, 1, 0))
-    return jnp.where(core == 0, before.astype(jnp.bfloat16), after)
-
-
-def kv_window(kv_pair, axis, core, width):
-    count = lax.axis_size(axis)
-    ring = [kv_pair]
-    for step in range(1, width // 2 + 1):
-        parity = 1 if step == width // 2 else None
-        ring.append(lax.ppermute(ring[-1], axis, shift_pairs(count, 2, parity)))
-    half = width // 2
     mine = jnp.stack(ring[:half])
     sent = jnp.where(core == 1, jnp.stack(ring[1 : half + 1]), mine)
-    swap = [(i, i ^ 1) for i in range(count)]
-    theirs = lax.ppermute(sent, axis, swap)
-    return jnp.stack([mine, theirs], axis=1).reshape((width,) + kv_pair.shape)
+    theirs = lax.ppermute(sent, axis, [(i, i ^ 1) for i in range(count)])
+    state = jnp.where(core == 0, before.astype(jnp.bfloat16), after)
+    return state, mine, theirs
 
 
 def join_states(earlier, later):
@@ -131,7 +131,10 @@
         light_q, light_k, light_v, log_decay, seg_tok, prev_last
     )
     core = position % 2
-    state_rounded = state_entering(element, ("grp", "seq"), core)
+    window_len = WINDOW_DEV
+    state_rounded, mine, theirs = exchange(
+        element, jnp.stack([soft_k, soft_v]), ("grp", "seq"), core, window_len
+    )
     inter_part = (
         jnp.einsum("thd,hde->the", queries, state_rounded, preferred_element_type=jnp.float32)
         * reach_gain.T[:, :, None]
@@ -140,23 +143,16 @@
     square_sum = lax.psum(jnp.sum(mixed * mixed, axis=1), "head")
     inv_norm = lax.rsqrt(square_sum / (LIGHTNING_HEADS * HEAD_DIM) + 1e-06)
     light_out = (mixed * inv_norm[:, None] * light_gain).astype(jnp.bfloat16)
-    kv_pair = jnp.stack([soft_k, soft_v])
-    window_len = min(WINDOW_DEV, lax.axis_size(("grp", "seq")))
-
-    window = kv_window(kv_pair, ("grp", "seq"), core, window_len)
     kv_heads = soft_k.shape[1] // HEAD_DIM
     group_size = soft_q.shape[1] // soft_k.shape[1]
     soft_queries = soft_q.reshape(tok_rows, kv_heads, group_size, HEAD_DIM)
     query_pos = row_start + jnp.arange(tok_rows, dtype=jnp.int32)
-    slots_per = max(1, 512 // tok_rows)
     running = (
         jnp.full((tok_rows, kv_heads, group_size), MASK_FILL, jnp.float32),
         jnp.zeros((tok_rows, kv_heads, group_size), jnp.float32),
         jnp.zeros((tok_rows, kv_heads, group_size, HEAD_DIM), jnp.float32),
     )
-    for first_slot in range(0, window_len, slots_per):
-        slot_list = list(range(first_slot, min(first_slot + slots_per, window_len)))
-        chosen = window[first_slot : first_slot + len(slot_list)]
+    for slot_list, chosen in ((range(0, window_len, 2), mine), (range(1, window_len, 2), theirs)):
         key_rows = chosen[:, 0].reshape(-1, kv_heads, HEAD_DIM)
         value_rows = chosen[:, 1].reshape(-1, kv_heads, HEAD_DIM)
         key_pos = jnp.concatenate(

time: 115 us -> 107 us (0.930)
  waiting for transfers between devices: 37.5 us -> 29.9 us
  other arithmetic: 16.4 us -> 12.9 us
  starting transfers between devices: 25.6 us -> 28.2 us
    ppermute x6 -> x4, waiting for transfers between devices: 22.1 us -> 0.81 us  [move(): return jax.tree.map(lambda part: lax.ppermute(part, axis, pairs), x)]
    ppermute x6 -> x8, waiting for transfers between devices: 15.5 us -> 29.1 us  [the longest x4 23.4 us: ring_step(): return lax.ppermute(ring[-1], axis, shift_pairs(count, 2, parity))]
    ppermute x6 -> x8, starting transfers between devices: 17.2 us -> 23.8 us  [the longest x1 11.5 us: exchange(): after = lax.ppermute(after, axis, shift_pairs(count, 1, 0))]
    ppermute x6 -> x4, starting transfers between devices: 8.45 us -> 4.41 us  [move(): return jax.tree.map(lambda part: lax.ppermute(part, axis, pairs), x)]
    add x3 -> x2, other arithmetic: 3.01 us -> 0.23 us  [join_states(): earlier[1] * later[0][:, None, None] + later[1]]
    reduce_sum x2, other arithmetic: 4.09 us -> 1.77 us  [absorb(): row_mass = row_mass * shrink + jnp.sum(exponent, axis=-1)]
    select_n x1, other arithmetic: 0.13 us -> 1.34 us  [exchange(): sent = jnp.where(core == 1, jnp.stack(ring[1:half + 1]), mine)]
    another operation x2 -> x1, other arithmetic: 2.08 us -> 0.89 us  [exchange(): mine = jnp.stack(ring[:half])]
  transfers between devices with their start and end apart: 12 -> 12, of which waited for: 3 -> 5; matrix products, arithmetic and copies ran while one was open for 27% -> 19% of each run, Pallas kernels for 0% -> 0%
where the time goes in v3:
time: 107 us
  waiting for transfers between devices  29.9 us (28%)
  starting transfers between devices  28.2 us (26%)
  other arithmetic  12.9 us (12%)
  local copies, waits for them, and re-layouts  12.1 us (11%)
  blocking collectives  10.5 us (10%)
  matrix products  10.4 us (10%)
  between operations  2.57 us (2%)
    ppermute x4, waiting for transfers between devices, ring_step(): return lax.ppermute(ring[-1], axis, shift_pairs(count, 2, parity))  23.4 us
    ppermute x1, starting transfers between devices, exchange(): after = lax.ppermute(after, axis, shift_pairs(count, 1, 0))  11.5 us
    psum x1, blocking collectives, body(): square_sum = lax.psum(jnp.sum(mixed * mixed, axis=1), 'head')  10.5 us
    ppermute x4, starting transfers between devices, ring_step(): return lax.ppermute(ring[-1], axis, shift_pairs(count, 2, parity))  8.31 us
    ppermute x1, waiting for transfers between devices, exchange(): before = lax.ppermute(wide_state, axis, shift_pairs(count, 1, 1))  5.61 us
    reshape x8, local copies, waits for them, and re-layouts, token_segments(): return jnp.repeat(blocks, BLOCK)  4.95 us
    ppermute x4, starting transfers between devices, move(): return jax.tree.map(lambda part: lax.ppermute(part, axis, pairs), x)  4.41 us
    dot_general x2, matrix products, absorb(): jnp.einsum('tkgd,skd->tkgs', queries, key_rows, preferred_element_type=jn...  3.53 us
  transfers between devices with their start and end apart: 12, of which 5 were waited for; matrix products, arithmetic and copies ran while one was open for 19% of the time, Pallas kernels for 0%

profile of v3, /device:TPU:24, one launch (start us, length us, event | category | flops | bytes accessed | tf_op | source)
XLA Modules:
  0.0 106.5 jit_solution(5154731823528611705)
XLA Ops:
  0.8 1.0 reduce_window_sum.11
  2.0 1.1 %copy.46 = bf16[128,1024]{0,1:T(8,128)(2,1)S(1)} copy(bf16[128,1024]{1,0:T(8,128)(2,1)} %param.10) | data formatting | bytes 524288 | tf_op jit(solution)/shard_map/reshape | solution.py:75
  3.2 1.7 %fusion.77 = (s32[1]{0:T(128)}, s32[1]{0:T(128)}, s32[1]{0:T(128)}, s32[1]{0:T(128)}, s32[1]{0:T(128)}, /*index=5*/s32[1]{0:T(128)}, s32[1]{0:T(128)}, s32[1]{0:T(128)}, s32[1]{0:T(128)}, s32[1]{0:T(128)}) fusion(s32[128]{0:T(128)} %param.17, s32[]{:T(128)S(6)} %select_n.138, s32[]{:T(128)S(6)} %select_n.140, s32[]{:T(128)S(6)} %select_n.135, ...), kind=kLoop, calls=%fused_computation.105 | loop fusion | bytes 120 | tf_op jit(solution)/shard_map/dynamic_slice | solution.py:67
  6.3 1.2 %fusion.45 = f32[8,128,128]{2,1,0:T(8,128)S(1)} fusion(bf16[128,8,128]{0,2,1:T(8,128)(2,1)S(1)} %bitcast.124, f32[128,8]{0,1:T(8,128)S(1)} %get-tuple-element.43, bf16[128,1024]{1,0:T(8,128)(2,1)} %param.11), kind=kOutput, calls=%fused_computation.48 | convolution fusion | flops 33947648 | bytes 1052672 | tf_op jit(solution)/shard_map/shd,she->hde/dot_general | solution.py:91
  7.5 1.8 %collective-permute-start.1 = (f32[8,128,128]{2,1,0:T(8,128)S(1)}, f32[8,128,128]{2,1,0:T(8,128)S(1)}, u32[]{:S(2)}, u32[]{:S(2)}) collective-permute-start(f32[8,128,128]{2,1,0:T(8,128)S(1)} %fusion.45), channel_id=1, source_target_pairs={{0,4},{8,12},{16,20},{24,28},{32,36},{40,44},{48,52},{56,60},{64,6... | collective-permute-start | bytes 1572872 | tf_op jit(solution)/shard_map/ppermute | solution.py:27
  9.2 0.9 fusion.74
  10.1 3.8 %collective-permute-start.2 = (bf16[2,128,256]{2,1,0:T(8,128)(2,1)S(1)}, bf16[2,128,256]{2,1,0:T(8,128)(2,1)S(1)}, u32[]{:S(2)}, u32[]{:S(2)}) collective-permute-start(bf16[2,128,256]{2,1,0:T(8,128)(2,1)S(1)} %get-tuple-element.39), channel_id=1, source_target_pairs={{0,8},{4,12},{8,16},{12,20},{16,24},{20,28},{24,32},{28,36},{32,40... | collective-permute-start | bytes 393224 | tf_op jit(solution)/shard_map/ppermute | solution.py:36
  14.0 1.3 %collective-permute-start = (f32[8]{0:T(128)S(1)}, f32[8]{0:T(128)S(1)}, u32[]{:S(2)}, u32[]{:S(2)}) collective-permute-start(f32[8]{0:T(128)S(1)} %broadcast_select_fusion), channel_id=1, source_target_pairs={{0,4},{8,12},{16,20},{24,28},{32,36},{40,44},{48,52},{56,60},{64,6... | collective-permute-start | bytes 104 | tf_op jit(solution)/shard_map/ppermute | solution.py:27
  15.3 0.8 collective-permute-done
  16.1 8.6 %collective-permute-done.2 = bf16[2,128,256]{2,1,0:T(8,128)(2,1)S(1)} collective-permute-done((bf16[2,128,256]{2,1,0:T(8,128)(2,1)S(1)}, bf16[2,128,256]{2,1,0:T(8,128)(2,1)S(1)}, u32[]{:S(2)}, u32[]{:S(2)}) %collective-permute-start.2) | collective-permute-done | bytes 131104 | tf_op jit(solution)/shard_map/ppermute | solution.py:36
  26.3 1.9 %collective-permute-start.5 = (bf16[2,128,256]{2,1,0:T(8,128)(2,1)}, bf16[2,128,256]{2,1,0:T(8,128)(2,1)S(1)}, u32[]{:S(2)}, u32[]{:S(2)}) collective-permute-start(bf16[2,128,256]{2,1,0:T(8,128)(2,1)} %copy-done.5), channel_id=1, source_target_pairs={{0,8},{4,12},{8,16},{12,20},{16,24},{20,28},{24,32},{28,36},{32,40... | collective-permute-start | bytes 393224 | tf_op jit(solution)/shard_map/ppermute | solution.py:36
  29.5 7.3 %collective-permute-done.5 = bf16[2,128,256]{2,1,0:T(8,128)(2,1)S(1)} collective-permute-done((bf16[2,128,256]{2,1,0:T(8,128)(2,1)}, bf16[2,128,256]{2,1,0:T(8,128)(2,1)S(1)}, u32[]{:S(2)}, u32[]{:S(2)}) %collective-permute-start.5) | collective-permute-done | bytes 131104 | tf_op jit(solution)/shard_map/ppermute | solution.py:36
  38.2 1.9 %collective-permute-start.7 = (bf16[2,128,256]{2,1,0:T(8,128)(2,1)S(1)}, bf16[2,128,256]{2,1,0:T(8,128)(2,1)S(1)}, u32[]{:S(2)}, u32[]{:S(2)}) collective-permute-start(bf16[2,128,256]{2,1,0:T(8,128)(2,1)S(1)} %collective-permute-done.5), channel_id=1, source_target_pairs={{0,8},{4,12},{8,16},{12,20},{16,24},{20,28},{24,32},{28,36},{32,40... | collective-permute-start | bytes 393224 | tf_op jit(solution)/shard_map/ppermute | solution.py:36
  41.3 7.5 %collective-permute-done.7 = bf16[2,128,256]{2,1,0:T(8,128)(2,1)S(1)} collective-permute-done((bf16[2,128,256]{2,1,0:T(8,128)(2,1)S(1)}, bf16[2,128,256]{2,1,0:T(8,128)(2,1)S(1)}, u32[]{:S(2)}, u32[]{:S(2)}) %collective-permute-start.7) | collective-permute-done | bytes 131104 | tf_op jit(solution)/shard_map/ppermute | solution.py:36
  49.6 1.3 %collective-permute-start.8 = (f32[8,128,128]{2,1,0:T(8,128)S(1)}, f32[8,128,128]{2,1,0:T(8,128)S(1)}, u32[]{:S(2)}, u32[]{:S(2)}) collective-permute-start(f32[8,128,128]{2,1,0:T(8,128)S(1)} %multiply_add_fusion), channel_id=1, source_target_pairs={{4,8},{12,16},{20,24},{28,32},{36,40},{44,48},{52,56},{60,64},{68,... | collective-permute-start | bytes 1572872 | tf_op jit(solution)/shard_map/ppermute | solution.py:50
  55.9 1.2 %add_compare_fusion = (pred[512]{0:T(512)(128)(4,1)}, pred[512]{0:T(512)(128)(4,1)}) fusion(s32[128]{0:T(128)S(1)} %reshape.275, s32[128]{0:T(128)S(1)} %reshape.274, s32[128]{0:T(128)S(1)} %reshape.273, s32[128]{0:T(128)S(1)} %reshape.272, s32[]{:T(128)} %bitcast.2, s32[128]{0:T(128)S(1)} %reshape.280, s32[128]{0:T(128)S(1)} %reshape.279, ...), kind=kLoop, calls=%fused_computation.81 | loop fusion | flops 4096 | bytes 5124 | tf_op jit(solution)/shard_map/eq | solution.py:173
  57.3 2.0 %convolution_bitcast_fusion.1 = f32[128,8,128]{0,2,1:T(8,128)} fusion(bf16[128,8,128]{0,2,1:T(8,128)(2,1)S(1)} %bitcast.125, f32[8,128]{1,0:T(8,128)S(1)} %reduce_window_sum.11, pred[128,128]{1,0:T(8,128)(4,1)} %iota_compare_fusion, bf16[128,1024]{1,0:T(8,128)(2,1)S(1)} %copy-done.4, bf16[128,1024]{1,0:T(8,128)(2,1)S(1)} %copy-done), kind=kOutput, calls=%fused_computation.26 | convolution fusion | flops 67633152 | bytes 1331200 | tf_op jit(solution)/shard_map/hts,shd->thd/dot_general | solution.py:83
  59.9 1.5 %and_and_fusion = (pred[128,512]{0,1:T(8,128)(4,1)S(1)}, pred[128,512]{0,1:T(8,128)(4,1)S(1)}) fusion(s32[128]{0:T(128)} %copy-done.8, s32[512]{0:T(512)S(1)} %get-tuple-element.29, pred[512]{0:T(512)(128)(4,1)} %get-tuple-element.64, pred[512]{0:T(512)(128)(4,1)} %get-tuple-element.28, pred[512]{0:T(512)(128)(4,1)} %get-tuple-element.63, ...), kind=kLoop, calls=%fused_computation.63 | loop fusion | flops 393216 | bytes 137728 | tf_op jit(solution)/shard_map/and | solution.py:171
  61.4 5.6 %collective-permute-done.8 = f32[8,128,128]{2,1,0:T(8,128)S(1)} collective-permute-done((f32[8,128,128]{2,1,0:T(8,128)S(1)}, f32[8,128,128]{2,1,0:T(8,128)S(1)}, u32[]{:S(2)}, u32[]{:S(2)}) %collective-permute-start.8) | collective-permute-done | bytes 524320 | tf_op jit(solution)/shard_map/ppermute | solution.py:50
  67.1 1.5 %add_convert_fusion = bf16[8,128,128]{2,1,0:T(8,128)(2,1)} fusion(f32[8,128,128]{2,1,0:T(8,128)S(1)} %fusion.45, f32[8,128,128]{2,1,0:T(8,128)S(1)} %collective-permute-done.8, f32[8]{0:T(128)} %copy-done.10), kind=kLoop, calls=%fused_computation.36 | loop fusion | flops 393216 | bytes 1310752 | tf_op jit(solution)/shard_map/convert_element_type | solution.py:53
  68.5 11.5 %collective-permute-start.10 = (bf16[8,128,128]{2,1,0:T(8,128)(2,1)}, bf16[8,128,128]{2,1,0:T(8,128)(2,1)}, u32[]{:S(2)}, u32[]{:S(2)}) collective-permute-start(bf16[8,128,128]{2,1,0:T(8,128)(2,1)} %add_convert_fusion), channel_id=1, source_target_pairs={{0,4},{8,12},{16,20},{24,28},{32,36},{40,44},{48,52},{56,60},{64,6... | collective-permute-start | bytes 786440 | tf_op jit(solution)/shard_map/ppermute | solution.py:54
  80.1 1.3 %maximum_select_fusion = (bf16[4,2,128,256]{3,2,1,0:T(8,128)(2,1)S(1)}, bf16[4,2,128,256]{3,2,1,0:T(8,128)(2,1)S(1)}) fusion(bf16[1,2,128,256]{3,2,1,0:T(8,128)(2,1)S(1)} %bitcast.133, bf16[1,2,128,256]{3,2,1,0:T(8,128)(2,1)} %bitcast.132, bf16[1,2,128,256]{3,2,1,0:T(8,128)(2,1)} %bitcast.131, bf16[1,2,128,256]{3,2,1,0:T(8,128)(2,1)} %bitcast.130, ...), kind=kLoop, calls=%fused_computation.33 | loop fusion | flops 1835008 | bytes 1703937 | tf_op jit(solution)/shard_map/jit(_where)/select_n | solution.py:56
  82.3 1.9 %collective-permute-start.11 = (bf16[4,2,128,256]{3,2,1,0:T(8,128)(2,1)S(1)}, bf16[4,2,128,256]{3,2,1,0:T(8,128)(2,1)S(1)}, u32[]{:S(2)}, u32[]{:S(2)}) collective-permute-start(bf16[4,2,128,256]{3,2,1,0:T(8,128)(2,1)S(1)} %get-tuple-element.36), channel_id=1, source_target_pairs={{0,4},{4,0},{8,12},{12,8},{16,20},{20,16},{24,28},{28,24},{32,36},... | collective-permute-start | bytes 1572872 | tf_op jit(solution)/shard_map/ppermute | solution.py:57
  84.2 2.7 %fusion.4 = (f32[128,2,8]{0,2,1:T(8,128)S(1)}, f32[2,512,128,8]{2,1,3,0:T(8,128)}) fusion(pred[128,512]{0,1:T(8,128)(4,1)S(1)} %get-tuple-element.46, bf16[128,2,8,128]{3,2,1,0:T(8,128)(2,1)S(1)} %bitcast.119, bf16[512,2,128,1]{2,1,0,3:T(2,128)(2,1)S(1)} %bitcast.122), kind=kOutput, calls=%fused_computation.8 | convolution fusion | flops 271579136 | bytes 5054464 | tf_op jit(solution)/shard_map/tkgd,skd->tkgs/dot_general | solution.py:103
  87.0 1.4 %multiply_reduce_fusion = (f32[128]{0:T(128)S(1)}, f32[128,8,128]{0,2,1:T(8,128)S(1)}) fusion(f32[128,8,128]{0,2,1:T(8,128)} %convolution_bitcast_fusion.1, f32[128,8]{0,1:T(8,128)S(1)} %get-tuple-element.44, bf16[8,128,128]{2,1,0:T(8,128)(2,1)} %collective-permute-done.10, f32[8,128,128]{2,1,0:T(8,128)S(1)} %collective-permute-done.8, pred[]{:T(512)S(6)} %eq.26, ...), kind=kOutput, calls=%fused_computation.35 | convolution fusion | flops 34340736 | bytes 2101761 | tf_op jit(solution)/shard_map/thd,hde->the/dot_general | solution.py:139
  88.6 10.5 %psum.7 = f32[128]{0:T(128)S(1)} all-reduce(f32[128]{0:T(128)S(1)} %get-tuple-element.57), channel_id=1, replica_groups=mesh['grp'=4,'seq'=32,'head'=4] {'head'}, use_global_device_ids=true, to_apply=%region_2.3 | all-reduce | flops 128 | bytes 1024 | tf_op jit(solution)/shard_map/psum | solution.py:143
  99.1 0.8 multiply_convert_fusion
  100.9 0.9 fusion.2
  102.3 0.9 fusion
  103.2 1.1 %fusion.30 = f32[128,2,8,128]{0,3,2,1:T(8,128)S(1)} fusion(f32[2,512,128,8]{2,1,3,0:T(8,128)S(1)} %copy-done.1, f32[128,2,8]{0,2,1:T(8,128)S(1)} %get-tuple-element.42, pred[128,512]{0,1:T(8,128)(4,1)S(1)} %get-tuple-element.46, f32[128,2,8]{0,2,1:T(8,128)S(1)} %get-tuple-element.27, f32[128,2,8]{0,2,1:T(8,128)S(1)} %get-tuple-element.40, ...), kind=kOutput, calls=%fused_computation.24 | convolution fusion | flops 273154048 | bytes 5595136 | tf_op jit(solution)/shard_map/tkgs,skd->tkgd/dot_general | solution.py:111
  104.3 1.2 %divide_convert_fusion = bf16[128,2,8,128]{0,3,2,1:T(8,128)(2,1)S(1)} fusion(f32[128,2,8,128]{0,3,2,1:T(8,128)S(1)} %fusion.30, f32[2,512,128,8]{2,1,3,0:T(8,128)S(1)} %get-tuple-element.62, f32[128,2,8]{0,2,1:T(8,128)S(1)} %get-tuple-element.41, pred[128,512]{0,1:T(8,128)(4,1)S(1)} %get-tuple-element.45, f32[128,2,8]{0,2,1:T(8,128)S(1)} %get-tuple-element.26, ...), kind=kOutput, calls=%fused_computation.31 | convolution fusion | flops 273416192 | bytes 6111232 | tf_op jit(solution)/shard_map/tkgs,skd->tkgd/dot_general | solution.py:111
  105.5 1.0 copy.38
  (70 shorter events, 14.7 us)
Async XLA Ops:
  0.6 56.6 %copy-start = (bf16[128,1024]{1,0:T(8,128)(2,1)S(1)}, bf16[128,1024]{1,0:T(8,128)(2,1)}, u32[]{:S(2)}) copy-start(bf16[128,1024]{1,0:T(8,128)(2,1)} %param.9) | copy-start | bytes 786436
  0.6 56.6 %copy-start.4 = (bf16[128,1024]{1,0:T(8,128)(2,1)S(1)}, bf16[128,1024]{1,0:T(8,128)(2,1)}, u32[]{:S(2)}) copy-start(bf16[128,1024]{1,0:T(8,128)(2,1)} %param.11) | copy-start | bytes 786436
  0.7 56.5 %copy-start.2 = (bf16[128,2048]{1,0:T(8,128)(2,1)S(1)}, bf16[128,2048]{1,0:T(8,128)(2,1)}, u32[]{:S(2)}) copy-start(bf16[128,2048]{1,0:T(8,128)(2,1)} %param.14) | copy-start | bytes 1572868
  7.5 17.9 %collective-permute-start.1 = (f32[8,128,128]{2,1,0:T(8,128)S(1)}, f32[8,128,128]{2,1,0:T(8,128)S(1)}, u32[]{:S(2)}, u32[]{:S(2)}) collective-permute-start(f32[8,128,128]{2,1,0:T(8,128)S(1)} %fusion.45), channel_id=1, source_target_pairs={{0,4},{8,12},{16,20},{24,28},{32,36},{40,44},{48,52},{56,60},{64,6... | collective-permute-start | bytes 1572872 | tf_op jit(solution)/shard_map/ppermute | solution.py:27
  10.1 14.6 %collective-permute-start.2 = (bf16[2,128,256]{2,1,0:T(8,128)(2,1)S(1)}, bf16[2,128,256]{2,1,0:T(8,128)(2,1)S(1)}, u32[]{:S(2)}, u32[]{:S(2)}) collective-permute-start(bf16[2,128,256]{2,1,0:T(8,128)(2,1)S(1)} %get-tuple-element.39), channel_id=1, source_target_pairs={{0,8},{4,12},{8,16},{12,20},{16,24},{20,28},{24,32},{28,36},{32,40... | collective-permute-start | bytes 393224 | tf_op jit(solution)/shard_map/ppermute | solution.py:36
  14.0 23.7 %copy-start.10 = (f32[8]{0:T(128)}, f32[8]{0:T(128)S(1)}, u32[]{:S(2)}) copy-start(f32[8]{0:T(128)S(1)} %broadcast_select_fusion) | copy-start | bytes 100
  14.0 2.1 %collective-permute-start = (f32[8]{0:T(128)S(1)}, f32[8]{0:T(128)S(1)}, u32[]{:S(2)}, u32[]{:S(2)}) collective-permute-start(f32[8]{0:T(128)S(1)} %broadcast_select_fusion), channel_id=1, source_target_pairs={{0,4},{8,12},{16,20},{24,28},{32,36},{40,44},{48,52},{56,60},{64,6... | collective-permute-start | bytes 104 | tf_op jit(solution)/shard_map/ppermute | solution.py:27
  16.1 8.6 %copy-start.11 = (f32[8]{0:T(128)}, f32[8]{0:T(128)S(1)}, u32[]{:S(2)}) copy-start(f32[8]{0:T(128)S(1)} %collective-permute-done) | copy-start | bytes 100
  24.7 0.7 copy-start.5
  25.5 11.3 %collective-permute-start.4 = (f32[8,128,128]{2,1,0:T(8,128)S(1)}, f32[8,128,128]{2,1,0:T(8,128)S(1)}, u32[]{:S(2)}, u32[]{:S(2)}) collective-permute-start(f32[8,128,128]{2,1,0:T(8,128)S(1)} %multiply_add_fusion.2), channel_id=1, source_target_pairs={{4,12},{12,20},{20,28},{28,36},{36,44},{44,52},{52,60},{60,68},{68... | collective-permute-start | bytes 1572872 | tf_op jit(solution)/shard_map/ppermute | solution.py:27
  26.2 24.7 %copy-start.8 = (s32[128]{0:T(128)}, s32[128]{0:T(128)S(1)}, u32[]{:S(2)}) copy-start(s32[128]{0:T(128)S(1)} %get-tuple-element.72) | copy-start | bytes 1540
  26.3 10.6 %collective-permute-start.5 = (bf16[2,128,256]{2,1,0:T(8,128)(2,1)}, bf16[2,128,256]{2,1,0:T(8,128)(2,1)S(1)}, u32[]{:S(2)}, u32[]{:S(2)}) collective-permute-start(bf16[2,128,256]{2,1,0:T(8,128)(2,1)} %copy-done.5), channel_id=1, source_target_pairs={{0,8},{4,12},{8,16},{12,20},{16,24},{20,28},{24,32},{28,36},{32,40... | collective-permute-start | bytes 393224 | tf_op jit(solution)/shard_map/ppermute | solution.py:36
  28.8 0.7 collective-permute-start.3
  36.8 14.1 %copy-start.6 = (bf16[2,128,256]{2,1,0:T(8,128)(2,1)}, bf16[2,128,256]{2,1,0:T(8,128)(2,1)S(1)}, u32[]{:S(2)}) copy-start(bf16[2,128,256]{2,1,0:T(8,128)(2,1)S(1)} %collective-permute-done.5) | copy-start | bytes 393220
  37.0 12.5 %collective-permute-start.6 = (f32[8,128,128]{2,1,0:T(8,128)S(1)}, f32[8,128,128]{2,1,0:T(8,128)S(1)}, u32[]{:S(2)}, u32[]{:S(2)}) collective-permute-start(f32[8,128,128]{2,1,0:T(8,128)S(1)} %multiply_add_fusion.1), channel_id=1, source_target_pairs={{4,20},{12,28},{20,36},{28,44},{36,52},{44,60},{52,68},{60,76},{68... | collective-permute-start | bytes 1572872 | tf_op jit(solution)/shard_map/ppermute | solution.py:46
  38.2 10.6 %collective-permute-start.7 = (bf16[2,128,256]{2,1,0:T(8,128)(2,1)S(1)}, bf16[2,128,256]{2,1,0:T(8,128)(2,1)S(1)}, u32[]{:S(2)}, u32[]{:S(2)}) collective-permute-start(bf16[2,128,256]{2,1,0:T(8,128)(2,1)S(1)} %collective-permute-done.5), channel_id=1, source_target_pairs={{0,8},{4,12},{8,16},{12,20},{16,24},{20,28},{24,32},{28,36},{32,40... | collective-permute-start | bytes 393224 | tf_op jit(solution)/shard_map/ppermute | solution.py:36
  48.8 0.6 copy-start.7
  49.6 17.5 %collective-permute-start.8 = (f32[8,128,128]{2,1,0:T(8,128)S(1)}, f32[8,128,128]{2,1,0:T(8,128)S(1)}, u32[]{:S(2)}, u32[]{:S(2)}) collective-permute-start(f32[8,128,128]{2,1,0:T(8,128)S(1)} %multiply_add_fusion), channel_id=1, source_target_pairs={{4,8},{12,16},{20,24},{28,32},{36,40},{44,48},{52,56},{60,64},{68,... | collective-permute-start | bytes 1572872 | tf_op jit(solution)/shard_map/ppermute | solution.py:50
  59.3 2.2 %collective-permute-start.9 = (bf16[2,128,256]{2,1,0:T(8,128)(2,1)}, bf16[2,128,256]{2,1,0:T(8,128)(2,1)S(1)}, u32[]{:S(2)}, u32[]{:S(2)}) collective-permute-start(bf16[2,128,256]{2,1,0:T(8,128)(2,1)} %copy-done.7), channel_id=1, source_target_pairs={{4,12},{12,20},{20,28},{28,36},{36,44},{44,52},{52,60},{60,68},{68... | collective-permute-start | bytes 393224 | tf_op jit(solution)/shard_map/ppermute | solution.py:36
  68.5 18.4 %collective-permute-start.10 = (bf16[8,128,128]{2,1,0:T(8,128)(2,1)}, bf16[8,128,128]{2,1,0:T(8,128)(2,1)}, u32[]{:S(2)}, u32[]{:S(2)}) collective-permute-start(bf16[8,128,128]{2,1,0:T(8,128)(2,1)} %add_convert_fusion), channel_id=1, source_target_pairs={{0,4},{8,12},{16,20},{24,28},{32,36},{40,44},{48,52},{56,60},{64,6... | collective-permute-start | bytes 786440 | tf_op jit(solution)/shard_map/ppermute | solution.py:54
  82.3 16.8 %copy-start.9 = (f32[1024]{0:T(1024)S(1)}, f32[1024]{0:T(1024)}, u32[]{:S(2)}) copy-start(f32[1024]{0:T(1024)} %param.13) | copy-start | bytes 12292
  82.3 17.6 %collective-permute-start.11 = (bf16[4,2,128,256]{3,2,1,0:T(8,128)(2,1)S(1)}, bf16[4,2,128,256]{3,2,1,0:T(8,128)(2,1)S(1)}, u32[]{:S(2)}, u32[]{:S(2)}) collective-permute-start(bf16[4,2,128,256]{3,2,1,0:T(8,128)(2,1)S(1)} %get-tuple-element.36), channel_id=1, source_target_pairs={{0,4},{4,0},{8,12},{12,8},{16,20},{20,16},{24,28},{28,24},{32,36},... | collective-permute-start | bytes 1572872 | tf_op jit(solution)/shard_map/ppermute | solution.py:57
  100.1 2.2 %copy-start.1 = (f32[2,512,128,8]{2,1,3,0:T(8,128)S(1)}, f32[2,512,128,8]{2,1,3,0:T(8,128)}, u32[]{:S(2)}) copy-start(f32[2,512,128,8]{2,1,3,0:T(8,128)} %get-tuple-element.60) | copy-start | bytes 12582916
  100.9 2.3 %copy-start.3 = (bf16[512,2,128]{2,1,0:T(2,128)(2,1)S(1)}, bf16[512,2,128]{2,1,0:T(2,128)(2,1)}, u32[]{:S(2)}) copy-start(bf16[512,2,128]{2,1,0:T(2,128)(2,1)} %reshape.285) | copy-start | bytes 786436

commit v4 on v3

--- a/solution.py
+++ b/solution.py
@@ -1,5 +1,3 @@
-from functools import partial
-
 import jax
 import jax.numpy as jnp
 from jax import lax
@@ -27,9 +25,10 @@
     return jax.tree.map(lambda part: lax.ppermute(part, axis, pairs), x)
 
 
-def exchange(element, kv_pair, axis, core, width):
+def exchange(element, kv_pair, axis, core, width, take, running):
     count = lax.axis_size(axis)
     half = width // 2
+    swap = [(i, i ^ 1) for i in range(count)]
     ring = [kv_pair]
 
     def ring_step(parity=None):
@@ -47,16 +46,40 @@
     got, kv_next = lax.optimization_barrier((got, ring_step()))
     ring.append(kv_next)
     wide_state = got * wide[0][:, None, None] + wide[1]
+    mine = jnp.stack(ring[:half])
+    sent = jnp.where(core == 1, jnp.stack(ring[1:half]), jnp.stack(ring[: half - 1]))
+    running = take(running, range(0, width, 2), mine)
     before = lax.ppermute(wide_state, axis, shift_pairs(count, 1, 1))
-    before, kv_next = lax.optimization_barrier((before, ring_step(1)))
-    ring.append(kv_next)
+    before, kv_next, theirs, running = lax.optimization_barrier(
+        (before, ring_step(1), lax.ppermute(sent, axis, swap), running)
+    )
+    ring.append(kv_next)
+    last = jnp.where(core == 1, ring[half], ring[half - 1])
+    running = take(running, range(1, width - 2, 2), theirs)
     after = (before * element[0][:, None, None] + element[1]).astype(jnp.bfloat16)
-    after = lax.ppermute(after, axis, shift_pairs(count, 1, 0))
-    mine = jnp.stack(ring[:half])
-    sent = jnp.where(core == 1, jnp.stack(ring[1 : half + 1]), mine)
-    theirs = lax.ppermute(sent, axis, [(i, i ^ 1) for i in range(count)])
+    after, last, running = lax.optimization_barrier(
+        (
+            lax.ppermute(after, axis, shift_pairs(count, 1, 0)),
+            lax.ppermute(last, axis, swap),
+            running,
+        )
+    )
+    running = take(running, [width - 1], last[None])
     state = jnp.where(core == 0, before.astype(jnp.bfloat16), after)
-    return state, mine, theirs
+    return state, running
+
+
+def sum_over(x, axis):
+    count, here = (lax.axis_size(axis), lax.axis_index(axis))
+    parts = [x] + [
+        lax.ppermute(x, axis, [(i, (i + by) % count) for i in range(count)])
+        for by in range(1, count)
+    ]
+    ordered = jnp.take(jnp.stack(parts), (here - jnp.arange(count)) % count, axis=0)
+    total = ordered[0]
+    for k in range(1, count):
+        total = total + ordered[k]
+    return total
 
 
 def join_states(earlier, later):
@@ -132,27 +155,12 @@
     )
     core = position % 2
     window_len = WINDOW_DEV
-    state_rounded, mine, theirs = exchange(
-        element, jnp.stack([soft_k, soft_v]), ("grp", "seq"), core, window_len
-    )
-    inter_part = (
-        jnp.einsum("thd,hde->the", queries, state_rounded, preferred_element_type=jnp.float32)
-        * reach_gain.T[:, :, None]
-    )
-    mixed = (intra_part + inter_part).reshape(tok_rows, -1)
-    square_sum = lax.psum(jnp.sum(mixed * mixed, axis=1), "head")
-    inv_norm = lax.rsqrt(square_sum / (LIGHTNING_HEADS * HEAD_DIM) + 1e-06)
-    light_out = (mixed * inv_norm[:, None] * light_gain).astype(jnp.bfloat16)
     kv_heads = soft_k.shape[1] // HEAD_DIM
     group_size = soft_q.shape[1] // soft_k.shape[1]
     soft_queries = soft_q.reshape(tok_rows, kv_heads, group_size, HEAD_DIM)
     query_pos = row_start + jnp.arange(tok_rows, dtype=jnp.int32)
-    running = (
-        jnp.full((tok_rows, kv_heads, group_size), MASK_FILL, jnp.float32),
-        jnp.zeros((tok_rows, kv_heads, group_size), jnp.float32),
-        jnp.zeros((tok_rows, kv_heads, group_size, HEAD_DIM), jnp.float32),
-    )
-    for slot_list, chosen in ((range(0, window_len, 2), mine), (range(1, window_len, 2), theirs)):
+
+    def take(running, slot_list, chosen):
         key_rows = chosen[:, 0].reshape(-1, kv_heads, HEAD_DIM)
         value_rows = chosen[:, 1].reshape(-1, kv_heads, HEAD_DIM)
         key_pos = jnp.concatenate(
@@ -172,10 +180,24 @@
             & (key_pos >= 0)[None, :]
             & (key_seg[None, :] == seg_tok[:, None])
         )
-        step_fn = partial(
-            absorb, queries=soft_queries, key_rows=key_rows, value_rows=value_rows, allowed=allowed
-        )
-        running = step_fn(running)
+        return absorb(running, soft_queries, key_rows, value_rows, allowed)
+
+    running = (
+        jnp.full((tok_rows, kv_heads, group_size), MASK_FILL, jnp.float32),
+        jnp.zeros((tok_rows, kv_heads, group_size), jnp.float32),
+        jnp.zeros((tok_rows, kv_heads, group_size, HEAD_DIM), jnp.float32),
+    )
+    state_rounded, running = exchange(
+        element, jnp.stack([soft_k, soft_v]), ("grp", "seq"), core, window_len, take, running
+    )
+    inter_part = (
+        jnp.einsum("thd,hde->the", queries, state_rounded, preferred_element_type=jnp.float32)
+        * reach_gain.T[:, :, None]
+    )
+    mixed = (intra_part + inter_part).reshape(tok_rows, -1)
+    square_sum = sum_over(jnp.sum(mixed * mixed, axis=1), "head")
+    inv_norm = lax.rsqrt(square_sum / (LIGHTNING_HEADS * HEAD_DIM) + 1e-06)
+    light_out = (mixed * inv_norm[:, None] * light_gain).astype(jnp.bfloat16)
     row_max, row_mass, weighted = running
     soft_out = (weighted / row_mass[..., None]).reshape(tok_rows, -1).astype(jnp.bfloat16)
     return (light_out, soft_out)

time: 107 us -> 104 us (0.972)
  blocking collectives: 10.5 us -> 0 us
  local copies, waits for them, and re-layouts: 12.1 us -> 16.8 us
  starting transfers between devices: 28.2 us -> 32.5 us
  other arithmetic: 12.9 us -> 9.06 us
  between operations: 2.57 us -> 4.03 us
    psum x1 -> x0, blocking collectives: 10.5 us -> none  [body(): square_sum = lax.psum(jnp.sum(mixed * mixed, axis=1), 'head')]
    ppermute x4, waiting for transfers between devices: 23.4 us -> 29.1 us  [ring_step(): return lax.ppermute(ring[-1], axis, shift_pairs(count, 2, parity))]
    ppermute x1, waiting for transfers between devices: 5.61 us -> 0.01 us  [exchange(): before = lax.ppermute(wide_state, axis, shift_pairs(count, 1, 1))]
    dot_general x2 -> x3, matrix products: 2.31 us -> 6.59 us  [absorb(): jnp.einsum('tkgs,skd->tkgd', exponent.astype(jnp.bfloat16), value_rows, p...]
    ppermute x2 -> x6, starting transfers between devices: 13.5 us -> 17 us  [the longest x3 10.2 us: sum_over(): lax.ppermute(x, axis, [(i, (i + by) % count) for i in range(count)])]
    unnamed x26 -> x20, local copies, waits for them, and re-layouts: 2.92 us -> 5.64 us
    slice x2 -> x6, local copies, waits for them, and re-layouts: 0.07 us -> 2.48 us  [the longest x4 2.18 us: take(): value_rows = chosen[:, 1].reshape(-1, kv_heads, HEAD_DIM)]
    add x1, other arithmetic: 0.12 us -> 1.97 us  [exchange(): wide_state = got * wide[0][:, None, None] + wide[1]]
  transfers between devices with their start and end apart: 12 -> 16, of which waited for: 5 -> 4; matrix products, arithmetic and copies ran while one was open for 19% -> 24% of each run, Pallas kernels for 0% -> 0%
where the time goes in v4:
time: 104 us; the launch traced here: 103 us
  starting transfers between devices  32.5 us (31%)
  waiting for transfers between devices  29.9 us (29%)
  local copies, waits for them, and re-layouts  16.8 us (16%)
  matrix products  10.5 us (10%)
  other arithmetic  9.06 us (9%)
  between operations  4.03 us (4%)
    ppermute x4, waiting for transfers between devices, ring_step(): return lax.ppermute(ring[-1], axis, shift_pairs(count, 2, parity))  29.1 us
    ppermute x3, starting transfers between devices, sum_over(): lax.ppermute(x, axis, [(i, (i + by) % count) for i in range(count)])  10.2 us
    ppermute x4, starting transfers between devices, ring_step(): return lax.ppermute(ring[-1], axis, shift_pairs(count, 2, parity))  8.34 us
    dot_general x3, matrix products, absorb(): jnp.einsum('tkgs,skd->tkgd', exponent.astype(jnp.bfloat16), value_rows, p...  6.59 us
    unnamed x20, local copies, waits for them, and re-layouts  5.64 us
    ppermute x4, starting transfers between devices, move(): return jax.tree.map(lambda part: lax.ppermute(part, axis, pairs), x)  4.42 us
    reshape x7, local copies, waits for them, and re-layouts, token_segments(): return jnp.repeat(blocks, BLOCK)  4.28 us
    ppermute x1, starting transfers between devices, exchange(): lax.ppermute(sent, axis, swap)  2.98 us
  transfers between devices with their start and end apart: 16, of which 4 were waited for; matrix products, arithmetic and copies ran while one was open for 24% of the time, Pallas kernels for 0%

profile of v4, /device:TPU:24, one launch (start us, length us, event | category | flops | bytes accessed | tf_op | source)
XLA Modules:
  0.0 102.8 jit_solution(12900591082399498883)
XLA Ops:
  0.8 1.0 reduce_window_sum.11
  2.1 1.7 %fusion.86 = (s32[1]{0:T(128)}, s32[1]{0:T(128)}, s32[1]{0:T(128)}, s32[1]{0:T(128)}, s32[1]{0:T(128)}, /*index=5*/s32[1]{0:T(128)}, s32[1]{0:T(128)}, s32[1]{0:T(128)}, s32[1]{0:T(128)}, s32[1]{0:T(128)}) fusion(s32[128]{0:T(128)} %param.17, s32[]{:T(128)S(6)} %select_n.204, s32[]{:T(128)S(6)} %select_n.191, s32[]{:T(128)S(6)} %select_n.189, ...), kind=kLoop, calls=%fused_computation.135 | loop fusion | bytes 120 | tf_op jit(solution)/shard_map/dynamic_slice | solution.py:90
  5.1 1.7 %collective-permute-start = (f32[8]{0:T(128)S(1)}, f32[8]{0:T(128)S(1)}, u32[]{:S(2)}, u32[]{:S(2)}) collective-permute-start(f32[8]{0:T(128)S(1)} %broadcast_select_fusion.2), channel_id=1, source_target_pairs={{0,4},{8,12},{16,20},{24,28},{32,36},{40,44},{48,52},{56,60},{64,6... | collective-permute-start | bytes 104 | tf_op jit(solution)/shard_map/ppermute | solution.py:25
  6.9 1.1 %copy.60 = bf16[128,1024]{0,1:T(8,128)(2,1)S(1)} copy(bf16[128,1024]{1,0:T(8,128)(2,1)} %param.10) | data formatting | bytes 524288 | tf_op jit(solution)/shard_map/reshape | solution.py:98
  8.2 1.3 %collective-permute-start.1 = (f32[8,128,128]{2,1,0:T(8,128)S(1)}, f32[8,128,128]{2,1,0:T(8,128)S(1)}, u32[]{:S(2)}, u32[]{:S(2)}) collective-permute-start(f32[8,128,128]{2,1,0:T(8,128)S(1)} %fusion.46), channel_id=1, source_target_pairs={{0,4},{8,12},{16,20},{24,28},{32,36},{40,44},{48,52},{56,60},{64,6... | collective-permute-start | bytes 1572872 | tf_op jit(solution)/shard_map/ppermute | solution.py:25
  9.6 1.0 copy.31
  10.5 1.0 copy.30
  11.5 3.8 %collective-permute-start.2 = (bf16[2,128,256]{1,2,0:T(8,128)(2,1)S(1)}, bf16[2,128,256]{1,2,0:T(8,128)(2,1)S(1)}, u32[]{:S(2)}, u32[]{:S(2)}) collective-permute-start(bf16[2,128,256]{1,2,0:T(8,128)(2,1)S(1)} %get-tuple-element.57), channel_id=1, source_target_pairs={{0,8},{4,12},{8,16},{12,20},{16,24},{20,28},{24,32},{28,36},{32,40... | collective-permute-start | bytes 393224 | tf_op jit(solution)/shard_map/ppermute | solution.py:35
  16.9 9.2 %collective-permute-done.2 = bf16[2,128,256]{1,2,0:T(8,128)(2,1)S(1)} collective-permute-done((bf16[2,128,256]{1,2,0:T(8,128)(2,1)S(1)}, bf16[2,128,256]{1,2,0:T(8,128)(2,1)S(1)}, u32[]{:S(2)}, u32[]{:S(2)}) %collective-permute-start.2) | collective-permute-done | bytes 131104 | tf_op jit(solution)/shard_map/ppermute | solution.py:35
  29.7 1.9 %collective-permute-start.5 = (bf16[2,128,256]{1,2,0:T(8,128)(2,1)S(1)}, bf16[2,128,256]{1,2,0:T(8,128)(2,1)S(1)}, u32[]{:S(2)}, u32[]{:S(2)}) collective-permute-start(bf16[2,128,256]{1,2,0:T(8,128)(2,1)S(1)} %collective-permute-done.2), channel_id=1, source_target_pairs={{0,8},{4,12},{8,16},{12,20},{16,24},{20,28},{24,32},{28,36},{32,40... | collective-permute-start | bytes 393224 | tf_op jit(solution)/shard_map/ppermute | solution.py:35
  32.4 7.7 %collective-permute-done.5 = bf16[2,128,256]{1,2,0:T(8,128)(2,1)S(1)} collective-permute-done((bf16[2,128,256]{1,2,0:T(8,128)(2,1)S(1)}, bf16[2,128,256]{1,2,0:T(8,128)(2,1)S(1)}, u32[]{:S(2)}, u32[]{:S(2)}) %collective-permute-start.5) | collective-permute-done | bytes 131104 | tf_op jit(solution)/shard_map/ppermute | solution.py:35
  40.2 1.5 %collective-permute-start.6 = (f32[8,128,128]{2,1,0:T(8,128)S(1)}, f32[8,128,128]{2,1,0:T(8,128)}, u32[]{:S(2)}, u32[]{:S(2)}) collective-permute-start(f32[8,128,128]{2,1,0:T(8,128)S(1)} %multiply_add_fusion.2), channel_id=1, source_target_pairs={{4,20},{12,28},{20,36},{28,44},{36,52},{44,60},{52,68},{60,76},{68... | collective-permute-start | bytes 1572872 | tf_op jit(solution)/shard_map/ppermute | solution.py:45
  45.0 1.9 %collective-permute-start.7 = (bf16[2,128,256]{1,2,0:T(8,128)(2,1)S(1)}, bf16[2,128,256]{1,2,0:T(8,128)(2,1)S(1)}, u32[]{:S(2)}, u32[]{:S(2)}) collective-permute-start(bf16[2,128,256]{1,2,0:T(8,128)(2,1)S(1)} %collective-permute-done.5), channel_id=1, source_target_pairs={{0,8},{4,12},{8,16},{12,20},{16,24},{20,28},{24,32},{28,36},{32,40... | collective-permute-start | bytes 393224 | tf_op jit(solution)/shard_map/ppermute | solution.py:35
  47.1 12.2 %collective-permute-done.7 = bf16[2,128,256]{1,2,0:T(8,128)(2,1)S(1)} collective-permute-done((bf16[2,128,256]{1,2,0:T(8,128)(2,1)S(1)}, bf16[2,128,256]{1,2,0:T(8,128)(2,1)S(1)}, u32[]{:S(2)}, u32[]{:S(2)}) %collective-permute-start.7) | collective-permute-done | bytes 131104 | tf_op jit(solution)/shard_map/ppermute | solution.py:35
  59.3 2.0 %multiply_add_fusion.1 = f32[8,128,128]{2,1,0:T(8,128)} fusion(f32[8,128,128]{2,1,0:T(8,128)S(1)} %multiply_add_fusion.2, f32[8,128,128]{2,1,0:T(8,128)} %collective-permute-done.6, f32[8]{0:T(128)S(1)} %mul.191), kind=kLoop, calls=%fused_computation.44 | loop fusion | flops 262144 | bytes 1572896 | tf_op jit(solution)/shard_map/add | solution.py:48
  61.2 1.3 %collective-permute-start.8 = (f32[8,128,128]{2,1,0:T(8,128)}, f32[8,128,128]{2,1,0:T(8,128)S(1)}, u32[]{:S(2)}, u32[]{:S(2)}) collective-permute-start(f32[8,128,128]{2,1,0:T(8,128)} %multiply_add_fusion.1), channel_id=1, source_target_pairs={{4,8},{12,16},{20,24},{28,32},{36,40},{44,48},{52,56},{60,64},{68,... | collective-permute-start | bytes 1572872 | tf_op jit(solution)/shard_map/ppermute | solution.py:52
  63.3 0.8 maximum_select_fusion
  64.1 3.0 %collective-permute-start.10 = (bf16[3,2,128,256]{2,3,1,0:T(8,128)(2,1)}, bf16[3,2,128,256]{2,3,1,0:T(8,128)(2,1)}, u32[]{:S(2)}, u32[]{:S(2)}) collective-permute-start(bf16[3,2,128,256]{2,3,1,0:T(8,128)(2,1)} %maximum_select_fusion), channel_id=1, source_target_pairs={{0,4},{4,0},{8,12},{12,8},{16,20},{20,16},{24,28},{28,24},{32,36},... | collective-permute-start | bytes 1179656 | tf_op jit(solution)/shard_map/ppermute | solution.py:54
  68.2 1.9 %copy-done.1 = f32[2,512,128,8]{2,1,3,0:T(8,128)} copy-done((f32[2,512,128,8]{2,1,3,0:T(8,128)}, f32[2,512,128,8]{2,1,3,0:T(8,128)S(1)}, u32[]{:S(2)}) %copy-start.1) | copy-done | bytes 4194328
  70.1 0.9 fusion.1
  71.3 4.3 %fusion.26 = f32[128,2,8,128]{0,3,2,1:T(8,128)} fusion(f32[2,512,128,8]{2,1,3,0:T(8,128)} %copy-done.1, f32[128,2,8]{0,2,1:T(8,128)S(1)} %broadcast_maximum_fusion, pred[128,512]{0,1:T(8,128)(4,1)S(1)} %and_and_fusion, f32[128,2,8]{0,2,1:T(8,128)S(1)} %get-tuple-element.58, bf16[512,2,128,1]{0,2,1,3:T(8,128)(2,1)S(1)} %reshape.391), kind=kOutput, calls=%fused_computation.27 | convolution fusion | flops 272891904 | bytes 5586944 | tf_op jit(solution)/shard_map/tkgs,skd->tkgd/dot_general | solution.py:134
  75.8 1.9 %collective-permute-start.11 = (bf16[8,128,128]{2,1,0:T(8,128)(2,1)S(1)}, bf16[8,128,128]{2,1,0:T(8,128)(2,1)S(1)}, u32[]{:S(2)}, u32[]{:S(2)}) collective-permute-start(bf16[8,128,128]{2,1,0:T(8,128)(2,1)S(1)} %add_convert_fusion), channel_id=1, source_target_pairs={{0,4},{8,12},{16,20},{24,28},{32,36},{40,44},{48,52},{56,60},{64,6... | collective-permute-start | bytes 786440 | tf_op jit(solution)/shard_map/ppermute | solution.py:62
  77.8 1.9 %collective-permute-start.12 = (bf16[2,128,256]{1,2,0:T(8,128)(2,1)S(1)}, bf16[2,128,256]{1,2,0:T(8,128)(2,1)S(1)}, u32[]{:S(2)}, u32[]{:S(2)}) collective-permute-start(bf16[2,128,256]{1,2,0:T(8,128)(2,1)S(1)} %broadcast_select_fusion), channel_id=1, source_target_pairs={{0,4},{4,0},{8,12},{12,8},{16,20},{20,16},{24,28},{28,24},{32,36},... | collective-permute-start | bytes 393224 | tf_op jit(solution)/shard_map/ppermute | solution.py:63
  79.7 1.1 %fusion.84 = (bf16[3,1,128,256]{2,3,1,0:T(8,128)(2,1)S(1)}, bf16[3,1,128,256]{2,3,1,0:T(8,128)(2,1)S(1)}) fusion(bf16[3,2,128,256]{2,3,1,0:T(8,128)(2,1)} %collective-permute-done.10), kind=kLoop, calls=%fused_computation.133 | loop fusion | bytes 786432 | tf_op jit(solution)/shard_map/slice | solution.py:165
  82.7 1.9 %multiply_add_fusion = f32[128,2,8,128]{0,3,2,1:T(8,128)} fusion(f32[128,2,8,128]{0,3,2,1:T(8,128)S(1)} %copy-done.3, f32[128,2,8]{0,2,1:T(8,128)S(1)} %get-tuple-element.47, f32[2,384,128,8]{2,1,3,0:T(8,128)S(1)} %get-tuple-element.75, f32[128,2,8]{0,2,1:T(8,128)S(1)} %max.38, pred[128,384]{0,1:T(8,128)(4,1)S(1)} %and_and_fusion.1, ...), kind=kOutput, calls=%fused_computation.36 | convolution fusion | flops 204996608 | bytes 5505024 | tf_op jit(solution)/shard_map/tkgs,skd->tkgd/dot_general | solution.py:134
  85.7 1.6 %multiply_reduce_fusion = (f32[128]{0:T(128)S(1)}, f32[128,8,128]{0,2,1:T(8,128)S(1)}) fusion(f32[128,8,128]{0,2,1:T(8,128)S(1)} %fusion.30, bf16[128,8,128]{0,2,1:T(8,128)(2,1)S(1)} %bitcast.158, f32[8,128]{1,0:T(8,128)S(1)} %reduce_window_sum.11, pred[128,128]{1,0:T(8,128)(4,1)S(1)} %iota_compare_fusion, bf16[128,1024]{1,0:T(8,128)(2,1)S(1)} %copy-done, ...), kind=kOutput, calls=%fused_computation.42 | convolution fusion | flops 68026240 | bytes 1856000 | tf_op jit(solution)/shard_map/hts,shd->thd/dot_general | solution.py:106
  87.2 4.7 %collective-permute-start.15 = (f32[128]{0:T(128)S(1)}, f32[128]{0:T(128)S(1)}, u32[]{:S(2)}, u32[]{:S(2)}) collective-permute-start(f32[128]{0:T(128)S(1)} %get-tuple-element.76), channel_id=1, source_target_pairs={{0,3},{1,0},{2,1},{3,2},{4,7},{5,4},{6,5},{7,6},{8,11},{9,8},{10,9... | collective-permute-start | bytes 1544 | tf_op jit(solution)/shard_map/ppermute | solution.py:75
  91.9 2.7 %collective-permute-start.14 = (f32[128]{0:T(128)S(1)}, f32[128]{0:T(128)S(1)}, u32[]{:S(2)}, u32[]{:S(2)}) collective-permute-start(f32[128]{0:T(128)S(1)} %get-tuple-element.76), channel_id=1, source_target_pairs={{0,2},{1,3},{2,0},{3,1},{4,6},{5,7},{6,4},{7,5},{8,10},{9,11},{10,... | collective-permute-start | bytes 1544 | tf_op jit(solution)/shard_map/ppermute | solution.py:75
  94.6 2.8 %collective-permute-start.13 = (f32[128]{0:T(128)S(1)}, f32[128]{0:T(128)S(1)}, u32[]{:S(2)}, u32[]{:S(2)}) collective-permute-start(f32[128]{0:T(128)S(1)} %get-tuple-element.76), channel_id=1, source_target_pairs={{0,1},{1,2},{2,3},{3,0},{4,5},{5,6},{6,7},{7,4},{8,9},{9,10},{10,1... | collective-permute-start | bytes 1544 | tf_op jit(solution)/shard_map/ppermute | solution.py:75
  97.4 0.9 fusion.85
  99.5 1.0 copy.49
  102.0 0.8 multiply_convert_fusion
  (96 shorter events, 16.2 us)
Async XLA Ops:
  0.6 7.4 %copy-start = (bf16[128,1024]{1,0:T(8,128)(2,1)S(1)}, bf16[128,1024]{1,0:T(8,128)(2,1)}, u32[]{:S(2)}) copy-start(bf16[128,1024]{1,0:T(8,128)(2,1)} %param.11) | copy-start | bytes 786436
  0.6 46.3 %copy-start.4 = (bf16[128,2048]{1,0:T(8,128)(2,1)S(1)}, bf16[128,2048]{1,0:T(8,128)(2,1)}, u32[]{:S(2)}) copy-start(bf16[128,2048]{1,0:T(8,128)(2,1)} %param.14) | copy-start | bytes 1572868
  5.1 11.9 %collective-permute-start = (f32[8]{0:T(128)S(1)}, f32[8]{0:T(128)S(1)}, u32[]{:S(2)}, u32[]{:S(2)}) collective-permute-start(f32[8]{0:T(128)S(1)} %broadcast_select_fusion.2), channel_id=1, source_target_pairs={{0,4},{8,12},{16,20},{24,28},{32,36},{40,44},{48,52},{56,60},{64,6... | collective-permute-start | bytes 104 | tf_op jit(solution)/shard_map/ppermute | solution.py:25
  8.2 17.9 %collective-permute-start.1 = (f32[8,128,128]{2,1,0:T(8,128)S(1)}, f32[8,128,128]{2,1,0:T(8,128)S(1)}, u32[]{:S(2)}, u32[]{:S(2)}) collective-permute-start(f32[8,128,128]{2,1,0:T(8,128)S(1)} %fusion.46), channel_id=1, source_target_pairs={{0,4},{8,12},{16,20},{24,28},{32,36},{40,44},{48,52},{56,60},{64,6... | collective-permute-start | bytes 1572872 | tf_op jit(solution)/shard_map/ppermute | solution.py:25
  11.5 14.6 %collective-permute-start.2 = (bf16[2,128,256]{1,2,0:T(8,128)(2,1)S(1)}, bf16[2,128,256]{1,2,0:T(8,128)(2,1)S(1)}, u32[]{:S(2)}, u32[]{:S(2)}) collective-permute-start(bf16[2,128,256]{1,2,0:T(8,128)(2,1)S(1)} %get-tuple-element.57), channel_id=1, source_target_pairs={{0,8},{4,12},{8,16},{12,20},{16,24},{20,28},{24,32},{28,36},{32,40... | collective-permute-start | bytes 393224 | tf_op jit(solution)/shard_map/ppermute | solution.py:35
  26.2 13.8 %collective-permute-start.4 = (f32[8,128,128]{2,1,0:T(8,128)S(1)}, f32[8,128,128]{2,1,0:T(8,128)S(1)}, u32[]{:S(2)}, u32[]{:S(2)}) collective-permute-start(f32[8,128,128]{2,1,0:T(8,128)S(1)} %multiply_add_fusion.3), channel_id=1, source_target_pairs={{4,12},{12,20},{20,28},{28,36},{36,44},{44,52},{52,60},{60,68},{68... | collective-permute-start | bytes 1572872 | tf_op jit(solution)/shard_map/ppermute | solution.py:25
  29.7 10.3 %collective-permute-start.5 = (bf16[2,128,256]{1,2,0:T(8,128)(2,1)S(1)}, bf16[2,128,256]{1,2,0:T(8,128)(2,1)S(1)}, u32[]{:S(2)}, u32[]{:S(2)}) collective-permute-start(bf16[2,128,256]{1,2,0:T(8,128)(2,1)S(1)} %collective-permute-done.2), channel_id=1, source_target_pairs={{0,8},{4,12},{8,16},{12,20},{16,24},{20,28},{24,32},{28,36},{32,40... | collective-permute-start | bytes 393224 | tf_op jit(solution)/shard_map/ppermute | solution.py:35
  31.7 0.7 collective-permute-start.3
  40.2 19.1 %collective-permute-start.6 = (f32[8,128,128]{2,1,0:T(8,128)S(1)}, f32[8,128,128]{2,1,0:T(8,128)}, u32[]{:S(2)}, u32[]{:S(2)}) collective-permute-start(f32[8,128,128]{2,1,0:T(8,128)S(1)} %multiply_add_fusion.2), channel_id=1, source_target_pairs={{4,20},{12,28},{20,36},{28,44},{36,52},{44,60},{52,68},{60,76},{68... | collective-permute-start | bytes 1572872 | tf_op jit(solution)/shard_map/ppermute | solution.py:45
  45.0 14.3 %collective-permute-start.7 = (bf16[2,128,256]{1,2,0:T(8,128)(2,1)S(1)}, bf16[2,128,256]{1,2,0:T(8,128)(2,1)S(1)}, u32[]{:S(2)}, u32[]{:S(2)}) collective-permute-start(bf16[2,128,256]{1,2,0:T(8,128)(2,1)S(1)} %collective-permute-done.5), channel_id=1, source_target_pairs={{0,8},{4,12},{8,16},{12,20},{16,24},{20,28},{24,32},{28,36},{32,40... | collective-permute-start | bytes 393224 | tf_op jit(solution)/shard_map/ppermute | solution.py:35
  61.2 14.4 %collective-permute-start.8 = (f32[8,128,128]{2,1,0:T(8,128)}, f32[8,128,128]{2,1,0:T(8,128)S(1)}, u32[]{:S(2)}, u32[]{:S(2)}) collective-permute-start(f32[8,128,128]{2,1,0:T(8,128)} %multiply_add_fusion.1), channel_id=1, source_target_pairs={{4,8},{12,16},{20,24},{28,32},{36,40},{44,48},{52,56},{60,64},{68,... | collective-permute-start | bytes 1572872 | tf_op jit(solution)/shard_map/ppermute | solution.py:52
  62.5 13.1 %collective-permute-start.9 = (bf16[2,128,256]{1,2,0:T(8,128)(2,1)S(1)}, bf16[2,128,256]{1,2,0:T(8,128)(2,1)S(1)}, u32[]{:S(2)}, u32[]{:S(2)}) collective-permute-start(bf16[2,128,256]{1,2,0:T(8,128)(2,1)S(1)} %collective-permute-done.7), channel_id=1, source_target_pairs={{4,12},{12,20},{20,28},{28,36},{36,44},{44,52},{52,60},{60,68},{68... | collective-permute-start | bytes 393224 | tf_op jit(solution)/shard_map/ppermute | solution.py:35
  64.1 11.5 %collective-permute-start.10 = (bf16[3,2,128,256]{2,3,1,0:T(8,128)(2,1)}, bf16[3,2,128,256]{2,3,1,0:T(8,128)(2,1)}, u32[]{:S(2)}, u32[]{:S(2)}) collective-permute-start(bf16[3,2,128,256]{2,3,1,0:T(8,128)(2,1)} %maximum_select_fusion), channel_id=1, source_target_pairs={{0,4},{4,0},{8,12},{12,8},{16,20},{20,16},{24,28},{28,24},{32,36},... | collective-permute-start | bytes 1179656 | tf_op jit(solution)/shard_map/ppermute | solution.py:54
  68.2 1.9 %copy-start.1 = (f32[2,512,128,8]{2,1,3,0:T(8,128)}, f32[2,512,128,8]{2,1,3,0:T(8,128)S(1)}, u32[]{:S(2)}) copy-start(f32[2,512,128,8]{2,1,3,0:T(8,128)S(1)} %get-tuple-element.73) | copy-start | bytes 12582916
  75.8 8.9 %collective-permute-start.11 = (bf16[8,128,128]{2,1,0:T(8,128)(2,1)S(1)}, bf16[8,128,128]{2,1,0:T(8,128)(2,1)S(1)}, u32[]{:S(2)}, u32[]{:S(2)}) collective-permute-start(bf16[8,128,128]{2,1,0:T(8,128)(2,1)S(1)} %add_convert_fusion), channel_id=1, source_target_pairs={{0,4},{8,12},{16,20},{24,28},{32,36},{40,44},{48,52},{56,60},{64,6... | collective-permute-start | bytes 786440 | tf_op jit(solution)/shard_map/ppermute | solution.py:62
  77.8 6.9 %collective-permute-start.12 = (bf16[2,128,256]{1,2,0:T(8,128)(2,1)S(1)}, bf16[2,128,256]{1,2,0:T(8,128)(2,1)S(1)}, u32[]{:S(2)}, u32[]{:S(2)}) collective-permute-start(bf16[2,128,256]{1,2,0:T(8,128)(2,1)S(1)} %broadcast_select_fusion), channel_id=1, source_target_pairs={{0,4},{4,0},{8,12},{12,8},{16,20},{20,16},{24,28},{28,24},{32,36},... | collective-permute-start | bytes 393224 | tf_op jit(solution)/shard_map/ppermute | solution.py:63
  81.3 1.4 %copy-start.3 = (f32[128,2,8,128]{0,3,2,1:T(8,128)S(1)}, f32[128,2,8,128]{0,3,2,1:T(8,128)}, u32[]{:S(2)}) copy-start(f32[128,2,8,128]{0,3,2,1:T(8,128)} %fusion.26) | copy-start | bytes 3145732
  82.7 2.7 %copy-start.5 = (bf16[128,1024]{1,0:T(8,128)(2,1)S(1)}, bf16[128,1024]{1,0:T(8,128)(2,1)}, u32[]{:S(2)}) copy-start(bf16[128,1024]{1,0:T(8,128)(2,1)} %param.9) | copy-start | bytes 786436
  84.7 0.7 copy-start.6
  85.7 13.2 %copy-start.2 = (f32[128,2,8,128]{0,3,2,1:T(8,128)S(1)}, f32[128,2,8,128]{0,3,2,1:T(8,128)}, u32[]{:S(2)}) copy-start(f32[128,2,8,128]{0,3,2,1:T(8,128)} %multiply_add_fusion) | copy-start | bytes 3145732
  87.2 13.2 %collective-permute-start.15 = (f32[128]{0:T(128)S(1)}, f32[128]{0:T(128)S(1)}, u32[]{:S(2)}, u32[]{:S(2)}) collective-permute-start(f32[128]{0:T(128)S(1)} %get-tuple-element.76), channel_id=1, source_target_pairs={{0,3},{1,0},{2,1},{3,2},{4,7},{5,4},{6,5},{7,6},{8,11},{9,8},{10,9... | collective-permute-start | bytes 1544 | tf_op jit(solution)/shard_map/ppermute | solution.py:75
  91.9 8.6 %collective-permute-start.14 = (f32[128]{0:T(128)S(1)}, f32[128]{0:T(128)S(1)}, u32[]{:S(2)}, u32[]{:S(2)}) collective-permute-start(f32[128]{0:T(128)S(1)} %get-tuple-element.76), channel_id=1, source_target_pairs={{0,2},{1,3},{2,0},{3,1},{4,6},{5,7},{6,4},{7,5},{8,10},{9,11},{10,... | collective-permute-start | bytes 1544 | tf_op jit(solution)/shard_map/ppermute | solution.py:75
  94.6 6.7 %collective-permute-start.13 = (f32[128]{0:T(128)S(1)}, f32[128]{0:T(128)S(1)}, u32[]{:S(2)}, u32[]{:S(2)}) collective-permute-start(f32[128]{0:T(128)S(1)} %get-tuple-element.76), channel_id=1, source_target_pairs={{0,1},{1,2},{2,3},{3,0},{4,5},{5,6},{6,7},{7,4},{8,9},{9,10},{10,1... | collective-permute-start | bytes 1544 | tf_op jit(solution)/shard_map/ppermute | solution.py:75
  98.9 3.1 %copy-start.7 = (f32[1024]{0:T(1024)S(1)}, f32[1024]{0:T(1024)}, u32[]{:S(2)}) copy-start(f32[1024]{0:T(1024)} %param.13) | copy-start | bytes 12292

commit v5 on v4

--- a/solution.py
+++ b/solution.py
@@ -21,10 +21,6 @@
     ]
 
 
-def move(x, axis, pairs):
-    return jax.tree.map(lambda part: lax.ppermute(part, axis, pairs), x)
-
-
 def exchange(element, kv_pair, axis, core, width, take, running):
     count = lax.axis_size(axis)
     half = width // 2
@@ -34,29 +30,45 @@
     def ring_step(parity=None):
         return lax.ppermute(ring[-1], axis, shift_pairs(count, 2, parity))
 
-    got = move(element, axis, shift_pairs(count, 1, 0))
+    gain, state = element
+    rows = state.shape[1]
+    packed = jnp.concatenate([state, jnp.broadcast_to(gain[:, None, None], state[:, :1].shape)], 1)
+    got = lax.ppermute(packed, axis, shift_pairs(count, 1, 0))
     got, kv_next = lax.optimization_barrier((got, ring_step()))
     ring.append(kv_next)
-    wide = join_states(got, element)
-    got = move(wide, axis, shift_pairs(count, 2, 1))
+    wide_state = got[:, :rows] * gain[:, None, None] + state
+    wide_gain = got[:, rows, 0] * gain
+    high = wide_gain.astype(jnp.bfloat16)
+    low = (wide_gain - high.astype(jnp.float32)).astype(jnp.bfloat16)
+    packed = jnp.concatenate(
+        [
+            wide_state.astype(jnp.bfloat16),
+            jnp.broadcast_to(high[:, None, None], state[:, :1].shape),
+            jnp.broadcast_to(low[:, None, None], state[:, :1].shape),
+        ],
+        1,
+    )
+    got = lax.ppermute(packed, axis, shift_pairs(count, 2, 1))
     got, kv_next = lax.optimization_barrier((got, ring_step()))
     ring.append(kv_next)
-    wide = join_states(got, wide)
-    got = lax.ppermute(wide[1], axis, shift_pairs(count, 4, 1))
+    got_gain = got[:, rows, 0].astype(jnp.float32) + got[:, rows + 1, 0].astype(jnp.float32)
+    wide_state = got[:, :rows].astype(jnp.float32) * wide_gain[:, None, None] + wide_state
+    wide_gain = got_gain * wide_gain
+    got = lax.ppermute(wide_state.astype(jnp.bfloat16), axis, shift_pairs(count, 4, 1))
     got, kv_next = lax.optimization_barrier((got, ring_step()))
     ring.append(kv_next)
-    wide_state = got * wide[0][:, None, None] + wide[1]
+    wide_state = got.astype(jnp.float32) * wide_gain[:, None, None] + wide_state
     mine = jnp.stack(ring[:half])
     sent = jnp.where(core == 1, jnp.stack(ring[1:half]), jnp.stack(ring[: half - 1]))
     running = take(running, range(0, width, 2), mine)
-    before = lax.ppermute(wide_state, axis, shift_pairs(count, 1, 1))
+    before = lax.ppermute(wide_state.astype(jnp.bfloat16), axis, shift_pairs(count, 1, 1))
     before, kv_next, theirs, running = lax.optimization_barrier(
         (before, ring_step(1), lax.ppermute(sent, axis, swap), running)
     )
     ring.append(kv_next)
     last = jnp.where(core == 1, ring[half], ring[half - 1])
     running = take(running, range(1, width - 2, 2), theirs)
-    after = (before * element[0][:, None, None] + element[1]).astype(jnp.bfloat16)
+    after = (before.astype(jnp.float32) * gain[:, None, None] + state).astype(jnp.bfloat16)
     after, last, running = lax.optimization_barrier(
         (
             lax.ppermute(after, axis, shift_pairs(count, 1, 0)),
@@ -65,25 +77,7 @@
         )
     )
     running = take(running, [width - 1], last[None])
-    state = jnp.where(core == 0, before.astype(jnp.bfloat16), after)
-    return state, running
-
-
-def sum_over(x, axis):
-    count, here = (lax.axis_size(axis), lax.axis_index(axis))
-    parts = [x] + [
-        lax.ppermute(x, axis, [(i, (i + by) % count) for i in range(count)])
-        for by in range(1, count)
-    ]
-    ordered = jnp.take(jnp.stack(parts), (here - jnp.arange(count)) % count, axis=0)
-    total = ordered[0]
-    for k in range(1, count):
-        total = total + ordered[k]
-    return total
-
-
-def join_states(earlier, later):
-    return (earlier[0] * later[0], earlier[1] * later[0][:, None, None] + later[1])
+    return jnp.where(core == 0, before, after), running
 
 
 def token_segments(segment_ids, row_start, tok_rows):
@@ -195,7 +189,7 @@
         * reach_gain.T[:, :, None]
     )
     mixed = (intra_part + inter_part).reshape(tok_rows, -1)
-    square_sum = sum_over(jnp.sum(mixed * mixed, axis=1), "head")
+    square_sum = lax.psum(jnp.sum(mixed * mixed, axis=1), "head")
     inv_norm = lax.rsqrt(square_sum / (LIGHTNING_HEADS * HEAD_DIM) + 1e-06)
     light_out = (mixed * inv_norm[:, None] * light_gain).astype(jnp.bfloat16)
     row_max, row_mass, weighted = running

time: 104 us -> 93.2 us (0.90)
  starting transfers between devices: 32.5 us -> 20.3 us
  blocking collectives: 0 us -> 10.5 us
  waiting for transfers between devices: 29.9 us -> 20.7 us
  other arithmetic: 9.06 us -> 12.9 us
  local copies, waits for them, and re-layouts: 16.8 us -> 13.7 us
    ppermute x9 -> x4, starting transfers between devices: 17.3 us -> 5.07 us  [the longest x1 1.76 us: exchange(): got = lax.ppermute(packed, axis, shift_pairs(count, 1, 0))]
    psum x0 -> x1, blocking collectives: none -> 10.5 us  [body(): square_sum = lax.psum(jnp.sum(mixed * mixed, axis=1), 'head')]
    ppermute x4, waiting for transfers between devices: 29.1 us -> 20.7 us  [ring_step(): return lax.ppermute(ring[-1], axis, shift_pairs(count, 2, parity))]
    convert_element_type x1 -> x5, other arithmetic: 0.14 us -> 3.13 us  [the longest x3 2.84 us: exchange(): wide_state.astype(jnp.bfloat16)]
    add x3 -> x0, other arithmetic: 2.21 us -> none  [the longest x1 1.97 us: exchange(): wide_state = got * wide[0][:, None, None] + wide[1]]
    slice x4, local copies, waits for them, and re-layouts: 2.18 us -> 0.28 us  [take(): value_rows = chosen[:, 1].reshape(-1, kv_heads, HEAD_DIM)]
    unnamed x20 -> x44, local copies, waits for them, and re-layouts: 5.64 us -> 4 us
  transfers between devices with their start and end apart: 16 -> 11, of which waited for: 4 -> 3; matrix products, arithmetic and copies ran while one was open for 24% -> 21% of each run, Pallas kernels for 0% -> 0%
where the time goes in v5:
time: 93.2 us; the launch traced here: 92.6 us
  waiting for transfers between devices  20.7 us (22%)
  starting transfers between devices  20.3 us (22%)
  local copies, waits for them, and re-layouts  13.7 us (15%)
  other arithmetic  12.9 us (14%)
  matrix products  10.5 us (11%)
  blocking collectives  10.5 us (11%)
  between operations  4 us (4%)
    ppermute x4, waiting for transfers between devices, ring_step(): return lax.ppermute(ring[-1], axis, shift_pairs(count, 2, parity))  20.7 us
    psum x1, blocking collectives, body(): square_sum = lax.psum(jnp.sum(mixed * mixed, axis=1), 'head')  10.5 us
    ppermute x4, starting transfers between devices, ring_step(): return lax.ppermute(ring[-1], axis, shift_pairs(count, 2, parity))  8.32 us
    dot_general x3, matrix products, absorb(): jnp.einsum('tkgs,skd->tkgd', exponent.astype(jnp.bfloat16), value_rows, p...  6.55 us
    reshape x7, local copies, waits for them, and re-layouts, token_segments(): return jnp.repeat(blocks, BLOCK)  4.33 us
    unnamed x44, local copies, waits for them, and re-layouts  4 us
    ppermute x1, starting transfers between devices, exchange(): lax.ppermute(sent, axis, swap)  3.07 us
    convert_element_type x3, other arithmetic, exchange(): wide_state.astype(jnp.bfloat16)  2.84 us
  transfers between devices with their start and end apart: 11, of which 3 were waited for; matrix products, arithmetic and copies ran while one was open for 21% of the time, Pallas kernels for 0%

profile of v5, /device:TPU:24, one launch (start us, length us, event | category | flops | bytes accessed | tf_op | source)
XLA Modules:
  0.0 92.6 jit_solution(17239464452166800069)
XLA Ops:
  0.8 1.0 %reduce_window_sum.11 = f32[8,128]{1,0:T(8,128)S(1)} reduce-window(f32[8,128]{1,0:T(8,128)} %param.12, f32[]{:T(128)} %constant.128.clone.1), window={size=1x128 pad=0_0x127_0}, to_apply=%region_0.1 | reduce-window | flops 130048 | bytes 8196 | tf_op jit(solution)/shard_map/jit(cumsum)/reduce_window_sum | solution.py:94
  1.8 1.7 %fusion.87 = (s32[1]{0:T(128)}, s32[1]{0:T(128)}, s32[1]{0:T(128)}, s32[1]{0:T(128)}, s32[1]{0:T(128)}, /*index=5*/s32[1]{0:T(128)}, s32[1]{0:T(128)}, s32[1]{0:T(128)}, s32[1]{0:T(128)}, s32[1]{0:T(128)}) fusion(s32[128]{0:T(128)} %param.17, s32[]{:T(128)S(6)} %select_n.180, s32[]{:T(128)S(6)} %select_n.172, s32[]{:T(128)S(6)} %select_n.170, ...), kind=kLoop, calls=%fused_computation.128 | loop fusion | bytes 120 | tf_op jit(solution)/shard_map/dynamic_slice | solution.py:84
  5.5 1.1 %copy.99 = bf16[128,1024]{0,1:T(8,128)(2,1)S(1)} copy(bf16[128,1024]{1,0:T(8,128)(2,1)} %param.10) | data formatting | bytes 524288 | tf_op jit(solution)/shard_map/reshape | solution.py:92
  7.0 0.9 copy.57
  7.9 1.8 %collective-permute-start = (f32[8,129,128]{2,0,1:T(8,128)}, f32[8,129,128]{2,0,1:T(8,128)S(1)}, u32[]{:S(2)}, u32[]{:S(2)}) collective-permute-start(f32[8,129,128]{2,0,1:T(8,128)} %copy.57), channel_id=1, source_target_pairs={{0,4},{8,12},{16,20},{24,28},{32,36},{40,44},{48,52},{56,60},{64,6... | collective-permute-start | bytes 1585160 | tf_op jit(solution)/shard_map/ppermute | solution.py:36
  9.9 3.8 %collective-permute-start.1 = (bf16[2,128,256]{1,2,0:T(8,128)(2,1)S(1)}, bf16[2,128,256]{1,2,0:T(8,128)(2,1)S(1)}, u32[]{:S(2)}, u32[]{:S(2)}) collective-permute-start(bf16[2,128,256]{1,2,0:T(8,128)(2,1)S(1)} %get-tuple-element.64), channel_id=1, source_target_pairs={{0,8},{4,12},{8,16},{12,20},{16,24},{20,28},{24,32},{28,36},{32,40... | collective-permute-start | bytes 393224 | tf_op jit(solution)/shard_map/ppermute | solution.py:31
  18.2 0.7 reshape.309
  19.8 4.7 %collective-permute-done.1 = bf16[2,128,256]{1,2,0:T(8,128)(2,1)S(1)} collective-permute-done((bf16[2,128,256]{1,2,0:T(8,128)(2,1)S(1)}, bf16[2,128,256]{1,2,0:T(8,128)(2,1)S(1)}, u32[]{:S(2)}, u32[]{:S(2)}) %collective-permute-start.1) | collective-permute-done | bytes 131104 | tf_op jit(solution)/shard_map/ppermute | solution.py:31
  25.1 0.7 collective-permute-start.2
  26.1 1.9 %collective-permute-start.3 = (bf16[2,128,256]{1,2,0:T(8,128)(2,1)S(1)}, bf16[2,128,256]{1,2,0:T(8,128)(2,1)S(1)}, u32[]{:S(2)}, u32[]{:S(2)}) collective-permute-start(bf16[2,128,256]{1,2,0:T(8,128)(2,1)S(1)} %collective-permute-done.1), channel_id=1, source_target_pairs={{0,8},{4,12},{8,16},{12,20},{16,24},{20,28},{24,32},{28,36},{32,40... | collective-permute-start | bytes 393224 | tf_op jit(solution)/shard_map/ppermute | solution.py:31
  29.3 7.0 %collective-permute-done.3 = bf16[2,128,256]{1,2,0:T(8,128)(2,1)S(1)} collective-permute-done((bf16[2,128,256]{1,2,0:T(8,128)(2,1)S(1)}, bf16[2,128,256]{1,2,0:T(8,128)(2,1)S(1)}, u32[]{:S(2)}, u32[]{:S(2)}) %collective-permute-start.3) | collective-permute-done | bytes 131104 | tf_op jit(solution)/shard_map/ppermute | solution.py:31
  37.0 0.8 fusion.47
  37.8 1.4 %collective-permute-start.4 = (bf16[8,128,128]{2,1,0:T(8,128)(2,1)}, bf16[8,128,128]{2,1,0:T(8,128)(2,1)}, u32[]{:S(2)}, u32[]{:S(2)}) collective-permute-start(bf16[8,128,128]{2,1,0:T(8,128)(2,1)} %fusion.47), channel_id=1, source_target_pairs={{4,20},{12,28},{20,36},{28,44},{36,52},{44,60},{52,68},{60,76},{68... | collective-permute-start | bytes 786440 | tf_op jit(solution)/shard_map/ppermute | solution.py:57
  39.2 1.9 %collective-permute-start.5 = (bf16[2,128,256]{1,2,0:T(8,128)(2,1)S(1)}, bf16[2,128,256]{1,2,0:T(8,128)(2,1)S(1)}, u32[]{:S(2)}, u32[]{:S(2)}) collective-permute-start(bf16[2,128,256]{1,2,0:T(8,128)(2,1)S(1)} %collective-permute-done.3), channel_id=1, source_target_pairs={{0,8},{4,12},{8,16},{12,20},{16,24},{20,28},{24,32},{28,36},{32,40... | collective-permute-start | bytes 393224 | tf_op jit(solution)/shard_map/ppermute | solution.py:31
  41.1 0.8 and_and_fusion.2
  42.6 9.0 %collective-permute-done.5 = bf16[2,128,256]{1,2,0:T(8,128)(2,1)S(1)} collective-permute-done((bf16[2,128,256]{1,2,0:T(8,128)(2,1)S(1)}, bf16[2,128,256]{1,2,0:T(8,128)(2,1)S(1)}, u32[]{:S(2)}, u32[]{:S(2)}) %collective-permute-start.5) | collective-permute-done | bytes 131104 | tf_op jit(solution)/shard_map/ppermute | solution.py:31
  51.6 1.9 %add_convert_fusion.1 = bf16[8,128,128]{2,1,0:T(8,128)(2,1)} fusion(bf16[8,128,128]{2,1,0:T(8,128)(2,1)} %collective-permute-done.4, f32[8,128,128]{2,1,0:T(8,128)S(1)} %get-tuple-element.53, f32[8]{0:T(128)} %get-tuple-element.42, f32[8]{0:T(128)} %copy-done.16, bf16[8,130,128]{2,1,0:T(8,128)(2,1)S(1)} %collective-permute-done.2), kind=kLoop, calls=%fused_computation.46 | loop fusion | flops 917504 | bytes 1310784 | tf_op jit(solution)/shard_map/convert_element_type | solution.py:64
  53.5 1.3 %collective-permute-start.6 = (bf16[8,128,128]{2,1,0:T(8,128)(2,1)}, bf16[8,128,128]{2,1,0:T(8,128)(2,1)S(1)}, u32[]{:S(2)}, u32[]{:S(2)}) collective-permute-start(bf16[8,128,128]{2,1,0:T(8,128)(2,1)} %add_convert_fusion.1), channel_id=1, source_target_pairs={{4,8},{12,16},{20,24},{28,32},{36,40},{44,48},{52,56},{60,64},{68,... | collective-permute-start | bytes 786440 | tf_op jit(solution)/shard_map/ppermute | solution.py:64
  54.8 0.7 collective-permute-start.7
  55.5 0.8 maximum_select_fusion
  56.3 3.1 %collective-permute-start.8 = (bf16[3,2,128,256]{2,3,1,0:T(8,128)(2,1)}, bf16[3,2,128,256]{2,3,1,0:T(8,128)(2,1)S(1)}, u32[]{:S(2)}, u32[]{:S(2)}) collective-permute-start(bf16[3,2,128,256]{2,3,1,0:T(8,128)(2,1)} %maximum_select_fusion), channel_id=1, source_target_pairs={{0,4},{4,0},{8,12},{12,8},{16,20},{20,16},{24,28},{28,24},{32,36},... | collective-permute-start | bytes 1179656 | tf_op jit(solution)/shard_map/ppermute | solution.py:66
  59.7 0.8 fusion.2
  60.5 1.9 %copy-done.1 = f32[2,512,128,8]{2,1,3,0:T(8,128)} copy-done((f32[2,512,128,8]{2,1,3,0:T(8,128)}, f32[2,512,128,8]{2,1,3,0:T(8,128)S(1)}, u32[]{:S(2)}) %copy-start.1) | copy-done | bytes 4194328
  62.4 0.9 fusion.1
  64.3 4.3 %fusion.26 = f32[128,2,8,128]{0,3,2,1:T(8,128)} fusion(f32[2,512,128,8]{2,1,3,0:T(8,128)} %copy-done.1, f32[128,2,8]{0,2,1:T(8,128)S(1)} %broadcast_maximum_fusion, pred[128,512]{0,1:T(8,128)(4,1)S(1)} %and_and_fusion, f32[128,2,8]{0,2,1:T(8,128)S(1)} %get-tuple-element.65, bf16[512,2,128,1]{0,2,1,3:T(8,128)(2,1)S(1)} %reshape.319), kind=kOutput, calls=%fused_computation.26 | convolution fusion | flops 272891904 | bytes 5586944 | tf_op jit(solution)/shard_map/tkgs,skd->tkgd/dot_general | solution.py:128
  68.7 1.9 %collective-permute-start.9 = (bf16[8,128,128]{2,1,0:T(8,128)(2,1)S(1)}, bf16[8,128,128]{2,1,0:T(8,128)(2,1)S(1)}, u32[]{:S(2)}, u32[]{:S(2)}) collective-permute-start(bf16[8,128,128]{2,1,0:T(8,128)(2,1)S(1)} %add_convert_fusion), channel_id=1, source_target_pairs={{0,4},{8,12},{16,20},{24,28},{32,36},{40,44},{48,52},{56,60},{64,6... | collective-permute-start | bytes 786440 | tf_op jit(solution)/shard_map/ppermute | solution.py:74
  70.7 1.9 %collective-permute-start.10 = (bf16[2,128,256]{1,2,0:T(8,128)(2,1)S(1)}, bf16[2,128,256]{1,2,0:T(8,128)(2,1)S(1)}, u32[]{:S(2)}, u32[]{:S(2)}) collective-permute-start(bf16[2,128,256]{1,2,0:T(8,128)(2,1)S(1)} %broadcast_select_fusion), channel_id=1, source_target_pairs={{0,4},{4,0},{8,12},{12,8},{16,20},{20,16},{24,28},{28,24},{32,36},... | collective-permute-start | bytes 393224 | tf_op jit(solution)/shard_map/ppermute | solution.py:75
  74.6 1.9 %multiply_add_fusion = f32[128,2,8,128]{0,3,2,1:T(8,128)} fusion(f32[128,2,8,128]{0,3,2,1:T(8,128)S(1)} %copy-done.2, f32[128,2,8]{0,2,1:T(8,128)S(1)} %get-tuple-element.49, f32[2,384,128,8]{2,1,3,0:T(8,128)S(1)} %get-tuple-element.83, f32[128,2,8]{0,2,1:T(8,128)S(1)} %max.38, pred[128,384]{0,1:T(8,128)(4,1)S(1)} %and_and_fusion.1, ...), kind=kOutput, calls=%fused_computation.35 | convolution fusion | flops 204996608 | bytes 5505024 | tf_op jit(solution)/shard_map/tkgs,skd->tkgd/dot_general | solution.py:128
  77.6 1.6 %multiply_reduce_fusion = (f32[128]{0:T(128)S(1)}, f32[128,8,128]{0,2,1:T(8,128)S(1)}) fusion(f32[128,8,128]{0,2,1:T(8,128)S(1)} %fusion.30, bf16[128,8,128]{0,2,1:T(8,128)(2,1)S(1)} %bitcast.152, f32[8,128]{1,0:T(8,128)S(1)} %copy-done.11, pred[128,128]{1,0:T(8,128)(4,1)S(1)} %copy-done.14, bf16[128,1024]{1,0:T(8,128)(2,1)S(1)} %copy-done, ...), kind=kOutput, calls=%fused_computation.44 | convolution fusion | flops 68026240 | bytes 1856000 | tf_op jit(solution)/shard_map/hts,shd->thd/dot_general | solution.py:100
  79.4 10.5 %psum.7 = f32[128]{0:T(128)S(1)} all-reduce(f32[128]{0:T(128)S(1)} %get-tuple-element.84), channel_id=1, replica_groups=mesh['grp'=4,'seq'=32,'head'=4] {'head'}, use_global_device_ids=true, to_apply=%region_6.7 | all-reduce | flops 128 | bytes 1024 | tf_op jit(solution)/shard_map/psum | solution.py:192
  90.8 1.0 %copy.80 = bf16[128,2048]{1,0:T(8,128)(2,1)} copy(bf16[128,2048]{0,1:T(8,128)(2,1)S(1)} %bitcast.156) | data formatting | bytes 1048576
  91.8 0.8 multiply_convert_fusion
  (113 shorter events, 14.3 us)
Async XLA Ops:
  0.6 6.0 %copy-start = (bf16[128,1024]{1,0:T(8,128)(2,1)S(1)}, bf16[128,1024]{1,0:T(8,128)(2,1)}, u32[]{:S(2)}) copy-start(bf16[128,1024]{1,0:T(8,128)(2,1)} %param.11) | copy-start | bytes 786436
  0.6 9.0 %copy-start.8 = (bf16[128,256]{1,0:T(8,128)(2,1)S(1)}, bf16[128,256]{1,0:T(8,128)(2,1)}, u32[]{:S(2)}) copy-start(bf16[128,256]{1,0:T(8,128)(2,1)} %param.16) | copy-start | bytes 196612
  0.7 9.1 %copy-start.9 = (bf16[128,256]{1,0:T(8,128)(2,1)S(1)}, bf16[128,256]{1,0:T(8,128)(2,1)}, u32[]{:S(2)}) copy-start(bf16[128,256]{1,0:T(8,128)(2,1)} %param.15) | copy-start | bytes 196612
  1.8 3.1 %copy-start.10 = (f32[8,128]{1,0:T(8,128)}, f32[8,128]{1,0:T(8,128)S(1)}, u32[]{:S(2)}) copy-start(f32[8,128]{1,0:T(8,128)S(1)} %reduce_window_sum.11) | copy-start | bytes 12292
  7.0 34.9 %copy-start.4 = (bf16[128,2048]{1,0:T(8,128)(2,1)S(1)}, bf16[128,2048]{1,0:T(8,128)(2,1)}, u32[]{:S(2)}) copy-start(bf16[128,2048]{1,0:T(8,128)(2,1)} %param.14) | copy-start | bytes 1572868
  7.9 16.6 %collective-permute-start = (f32[8,129,128]{2,0,1:T(8,128)}, f32[8,129,128]{2,0,1:T(8,128)S(1)}, u32[]{:S(2)}, u32[]{:S(2)}) collective-permute-start(f32[8,129,128]{2,0,1:T(8,128)} %copy.57), channel_id=1, source_target_pairs={{0,4},{8,12},{16,20},{24,28},{32,36},{40,44},{48,52},{56,60},{64,6... | collective-permute-start | bytes 1585160 | tf_op jit(solution)/shard_map/ppermute | solution.py:36
  9.9 14.6 %collective-permute-start.1 = (bf16[2,128,256]{1,2,0:T(8,128)(2,1)S(1)}, bf16[2,128,256]{1,2,0:T(8,128)(2,1)S(1)}, u32[]{:S(2)}, u32[]{:S(2)}) collective-permute-start(bf16[2,128,256]{1,2,0:T(8,128)(2,1)S(1)} %get-tuple-element.64), channel_id=1, source_target_pairs={{0,8},{4,12},{8,16},{12,20},{16,24},{20,28},{24,32},{28,36},{32,40... | collective-permute-start | bytes 393224 | tf_op jit(solution)/shard_map/ppermute | solution.py:31
  13.8 11.4 %copy-start.18 = (f32[8]{0:T(128)}, f32[8]{0:T(128)S(1)}, u32[]{:S(2)}) copy-start(f32[8]{0:T(128)S(1)} %broadcast_select_fusion.1) | copy-start | bytes 100
  13.8 12.2 %copy-start.15 = (s32[128]{0:T(128)}, s32[128]{0:T(128)S(1)}, u32[]{:S(2)}) copy-start(s32[128]{0:T(128)S(1)} %get-tuple-element.91) | copy-start | bytes 1540
  25.1 11.2 %collective-permute-start.2 = (bf16[8,130,128]{2,1,0:T(8,128)(2,1)S(1)}, bf16[8,130,128]{2,1,0:T(8,128)(2,1)S(1)}, u32[]{:S(2)}, u32[]{:S(2)}) collective-permute-start(bf16[8,130,128]{2,1,0:T(8,128)(2,1)S(1)} %pad_maximum_fusion.2), channel_id=1, source_target_pairs={{4,12},{12,20},{20,28},{28,36},{36,44},{44,52},{52,60},{60,68},{68... | collective-permute-start | bytes 798728 | tf_op jit(solution)/shard_map/ppermute | solution.py:51
  26.1 10.2 %collective-permute-start.3 = (bf16[2,128,256]{1,2,0:T(8,128)(2,1)S(1)}, bf16[2,128,256]{1,2,0:T(8,128)(2,1)S(1)}, u32[]{:S(2)}, u32[]{:S(2)}) collective-permute-start(bf16[2,128,256]{1,2,0:T(8,128)(2,1)S(1)} %collective-permute-done.1), channel_id=1, source_target_pairs={{0,8},{4,12},{8,16},{12,20},{16,24},{20,28},{24,32},{28,36},{32,40... | collective-permute-start | bytes 393224 | tf_op jit(solution)/shard_map/ppermute | solution.py:31
  37.0 0.8 copy-start.16
  37.8 13.8 %collective-permute-start.4 = (bf16[8,128,128]{2,1,0:T(8,128)(2,1)}, bf16[8,128,128]{2,1,0:T(8,128)(2,1)}, u32[]{:S(2)}, u32[]{:S(2)}) collective-permute-start(bf16[8,128,128]{2,1,0:T(8,128)(2,1)} %fusion.47), channel_id=1, source_target_pairs={{4,20},{12,28},{20,36},{28,44},{36,52},{44,60},{52,68},{60,76},{68... | collective-permute-start | bytes 786440 | tf_op jit(solution)/shard_map/ppermute | solution.py:57
  39.2 12.4 %collective-permute-start.5 = (bf16[2,128,256]{1,2,0:T(8,128)(2,1)S(1)}, bf16[2,128,256]{1,2,0:T(8,128)(2,1)S(1)}, u32[]{:S(2)}, u32[]{:S(2)}) collective-permute-start(bf16[2,128,256]{1,2,0:T(8,128)(2,1)S(1)} %collective-permute-done.3), channel_id=1, source_target_pairs={{0,8},{4,12},{8,16},{12,20},{16,24},{20,28},{24,32},{28,36},{32,40... | collective-permute-start | bytes 393224 | tf_op jit(solution)/shard_map/ppermute | solution.py:31
  53.5 15.1 %collective-permute-start.6 = (bf16[8,128,128]{2,1,0:T(8,128)(2,1)}, bf16[8,128,128]{2,1,0:T(8,128)(2,1)S(1)}, u32[]{:S(2)}, u32[]{:S(2)}) collective-permute-start(bf16[8,128,128]{2,1,0:T(8,128)(2,1)} %add_convert_fusion.1), channel_id=1, source_target_pairs={{4,8},{12,16},{20,24},{28,32},{36,40},{44,48},{52,56},{60,64},{68,... | collective-permute-start | bytes 786440 | tf_op jit(solution)/shard_map/ppermute | solution.py:64
  54.8 13.8 %collective-permute-start.7 = (bf16[2,128,256]{1,2,0:T(8,128)(2,1)S(1)}, bf16[2,128,256]{1,2,0:T(8,128)(2,1)S(1)}, u32[]{:S(2)}, u32[]{:S(2)}) collective-permute-start(bf16[2,128,256]{1,2,0:T(8,128)(2,1)S(1)} %collective-permute-done.5), channel_id=1, source_target_pairs={{4,12},{12,20},{20,28},{28,36},{36,44},{44,52},{52,60},{60,68},{68... | collective-permute-start | bytes 393224 | tf_op jit(solution)/shard_map/ppermute | solution.py:31
  56.3 12.2 %collective-permute-start.8 = (bf16[3,2,128,256]{2,3,1,0:T(8,128)(2,1)}, bf16[3,2,128,256]{2,3,1,0:T(8,128)(2,1)S(1)}, u32[]{:S(2)}, u32[]{:S(2)}) collective-permute-start(bf16[3,2,128,256]{2,3,1,0:T(8,128)(2,1)} %maximum_select_fusion), channel_id=1, source_target_pairs={{0,4},{4,0},{8,12},{12,8},{16,20},{20,16},{24,28},{28,24},{32,36},... | collective-permute-start | bytes 1179656 | tf_op jit(solution)/shard_map/ppermute | solution.py:66
  60.5 1.9 %copy-start.1 = (f32[2,512,128,8]{2,1,3,0:T(8,128)}, f32[2,512,128,8]{2,1,3,0:T(8,128)S(1)}, u32[]{:S(2)}) copy-start(f32[2,512,128,8]{2,1,3,0:T(8,128)S(1)} %get-tuple-element.81) | copy-start | bytes 12582916
  64.2 4.3 %copy-start.19 = (f32[8]{0:T(128)S(1)}, f32[8]{0:T(128)}, u32[]{:S(2)}) copy-start(f32[8]{0:T(128)} %copy-done.18) | copy-start | bytes 100
  68.7 7.9 %collective-permute-start.9 = (bf16[8,128,128]{2,1,0:T(8,128)(2,1)S(1)}, bf16[8,128,128]{2,1,0:T(8,128)(2,1)S(1)}, u32[]{:S(2)}, u32[]{:S(2)}) collective-permute-start(bf16[8,128,128]{2,1,0:T(8,128)(2,1)S(1)} %add_convert_fusion), channel_id=1, source_target_pairs={{0,4},{8,12},{16,20},{24,28},{32,36},{40,44},{48,52},{56,60},{64,6... | collective-permute-start | bytes 786440 | tf_op jit(solution)/shard_map/ppermute | solution.py:74
  70.7 5.9 %collective-permute-start.10 = (bf16[2,128,256]{1,2,0:T(8,128)(2,1)S(1)}, bf16[2,128,256]{1,2,0:T(8,128)(2,1)S(1)}, u32[]{:S(2)}, u32[]{:S(2)}) collective-permute-start(bf16[2,128,256]{1,2,0:T(8,128)(2,1)S(1)} %broadcast_select_fusion), channel_id=1, source_target_pairs={{0,4},{4,0},{8,12},{12,8},{16,20},{20,16},{24,28},{28,24},{32,36},... | collective-permute-start | bytes 393224 | tf_op jit(solution)/shard_map/ppermute | solution.py:75
  73.2 1.3 %copy-start.12 = (f32[128,2,8]{0,2,1:T(8,128)S(1)}, f32[128,2,8]{0,2,1:T(8,128)}, u32[]{:S(2)}) copy-start(f32[128,2,8]{0,2,1:T(8,128)} %get-tuple-element.29) | copy-start | bytes 24580
  73.2 1.4 %copy-start.2 = (f32[128,2,8,128]{0,3,2,1:T(8,128)S(1)}, f32[128,2,8,128]{0,3,2,1:T(8,128)}, u32[]{:S(2)}) copy-start(f32[128,2,8,128]{0,3,2,1:T(8,128)} %fusion.26) | copy-start | bytes 3145732
  74.6 2.7 %copy-start.5 = (bf16[128,1024]{1,0:T(8,128)(2,1)S(1)}, bf16[128,1024]{1,0:T(8,128)(2,1)}, u32[]{:S(2)}) copy-start(bf16[128,1024]{1,0:T(8,128)(2,1)} %param.9) | copy-start | bytes 786436
  74.6 2.7 %copy-start.13 = (f32[128,8]{0,1:T(8,128)S(1)}, f32[128,8]{0,1:T(8,128)}, u32[]{:S(2)}) copy-start(f32[128,8]{0,1:T(8,128)} %get-tuple-element.69) | copy-start | bytes 12292
  74.6 3.0 %copy-start.11 = (f32[8,128]{1,0:T(8,128)S(1)}, f32[8,128]{1,0:T(8,128)}, u32[]{:S(2)}) copy-start(f32[8,128]{1,0:T(8,128)} %copy-done.10) | copy-start | bytes 12292
  74.6 3.0 %copy-start.14 = (pred[128,128]{1,0:T(8,128)(4,1)S(1)}, pred[128,128]{1,0:T(8,128)(4,1)}, u32[]{:S(2)}) copy-start(pred[128,128]{1,0:T(8,128)(4,1)} %iota_compare_fusion) | copy-start | bytes 49156
  76.6 0.7 copy-start.6
  77.2 12.6 %copy-start.7 = (bf16[2,128,256]{1,2,0:T(8,128)(2,1)S(1)}, bf16[2,128,256]{1,2,0:T(8,128)(2,1)}, u32[]{:S(2)}) copy-start(bf16[2,128,256]{1,2,0:T(8,128)(2,1)} %copy-done.6) | copy-start | bytes 393220
  77.6 12.9 %copy-start.3 = (f32[128,2,8,128]{0,3,2,1:T(8,128)S(1)}, f32[128,2,8,128]{0,3,2,1:T(8,128)}, u32[]{:S(2)}) copy-start(f32[128,2,8,128]{0,3,2,1:T(8,128)} %multiply_add_fusion) | copy-start | bytes 3145732
  90.4 1.4 %copy-start.17 = (f32[1024]{0:T(1024)S(1)}, f32[1024]{0:T(1024)}, u32[]{:S(2)}) copy-start(f32[1024]{0:T(1024)} %param.13) | copy-start | bytes 12292

commit v6 on v5

--- a/solution.py
+++ b/solution.py
@@ -23,61 +23,64 @@
 
 def exchange(element, kv_pair, axis, core, width, take, running):
     count = lax.axis_size(axis)
-    half = width // 2
     swap = [(i, i ^ 1) for i in range(count)]
     ring = [kv_pair]
 
-    def ring_step(parity=None):
-        return lax.ppermute(ring[-1], axis, shift_pairs(count, 2, parity))
+    def ring_step():
+        return lax.ppermute(ring[-1], axis, shift_pairs(count, 2))
 
     gain, state = element
     rows = state.shape[1]
-    packed = jnp.concatenate([state, jnp.broadcast_to(gain[:, None, None], state[:, :1].shape)], 1)
-    got = lax.ppermute(packed, axis, shift_pairs(count, 1, 0))
-    got, kv_next = lax.optimization_barrier((got, ring_step()))
+    row_of = lambda v: jnp.broadcast_to(v[:, None, None], state[:, :1].shape)
+    packed = jnp.concatenate([state, row_of(gain)], 1)
+    partner, kv_next = lax.optimization_barrier(
+        (lax.ppermute(packed, axis, shift_pairs(count, 1, 0)), ring_step())
+    )
     ring.append(kv_next)
-    wide_state = got[:, :rows] * gain[:, None, None] + state
-    wide_gain = got[:, rows, 0] * gain
+    partner_state, partner_gain = partner[:, :rows], partner[:, rows, 0]
+    wide_state = partner_state * gain[:, None, None] + state
+    wide_gain = partner_gain * gain
     high = wide_gain.astype(jnp.bfloat16)
     low = (wide_gain - high.astype(jnp.float32)).astype(jnp.bfloat16)
-    packed = jnp.concatenate(
-        [
-            wide_state.astype(jnp.bfloat16),
-            jnp.broadcast_to(high[:, None, None], state[:, :1].shape),
-            jnp.broadcast_to(low[:, None, None], state[:, :1].shape),
-        ],
-        1,
-    )
-    got = lax.ppermute(packed, axis, shift_pairs(count, 2, 1))
-    got, kv_next = lax.optimization_barrier((got, ring_step()))
+    packed = jnp.concatenate([wide_state.astype(jnp.bfloat16), row_of(high), row_of(low)], 1)
+    got, kv_next = lax.optimization_barrier(
+        (lax.ppermute(packed, axis, shift_pairs(count, 2, 1)), ring_step())
+    )
     ring.append(kv_next)
     got_gain = got[:, rows, 0].astype(jnp.float32) + got[:, rows + 1, 0].astype(jnp.float32)
     wide_state = got[:, :rows].astype(jnp.float32) * wide_gain[:, None, None] + wide_state
     wide_gain = got_gain * wide_gain
-    got = lax.ppermute(wide_state.astype(jnp.bfloat16), axis, shift_pairs(count, 4, 1))
-    got, kv_next = lax.optimization_barrier((got, ring_step()))
+    sent = jnp.where(core == 1, jnp.stack(ring[1:3]), jnp.stack(ring[0:2]))
+    running = take(running, [0, 2, 4], jnp.stack(ring[0:3]))
+    got, kv_next, theirs, running = lax.optimization_barrier(
+        (
+            lax.ppermute(wide_state.astype(jnp.bfloat16), axis, shift_pairs(count, 4, 1)),
+            ring_step(),
+            lax.ppermute(sent, axis, swap),
+            running,
+        )
+    )
     ring.append(kv_next)
-    wide_state = got.astype(jnp.float32) * wide_gain[:, None, None] + wide_state
-    mine = jnp.stack(ring[:half])
-    sent = jnp.where(core == 1, jnp.stack(ring[1:half]), jnp.stack(ring[: half - 1]))
-    running = take(running, range(0, width, 2), mine)
-    before = lax.ppermute(wide_state.astype(jnp.bfloat16), axis, shift_pairs(count, 1, 1))
-    before, kv_next, theirs, running = lax.optimization_barrier(
-        (before, ring_step(1), lax.ppermute(sent, axis, swap), running)
-    )
-    ring.append(kv_next)
-    last = jnp.where(core == 1, ring[half], ring[half - 1])
-    running = take(running, range(1, width - 2, 2), theirs)
-    after = (before.astype(jnp.float32) * gain[:, None, None] + state).astype(jnp.bfloat16)
-    after, last, running = lax.optimization_barrier(
+    outgoing = (got.astype(jnp.float32) * wide_gain[:, None, None] + wide_state).astype(jnp.bfloat16)
+    cross = jnp.concatenate([outgoing.reshape(-1, HEAD_DIM), ring[3].reshape(-1, HEAD_DIM)])
+    sent = jnp.where(core == 1, jnp.stack([ring[3], ring[3]]), jnp.stack(ring[2:4]))
+    running = take(running, [6, 1, 3], jnp.concatenate([ring[3][None], theirs]))
+    cross, ahead, theirs, running = lax.optimization_barrier(
         (
-            lax.ppermute(after, axis, shift_pairs(count, 1, 0)),
-            lax.ppermute(last, axis, swap),
+            lax.ppermute(cross, axis, shift_pairs(count, 1, 1)),
+            lax.ppermute(outgoing, axis, shift_pairs(count, 2, 1)),
+            lax.ppermute(sent, axis, swap),
             running,
         )
     )
-    running = take(running, [width - 1], last[None])
-    return jnp.where(core == 0, before, after), running
+    split = outgoing.size // HEAD_DIM
+    behind = cross[:split].reshape(outgoing.shape)
+    after = ahead.astype(jnp.float32) * partner_gain[:, None, None] + partner_state
+    last = jnp.where(
+        core == 0, jnp.stack([theirs[0], cross[split:].reshape(kv_pair.shape)]), theirs
+    )
+    running = take(running, [5, 7], last)
+    return jnp.where(core == 0, behind, after.astype(jnp.bfloat16)), running
 
 
 def token_segments(segment_ids, row_start, tok_rows):

time: 93.2 us -> 103 us (1.11)
  waiting for transfers between devices: 20.7 us -> 10 us
  other arithmetic: 12.9 us -> 22.2 us
  local copies, waits for them, and re-layouts: 13.7 us -> 19.1 us
  matrix products: 10.5 us -> 13.8 us
  starting transfers between devices: 20.3 us -> 22.9 us
  between operations: 4 us -> 2.73 us
    ppermute x9 -> x7, waiting for transfers between devices: 20.7 us -> 10 us  [the longest x3 10 us: ring_step(): return lax.ppermute(ring[-1], axis, shift_pairs(count, 2))]
    ppermute x1 -> x2, starting transfers between devices: 3.07 us -> 8.82 us  [exchange(): lax.ppermute(sent, axis, swap)]
    concatenate x2 -> x4, other arithmetic: 0.07 us -> 3.48 us  [the longest x1 1.72 us: exchange(): jnp.concatenate([outgoing.reshape(-1, HEAD_DIM), ring[3].reshape(-1, HEAD...]
    slice x3 -> x4, local copies, waits for them, and re-layouts: 0.29 us -> 3.48 us  [the longest x1 0.97 us: exchange(): behind = cross[:split].reshape(outgoing.shape)]
    ppermute x9 -> x7, starting transfers between devices: 15.9 us -> 12.8 us  [the longest x3 7.64 us: ring_step(): return lax.ppermute(ring[-1], axis, shift_pairs(count, 2))]
    another operation x3, local copies, waits for them, and re-layouts: 0.45 us -> 3.33 us  [take(): value_rows = chosen[:, 1].reshape(-1, kv_heads, HEAD_DIM)]
    select_n x2 -> x4, other arithmetic: 0.83 us -> 3.39 us  [the longest x1 1.64 us: exchange(): sent = jnp.where(core == 1, jnp.stack(ring[1:3]), jnp.stack(ring[0:2]))]
    dot_general x3, matrix products: 1.8 us -> 3.96 us  [absorb(): jnp.einsum('tkgd,skd->tkgs', queries, key_rows, preferred_element_type=jn...]
  transfers between devices with their start and end apart: 11 -> 10, of which waited for: 3 -> 2; matrix products, arithmetic and copies ran while one was open for 21% -> 36% of each run, Pallas kernels for 0% -> 0%
where the time goes in v6:
time: 103 us; the launch traced here: 101 us
  starting transfers between devices  22.9 us (22%)
  other arithmetic  22.2 us (22%)
  local copies, waits for them, and re-layouts  19.1 us (19%)
  matrix products  13.8 us (13%)
  blocking collectives  10.5 us (10%)
  waiting for transfers between devices  10 us (10%)
  between operations  2.73 us (3%)
    psum x1, blocking collectives, body(): square_sum = lax.psum(jnp.sum(mixed * mixed, axis=1), 'head')  10.5 us
    ppermute x3, waiting for transfers between devices, ring_step(): return lax.ppermute(ring[-1], axis, shift_pairs(count, 2))  10 us
    ppermute x2, starting transfers between devices, exchange(): lax.ppermute(sent, axis, swap)  8.82 us
    ppermute x3, starting transfers between devices, ring_step(): return lax.ppermute(ring[-1], axis, shift_pairs(count, 2))  7.64 us
    dot_general x3, matrix products, absorb(): jnp.einsum('tkgs,skd->tkgd', exponent.astype(jnp.bfloat16), value_rows, p...  6.62 us
    reshape x7, local copies, waits for them, and re-layouts, token_segments(): return jnp.repeat(blocks, BLOCK)  4.32 us
    dot_general x3, matrix products, absorb(): jnp.einsum('tkgd,skd->tkgs', queries, key_rows, preferred_element_type=jn...  3.96 us
    another operation x3, local copies, waits for them, and re-layouts, take(): value_rows = chosen[:, 1].reshape(-1, kv_heads, HEAD_DIM)  3.33 us
  transfers between devices with their start and end apart: 10, of which 2 were waited for; matrix products, arithmetic and copies ran while one was open for 36% of the time, Pallas kernels for 0%

profile of v6, /device:TPU:24, one launch (start us, length us, event | category | flops | bytes accessed | tf_op | source)
XLA Modules:
  0.0 101.4 jit_solution(1524966912720622625)
XLA Ops:
  0.8 1.1 %copy.96 = bf16[128,1024]{0,1:T(8,128)(2,1)S(1)} copy(bf16[128,1024]{1,0:T(8,128)(2,1)} %param.10) | data formatting | bytes 524288 | tf_op jit(solution)/shard_map/reshape | solution.py:95
  3.0 1.7 %fusion.90 = (s32[1]{0:T(128)}, s32[1]{0:T(128)}, s32[1]{0:T(128)}, s32[1]{0:T(128)}, s32[1]{0:T(128)}, /*index=5*/s32[1]{0:T(128)}, s32[1]{0:T(128)}, s32[1]{0:T(128)}, s32[1]{0:T(128)}, s32[1]{0:T(128)}) fusion(s32[128]{0:T(128)} %param.17, s32[]{:T(128)S(6)} %select_n.180, s32[]{:T(128)S(6)} %select_n.172, s32[]{:T(128)S(6)} %select_n.170, ...), kind=kLoop, calls=%fused_computation.139 | loop fusion | bytes 120 | tf_op jit(solution)/shard_map/dynamic_slice | solution.py:87
  6.7 1.8 %collective-permute-start = (f32[8,129,128]{2,0,1:T(8,128)S(1)}, f32[8,129,128]{2,0,1:T(8,128)S(1)}, u32[]{:S(2)}, u32[]{:S(2)}) collective-permute-start(f32[8,129,128]{2,0,1:T(8,128)S(1)} %copy.53), channel_id=1, source_target_pairs={{0,4},{8,12},{16,20},{24,28},{32,36},{40,44},{48,52},{56,60},{64,6... | collective-permute-start | bytes 1585160 | tf_op jit(solution)/shard_map/ppermute | solution.py:37
  8.5 3.8 %collective-permute-start.1 = (bf16[2,128,256]{2,1,0:T(8,128)(2,1)S(1)}, bf16[2,128,256]{2,1,0:T(8,128)(2,1)S(1)}, u32[]{:S(2)}, u32[]{:S(2)}) collective-permute-start(bf16[2,128,256]{2,1,0:T(8,128)(2,1)S(1)} %get-tuple-element.60), channel_id=1, source_target_pairs={{0,8},{4,12},{8,16},{12,20},{16,24},{20,28},{24,32},{28,36},{32,40... | collective-permute-start | bytes 393224 | tf_op jit(solution)/shard_map/ppermute | solution.py:30
  17.6 1.3 %pad_compare_fusion = pred[256]{0:T(512)(128)(4,1)S(1)} fusion(s32[128]{0:T(128)S(1)} %reshape.341, s32[]{:T(128)} %bitcast.31, s32[]{:T(128)} %bitcast.2), kind=kLoop, calls=%fused_computation.114 | loop fusion | flops 256 | bytes 776 | tf_op jit(solution)/shard_map/eq | solution.py:178
  18.8 1.1 %and_and_fusion = (pred[128,384]{0,1:T(8,128)(4,1)}, pred[128,384]{0,1:T(8,128)(4,1)}) fusion(s32[128]{0:T(128)S(1)} %iota_add_fusion.7, s32[384]{0:T(512)S(1)} %pad_add_fusion.1, pred[384]{0:T(512)(128)(4,1)S(1)} %get-tuple-element.87, pred[384]{0:T(512)(128)(4,1)S(1)} %broadcast_compare_fusion, pred[384]{0:T(512)(128)(4,1)S(1)} %get-tuple-element.86, ...), kind=kLoop, calls=%fused_computation.87 | loop fusion | flops 294912 | bytes 103424 | tf_op jit(solution)/shard_map/and | solution.py:176
  20.0 3.1 %collective-permute-done.1 = bf16[2,128,256]{2,1,0:T(8,128)(2,1)S(1)} collective-permute-done((bf16[2,128,256]{2,1,0:T(8,128)(2,1)S(1)}, bf16[2,128,256]{2,1,0:T(8,128)(2,1)S(1)}, u32[]{:S(2)}, u32[]{:S(2)}) %collective-permute-start.1) | collective-permute-done | bytes 131104 | tf_op jit(solution)/shard_map/ppermute | solution.py:30
  25.2 1.9 %collective-permute-start.3 = (bf16[2,128,256]{2,1,0:T(8,128)(2,1)S(1)}, bf16[2,128,256]{2,1,0:T(8,128)(2,1)}, u32[]{:S(2)}, u32[]{:S(2)}) collective-permute-start(bf16[2,128,256]{2,1,0:T(8,128)(2,1)S(1)} %collective-permute-done.1), channel_id=1, source_target_pairs={{0,8},{4,12},{8,16},{12,20},{16,24},{20,28},{24,32},{28,36},{32,40... | collective-permute-start | bytes 393224 | tf_op jit(solution)/shard_map/ppermute | solution.py:30
  29.3 6.9 %collective-permute-done.3 = bf16[2,128,256]{2,1,0:T(8,128)(2,1)} collective-permute-done((bf16[2,128,256]{2,1,0:T(8,128)(2,1)S(1)}, bf16[2,128,256]{2,1,0:T(8,128)(2,1)}, u32[]{:S(2)}, u32[]{:S(2)}) %collective-permute-start.3) | collective-permute-done | bytes 131104 | tf_op jit(solution)/shard_map/ppermute | solution.py:30
  37.8 1.4 %collective-permute-start.4 = (bf16[8,128,128]{2,1,0:T(8,128)(2,1)}, bf16[8,128,128]{2,1,0:T(8,128)(2,1)}, u32[]{:S(2)}, u32[]{:S(2)}) collective-permute-start(bf16[8,128,128]{2,1,0:T(8,128)(2,1)} %fusion.42), channel_id=1, source_target_pairs={{4,20},{12,28},{20,36},{28,44},{36,52},{44,60},{52,68},{60,76},{68... | collective-permute-start | bytes 786440 | tf_op jit(solution)/shard_map/ppermute | solution.py:57
  39.2 1.9 %collective-permute-start.5 = (bf16[2,128,256]{2,1,0:T(8,128)(2,1)}, bf16[2,128,256]{2,1,0:T(8,128)(2,1)S(1)}, u32[]{:S(2)}, u32[]{:S(2)}) collective-permute-start(bf16[2,128,256]{2,1,0:T(8,128)(2,1)} %collective-permute-done.3), channel_id=1, source_target_pairs={{0,8},{4,12},{8,16},{12,20},{16,24},{20,28},{24,32},{28,36},{32,40... | collective-permute-start | bytes 393224 | tf_op jit(solution)/shard_map/ppermute | solution.py:30
  42.1 1.6 %maximum_select_fusion = bf16[2,2,128,256]{3,2,1,0:T(8,128)(2,1)} fusion(bf16[1,2,128,256]{3,2,1,0:T(8,128)(2,1)} %bitcast.8, bf16[1,2,128,256]{3,2,1,0:T(8,128)(2,1)S(1)} %bitcast.143, bf16[1,2,128,256]{3,2,1,0:T(8,128)(2,1)S(1)} %get-tuple-element.59, pred[]{:T(512)S(6)} %eq.36), kind=kLoop, calls=%fused_computation.68 | loop fusion | flops 393216 | bytes 655361 | tf_op jit(solution)/shard_map/jit(_where)/select_n | solution.py:53
  43.8 2.6 %collective-permute-start.6 = (bf16[2,2,128,256]{3,2,1,0:T(8,128)(2,1)}, bf16[2,2,128,256]{3,2,1,0:T(8,128)(2,1)}, u32[]{:S(2)}, u32[]{:S(2)}) collective-permute-start(bf16[2,2,128,256]{3,2,1,0:T(8,128)(2,1)} %maximum_select_fusion), channel_id=1, source_target_pairs={{0,4},{4,0},{8,12},{12,8},{16,20},{20,16},{24,28},{28,24},{32,36},... | collective-permute-start | bytes 786440 | tf_op jit(solution)/shard_map/ppermute | solution.py:59
  47.8 1.7 %fusion.4 = (f32[128,2,8]{0,2,1:T(8,128)S(1)}, f32[2,384,128,8]{2,1,3,0:T(8,128)S(1)}) fusion(pred[128,384]{0,1:T(8,128)(4,1)} %get-tuple-element.77, bf16[128,2,8,128]{3,2,1,0:T(8,128)(2,1)} %bitcast.127, bf16[384,2,128,1]{2,1,0,3:T(2,128)(2,1)} %bitcast.137), kind=kOutput, calls=%fused_computation.8 | convolution fusion | flops 203683840 | bytes 3923968 | tf_op jit(solution)/shard_map/tkgd,skd->tkgs/dot_general | solution.py:123
  49.5 1.4 %fusion.1 = f32[128,2,8]{0,2,1:T(8,128)S(1)} fusion(f32[2,384,128,8]{2,1,3,0:T(8,128)S(1)} %get-tuple-element.79, f32[128,2,8]{0,2,1:T(8,128)S(1)} %broadcast_maximum_fusion, pred[128,384]{0,1:T(8,128)(4,1)} %get-tuple-element.77), kind=kLoop, calls=%fused_computation.5 | loop fusion | flops 3143680 | bytes 3211264 | tf_op jit(solution)/shard_map/reduce_sum | solution.py:130
  51.6 1.6 %reshape_squeeze.19 = bf16[384,2,128]{2,1,0:T(2,128)(2,1)} reshape(bf16[3,1,128,256]{3,2,1,0:T(8,128)(2,1)} %get-tuple-element.55) | data formatting | bytes 393216 | tf_op jit(solution)/shard_map/reshape;squeeze | solution.py:162
  53.2 2.8 %fusion.23 = f32[128,2,8,128]{0,3,2,1:T(8,128)} fusion(f32[2,384,128,8]{2,1,3,0:T(8,128)S(1)} %get-tuple-element.79, f32[128,2,8]{0,2,1:T(8,128)S(1)} %broadcast_maximum_fusion, pred[128,384]{0,1:T(8,128)(4,1)} %get-tuple-element.77, f32[128,2,8]{0,2,1:T(8,128)} %get-tuple-element.61, bf16[384,2,128,1]{2,1,0,3:T(2,128)(2,1)} %bitcast.144), kind=kOutput, calls=%fused_computation.26 | convolution fusion | flops 204734464 | bytes 4456448 | tf_op jit(solution)/shard_map/tkgs,skd->tkgd/dot_general | solution.py:131
  56.1 2.1 %add_convert_fusion.1 = bf16[8,128,128]{2,1,0:T(8,128)(2,1)} fusion(bf16[8,128,128]{2,1,0:T(8,128)(2,1)} %collective-permute-done.4, f32[8,128,128]{2,1,0:T(8,128)} %copy-done.2, f32[8]{0:T(128)} %get-tuple-element.40, f32[8]{0:T(128)} %copy-done.16, bf16[8,130,128]{2,1,0:T(8,128)(2,1)} %copy-done.7), kind=kLoop, calls=%fused_computation.41 | loop fusion | flops 917504 | bytes 1310784 | tf_op jit(solution)/shard_map/convert_element_type | solution.py:64
  58.2 1.4 %collective-permute-start.8 = (bf16[8,128,128]{2,1,0:T(8,128)(2,1)}, bf16[8,128,128]{2,1,0:T(8,128)(2,1)}, u32[]{:S(2)}, u32[]{:S(2)}) collective-permute-start(bf16[8,128,128]{2,1,0:T(8,128)(2,1)} %add_convert_fusion.1), channel_id=1, source_target_pairs={{4,12},{12,20},{20,28},{28,36},{36,44},{44,52},{52,60},{60,68},{68... | collective-permute-start | bytes 786440 | tf_op jit(solution)/shard_map/ppermute | solution.py:71
  59.6 1.7 %pad_maximum_fusion.2 = bf16[1536,128]{1,0:T(8,128)(2,1)} fusion(bf16[512,128]{1,0:T(8,128)(2,1)S(1)} %reshape.335, bf16[1024,128]{1,0:T(8,128)(2,1)} %bitcast.17), kind=kLoop, calls=%fused_computation.54 | loop fusion | flops 786432 | bytes 786432 | tf_op jit(solution)/shard_map/concatenate | solution.py:65
  61.3 1.3 %collective-permute-start.7 = (bf16[1536,128]{1,0:T(8,128)(2,1)}, bf16[1536,128]{1,0:T(8,128)(2,1)}, u32[]{:S(2)}, u32[]{:S(2)}) collective-permute-start(bf16[1536,128]{1,0:T(8,128)(2,1)} %pad_maximum_fusion.2), channel_id=1, source_target_pairs={{4,8},{12,16},{20,24},{28,32},{36,40},{44,48},{52,56},{60,64},{68,... | collective-permute-start | bytes 1179656 | tf_op jit(solution)/shard_map/ppermute | solution.py:70
  62.6 1.6 %fusion.43 = bf16[2,2,128,256]{3,2,1,0:T(8,128)(2,1)} fusion(bf16[1,2,128,256]{3,2,1,0:T(8,128)(2,1)S(1)} %bitcast.130, bf16[1,2,128,256]{3,2,1,0:T(8,128)(2,1)} %bitcast.8, pred[]{:T(512)S(6)} %eq.36), kind=kLoop, calls=%fused_computation.61 | loop fusion | flops 393216 | bytes 524289 | tf_op jit(solution)/shard_map/jit(_where)/select_n | solution.py:66
  64.2 6.3 %collective-permute-start.9 = (bf16[2,2,128,256]{3,2,1,0:T(8,128)(2,1)}, bf16[2,2,128,256]{3,2,1,0:T(8,128)(2,1)}, u32[]{:S(2)}, u32[]{:S(2)}) collective-permute-start(bf16[2,2,128,256]{3,2,1,0:T(8,128)(2,1)} %fusion.43), channel_id=1, source_target_pairs={{0,4},{4,0},{8,12},{12,8},{16,20},{20,16},{24,28},{28,24},{32,36},... | collective-permute-start | bytes 786440 | tf_op jit(solution)/shard_map/ppermute | solution.py:72
  70.5 1.7 %pad_maximum_fusion.6 = (bf16[3,1,128,256]{3,2,1,0:T(8,128)(2,1)}, bf16[3,1,128,256]{3,2,1,0:T(8,128)(2,1)S(1)}) fusion(bf16[2,2,128,256]{3,2,1,0:T(8,128)(2,1)} %collective-permute-done.6, bf16[1,2,128,256]{3,2,1,0:T(8,128)(2,1)S(1)} %bitcast.131), kind=kLoop, calls=%fused_computation.82 | loop fusion | flops 196608 | bytes 786432 | tf_op jit(solution)/shard_map/concatenate | solution.py:67
  72.9 1.7 %fusion.5 = (f32[128,2,8]{0,2,1:T(8,128)S(1)}, f32[2,384,128,8]{2,1,3,0:T(8,128)S(1)}) fusion(pred[128,384]{0,1:T(8,128)(4,1)} %get-tuple-element.76, bf16[128,2,8,128]{3,2,1,0:T(8,128)(2,1)} %bitcast.128, bf16[384,2,128,1]{2,1,0,3:T(2,128)(2,1)} %bitcast.136), kind=kOutput, calls=%fused_computation.9 | convolution fusion | flops 203683840 | bytes 3923968 | tf_op jit(solution)/shard_map/tkgd,skd->tkgs/dot_general | solution.py:123
  74.7 1.4 %fusion.3 = f32[128,2,8]{0,2,1:T(8,128)S(1)} fusion(f32[2,384,128,8]{2,1,3,0:T(8,128)S(1)} %get-tuple-element.81, f32[128,2,8]{0,2,1:T(8,128)S(1)} %max.37, pred[128,384]{0,1:T(8,128)(4,1)} %get-tuple-element.76), kind=kLoop, calls=%fused_computation.7 | loop fusion | flops 3143680 | bytes 3211264 | tf_op jit(solution)/shard_map/reduce_sum | solution.py:130
  76.2 1.7 %reshape_squeeze.21 = bf16[384,2,128]{2,1,0:T(2,128)(2,1)} reshape(bf16[3,1,128,256]{3,2,1,0:T(8,128)(2,1)} %get-tuple-element.53) | data formatting | bytes 393216 | tf_op jit(solution)/shard_map/reshape;squeeze | solution.py:162
  77.8 3.3 %multiply_add_fusion = f32[128,2,8,128]{0,3,2,1:T(8,128)} fusion(f32[128,2,8,128]{0,3,2,1:T(8,128)} %fusion.23, f32[128,2,8]{0,2,1:T(8,128)S(1)} %get-tuple-element.47, f32[2,384,128,8]{2,1,3,0:T(8,128)S(1)} %get-tuple-element.81, f32[128,2,8]{0,2,1:T(8,128)S(1)} %max.37, pred[128,384]{0,1:T(8,128)(4,1)S(1)} %copy-done.8, bf16[384,2,128,1]{2,1,0,3:T(2,128)(2,1)} %bitcast.135), kind=kOutput, calls=%fused_computation.36 | convolution fusion | flops 204996608 | bytes 5505024 | tf_op jit(solution)/shard_map/tkgs,skd->tkgd/dot_general | solution.py:131
  83.1 1.4 %fusion.30 = f32[128,8,128]{0,2,1:T(8,128)S(1)} fusion(bf16[8,128,128]{2,1,0:T(8,128)(2,1)S(1)} %bitcast.132, f32[8,129,128]{2,1,0:T(8,128)S(1)} %copy-done.4, bf16[8,128,128]{2,1,0:T(8,128)(2,1)} %collective-permute-done.8, f32[128,8]{0,1:T(8,128)S(1)} %get-tuple-element.63, f32[8]{0:T(128)S(1)} %copy-done.18, pred[]{:T(512)S(6)} %eq.34, ...), kind=kOutput, calls=%fused_computation.31 | convolution fusion | flops 34340864 | bytes 1839617 | tf_op jit(solution)/shard_map/thd,hde->the/dot_general | solution.py:191
  84.5 1.5 %multiply_reduce_fusion = (f32[128]{0:T(128)S(1)}, f32[128,8,128]{0,2,1:T(8,128)S(1)}) fusion(f32[128,8,128]{0,2,1:T(8,128)S(1)} %fusion.30, bf16[128,8,128]{0,2,1:T(8,128)(2,1)} %bitcast.134, f32[8,128]{1,0:T(8,128)S(1)} %reduce_window_sum.11, pred[128,128]{1,0:T(8,128)(4,1)S(1)} %copy-done.15, bf16[128,1024]{1,0:T(8,128)(2,1)S(1)} %copy-done, ...), kind=kOutput, calls=%fused_computation.39 | convolution fusion | flops 68026240 | bytes 1856000 | tf_op jit(solution)/shard_map/hts,shd->thd/dot_general | solution.py:103
  86.3 10.5 %psum.7 = f32[128]{0:T(128)S(1)} all-reduce(f32[128]{0:T(128)S(1)} %get-tuple-element.82), channel_id=1, replica_groups=mesh['grp'=4,'seq'=32,'head'=4] {'head'}, use_global_device_ids=true, to_apply=%region_6.7 | all-reduce | flops 128 | bytes 1024 | tf_op jit(solution)/shard_map/psum | solution.py:195
  99.6 1.0 copy.72
  (112 shorter events, 22.1 us)
Async XLA Ops:
  0.6 5.6 %copy-start = (bf16[128,1024]{1,0:T(8,128)(2,1)S(1)}, bf16[128,1024]{1,0:T(8,128)(2,1)}, u32[]{:S(2)}) copy-start(bf16[128,1024]{1,0:T(8,128)(2,1)} %param.11) | copy-start | bytes 786436
  0.6 7.9 %copy-start.12 = (bf16[128,256]{1,0:T(8,128)(2,1)S(1)}, bf16[128,256]{1,0:T(8,128)(2,1)}, u32[]{:S(2)}) copy-start(bf16[128,256]{1,0:T(8,128)(2,1)} %param.16) | copy-start | bytes 196612
  0.7 7.9 %copy-start.13 = (bf16[128,256]{1,0:T(8,128)(2,1)S(1)}, bf16[128,256]{1,0:T(8,128)(2,1)}, u32[]{:S(2)}) copy-start(bf16[128,256]{1,0:T(8,128)(2,1)} %param.15) | copy-start | bytes 196612
  1.9 21.2 %copy-start.5 = (bf16[128,1024]{0,1:T(8,128)(2,1)}, bf16[128,1024]{0,1:T(8,128)(2,1)S(1)}, u32[]{:S(2)}) copy-start(bf16[128,1024]{0,1:T(8,128)(2,1)S(1)} %copy.96) | copy-start | bytes 786436
  6.6 21.2 %copy-start.9 = (bf16[128,2048]{1,0:T(8,128)(2,1)S(1)}, bf16[128,2048]{1,0:T(8,128)(2,1)}, u32[]{:S(2)}) copy-start(bf16[128,2048]{1,0:T(8,128)(2,1)} %param.14) | copy-start | bytes 1572868
  6.7 16.4 %collective-permute-start = (f32[8,129,128]{2,0,1:T(8,128)S(1)}, f32[8,129,128]{2,0,1:T(8,128)S(1)}, u32[]{:S(2)}, u32[]{:S(2)}) collective-permute-start(f32[8,129,128]{2,0,1:T(8,128)S(1)} %copy.53), channel_id=1, source_target_pairs={{0,4},{8,12},{16,20},{24,28},{32,36},{40,44},{48,52},{56,60},{64,6... | collective-permute-start | bytes 1585160 | tf_op jit(solution)/shard_map/ppermute | solution.py:37
  8.5 14.6 %collective-permute-start.1 = (bf16[2,128,256]{2,1,0:T(8,128)(2,1)S(1)}, bf16[2,128,256]{2,1,0:T(8,128)(2,1)S(1)}, u32[]{:S(2)}, u32[]{:S(2)}) collective-permute-start(bf16[2,128,256]{2,1,0:T(8,128)(2,1)S(1)} %get-tuple-element.60), channel_id=1, source_target_pairs={{0,8},{4,12},{8,16},{12,20},{16,24},{20,28},{24,32},{28,36},{32,40... | collective-permute-start | bytes 393224 | tf_op jit(solution)/shard_map/ppermute | solution.py:30
  23.3 23.8 %copy-start.3 = (f32[8,129,128]{2,1,0:T(8,128)}, f32[8,129,128]{2,1,0:T(8,128)S(1)}, u32[]{:S(2)}) copy-start(f32[8,129,128]{2,1,0:T(8,128)S(1)} %copy.54) | copy-start | bytes 1585156
  23.4 24.4 %copy-start.2 = (f32[8,128,128]{2,1,0:T(8,128)}, f32[8,128,128]{2,1,0:T(8,128)S(1)}, u32[]{:S(2)}) copy-start(f32[8,128,128]{2,1,0:T(8,128)S(1)} %get-tuple-element.49) | copy-start | bytes 1572868
  23.8 12.5 %collective-permute-start.2 = (bf16[8,130,128]{2,1,0:T(8,128)(2,1)S(1)}, bf16[8,130,128]{2,1,0:T(8,128)(2,1)S(1)}, u32[]{:S(2)}, u32[]{:S(2)}) collective-permute-start(bf16[8,130,128]{2,1,0:T(8,128)(2,1)S(1)} %pad_maximum_fusion.5), channel_id=1, source_target_pairs={{4,12},{12,20},{20,28},{28,36},{36,44},{44,52},{52,60},{60,68},{68... | collective-permute-start | bytes 798728 | tf_op jit(solution)/shard_map/ppermute | solution.py:47
  25.2 11.0 %collective-permute-start.3 = (bf16[2,128,256]{2,1,0:T(8,128)(2,1)S(1)}, bf16[2,128,256]{2,1,0:T(8,128)(2,1)}, u32[]{:S(2)}, u32[]{:S(2)}) collective-permute-start(bf16[2,128,256]{2,1,0:T(8,128)(2,1)S(1)} %collective-permute-done.1), channel_id=1, source_target_pairs={{0,8},{4,12},{8,16},{12,20},{16,24},{20,28},{24,32},{28,36},{32,40... | collective-permute-start | bytes 393224 | tf_op jit(solution)/shard_map/ppermute | solution.py:30
  36.2 4.9 %copy-start.7 = (bf16[8,130,128]{2,1,0:T(8,128)(2,1)}, bf16[8,130,128]{2,1,0:T(8,128)(2,1)S(1)}, u32[]{:S(2)}) copy-start(bf16[8,130,128]{2,1,0:T(8,128)(2,1)S(1)} %collective-permute-done.2) | copy-start | bytes 798724
  37.0 4.1 %copy-start.16 = (f32[8]{0:T(128)}, f32[8]{0:T(128)S(1)}, u32[]{:S(2)}) copy-start(f32[8]{0:T(128)S(1)} %get-tuple-element.41) | copy-start | bytes 100
  37.8 18.3 %collective-permute-start.4 = (bf16[8,128,128]{2,1,0:T(8,128)(2,1)}, bf16[8,128,128]{2,1,0:T(8,128)(2,1)}, u32[]{:S(2)}, u32[]{:S(2)}) collective-permute-start(bf16[8,128,128]{2,1,0:T(8,128)(2,1)} %fusion.42), channel_id=1, source_target_pairs={{4,20},{12,28},{20,36},{28,44},{36,52},{44,60},{52,68},{60,76},{68... | collective-permute-start | bytes 786440 | tf_op jit(solution)/shard_map/ppermute | solution.py:57
  39.2 16.9 %collective-permute-start.5 = (bf16[2,128,256]{2,1,0:T(8,128)(2,1)}, bf16[2,128,256]{2,1,0:T(8,128)(2,1)S(1)}, u32[]{:S(2)}, u32[]{:S(2)}) collective-permute-start(bf16[2,128,256]{2,1,0:T(8,128)(2,1)} %collective-permute-done.3), channel_id=1, source_target_pairs={{0,8},{4,12},{8,16},{12,20},{16,24},{20,28},{24,32},{28,36},{32,40... | collective-permute-start | bytes 393224 | tf_op jit(solution)/shard_map/ppermute | solution.py:30
  43.8 12.3 %collective-permute-start.6 = (bf16[2,2,128,256]{3,2,1,0:T(8,128)(2,1)}, bf16[2,2,128,256]{3,2,1,0:T(8,128)(2,1)}, u32[]{:S(2)}, u32[]{:S(2)}) collective-permute-start(bf16[2,2,128,256]{3,2,1,0:T(8,128)(2,1)} %maximum_select_fusion), channel_id=1, source_target_pairs={{0,4},{4,0},{8,12},{12,8},{16,20},{20,16},{24,28},{28,24},{32,36},... | collective-permute-start | bytes 786440 | tf_op jit(solution)/shard_map/ppermute | solution.py:59
  58.2 22.9 %collective-permute-start.8 = (bf16[8,128,128]{2,1,0:T(8,128)(2,1)}, bf16[8,128,128]{2,1,0:T(8,128)(2,1)}, u32[]{:S(2)}, u32[]{:S(2)}) collective-permute-start(bf16[8,128,128]{2,1,0:T(8,128)(2,1)} %add_convert_fusion.1), channel_id=1, source_target_pairs={{4,12},{12,20},{20,28},{28,36},{36,44},{44,52},{52,60},{60,68},{68... | collective-permute-start | bytes 786440 | tf_op jit(solution)/shard_map/ppermute | solution.py:71
  61.3 19.8 %collective-permute-start.7 = (bf16[1536,128]{1,0:T(8,128)(2,1)}, bf16[1536,128]{1,0:T(8,128)(2,1)}, u32[]{:S(2)}, u32[]{:S(2)}) collective-permute-start(bf16[1536,128]{1,0:T(8,128)(2,1)} %pad_maximum_fusion.2), channel_id=1, source_target_pairs={{4,8},{12,16},{20,24},{28,32},{36,40},{44,48},{52,56},{60,64},{68,... | collective-permute-start | bytes 1179656 | tf_op jit(solution)/shard_map/ppermute | solution.py:70
  64.2 16.9 %collective-permute-start.9 = (bf16[2,2,128,256]{3,2,1,0:T(8,128)(2,1)}, bf16[2,2,128,256]{3,2,1,0:T(8,128)(2,1)}, u32[]{:S(2)}, u32[]{:S(2)}) collective-permute-start(bf16[2,2,128,256]{3,2,1,0:T(8,128)(2,1)} %fusion.43), channel_id=1, source_target_pairs={{0,4},{4,0},{8,12},{12,8},{16,20},{20,16},{24,28},{28,24},{32,36},... | collective-permute-start | bytes 786440 | tf_op jit(solution)/shard_map/ppermute | solution.py:72
  72.9 3.2 %copy-start.14 = (f32[128,2,8]{0,2,1:T(8,128)S(1)}, f32[128,2,8]{0,2,1:T(8,128)}, u32[]{:S(2)}) copy-start(f32[128,2,8]{0,2,1:T(8,128)} %get-tuple-element.26) | copy-start | bytes 24580
  72.9 4.9 %copy-start.8 = (pred[128,384]{0,1:T(8,128)(4,1)S(1)}, pred[128,384]{0,1:T(8,128)(4,1)}, u32[]{:S(2)}) copy-start(pred[128,384]{0,1:T(8,128)(4,1)} %get-tuple-element.76) | copy-start | bytes 147460
  77.8 5.2 %copy-start.4 = (f32[8,129,128]{2,1,0:T(8,128)S(1)}, f32[8,129,128]{2,1,0:T(8,128)}, u32[]{:S(2)}) copy-start(f32[8,129,128]{2,1,0:T(8,128)} %copy-done.3) | copy-start | bytes 1585156
  77.8 5.2 %copy-start.10 = (bf16[128,1024]{1,0:T(8,128)(2,1)S(1)}, bf16[128,1024]{1,0:T(8,128)(2,1)}, u32[]{:S(2)}) copy-start(bf16[128,1024]{1,0:T(8,128)(2,1)} %param.9) | copy-start | bytes 786436
  77.8 5.2 %copy-start.18 = (f32[8]{0:T(128)S(1)}, f32[8]{0:T(128)}, u32[]{:S(2)}) copy-start(f32[8]{0:T(128)} %slice_reduce_fusion.1) | copy-start | bytes 100
  77.8 6.7 %copy-start.15 = (pred[128,128]{1,0:T(8,128)(4,1)S(1)}, pred[128,128]{1,0:T(8,128)(4,1)}, u32[]{:S(2)}) copy-start(pred[128,128]{1,0:T(8,128)(4,1)} %iota_compare_fusion) | copy-start | bytes 49156
  83.1 14.9 %copy-start.1 = (bf16[16,8,16,128]{3,2,1,0:T(8,128)(2,1)S(1)}, bf16[16,8,16,128]{3,2,1,0:T(8,128)(2,1)}, u32[]{:S(2)}) copy-start(bf16[16,8,16,128]{3,2,1,0:T(8,128)(2,1)} %copy.99) | copy-start | bytes 1572868
  83.1 14.9 %copy-start.11 = (pred[128,256]{0,1:T(8,128)(4,1)S(1)}, pred[128,256]{0,1:T(8,128)(4,1)}, u32[]{:S(2)}) copy-start(pred[128,256]{0,1:T(8,128)(4,1)} %and_and_fusion.2) | copy-start | bytes 98308
  97.8 1.2 %copy-start.6 = (f32[128,2,8,128]{0,3,2,1:T(8,128)S(1)}, f32[128,2,8,128]{0,3,2,1:T(8,128)}, u32[]{:S(2)}) copy-start(f32[128,2,8,128]{0,3,2,1:T(8,128)} %multiply_add_fusion) | copy-start | bytes 3145732
  99.1 1.5 %copy-start.17 = (f32[1024]{0:T(1024)S(1)}, f32[1024]{0:T(1024)}, u32[]{:S(2)}) copy-start(f32[1024]{0:T(1024)} %param.13) | copy-start | bytes 12292

commit v7 on v5

--- a/solution.py
+++ b/solution.py
@@ -80,12 +80,7 @@
     return jnp.where(core == 0, before, after), running
 
 
-def token_segments(segment_ids, row_start, tok_rows):
-    blocks = lax.dynamic_slice_in_dim(segment_ids, row_start // BLOCK, tok_rows // BLOCK)
-    return jnp.repeat(blocks, BLOCK)
-
-
-def lightning_local(light_q, light_k, light_v, log_decay, seg_tok, prev_last):
+def lightning_local(light_q, light_k, light_v, log_decay, joined):
     tok_rows, feat_width = light_q.shape
     head_count = feat_width // HEAD_DIM
     queries = light_q.reshape(tok_rows, head_count, HEAD_DIM)
@@ -93,25 +88,16 @@
     value_rows = light_v.reshape(tok_rows, head_count, HEAD_DIM)
     levels = jnp.cumsum(log_decay, axis=1)
     offsets = jnp.arange(tok_rows, dtype=jnp.int32)
-    allowed = (offsets[:, None] >= offsets[None, :]) & (seg_tok[:, None] == seg_tok[None, :])
+    allowed = offsets[:, None] >= offsets[None, :]
     decays = jnp.exp(jnp.where(allowed[None], levels[:, :, None] - levels[:, None, :], NEG_FLOOR))
     scores = jnp.einsum("thd,shd->hts", queries, key_rows, preferred_element_type=jnp.float32)
     weights = (scores * decays).astype(jnp.bfloat16)
     intra_part = jnp.einsum("hts,shd->thd", weights, value_rows, preferred_element_type=jnp.float32)
-    last_seg = seg_tok[tok_rows - 1]
-    tail_gain = jnp.exp(
-        jnp.where(
-            (seg_tok == last_seg)[None, :], levels[:, tok_rows - 1 : tok_rows] - levels, NEG_FLOOR
-        )
-    )
+    tail_gain = jnp.exp(levels[:, tok_rows - 1 : tok_rows] - levels)
     keyed = (key_rows * tail_gain.T[:, :, None]).astype(jnp.bfloat16)
     local_state = jnp.einsum("shd,she->hde", keyed, value_rows, preferred_element_type=jnp.float32)
-    first_seg = seg_tok[0]
-    joined = (first_seg == prev_last) & jnp.all(seg_tok == first_seg)
     carry_gain = jnp.where(joined, jnp.exp(levels[:, tok_rows - 1]), 0.0)
-    reach_gain = jnp.where(
-        ((seg_tok == first_seg) & (first_seg == prev_last))[None, :], jnp.exp(levels), 0.0
-    )
+    reach_gain = jnp.where(joined, jnp.exp(levels), 0.0)
     return (intra_part, (carry_gain, local_state), reach_gain, queries)
 
 
@@ -137,42 +123,36 @@
 
 def body(light_q, light_k, light_v, log_decay, light_gain, soft_q, soft_k, soft_v, segment_ids):
     tok_rows = light_q.shape[0]
+    assert tok_rows == BLOCK
     position = lax.axis_index(("grp", "seq"))
-    row_start = position * tok_rows
-    seg_tok = token_segments(segment_ids, row_start, tok_rows)
-    prev_index = jnp.maximum(position * (tok_rows // BLOCK) - 1, 0)
-    prev_last = jnp.where(
-        position > 0, lax.dynamic_index_in_dim(segment_ids, prev_index, keepdims=False), -1
-    )
+    here_seg = segment_ids[position]
+    joined = (position > 0) & (segment_ids[jnp.maximum(position - 1, 0)] == here_seg)
     intra_part, element, reach_gain, queries = lightning_local(
-        light_q, light_k, light_v, log_decay, seg_tok, prev_last
+        light_q, light_k, light_v, log_decay, joined
     )
     core = position % 2
     window_len = WINDOW_DEV
     kv_heads = soft_k.shape[1] // HEAD_DIM
     group_size = soft_q.shape[1] // soft_k.shape[1]
     soft_queries = soft_q.reshape(tok_rows, kv_heads, group_size, HEAD_DIM)
-    query_pos = row_start + jnp.arange(tok_rows, dtype=jnp.int32)
+
+    causal = jnp.arange(tok_rows)[:, None] >= jnp.arange(tok_rows)[None, :]
 
     def take(running, slot_list, chosen):
         key_rows = chosen[:, 0].reshape(-1, kv_heads, HEAD_DIM)
         value_rows = chosen[:, 1].reshape(-1, kv_heads, HEAD_DIM)
-        key_pos = jnp.concatenate(
+        allowed = jnp.concatenate(
             [
-                (position - source) * tok_rows + jnp.arange(tok_rows, dtype=jnp.int32)
+                causal
+                if source == 0
+                else jnp.broadcast_to(
+                    (position >= source)
+                    & (segment_ids[jnp.maximum(position - source, 0)] == here_seg),
+                    causal.shape,
+                )
                 for source in slot_list
-            ]
-        )
-        key_seg = jnp.concatenate(
-            [
-                token_segments(segment_ids, jnp.maximum(position - source, 0) * tok_rows, tok_rows)
-                for source in slot_list
-            ]
-        )
-        allowed = (
-            (key_pos[None, :] <= query_pos[:, None])
-            & (key_pos >= 0)[None, :]
-            & (key_seg[None, :] == seg_tok[:, None])
+            ],
+            axis=1,
         )
         return absorb(running, soft_queries, key_rows, value_rows, allowed)
 

time: 93.2 us -> 94.7 us (1.016)
  starting transfers between devices: 20.3 us -> 28.1 us
  between operations: 4 us -> 10 us
  local copies, waits for them, and re-layouts: 13.7 us -> 8.84 us
  waiting for transfers between devices: 20.7 us -> 16 us
  other arithmetic: 12.9 us -> 9.97 us
    ppermute x1, starting transfers between devices: 3.07 us -> 9.34 us  [exchange(): lax.ppermute(sent, axis, swap)]
    ppermute x4, waiting for transfers between devices: 20.7 us -> 16 us  [ring_step(): return lax.ppermute(ring[-1], axis, shift_pairs(count, 2, parity))]
    reshape x7 -> x0, local copies, waits for them, and re-layouts: 4.33 us -> none  [token_segments(): return jnp.repeat(blocks, BLOCK)]
    eq x2 -> x0, other arithmetic: 1.26 us -> none  [take(): key_seg[None, :] == seg_tok[:, None]]
    and x3 -> x0, other arithmetic: 1.26 us -> none  [take(): (key_pos[None, :] <= query_pos[:, None]) & (key_pos >= 0)[None, :]]
    unnamed x44 -> x30, local copies, waits for them, and re-layouts: 4 us -> 3.31 us
  transfers between devices with their start and end apart: 11 -> 11, of which waited for: 3 -> 3; matrix products, arithmetic and copies ran while one was open for 21% -> 16% of each run, Pallas kernels for 0% -> 0%
where the time goes in v7:
time: 94.7 us; the launch traced here: 94 us
  starting transfers between devices  28.1 us (30%)
  waiting for transfers between devices  16 us (17%)
  matrix products  10.6 us (11%)
  blocking collectives  10.5 us (11%)
  between operations  10 us (11%)
  other arithmetic  9.97 us (11%)
  local copies, waits for them, and re-layouts  8.84 us (9%)
    ppermute x4, waiting for transfers between devices, ring_step(): return lax.ppermute(ring[-1], axis, shift_pairs(count, 2, parity))  16 us
    psum x1, blocking collectives, body(): square_sum = lax.psum(jnp.sum(mixed * mixed, axis=1), 'head')  10.5 us
    ppermute x1, starting transfers between devices, exchange(): lax.ppermute(sent, axis, swap)  9.34 us
    ppermute x4, starting transfers between devices, ring_step(): return lax.ppermute(ring[-1], axis, shift_pairs(count, 2, parity))  8.95 us
    dot_general x3, matrix products, absorb(): jnp.einsum('tkgs,skd->tkgd', exponent.astype(jnp.bfloat16), value_rows, p...  6.64 us
    unnamed x30, local copies, waits for them, and re-layouts  3.31 us
    convert_element_type x3, other arithmetic, exchange(): wide_state.astype(jnp.bfloat16)  2.82 us
    ppermute x1, starting transfers between devices, exchange(): lax.ppermute(last, axis, swap)  2.82 us
  transfers between devices with their start and end apart: 11, of which 3 were waited for; matrix products, arithmetic and copies ran while one was open for 16% of the time, Pallas kernels for 0%

profile of v7, /device:TPU:24, one launch (start us, length us, event | category | flops | bytes accessed | tf_op | source)
XLA Modules:
  0.0 94.0 jit_solution(5963261859242828316)
XLA Ops:
  0.7 1.6 %fusion.87 = (s32[1]{0:T(128)}, s32[1]{0:T(128)}, s32[1]{0:T(128)}, s32[1]{0:T(128)}, s32[1]{0:T(128)}, /*index=5*/s32[1]{0:T(128)}, s32[1]{0:T(128)}, s32[1]{0:T(128)}) fusion(s32[128]{0:T(128)} %param.17, s32[]{:T(128)S(6)} %max.35, s32[]{:T(128)S(6)} %max.32, s32[]{:T(128)S(6)} %max.31, s32[]{:T(128)S(6)} %max.30, s32[]{:T(128)S(6)} %max.29, ...), kind=kLoop, calls=%fused_computation.112 | loop fusion | bytes 96 | tf_op jit(solution)/shard_map/dynamic_slice | solution.py:150
  3.6 1.0 %reduce_window_sum.11 = f32[8,128]{1,0:T(8,128)S(1)} reduce-window(f32[8,128]{1,0:T(8,128)} %param.12, f32[]{:T(128)} %constant.56.clone.1), window={size=1x128 pad=0_0x127_0}, to_apply=%region_0.0 | reduce-window | flops 130048 | bytes 8196 | tf_op jit(solution)/shard_map/jit(cumsum)/reduce_window_sum | solution.py:89
  5.4 1.1 %copy.102 = bf16[128,1024]{0,1:T(8,128)(2,1)S(1)} copy(bf16[128,1024]{1,0:T(8,128)(2,1)} %param.10) | data formatting | bytes 524288 | tf_op jit(solution)/shard_map/reshape | solution.py:87
  6.9 0.9 copy.59
  7.8 1.8 %collective-permute-start = (f32[8,129,128]{2,0,1:T(8,128)}, f32[8,129,128]{2,0,1:T(8,128)S(1)}, u32[]{:S(2)}, u32[]{:S(2)}) collective-permute-start(f32[8,129,128]{2,0,1:T(8,128)} %copy.59), channel_id=1, source_target_pairs={{0,4},{8,12},{16,20},{24,28},{32,36},{40,44},{48,52},{56,60},{64,6... | collective-permute-start | bytes 1585160 | tf_op jit(solution)/shard_map/ppermute | solution.py:36
  9.8 3.8 %collective-permute-start.1 = (bf16[2,128,256]{1,2,0:T(8,128)(2,1)S(1)}, bf16[2,128,256]{1,2,0:T(8,128)(2,1)S(1)}, u32[]{:S(2)}, u32[]{:S(2)}) collective-permute-start(bf16[2,128,256]{1,2,0:T(8,128)(2,1)S(1)} %get-tuple-element.62), channel_id=1, source_target_pairs={{0,8},{4,12},{8,16},{12,20},{16,24},{20,28},{24,32},{28,36},{32,40... | collective-permute-start | bytes 393224 | tf_op jit(solution)/shard_map/ppermute | solution.py:31
  13.7 10.7 %collective-permute-done.1 = bf16[2,128,256]{1,2,0:T(8,128)(2,1)S(1)} collective-permute-done((bf16[2,128,256]{1,2,0:T(8,128)(2,1)S(1)}, bf16[2,128,256]{1,2,0:T(8,128)(2,1)S(1)}, u32[]{:S(2)}, u32[]{:S(2)}) %collective-permute-start.1) | collective-permute-done | bytes 131104 | tf_op jit(solution)/shard_map/ppermute | solution.py:31
  25.0 0.7 pad_maximum_fusion.2
  26.4 1.9 %collective-permute-start.3 = (bf16[2,128,256]{1,2,0:T(8,128)(2,1)S(1)}, bf16[2,128,256]{1,2,0:T(8,128)(2,1)S(1)}, u32[]{:S(2)}, u32[]{:S(2)}) collective-permute-start(bf16[2,128,256]{1,2,0:T(8,128)(2,1)S(1)} %collective-permute-done.1), channel_id=1, source_target_pairs={{0,8},{4,12},{8,16},{12,20},{16,24},{20,28},{24,32},{28,36},{32,40... | collective-permute-start | bytes 393224 | tf_op jit(solution)/shard_map/ppermute | solution.py:31
  32.2 4.5 %collective-permute-done.3 = bf16[2,128,256]{1,2,0:T(8,128)(2,1)S(1)} collective-permute-done((bf16[2,128,256]{1,2,0:T(8,128)(2,1)S(1)}, bf16[2,128,256]{1,2,0:T(8,128)(2,1)S(1)}, u32[]{:S(2)}, u32[]{:S(2)}) %collective-permute-start.3) | collective-permute-done | bytes 131104 | tf_op jit(solution)/shard_map/ppermute | solution.py:31
  36.8 1.9 %collective-permute-start.5 = (bf16[2,128,256]{1,2,0:T(8,128)(2,1)S(1)}, bf16[2,128,256]{1,2,0:T(8,128)(2,1)S(1)}, u32[]{:S(2)}, u32[]{:S(2)}) collective-permute-start(bf16[2,128,256]{1,2,0:T(8,128)(2,1)S(1)} %collective-permute-done.3), channel_id=1, source_target_pairs={{0,8},{4,12},{8,16},{12,20},{16,24},{20,28},{24,32},{28,36},{32,40... | collective-permute-start | bytes 393224 | tf_op jit(solution)/shard_map/ppermute | solution.py:31
  38.8 0.8 fusion.47
  39.7 1.3 %collective-permute-start.4 = (bf16[8,128,128]{2,1,0:T(8,128)(2,1)}, bf16[8,128,128]{2,1,0:T(8,128)(2,1)}, u32[]{:S(2)}, u32[]{:S(2)}) collective-permute-start(bf16[8,128,128]{2,1,0:T(8,128)(2,1)} %fusion.47), channel_id=1, source_target_pairs={{4,20},{12,28},{20,36},{28,44},{36,52},{44,60},{52,68},{60,76},{68... | collective-permute-start | bytes 786440 | tf_op jit(solution)/shard_map/ppermute | solution.py:57
  45.6 0.7 collective-permute-done.5
  46.3 1.3 %collective-permute-start.7 = (bf16[2,128,256]{1,2,0:T(8,128)(2,1)S(1)}, bf16[2,128,256]{1,2,0:T(8,128)(2,1)}, u32[]{:S(2)}, u32[]{:S(2)}) collective-permute-start(bf16[2,128,256]{1,2,0:T(8,128)(2,1)S(1)} %collective-permute-done.5), channel_id=1, source_target_pairs={{4,12},{12,20},{20,28},{28,36},{36,44},{44,52},{52,60},{60,68},{68... | collective-permute-start | bytes 393224 | tf_op jit(solution)/shard_map/ppermute | solution.py:31
  47.6 1.8 %add_convert_fusion.1 = bf16[8,128,128]{2,1,0:T(8,128)(2,1)} fusion(bf16[8,128,128]{2,1,0:T(8,128)(2,1)} %collective-permute-done.4, f32[8,128,128]{2,1,0:T(8,128)S(1)} %get-tuple-element.51, f32[8]{0:T(128)S(1)} %get-tuple-element.42, f32[8]{0:T(128)S(1)} %get-tuple-element.43, bf16[8,130,128]{2,1,0:T(8,128)(2,1)S(1)} %collective-permute-done.2), kind=kLoop, calls=%fused_computation.46 | loop fusion | flops 917504 | bytes 1310784 | tf_op jit(solution)/shard_map/convert_element_type | solution.py:64
  49.4 1.3 %collective-permute-start.6 = (bf16[8,128,128]{2,1,0:T(8,128)(2,1)}, bf16[8,128,128]{2,1,0:T(8,128)(2,1)S(1)}, u32[]{:S(2)}, u32[]{:S(2)}) collective-permute-start(bf16[8,128,128]{2,1,0:T(8,128)(2,1)} %add_convert_fusion.1), channel_id=1, source_target_pairs={{4,8},{12,16},{20,24},{28,32},{36,40},{44,48},{52,56},{60,64},{68,... | collective-permute-start | bytes 786440 | tf_op jit(solution)/shard_map/ppermute | solution.py:64
  50.8 0.8 maximum_select_fusion
  51.9 9.3 %collective-permute-start.8 = (bf16[3,2,128,256]{2,3,1,0:T(8,128)(2,1)}, bf16[3,2,128,256]{2,3,1,0:T(8,128)(2,1)S(1)}, u32[]{:S(2)}, u32[]{:S(2)}) collective-permute-start(bf16[3,2,128,256]{2,3,1,0:T(8,128)(2,1)} %maximum_select_fusion), channel_id=1, source_target_pairs={{0,4},{4,0},{8,12},{12,8},{16,20},{20,16},{24,28},{28,24},{32,36},... | collective-permute-start | bytes 1179656 | tf_op jit(solution)/shard_map/ppermute | solution.py:66
  61.2 0.8 fusion.2
  62.0 1.9 %copy-done.1 = f32[2,512,128,8]{2,1,3,0:T(8,128)} copy-done((f32[2,512,128,8]{2,1,3,0:T(8,128)}, f32[2,512,128,8]{2,1,3,0:T(8,128)S(1)}, u32[]{:S(2)}) %copy-start.1) | copy-done | bytes 4194328
  63.9 0.9 fusion.1
  65.2 4.3 %fusion.26 = f32[128,2,8,128]{0,3,2,1:T(8,128)} fusion(f32[2,512,128,8]{2,1,3,0:T(8,128)} %copy-done.1, f32[128,2,8]{0,2,1:T(8,128)S(1)} %broadcast_maximum_fusion, pred[128,512]{0,1:T(8,128)(4,1)S(1)} %copy.65, f32[128,2,8]{0,2,1:T(8,128)S(1)} %get-tuple-element.63, bf16[512,2,128,1]{0,2,1,3:T(8,128)(2,1)S(1)} %reshape.93), kind=kOutput, calls=%fused_computation.26 | convolution fusion | flops 272891904 | bytes 5586944 | tf_op jit(solution)/shard_map/tkgs,skd->tkgd/dot_general | solution.py:114
  69.7 2.8 %collective-permute-start.10 = (bf16[2,128,256]{1,2,0:T(8,128)(2,1)S(1)}, bf16[2,128,256]{1,2,0:T(8,128)(2,1)S(1)}, u32[]{:S(2)}, u32[]{:S(2)}) collective-permute-start(bf16[2,128,256]{1,2,0:T(8,128)(2,1)S(1)} %broadcast_select_fusion), channel_id=1, source_target_pairs={{0,4},{4,0},{8,12},{12,8},{16,20},{20,16},{24,28},{28,24},{32,36},... | collective-permute-start | bytes 393224 | tf_op jit(solution)/shard_map/ppermute | solution.py:75
  72.5 1.9 %collective-permute-start.9 = (bf16[8,128,128]{2,1,0:T(8,128)(2,1)S(1)}, bf16[8,128,128]{2,1,0:T(8,128)(2,1)S(1)}, u32[]{:S(2)}, u32[]{:S(2)}) collective-permute-start(bf16[8,128,128]{2,1,0:T(8,128)(2,1)S(1)} %add_convert_fusion), channel_id=1, source_target_pairs={{0,4},{8,12},{16,20},{24,28},{32,36},{40,44},{48,52},{56,60},{64,6... | collective-permute-start | bytes 786440 | tf_op jit(solution)/shard_map/ppermute | solution.py:74
  75.1 0.7 fusion.5
  75.8 0.7 fusion.4
  76.6 2.0 %multiply_add_fusion = f32[128,2,8,128]{0,3,2,1:T(8,128)} fusion(f32[128,2,8,128]{0,3,2,1:T(8,128)S(1)} %copy-done.2, f32[128,2,8]{0,2,1:T(8,128)S(1)} %get-tuple-element.49, f32[2,384,128,8]{2,1,3,0:T(8,128)S(1)} %get-tuple-element.79, f32[128,2,8]{0,2,1:T(8,128)S(1)} %max.34, pred[384]{0:T(512)(128)(4,1)S(1)} %copy-done.11, ...), kind=kOutput, calls=%fused_computation.35 | convolution fusion | flops 204996608 | bytes 5456256 | tf_op jit(solution)/shard_map/tkgs,skd->tkgd/dot_general | solution.py:114
  79.0 1.6 %multiply_reduce_fusion = (f32[128]{0:T(128)S(1)}, f32[128,8,128]{0,2,1:T(8,128)S(1)}) fusion(f32[128,8,128]{0,2,1:T(8,128)S(1)} %fusion.30, bf16[128,8,128]{0,2,1:T(8,128)(2,1)S(1)} %bitcast.147, f32[8,128]{1,0:T(8,128)S(1)} %copy-done.9, pred[128,128]{1,0:T(8,128)(4,1)S(1)} %iota_compare_fusion, bf16[128,1024]{1,0:T(8,128)(2,1)S(1)} %copy-done, ...), kind=kOutput, calls=%fused_computation.44 | convolution fusion | flops 68026240 | bytes 1856000 | tf_op jit(solution)/shard_map/hts,shd->thd/dot_general | solution.py:95
  80.5 10.5 %psum.7 = f32[128]{0:T(128)S(1)} all-reduce(f32[128]{0:T(128)S(1)} %get-tuple-element.80), channel_id=1, replica_groups=mesh['grp'=4,'seq'=32,'head'=4] {'head'}, use_global_device_ids=true, to_apply=%region_6.7 | all-reduce | flops 128 | bytes 1024 | tf_op jit(solution)/shard_map/psum | solution.py:172
  92.2 1.0 %copy.83 = bf16[128,2048]{1,0:T(8,128)(2,1)} copy(bf16[128,2048]{0,1:T(8,128)(2,1)S(1)} %bitcast.151) | data formatting | bytes 1048576
  93.2 0.8 multiply_convert_fusion
  (90 shorter events, 6.6 us)
Async XLA Ops:
  0.6 5.9 %copy-start = (bf16[128,1024]{1,0:T(8,128)(2,1)S(1)}, bf16[128,1024]{1,0:T(8,128)(2,1)}, u32[]{:S(2)}) copy-start(bf16[128,1024]{1,0:T(8,128)(2,1)} %param.11) | copy-start | bytes 786436
  0.6 8.9 %copy-start.6 = (bf16[128,256]{1,0:T(8,128)(2,1)S(1)}, bf16[128,256]{1,0:T(8,128)(2,1)}, u32[]{:S(2)}) copy-start(bf16[128,256]{1,0:T(8,128)(2,1)} %param.15) | copy-start | bytes 196612
  0.7 9.0 %copy-start.7 = (bf16[128,256]{1,0:T(8,128)(2,1)S(1)}, bf16[128,256]{1,0:T(8,128)(2,1)}, u32[]{:S(2)}) copy-start(bf16[128,256]{1,0:T(8,128)(2,1)} %param.16) | copy-start | bytes 196612
  4.6 5.2 %copy-start.8 = (f32[8,128]{1,0:T(8,128)}, f32[8,128]{1,0:T(8,128)S(1)}, u32[]{:S(2)}) copy-start(f32[8,128]{1,0:T(8,128)S(1)} %reduce_window_sum.11) | copy-start | bytes 12292
  6.9 38.0 %copy-start.4 = (bf16[128,2048]{1,0:T(8,128)(2,1)S(1)}, bf16[128,2048]{1,0:T(8,128)(2,1)}, u32[]{:S(2)}) copy-start(bf16[128,2048]{1,0:T(8,128)(2,1)} %param.14) | copy-start | bytes 1572868
  7.8 16.7 %collective-permute-start = (f32[8,129,128]{2,0,1:T(8,128)}, f32[8,129,128]{2,0,1:T(8,128)S(1)}, u32[]{:S(2)}, u32[]{:S(2)}) collective-permute-start(f32[8,129,128]{2,0,1:T(8,128)} %copy.59), channel_id=1, source_target_pairs={{0,4},{8,12},{16,20},{24,28},{32,36},{40,44},{48,52},{56,60},{64,6... | collective-permute-start | bytes 1585160 | tf_op jit(solution)/shard_map/ppermute | solution.py:36
  9.8 14.6 %collective-permute-start.1 = (bf16[2,128,256]{1,2,0:T(8,128)(2,1)S(1)}, bf16[2,128,256]{1,2,0:T(8,128)(2,1)S(1)}, u32[]{:S(2)}, u32[]{:S(2)}) collective-permute-start(bf16[2,128,256]{1,2,0:T(8,128)(2,1)S(1)} %get-tuple-element.62), channel_id=1, source_target_pairs={{0,8},{4,12},{8,16},{12,20},{16,24},{20,28},{24,32},{28,36},{32,40... | collective-permute-start | bytes 393224 | tf_op jit(solution)/shard_map/ppermute | solution.py:31
  25.7 11.0 %collective-permute-start.2 = (bf16[8,130,128]{2,1,0:T(8,128)(2,1)}, bf16[8,130,128]{2,1,0:T(8,128)(2,1)S(1)}, u32[]{:S(2)}, u32[]{:S(2)}) collective-permute-start(bf16[8,130,128]{2,1,0:T(8,128)(2,1)} %pad_maximum_fusion.2), channel_id=1, source_target_pairs={{4,12},{12,20},{20,28},{28,36},{36,44},{44,52},{52,60},{60,68},{68... | collective-permute-start | bytes 798728 | tf_op jit(solution)/shard_map/ppermute | solution.py:51
  26.4 10.4 %collective-permute-start.3 = (bf16[2,128,256]{1,2,0:T(8,128)(2,1)S(1)}, bf16[2,128,256]{1,2,0:T(8,128)(2,1)S(1)}, u32[]{:S(2)}, u32[]{:S(2)}) collective-permute-start(bf16[2,128,256]{1,2,0:T(8,128)(2,1)S(1)} %collective-permute-done.1), channel_id=1, source_target_pairs={{0,8},{4,12},{8,16},{12,20},{16,24},{20,28},{24,32},{28,36},{32,40... | collective-permute-start | bytes 393224 | tf_op jit(solution)/shard_map/ppermute | solution.py:31
  36.8 9.5 %collective-permute-start.5 = (bf16[2,128,256]{1,2,0:T(8,128)(2,1)S(1)}, bf16[2,128,256]{1,2,0:T(8,128)(2,1)S(1)}, u32[]{:S(2)}, u32[]{:S(2)}) collective-permute-start(bf16[2,128,256]{1,2,0:T(8,128)(2,1)S(1)} %collective-permute-done.3), channel_id=1, source_target_pairs={{0,8},{4,12},{8,16},{12,20},{16,24},{20,28},{24,32},{28,36},{32,40... | collective-permute-start | bytes 393224 | tf_op jit(solution)/shard_map/ppermute | solution.py:31
  39.7 6.6 %collective-permute-start.4 = (bf16[8,128,128]{2,1,0:T(8,128)(2,1)}, bf16[8,128,128]{2,1,0:T(8,128)(2,1)}, u32[]{:S(2)}, u32[]{:S(2)}) collective-permute-start(bf16[8,128,128]{2,1,0:T(8,128)(2,1)} %fusion.47), channel_id=1, source_target_pairs={{4,20},{12,28},{20,36},{28,44},{36,52},{44,60},{52,68},{60,76},{68... | collective-permute-start | bytes 786440 | tf_op jit(solution)/shard_map/ppermute | solution.py:57
  46.3 23.2 %collective-permute-start.7 = (bf16[2,128,256]{1,2,0:T(8,128)(2,1)S(1)}, bf16[2,128,256]{1,2,0:T(8,128)(2,1)}, u32[]{:S(2)}, u32[]{:S(2)}) collective-permute-start(bf16[2,128,256]{1,2,0:T(8,128)(2,1)S(1)} %collective-permute-done.5), channel_id=1, source_target_pairs={{4,12},{12,20},{20,28},{28,36},{36,44},{44,52},{52,60},{60,68},{68... | collective-permute-start | bytes 393224 | tf_op jit(solution)/shard_map/ppermute | solution.py:31
  49.4 20.1 %collective-permute-start.6 = (bf16[8,128,128]{2,1,0:T(8,128)(2,1)}, bf16[8,128,128]{2,1,0:T(8,128)(2,1)S(1)}, u32[]{:S(2)}, u32[]{:S(2)}) collective-permute-start(bf16[8,128,128]{2,1,0:T(8,128)(2,1)} %add_convert_fusion.1), channel_id=1, source_target_pairs={{4,8},{12,16},{20,24},{28,32},{36,40},{44,48},{52,56},{60,64},{68,... | collective-permute-start | bytes 786440 | tf_op jit(solution)/shard_map/ppermute | solution.py:64
  51.9 17.6 %collective-permute-start.8 = (bf16[3,2,128,256]{2,3,1,0:T(8,128)(2,1)}, bf16[3,2,128,256]{2,3,1,0:T(8,128)(2,1)S(1)}, u32[]{:S(2)}, u32[]{:S(2)}) collective-permute-start(bf16[3,2,128,256]{2,3,1,0:T(8,128)(2,1)} %maximum_select_fusion), channel_id=1, source_target_pairs={{0,4},{4,0},{8,12},{12,8},{16,20},{20,16},{24,28},{28,24},{32,36},... | collective-permute-start | bytes 1179656 | tf_op jit(solution)/shard_map/ppermute | solution.py:66
  62.0 1.9 %copy-start.1 = (f32[2,512,128,8]{2,1,3,0:T(8,128)}, f32[2,512,128,8]{2,1,3,0:T(8,128)S(1)}, u32[]{:S(2)}) copy-start(f32[2,512,128,8]{2,1,3,0:T(8,128)S(1)} %get-tuple-element.77) | copy-start | bytes 12582916
  69.5 5.6 %copy-start.11 = (pred[384]{0:T(512)(128)(4,1)S(1)}, pred[384]{0:T(512)(128)(4,1)}, u32[]{:S(2)}) copy-start(pred[384]{0:T(512)(128)(4,1)} %add_add_fusion.1) | copy-start | bytes 1156
  69.7 8.9 %collective-permute-start.10 = (bf16[2,128,256]{1,2,0:T(8,128)(2,1)S(1)}, bf16[2,128,256]{1,2,0:T(8,128)(2,1)S(1)}, u32[]{:S(2)}, u32[]{:S(2)}) collective-permute-start(bf16[2,128,256]{1,2,0:T(8,128)(2,1)S(1)} %broadcast_select_fusion), channel_id=1, source_target_pairs={{0,4},{4,0},{8,12},{12,8},{16,20},{20,16},{24,28},{28,24},{32,36},... | collective-permute-start | bytes 393224 | tf_op jit(solution)/shard_map/ppermute | solution.py:75
  72.5 6.1 %collective-permute-start.9 = (bf16[8,128,128]{2,1,0:T(8,128)(2,1)S(1)}, bf16[8,128,128]{2,1,0:T(8,128)(2,1)S(1)}, u32[]{:S(2)}, u32[]{:S(2)}) collective-permute-start(bf16[8,128,128]{2,1,0:T(8,128)(2,1)S(1)} %add_convert_fusion), channel_id=1, source_target_pairs={{0,4},{8,12},{16,20},{24,28},{32,36},{40,44},{48,52},{56,60},{64,6... | collective-permute-start | bytes 786440 | tf_op jit(solution)/shard_map/ppermute | solution.py:74
  75.1 1.5 %copy-start.2 = (f32[128,2,8,128]{0,3,2,1:T(8,128)S(1)}, f32[128,2,8,128]{0,3,2,1:T(8,128)}, u32[]{:S(2)}) copy-start(f32[128,2,8,128]{0,3,2,1:T(8,128)} %fusion.26) | copy-start | bytes 3145732
  76.5 2.1 %copy-start.5 = (bf16[128,1024]{1,0:T(8,128)(2,1)S(1)}, bf16[128,1024]{1,0:T(8,128)(2,1)}, u32[]{:S(2)}) copy-start(bf16[128,1024]{1,0:T(8,128)(2,1)} %param.9) | copy-start | bytes 786436
  76.5 2.1 %copy-start.10 = (f32[128,8]{0,1:T(8,128)S(1)}, f32[128,8]{0,1:T(8,128)}, u32[]{:S(2)}) copy-start(f32[128,8]{0,1:T(8,128)} %get-tuple-element.67) | copy-start | bytes 12292
  76.6 2.4 %copy-start.9 = (f32[8,128]{1,0:T(8,128)S(1)}, f32[8,128]{1,0:T(8,128)}, u32[]{:S(2)}) copy-start(f32[8,128]{1,0:T(8,128)} %copy-done.8) | copy-start | bytes 12292
  78.9 12.9 %copy-start.3 = (f32[128,2,8,128]{0,3,2,1:T(8,128)S(1)}, f32[128,2,8,128]{0,3,2,1:T(8,128)}, u32[]{:S(2)}) copy-start(f32[128,2,8,128]{0,3,2,1:T(8,128)} %multiply_add_fusion) | copy-start | bytes 3145732
  91.8 1.4 %copy-start.12 = (f32[1024]{0:T(1024)S(1)}, f32[1024]{0:T(1024)}, u32[]{:S(2)}) copy-start(f32[1024]{0:T(1024)} %param.13) | copy-start | bytes 12292

commit v8 on v7

--- a/solution.py
+++ b/solution.py
@@ -60,13 +60,13 @@
     wide_state = got.astype(jnp.float32) * wide_gain[:, None, None] + wide_state
     mine = jnp.stack(ring[:half])
     sent = jnp.where(core == 1, jnp.stack(ring[1:half]), jnp.stack(ring[: half - 1]))
-    running = take(running, range(0, width, 2), mine)
     before = lax.ppermute(wide_state.astype(jnp.bfloat16), axis, shift_pairs(count, 1, 1))
-    before, kv_next, theirs, running = lax.optimization_barrier(
-        (before, ring_step(1), lax.ppermute(sent, axis, swap), running)
+    before, kv_next, theirs = lax.optimization_barrier(
+        (before, ring_step(1), lax.ppermute(sent, axis, swap))
     )
     ring.append(kv_next)
     last = jnp.where(core == 1, ring[half], ring[half - 1])
+    running = take(running, range(0, width, 2), mine)
     running = take(running, range(1, width - 2, 2), theirs)
     after = (before.astype(jnp.float32) * gain[:, None, None] + state).astype(jnp.bfloat16)
     after, last, running = lax.optimization_barrier(

time: 94.7 us -> 95.7 us (1.011)
  waiting for transfers between devices: 16 us -> 18.2 us
  other arithmetic: 9.97 us -> 11.2 us
  matrix products: 10.6 us -> 9.4 us
    dot_general x3, matrix products: 6.64 us -> 3.54 us  [absorb(): jnp.einsum('tkgs,skd->tkgd', exponent.astype(jnp.bfloat16), value_rows, p...]
    reduce_sum x3, other arithmetic: 1.78 us -> 4.07 us  [absorb(): row_mass = row_mass * shrink + jnp.sum(exponent, axis=-1)]
    dot_general x3, matrix products: 1.84 us -> 3.75 us  [absorb(): jnp.einsum('tkgd,skd->tkgs', queries, key_rows, preferred_element_type=jn...]
    ppermute x1, waiting for transfers between devices: 0.01 us -> 1.58 us  [exchange(): lax.ppermute(wide_state.astype(jnp.bfloat16), axis, shift_pairs(count, 1,...]
    unnamed x30 -> x24, local copies, waits for them, and re-layouts: 3.31 us -> 1.79 us
  transfers between devices with their start and end apart: 11 -> 11, of which waited for: 3 -> 4; matrix products, arithmetic and copies ran while one was open for 16% -> 17% of each run, Pallas kernels for 0% -> 0%
where the time goes in v8:
time: 95.7 us; the launch traced here: 95 us
  starting transfers between devices  27.7 us (29%)
  waiting for transfers between devices  18.2 us (19%)
  other arithmetic  11.2 us (12%)
  blocking collectives  10.5 us (11%)
  between operations  9.8 us (10%)
  matrix products  9.4 us (10%)
  local copies, waits for them, and re-layouts  8.23 us (9%)
    ppermute x4, waiting for transfers between devices, ring_step(): return lax.ppermute(ring[-1], axis, shift_pairs(count, 2, parity))  16.6 us
    psum x1, blocking collectives, body(): square_sum = lax.psum(jnp.sum(mixed * mixed, axis=1), 'head')  10.5 us
    ppermute x1, starting transfers between devices, exchange(): lax.ppermute(sent, axis, swap)  9.33 us
    ppermute x4, starting transfers between devices, ring_step(): return lax.ppermute(ring[-1], axis, shift_pairs(count, 2, parity))  8.96 us
    reduce_sum x3, other arithmetic, absorb(): row_mass = row_mass * shrink + jnp.sum(exponent, axis=-1)  4.07 us
    dot_general x3, matrix products, absorb(): jnp.einsum('tkgd,skd->tkgs', queries, key_rows, preferred_element_type=jn...  3.75 us
    dot_general x3, matrix products, absorb(): jnp.einsum('tkgs,skd->tkgd', exponent.astype(jnp.bfloat16), value_rows, p...  3.54 us
    convert_element_type x3, other arithmetic, exchange(): wide_state.astype(jnp.bfloat16)  2.82 us
  transfers between devices with their start and end apart: 11, of which 4 were waited for; matrix products, arithmetic and copies ran while one was open for 17% of the time, Pallas kernels for 0%

profile of v8, /device:TPU:24, one launch (start us, length us, event | category | flops | bytes accessed | tf_op | source)
XLA Modules:
  0.0 95.0 jit_solution(16894926588817561190)
XLA Ops:
  0.7 1.7 %fusion.89 = (s32[1]{0:T(128)}, s32[1]{0:T(128)}, s32[1]{0:T(128)}, s32[1]{0:T(128)}, s32[1]{0:T(128)}, /*index=5*/s32[1]{0:T(128)}, s32[1]{0:T(128)}, s32[1]{0:T(128)}) fusion(s32[128]{0:T(128)} %param.17, s32[]{:T(128)S(6)} %max.42, s32[]{:T(128)S(6)} %max.39, s32[]{:T(128)S(6)} %max.38, s32[]{:T(128)S(6)} %max.37, s32[]{:T(128)S(6)} %max.36, ...), kind=kLoop, calls=%fused_computation.113 | loop fusion | bytes 96 | tf_op jit(solution)/shard_map/dynamic_slice | solution.py:150
  3.6 1.0 %reduce_window_sum.11 = f32[8,128]{1,0:T(8,128)S(1)} reduce-window(f32[8,128]{1,0:T(8,128)} %param.12, f32[]{:T(128)} %constant.56.clone.1), window={size=1x128 pad=0_0x127_0}, to_apply=%region_0.0 | reduce-window | flops 130048 | bytes 8196 | tf_op jit(solution)/shard_map/jit(cumsum)/reduce_window_sum | solution.py:89
  5.2 1.1 %copy.102 = bf16[128,1024]{0,1:T(8,128)(2,1)S(1)} copy(bf16[128,1024]{1,0:T(8,128)(2,1)} %param.10) | data formatting | bytes 524288 | tf_op jit(solution)/shard_map/reshape | solution.py:87
  6.7 0.9 copy.59
  7.6 1.8 %collective-permute-start = (f32[8,129,128]{2,0,1:T(8,128)}, f32[8,129,128]{2,0,1:T(8,128)S(1)}, u32[]{:S(2)}, u32[]{:S(2)}) collective-permute-start(f32[8,129,128]{2,0,1:T(8,128)} %copy.59), channel_id=1, source_target_pairs={{0,4},{8,12},{16,20},{24,28},{32,36},{40,44},{48,52},{56,60},{64,6... | collective-permute-start | bytes 1585160 | tf_op jit(solution)/shard_map/ppermute | solution.py:36
  9.7 3.8 %collective-permute-start.1 = (bf16[2,128,256]{1,2,0:T(8,128)(2,1)S(1)}, bf16[2,128,256]{1,2,0:T(8,128)(2,1)S(1)}, u32[]{:S(2)}, u32[]{:S(2)}) collective-permute-start(bf16[2,128,256]{1,2,0:T(8,128)(2,1)S(1)} %get-tuple-element.56), channel_id=1, source_target_pairs={{0,8},{4,12},{8,16},{12,20},{16,24},{20,28},{24,32},{28,36},{32,40... | collective-permute-start | bytes 393224 | tf_op jit(solution)/shard_map/ppermute | solution.py:31
  13.5 10.7 %collective-permute-done.1 = bf16[2,128,256]{1,2,0:T(8,128)(2,1)S(1)} collective-permute-done((bf16[2,128,256]{1,2,0:T(8,128)(2,1)S(1)}, bf16[2,128,256]{1,2,0:T(8,128)(2,1)S(1)}, u32[]{:S(2)}, u32[]{:S(2)}) %collective-permute-start.1) | collective-permute-done | bytes 131104 | tf_op jit(solution)/shard_map/ppermute | solution.py:31
  25.5 1.9 %collective-permute-start.3 = (bf16[2,128,256]{1,2,0:T(8,128)(2,1)S(1)}, bf16[2,128,256]{1,2,0:T(8,128)(2,1)S(1)}, u32[]{:S(2)}, u32[]{:S(2)}) collective-permute-start(bf16[2,128,256]{1,2,0:T(8,128)(2,1)S(1)} %collective-permute-done.1), channel_id=1, source_target_pairs={{0,8},{4,12},{8,16},{12,20},{16,24},{20,28},{24,32},{28,36},{32,40... | collective-permute-start | bytes 393224 | tf_op jit(solution)/shard_map/ppermute | solution.py:31
  31.3 4.6 %collective-permute-done.3 = bf16[2,128,256]{1,2,0:T(8,128)(2,1)S(1)} collective-permute-done((bf16[2,128,256]{1,2,0:T(8,128)(2,1)S(1)}, bf16[2,128,256]{1,2,0:T(8,128)(2,1)S(1)}, u32[]{:S(2)}, u32[]{:S(2)}) %collective-permute-start.3) | collective-permute-done | bytes 131104 | tf_op jit(solution)/shard_map/ppermute | solution.py:31
  35.9 1.9 %collective-permute-start.5 = (bf16[2,128,256]{1,2,0:T(8,128)(2,1)S(1)}, bf16[2,128,256]{1,2,0:T(8,128)(2,1)S(1)}, u32[]{:S(2)}, u32[]{:S(2)}) collective-permute-start(bf16[2,128,256]{1,2,0:T(8,128)(2,1)S(1)} %collective-permute-done.3), channel_id=1, source_target_pairs={{0,8},{4,12},{8,16},{12,20},{16,24},{20,28},{24,32},{28,36},{32,40... | collective-permute-start | bytes 393224 | tf_op jit(solution)/shard_map/ppermute | solution.py:31
  38.0 0.8 fusion.53
  38.8 1.3 %collective-permute-start.4 = (bf16[8,128,128]{2,1,0:T(8,128)(2,1)}, bf16[8,128,128]{2,1,0:T(8,128)(2,1)}, u32[]{:S(2)}, u32[]{:S(2)}) collective-permute-start(bf16[8,128,128]{2,1,0:T(8,128)(2,1)} %fusion.53), channel_id=1, source_target_pairs={{4,20},{12,28},{20,36},{28,44},{36,52},{44,60},{52,68},{60,76},{68... | collective-permute-start | bytes 786440 | tf_op jit(solution)/shard_map/ppermute | solution.py:57
  44.2 1.2 %collective-permute-done.5 = bf16[2,128,256]{1,2,0:T(8,128)(2,1)S(1)} collective-permute-done((bf16[2,128,256]{1,2,0:T(8,128)(2,1)S(1)}, bf16[2,128,256]{1,2,0:T(8,128)(2,1)S(1)}, u32[]{:S(2)}, u32[]{:S(2)}) %collective-permute-start.5) | collective-permute-done | bytes 131104 | tf_op jit(solution)/shard_map/ppermute | solution.py:31
  45.4 1.3 %collective-permute-start.7 = (bf16[2,128,256]{1,2,0:T(8,128)(2,1)S(1)}, bf16[2,128,256]{1,2,0:T(8,128)(2,1)}, u32[]{:S(2)}, u32[]{:S(2)}) collective-permute-start(bf16[2,128,256]{1,2,0:T(8,128)(2,1)S(1)} %collective-permute-done.5), channel_id=1, source_target_pairs={{4,12},{12,20},{20,28},{28,36},{36,44},{44,52},{52,60},{60,68},{68... | collective-permute-start | bytes 393224 | tf_op jit(solution)/shard_map/ppermute | solution.py:31
  46.7 1.8 %add_convert_fusion.1 = bf16[8,128,128]{2,1,0:T(8,128)(2,1)} fusion(bf16[8,128,128]{2,1,0:T(8,128)(2,1)} %collective-permute-done.4, f32[8,128,128]{2,1,0:T(8,128)S(1)} %get-tuple-element.45, f32[8]{0:T(128)S(1)} %get-tuple-element.36, f32[8]{0:T(128)S(1)} %get-tuple-element.37, bf16[8,130,128]{2,1,0:T(8,128)(2,1)S(1)} %collective-permute-done.2), kind=kLoop, calls=%fused_computation.47 | loop fusion | flops 917504 | bytes 1310784 | tf_op jit(solution)/shard_map/convert_element_type | solution.py:63
  48.6 1.3 %collective-permute-start.6 = (bf16[8,128,128]{2,1,0:T(8,128)(2,1)}, bf16[8,128,128]{2,1,0:T(8,128)(2,1)S(1)}, u32[]{:S(2)}, u32[]{:S(2)}) collective-permute-start(bf16[8,128,128]{2,1,0:T(8,128)(2,1)} %add_convert_fusion.1), channel_id=1, source_target_pairs={{4,8},{12,16},{20,24},{28,32},{36,40},{44,48},{52,56},{60,64},{68,... | collective-permute-start | bytes 786440 | tf_op jit(solution)/shard_map/ppermute | solution.py:63
  49.9 0.8 maximum_select_fusion
  50.8 9.3 %collective-permute-start.8 = (bf16[3,2,128,256]{2,3,1,0:T(8,128)(2,1)}, bf16[3,2,128,256]{2,3,1,0:T(8,128)(2,1)S(1)}, u32[]{:S(2)}, u32[]{:S(2)}) collective-permute-start(bf16[3,2,128,256]{2,3,1,0:T(8,128)(2,1)} %maximum_select_fusion), channel_id=1, source_target_pairs={{0,4},{4,0},{8,12},{12,8},{16,20},{20,16},{24,28},{28,24},{32,36},... | collective-permute-start | bytes 1179656 | tf_op jit(solution)/shard_map/ppermute | solution.py:65
  60.4 2.7 %fusion.2 = (f32[128,2,8]{0,2,1:T(8,128)S(1)}, f32[2,512,128,8]{2,1,3,0:T(8,128)}) fusion(pred[128,512]{0,1:T(8,128)(4,1)S(1)} %copy.65, bf16[128,2,8,128]{3,2,1,0:T(8,128)(2,1)S(1)} %bitcast.142, bf16[512,2,128,1]{2,1,0,3:T(2,128)(2,1)S(1)} %bitcast.147), kind=kOutput, calls=%fused_computation.4 | convolution fusion | flops 271579136 | bytes 5054464 | tf_op jit(solution)/shard_map/tkgd,skd->tkgs/dot_general | solution.py:106
  63.4 1.6 %collective-permute-done.6 = bf16[8,128,128]{2,1,0:T(8,128)(2,1)S(1)} collective-permute-done((bf16[8,128,128]{2,1,0:T(8,128)(2,1)}, bf16[8,128,128]{2,1,0:T(8,128)(2,1)S(1)}, u32[]{:S(2)}, u32[]{:S(2)}) %collective-permute-start.6) | collective-permute-done | bytes 262176 | tf_op jit(solution)/shard_map/ppermute | solution.py:63
  65.0 0.8 add_convert_fusion
  65.8 1.9 %collective-permute-start.10 = (bf16[2,128,256]{1,2,0:T(8,128)(2,1)S(1)}, bf16[2,128,256]{1,2,0:T(8,128)(2,1)}, u32[]{:S(2)}, u32[]{:S(2)}) collective-permute-start(bf16[2,128,256]{1,2,0:T(8,128)(2,1)S(1)} %broadcast_select_fusion), channel_id=1, source_target_pairs={{0,4},{4,0},{8,12},{12,8},{16,20},{20,16},{24,28},{28,24},{32,36},... | collective-permute-start | bytes 393224 | tf_op jit(solution)/shard_map/ppermute | solution.py:75
  67.8 2.4 %collective-permute-start.9 = (bf16[8,128,128]{2,1,0:T(8,128)(2,1)}, bf16[8,128,128]{2,1,0:T(8,128)(2,1)S(1)}, u32[]{:S(2)}, u32[]{:S(2)}) collective-permute-start(bf16[8,128,128]{2,1,0:T(8,128)(2,1)} %add_convert_fusion), channel_id=1, source_target_pairs={{0,4},{8,12},{16,20},{24,28},{32,36},{40,44},{48,52},{56,60},{64,6... | collective-permute-start | bytes 786440 | tf_op jit(solution)/shard_map/ppermute | solution.py:74
  71.5 3.2 %fusion.1 = f32[128,2,8]{0,2,1:T(8,128)S(1)} fusion(f32[2,512,128,8]{2,1,3,0:T(8,128)} %get-tuple-element.72, f32[128,2,8]{0,2,1:T(8,128)S(1)} %get-tuple-element.59, pred[128,512]{0,1:T(8,128)(4,1)S(1)} %copy.65), kind=kLoop, calls=%fused_computation.3 | loop fusion | flops 4192256 | bytes 4276224 | tf_op jit(solution)/shard_map/reduce_sum | solution.py:113
  74.7 0.7 fusion.4
  75.5 1.2 %fusion.32 = f32[128,2,8,128]{0,3,2,1:T(8,128)S(1)} fusion(f32[2,512,128,8]{2,1,3,0:T(8,128)S(1)} %copy-done.1, f32[128,2,8]{0,2,1:T(8,128)S(1)} %get-tuple-element.59, pred[128,512]{0,1:T(8,128)(4,1)S(1)} %copy.65, f32[128,2,8]{0,2,1:T(8,128)S(1)} %get-tuple-element.43, f32[128,2,8]{0,2,1:T(8,128)S(1)} %get-tuple-element.57, ...), kind=kOutput, calls=%fused_computation.28 | convolution fusion | flops 273154048 | bytes 5595136 | tf_op jit(solution)/shard_map/tkgs,skd->tkgd/dot_general | solution.py:114
  76.7 2.0 %fusion.21 = f32[128,2,8,128]{0,3,2,1:T(8,128)} fusion(f32[128,2,8,128]{0,3,2,1:T(8,128)S(1)} %fusion.32, f32[2,384,128,8]{2,1,3,0:T(8,128)S(1)} %get-tuple-element.74, f32[128,2,8]{0,2,1:T(8,128)S(1)} %get-tuple-element.27, pred[384]{0:T(512)(128)(4,1)S(1)} %add_add_fusion.1, bf16[384,2,128,1]{0,2,1,3:T(8,128)(2,1)S(1)} %reshape.104), kind=kOutput, calls=%fused_computation.22 | convolution fusion | flops 204734464 | bytes 5448064 | tf_op jit(solution)/shard_map/tkgs,skd->tkgd/dot_general | solution.py:114
  79.1 1.6 %multiply_reduce_fusion = (f32[128]{0:T(128)S(1)}, f32[128,8,128]{0,2,1:T(8,128)S(1)}) fusion(f32[128,8,128]{0,2,1:T(8,128)S(1)} %fusion.36, bf16[128,8,128]{0,2,1:T(8,128)(2,1)S(1)} %bitcast.149, f32[8,128]{1,0:T(8,128)S(1)} %copy-done.8, pred[128,128]{1,0:T(8,128)(4,1)S(1)} %iota_compare_fusion, bf16[128,1024]{1,0:T(8,128)(2,1)S(1)} %copy-done, ...), kind=kOutput, calls=%fused_computation.45 | convolution fusion | flops 68026240 | bytes 1856000 | tf_op jit(solution)/shard_map/hts,shd->thd/dot_general | solution.py:95
  80.6 10.5 %psum.7 = f32[128]{0:T(128)S(1)} all-reduce(f32[128]{0:T(128)S(1)} %get-tuple-element.75), channel_id=1, replica_groups=mesh['grp'=4,'seq'=32,'head'=4] {'head'}, use_global_device_ids=true, to_apply=%region_6.7 | all-reduce | flops 128 | bytes 1024 | tf_op jit(solution)/shard_map/psum | solution.py:172
  91.3 0.9 fusion.88
  93.1 1.0 %copy.83 = bf16[128,2048]{1,0:T(8,128)(2,1)} copy(bf16[128,2048]{0,1:T(8,128)(2,1)S(1)} %bitcast.153) | data formatting | bytes 1048576
  94.2 0.8 multiply_convert_fusion
  (82 shorter events, 6.4 us)
Async XLA Ops:
  0.6 5.7 %copy-start = (bf16[128,1024]{1,0:T(8,128)(2,1)S(1)}, bf16[128,1024]{1,0:T(8,128)(2,1)}, u32[]{:S(2)}) copy-start(bf16[128,1024]{1,0:T(8,128)(2,1)} %param.11) | copy-start | bytes 786436
  0.6 8.7 %copy-start.5 = (bf16[128,256]{1,0:T(8,128)(2,1)S(1)}, bf16[128,256]{1,0:T(8,128)(2,1)}, u32[]{:S(2)}) copy-start(bf16[128,256]{1,0:T(8,128)(2,1)} %param.15) | copy-start | bytes 196612
  0.7 8.9 %copy-start.6 = (bf16[128,256]{1,0:T(8,128)(2,1)S(1)}, bf16[128,256]{1,0:T(8,128)(2,1)}, u32[]{:S(2)}) copy-start(bf16[128,256]{1,0:T(8,128)(2,1)} %param.16) | copy-start | bytes 196612
  4.6 0.6 copy-start.7
  6.7 37.3 %copy-start.3 = (bf16[128,2048]{1,0:T(8,128)(2,1)S(1)}, bf16[128,2048]{1,0:T(8,128)(2,1)}, u32[]{:S(2)}) copy-start(bf16[128,2048]{1,0:T(8,128)(2,1)} %param.14) | copy-start | bytes 1572868
  7.6 16.6 %collective-permute-start = (f32[8,129,128]{2,0,1:T(8,128)}, f32[8,129,128]{2,0,1:T(8,128)S(1)}, u32[]{:S(2)}, u32[]{:S(2)}) collective-permute-start(f32[8,129,128]{2,0,1:T(8,128)} %copy.59), channel_id=1, source_target_pairs={{0,4},{8,12},{16,20},{24,28},{32,36},{40,44},{48,52},{56,60},{64,6... | collective-permute-start | bytes 1585160 | tf_op jit(solution)/shard_map/ppermute | solution.py:36
  9.7 14.6 %collective-permute-start.1 = (bf16[2,128,256]{1,2,0:T(8,128)(2,1)S(1)}, bf16[2,128,256]{1,2,0:T(8,128)(2,1)S(1)}, u32[]{:S(2)}, u32[]{:S(2)}) collective-permute-start(bf16[2,128,256]{1,2,0:T(8,128)(2,1)S(1)} %get-tuple-element.56), channel_id=1, source_target_pairs={{0,8},{4,12},{8,16},{12,20},{16,24},{20,28},{24,32},{28,36},{32,40... | collective-permute-start | bytes 393224 | tf_op jit(solution)/shard_map/ppermute | solution.py:31
  24.9 11.1 %collective-permute-start.2 = (bf16[8,130,128]{2,1,0:T(8,128)(2,1)S(1)}, bf16[8,130,128]{2,1,0:T(8,128)(2,1)S(1)}, u32[]{:S(2)}, u32[]{:S(2)}) collective-permute-start(bf16[8,130,128]{2,1,0:T(8,128)(2,1)S(1)} %pad_maximum_fusion.2), channel_id=1, source_target_pairs={{4,12},{12,20},{20,28},{28,36},{36,44},{44,52},{52,60},{60,68},{68... | collective-permute-start | bytes 798728 | tf_op jit(solution)/shard_map/ppermute | solution.py:51
  25.5 10.4 %collective-permute-start.3 = (bf16[2,128,256]{1,2,0:T(8,128)(2,1)S(1)}, bf16[2,128,256]{1,2,0:T(8,128)(2,1)S(1)}, u32[]{:S(2)}, u32[]{:S(2)}) collective-permute-start(bf16[2,128,256]{1,2,0:T(8,128)(2,1)S(1)} %collective-permute-done.1), channel_id=1, source_target_pairs={{0,8},{4,12},{8,16},{12,20},{16,24},{20,28},{24,32},{28,36},{32,40... | collective-permute-start | bytes 393224 | tf_op jit(solution)/shard_map/ppermute | solution.py:31
  35.9 9.5 %collective-permute-start.5 = (bf16[2,128,256]{1,2,0:T(8,128)(2,1)S(1)}, bf16[2,128,256]{1,2,0:T(8,128)(2,1)S(1)}, u32[]{:S(2)}, u32[]{:S(2)}) collective-permute-start(bf16[2,128,256]{1,2,0:T(8,128)(2,1)S(1)} %collective-permute-done.3), channel_id=1, source_target_pairs={{0,8},{4,12},{8,16},{12,20},{16,24},{20,28},{24,32},{28,36},{32,40... | collective-permute-start | bytes 393224 | tf_op jit(solution)/shard_map/ppermute | solution.py:31
  38.8 6.6 %collective-permute-start.4 = (bf16[8,128,128]{2,1,0:T(8,128)(2,1)}, bf16[8,128,128]{2,1,0:T(8,128)(2,1)}, u32[]{:S(2)}, u32[]{:S(2)}) collective-permute-start(bf16[8,128,128]{2,1,0:T(8,128)(2,1)} %fusion.53), channel_id=1, source_target_pairs={{4,20},{12,28},{20,36},{28,44},{36,52},{44,60},{52,68},{60,76},{68... | collective-permute-start | bytes 786440 | tf_op jit(solution)/shard_map/ppermute | solution.py:57
  45.4 17.9 %collective-permute-start.7 = (bf16[2,128,256]{1,2,0:T(8,128)(2,1)S(1)}, bf16[2,128,256]{1,2,0:T(8,128)(2,1)}, u32[]{:S(2)}, u32[]{:S(2)}) collective-permute-start(bf16[2,128,256]{1,2,0:T(8,128)(2,1)S(1)} %collective-permute-done.5), channel_id=1, source_target_pairs={{4,12},{12,20},{20,28},{28,36},{36,44},{44,52},{52,60},{60,68},{68... | collective-permute-start | bytes 393224 | tf_op jit(solution)/shard_map/ppermute | solution.py:31
  48.6 16.4 %collective-permute-start.6 = (bf16[8,128,128]{2,1,0:T(8,128)(2,1)}, bf16[8,128,128]{2,1,0:T(8,128)(2,1)S(1)}, u32[]{:S(2)}, u32[]{:S(2)}) collective-permute-start(bf16[8,128,128]{2,1,0:T(8,128)(2,1)} %add_convert_fusion.1), channel_id=1, source_target_pairs={{4,8},{12,16},{20,24},{28,32},{36,40},{44,48},{52,56},{60,64},{68,... | collective-permute-start | bytes 786440 | tf_op jit(solution)/shard_map/ppermute | solution.py:63
  50.8 14.2 %collective-permute-start.8 = (bf16[3,2,128,256]{2,3,1,0:T(8,128)(2,1)}, bf16[3,2,128,256]{2,3,1,0:T(8,128)(2,1)S(1)}, u32[]{:S(2)}, u32[]{:S(2)}) collective-permute-start(bf16[3,2,128,256]{2,3,1,0:T(8,128)(2,1)} %maximum_select_fusion), channel_id=1, source_target_pairs={{0,4},{4,0},{8,12},{12,8},{16,20},{20,16},{24,28},{28,24},{32,36},... | collective-permute-start | bytes 1179656 | tf_op jit(solution)/shard_map/ppermute | solution.py:65
  65.8 12.9 %collective-permute-start.10 = (bf16[2,128,256]{1,2,0:T(8,128)(2,1)S(1)}, bf16[2,128,256]{1,2,0:T(8,128)(2,1)}, u32[]{:S(2)}, u32[]{:S(2)}) collective-permute-start(bf16[2,128,256]{1,2,0:T(8,128)(2,1)S(1)} %broadcast_select_fusion), channel_id=1, source_target_pairs={{0,4},{4,0},{8,12},{12,8},{16,20},{20,16},{24,28},{28,24},{32,36},... | collective-permute-start | bytes 393224 | tf_op jit(solution)/shard_map/ppermute | solution.py:75
  67.8 10.9 %collective-permute-start.9 = (bf16[8,128,128]{2,1,0:T(8,128)(2,1)}, bf16[8,128,128]{2,1,0:T(8,128)(2,1)S(1)}, u32[]{:S(2)}, u32[]{:S(2)}) collective-permute-start(bf16[8,128,128]{2,1,0:T(8,128)(2,1)} %add_convert_fusion), channel_id=1, source_target_pairs={{0,4},{8,12},{16,20},{24,28},{32,36},{40,44},{48,52},{56,60},{64,6... | collective-permute-start | bytes 786440 | tf_op jit(solution)/shard_map/ppermute | solution.py:74
  71.5 3.9 %copy-start.1 = (f32[2,512,128,8]{2,1,3,0:T(8,128)S(1)}, f32[2,512,128,8]{2,1,3,0:T(8,128)}, u32[]{:S(2)}) copy-start(f32[2,512,128,8]{2,1,3,0:T(8,128)} %get-tuple-element.72) | copy-start | bytes 12582916
  76.7 2.1 %copy-start.4 = (bf16[128,1024]{1,0:T(8,128)(2,1)S(1)}, bf16[128,1024]{1,0:T(8,128)(2,1)}, u32[]{:S(2)}) copy-start(bf16[128,1024]{1,0:T(8,128)(2,1)} %param.9) | copy-start | bytes 786436
  76.7 2.4 %copy-start.8 = (f32[8,128]{1,0:T(8,128)S(1)}, f32[8,128]{1,0:T(8,128)}, u32[]{:S(2)}) copy-start(f32[8,128]{1,0:T(8,128)} %copy-done.7) | copy-start | bytes 12292
  79.1 13.7 %copy-start.2 = (f32[128,2,8,128]{0,3,2,1:T(8,128)S(1)}, f32[128,2,8,128]{0,3,2,1:T(8,128)}, u32[]{:S(2)}) copy-start(f32[128,2,8,128]{0,3,2,1:T(8,128)} %fusion.21) | copy-start | bytes 3145732
  92.8 1.4 %copy-start.9 = (f32[1024]{0:T(1024)S(1)}, f32[1024]{0:T(1024)}, u32[]{:S(2)}) copy-start(f32[1024]{0:T(1024)} %param.13) | copy-start | bytes 12292

commit v9 on v8

--- a/solution.py
+++ b/solution.py
@@ -2,6 +2,7 @@
 import jax.numpy as jnp
 from jax import lax
 from jax.sharding import PartitionSpec as P
+
 
 LIGHTNING_HEADS = 32
 HEAD_DIM = 128
@@ -33,8 +34,9 @@
     gain, state = element
     rows = state.shape[1]
     packed = jnp.concatenate([state, jnp.broadcast_to(gain[:, None, None], state[:, :1].shape)], 1)
+    kv_next = ring_step()
     got = lax.ppermute(packed, axis, shift_pairs(count, 1, 0))
-    got, kv_next = lax.optimization_barrier((got, ring_step()))
+    got, kv_next = lax.optimization_barrier((got, kv_next))
     ring.append(kv_next)
     wide_state = got[:, :rows] * gain[:, None, None] + state
     wide_gain = got[:, rows, 0] * gain
@@ -172,7 +174,7 @@
     square_sum = lax.psum(jnp.sum(mixed * mixed, axis=1), "head")
     inv_norm = lax.rsqrt(square_sum / (LIGHTNING_HEADS * HEAD_DIM) + 1e-06)
     light_out = (mixed * inv_norm[:, None] * light_gain).astype(jnp.bfloat16)
-    row_max, row_mass, weighted = running
+    _, row_mass, weighted = running
     soft_out = (weighted / row_mass[..., None]).reshape(tok_rows, -1).astype(jnp.bfloat16)
     return (light_out, soft_out)
 
@@ -189,6 +191,7 @@
         P(("grp", "seq"), "head"),
         P(),
     )
+
     return jax.shard_map(
         body,
         mesh=mesh,

time: 95.7 us -> 95.7 us (level)
  no operation moved by 1% of the time
where the time goes in v9:
time: 95.7 us; the launch traced here: 95 us
  starting transfers between devices  27.7 us (29%)
  waiting for transfers between devices  18.2 us (19%)
  other arithmetic  11.2 us (12%)
  blocking collectives  10.5 us (11%)
  between operations  9.8 us (10%)
  matrix products  9.4 us (10%)
  local copies, waits for them, and re-layouts  8.23 us (9%)
    ppermute x4, waiting for transfers between devices, ring_step(): return lax.ppermute(ring[-1], axis, shift_pairs(count, 2, parity))  16.6 us
    psum x1, blocking collectives, body(): square_sum = lax.psum(jnp.sum(mixed * mixed, axis=1), 'head')  10.5 us
    ppermute x1, starting transfers between devices, exchange(): lax.ppermute(sent, axis, swap)  9.33 us
    ppermute x4, starting transfers between devices, ring_step(): return lax.ppermute(ring[-1], axis, shift_pairs(count, 2, parity))  8.96 us
    reduce_sum x3, other arithmetic, absorb(): row_mass = row_mass * shrink + jnp.sum(exponent, axis=-1)  4.07 us
    dot_general x3, matrix products, absorb(): jnp.einsum('tkgd,skd->tkgs', queries, key_rows, preferred_element_type=jn...  3.75 us
    dot_general x3, matrix products, absorb(): jnp.einsum('tkgs,skd->tkgd', exponent.astype(jnp.bfloat16), value_rows, p...  3.54 us
    convert_element_type x3, other arithmetic, exchange(): wide_state.astype(jnp.bfloat16)  2.82 us
  transfers between devices with their start and end apart: 11, of which 4 were waited for; matrix products, arithmetic and copies ran while one was open for 17% of the time, Pallas kernels for 0%

profile of v9, /device:TPU:24, one launch (start us, length us, event | category | flops | bytes accessed | tf_op | source)
XLA Modules:
  0.0 95.0 jit_solution(16894926588817561190)
XLA Ops:
  0.7 1.7 %fusion.89 = (s32[1]{0:T(128)}, s32[1]{0:T(128)}, s32[1]{0:T(128)}, s32[1]{0:T(128)}, s32[1]{0:T(128)}, /*index=5*/s32[1]{0:T(128)}, s32[1]{0:T(128)}, s32[1]{0:T(128)}) fusion(s32[128]{0:T(128)} %param.17, s32[]{:T(128)S(6)} %max.42, s32[]{:T(128)S(6)} %max.39, s32[]{:T(128)S(6)} %max.38, s32[]{:T(128)S(6)} %max.37, s32[]{:T(128)S(6)} %max.36, ...), kind=kLoop, calls=%fused_computation.113 | loop fusion | bytes 96 | tf_op jit(solution)/shard_map/dynamic_slice | solution.py:152
  3.6 1.0 %reduce_window_sum.11 = f32[8,128]{1,0:T(8,128)S(1)} reduce-window(f32[8,128]{1,0:T(8,128)} %param.12, f32[]{:T(128)} %constant.56.clone.1), window={size=1x128 pad=0_0x127_0}, to_apply=%region_0.0 | reduce-window | flops 130048 | bytes 8196 | tf_op jit(solution)/shard_map/jit(cumsum)/reduce_window_sum | solution.py:91
  5.2 1.1 %copy.102 = bf16[128,1024]{0,1:T(8,128)(2,1)S(1)} copy(bf16[128,1024]{1,0:T(8,128)(2,1)} %param.10) | data formatting | bytes 524288 | tf_op jit(solution)/shard_map/reshape | solution.py:89
  6.7 0.9 copy.59
  7.6 1.8 %collective-permute-start = (f32[8,129,128]{2,0,1:T(8,128)}, f32[8,129,128]{2,0,1:T(8,128)S(1)}, u32[]{:S(2)}, u32[]{:S(2)}) collective-permute-start(f32[8,129,128]{2,0,1:T(8,128)} %copy.59), channel_id=1, source_target_pairs={{0,4},{8,12},{16,20},{24,28},{32,36},{40,44},{48,52},{56,60},{64,6... | collective-permute-start | bytes 1585160 | tf_op jit(solution)/shard_map/ppermute | solution.py:38
  9.7 3.8 %collective-permute-start.1 = (bf16[2,128,256]{1,2,0:T(8,128)(2,1)S(1)}, bf16[2,128,256]{1,2,0:T(8,128)(2,1)S(1)}, u32[]{:S(2)}, u32[]{:S(2)}) collective-permute-start(bf16[2,128,256]{1,2,0:T(8,128)(2,1)S(1)} %get-tuple-element.56), channel_id=1, source_target_pairs={{0,8},{4,12},{8,16},{12,20},{16,24},{20,28},{24,32},{28,36},{32,40... | collective-permute-start | bytes 393224 | tf_op jit(solution)/shard_map/ppermute | solution.py:32
  13.5 10.7 %collective-permute-done.1 = bf16[2,128,256]{1,2,0:T(8,128)(2,1)S(1)} collective-permute-done((bf16[2,128,256]{1,2,0:T(8,128)(2,1)S(1)}, bf16[2,128,256]{1,2,0:T(8,128)(2,1)S(1)}, u32[]{:S(2)}, u32[]{:S(2)}) %collective-permute-start.1) | collective-permute-done | bytes 131104 | tf_op jit(solution)/shard_map/ppermute | solution.py:32
  25.5 1.9 %collective-permute-start.3 = (bf16[2,128,256]{1,2,0:T(8,128)(2,1)S(1)}, bf16[2,128,256]{1,2,0:T(8,128)(2,1)S(1)}, u32[]{:S(2)}, u32[]{:S(2)}) collective-permute-start(bf16[2,128,256]{1,2,0:T(8,128)(2,1)S(1)} %collective-permute-done.1), channel_id=1, source_target_pairs={{0,8},{4,12},{8,16},{12,20},{16,24},{20,28},{24,32},{28,36},{32,40... | collective-permute-start | bytes 393224 | tf_op jit(solution)/shard_map/ppermute | solution.py:32
  31.3 4.6 %collective-permute-done.3 = bf16[2,128,256]{1,2,0:T(8,128)(2,1)S(1)} collective-permute-done((bf16[2,128,256]{1,2,0:T(8,128)(2,1)S(1)}, bf16[2,128,256]{1,2,0:T(8,128)(2,1)S(1)}, u32[]{:S(2)}, u32[]{:S(2)}) %collective-permute-start.3) | collective-permute-done | bytes 131104 | tf_op jit(solution)/shard_map/ppermute | solution.py:32
  35.9 1.9 %collective-permute-start.5 = (bf16[2,128,256]{1,2,0:T(8,128)(2,1)S(1)}, bf16[2,128,256]{1,2,0:T(8,128)(2,1)S(1)}, u32[]{:S(2)}, u32[]{:S(2)}) collective-permute-start(bf16[2,128,256]{1,2,0:T(8,128)(2,1)S(1)} %collective-permute-done.3), channel_id=1, source_target_pairs={{0,8},{4,12},{8,16},{12,20},{16,24},{20,28},{24,32},{28,36},{32,40... | collective-permute-start | bytes 393224 | tf_op jit(solution)/shard_map/ppermute | solution.py:32
  38.0 0.8 fusion.53
  38.8 1.3 %collective-permute-start.4 = (bf16[8,128,128]{2,1,0:T(8,128)(2,1)}, bf16[8,128,128]{2,1,0:T(8,128)(2,1)}, u32[]{:S(2)}, u32[]{:S(2)}) collective-permute-start(bf16[8,128,128]{2,1,0:T(8,128)(2,1)} %fusion.53), channel_id=1, source_target_pairs={{4,20},{12,28},{20,36},{28,44},{36,52},{44,60},{52,68},{60,76},{68... | collective-permute-start | bytes 786440 | tf_op jit(solution)/shard_map/ppermute | solution.py:59
  44.2 1.2 %collective-permute-done.5 = bf16[2,128,256]{1,2,0:T(8,128)(2,1)S(1)} collective-permute-done((bf16[2,128,256]{1,2,0:T(8,128)(2,1)S(1)}, bf16[2,128,256]{1,2,0:T(8,128)(2,1)S(1)}, u32[]{:S(2)}, u32[]{:S(2)}) %collective-permute-start.5) | collective-permute-done | bytes 131104 | tf_op jit(solution)/shard_map/ppermute | solution.py:32
  45.4 1.3 %collective-permute-start.7 = (bf16[2,128,256]{1,2,0:T(8,128)(2,1)S(1)}, bf16[2,128,256]{1,2,0:T(8,128)(2,1)}, u32[]{:S(2)}, u32[]{:S(2)}) collective-permute-start(bf16[2,128,256]{1,2,0:T(8,128)(2,1)S(1)} %collective-permute-done.5), channel_id=1, source_target_pairs={{4,12},{12,20},{20,28},{28,36},{36,44},{44,52},{52,60},{60,68},{68... | collective-permute-start | bytes 393224 | tf_op jit(solution)/shard_map/ppermute | solution.py:32
  46.7 1.8 %add_convert_fusion.1 = bf16[8,128,128]{2,1,0:T(8,128)(2,1)} fusion(bf16[8,128,128]{2,1,0:T(8,128)(2,1)} %collective-permute-done.4, f32[8,128,128]{2,1,0:T(8,128)S(1)} %get-tuple-element.45, f32[8]{0:T(128)S(1)} %get-tuple-element.36, f32[8]{0:T(128)S(1)} %get-tuple-element.37, bf16[8,130,128]{2,1,0:T(8,128)(2,1)S(1)} %collective-permute-done.2), kind=kLoop, calls=%fused_computation.47 | loop fusion | flops 917504 | bytes 1310784 | tf_op jit(solution)/shard_map/convert_element_type | solution.py:65
  48.6 1.3 %collective-permute-start.6 = (bf16[8,128,128]{2,1,0:T(8,128)(2,1)}, bf16[8,128,128]{2,1,0:T(8,128)(2,1)S(1)}, u32[]{:S(2)}, u32[]{:S(2)}) collective-permute-start(bf16[8,128,128]{2,1,0:T(8,128)(2,1)} %add_convert_fusion.1), channel_id=1, source_target_pairs={{4,8},{12,16},{20,24},{28,32},{36,40},{44,48},{52,56},{60,64},{68,... | collective-permute-start | bytes 786440 | tf_op jit(solution)/shard_map/ppermute | solution.py:65
  49.9 0.8 maximum_select_fusion
  50.8 9.3 %collective-permute-start.8 = (bf16[3,2,128,256]{2,3,1,0:T(8,128)(2,1)}, bf16[3,2,128,256]{2,3,1,0:T(8,128)(2,1)S(1)}, u32[]{:S(2)}, u32[]{:S(2)}) collective-permute-start(bf16[3,2,128,256]{2,3,1,0:T(8,128)(2,1)} %maximum_select_fusion), channel_id=1, source_target_pairs={{0,4},{4,0},{8,12},{12,8},{16,20},{20,16},{24,28},{28,24},{32,36},... | collective-permute-start | bytes 1179656 | tf_op jit(solution)/shard_map/ppermute | solution.py:67
  60.4 2.7 %fusion.2 = (f32[128,2,8]{0,2,1:T(8,128)S(1)}, f32[2,512,128,8]{2,1,3,0:T(8,128)}) fusion(pred[128,512]{0,1:T(8,128)(4,1)S(1)} %copy.65, bf16[128,2,8,128]{3,2,1,0:T(8,128)(2,1)S(1)} %bitcast.142, bf16[512,2,128,1]{2,1,0,3:T(2,128)(2,1)S(1)} %bitcast.147), kind=kOutput, calls=%fused_computation.4 | convolution fusion | flops 271579136 | bytes 5054464 | tf_op jit(solution)/shard_map/tkgd,skd->tkgs/dot_general | solution.py:108
  63.4 1.6 %collective-permute-done.6 = bf16[8,128,128]{2,1,0:T(8,128)(2,1)S(1)} collective-permute-done((bf16[8,128,128]{2,1,0:T(8,128)(2,1)}, bf16[8,128,128]{2,1,0:T(8,128)(2,1)S(1)}, u32[]{:S(2)}, u32[]{:S(2)}) %collective-permute-start.6) | collective-permute-done | bytes 262176 | tf_op jit(solution)/shard_map/ppermute | solution.py:65
  65.0 0.8 add_convert_fusion
  65.8 1.9 %collective-permute-start.10 = (bf16[2,128,256]{1,2,0:T(8,128)(2,1)S(1)}, bf16[2,128,256]{1,2,0:T(8,128)(2,1)}, u32[]{:S(2)}, u32[]{:S(2)}) collective-permute-start(bf16[2,128,256]{1,2,0:T(8,128)(2,1)S(1)} %broadcast_select_fusion), channel_id=1, source_target_pairs={{0,4},{4,0},{8,12},{12,8},{16,20},{20,16},{24,28},{28,24},{32,36},... | collective-permute-start | bytes 393224 | tf_op jit(solution)/shard_map/ppermute | solution.py:77
  67.8 2.4 %collective-permute-start.9 = (bf16[8,128,128]{2,1,0:T(8,128)(2,1)}, bf16[8,128,128]{2,1,0:T(8,128)(2,1)S(1)}, u32[]{:S(2)}, u32[]{:S(2)}) collective-permute-start(bf16[8,128,128]{2,1,0:T(8,128)(2,1)} %add_convert_fusion), channel_id=1, source_target_pairs={{0,4},{8,12},{16,20},{24,28},{32,36},{40,44},{48,52},{56,60},{64,6... | collective-permute-start | bytes 786440 | tf_op jit(solution)/shard_map/ppermute | solution.py:76
  71.5 3.2 %fusion.1 = f32[128,2,8]{0,2,1:T(8,128)S(1)} fusion(f32[2,512,128,8]{2,1,3,0:T(8,128)} %get-tuple-element.72, f32[128,2,8]{0,2,1:T(8,128)S(1)} %get-tuple-element.59, pred[128,512]{0,1:T(8,128)(4,1)S(1)} %copy.65), kind=kLoop, calls=%fused_computation.3 | loop fusion | flops 4192256 | bytes 4276224 | tf_op jit(solution)/shard_map/reduce_sum | solution.py:115
  74.7 0.7 fusion.4
  75.5 1.2 %fusion.32 = f32[128,2,8,128]{0,3,2,1:T(8,128)S(1)} fusion(f32[2,512,128,8]{2,1,3,0:T(8,128)S(1)} %copy-done.1, f32[128,2,8]{0,2,1:T(8,128)S(1)} %get-tuple-element.59, pred[128,512]{0,1:T(8,128)(4,1)S(1)} %copy.65, f32[128,2,8]{0,2,1:T(8,128)S(1)} %get-tuple-element.43, f32[128,2,8]{0,2,1:T(8,128)S(1)} %get-tuple-element.57, ...), kind=kOutput, calls=%fused_computation.28 | convolution fusion | flops 273154048 | bytes 5595136 | tf_op jit(solution)/shard_map/tkgs,skd->tkgd/dot_general | solution.py:116
  76.7 2.0 %fusion.21 = f32[128,2,8,128]{0,3,2,1:T(8,128)} fusion(f32[128,2,8,128]{0,3,2,1:T(8,128)S(1)} %fusion.32, f32[2,384,128,8]{2,1,3,0:T(8,128)S(1)} %get-tuple-element.74, f32[128,2,8]{0,2,1:T(8,128)S(1)} %get-tuple-element.27, pred[384]{0:T(512)(128)(4,1)S(1)} %add_add_fusion.1, bf16[384,2,128,1]{0,2,1,3:T(8,128)(2,1)S(1)} %reshape.104), kind=kOutput, calls=%fused_computation.22 | convolution fusion | flops 204734464 | bytes 5448064 | tf_op jit(solution)/shard_map/tkgs,skd->tkgd/dot_general | solution.py:116
  79.1 1.6 %multiply_reduce_fusion = (f32[128]{0:T(128)S(1)}, f32[128,8,128]{0,2,1:T(8,128)S(1)}) fusion(f32[128,8,128]{0,2,1:T(8,128)S(1)} %fusion.36, bf16[128,8,128]{0,2,1:T(8,128)(2,1)S(1)} %bitcast.149, f32[8,128]{1,0:T(8,128)S(1)} %copy-done.8, pred[128,128]{1,0:T(8,128)(4,1)S(1)} %iota_compare_fusion, bf16[128,1024]{1,0:T(8,128)(2,1)S(1)} %copy-done, ...), kind=kOutput, calls=%fused_computation.45 | convolution fusion | flops 68026240 | bytes 1856000 | tf_op jit(solution)/shard_map/hts,shd->thd/dot_general | solution.py:97
  80.6 10.5 %psum.7 = f32[128]{0:T(128)S(1)} all-reduce(f32[128]{0:T(128)S(1)} %get-tuple-element.75), channel_id=1, replica_groups=mesh['grp'=4,'seq'=32,'head'=4] {'head'}, use_global_device_ids=true, to_apply=%region_6.7 | all-reduce | flops 128 | bytes 1024 | tf_op jit(solution)/shard_map/psum | solution.py:174
  91.3 0.9 fusion.88
  93.1 1.0 %copy.83 = bf16[128,2048]{1,0:T(8,128)(2,1)} copy(bf16[128,2048]{0,1:T(8,128)(2,1)S(1)} %bitcast.153) | data formatting | bytes 1048576
  94.2 0.8 multiply_convert_fusion
  (82 shorter events, 6.4 us)
Async XLA Ops:
  0.6 5.7 %copy-start = (bf16[128,1024]{1,0:T(8,128)(2,1)S(1)}, bf16[128,1024]{1,0:T(8,128)(2,1)}, u32[]{:S(2)}) copy-start(bf16[128,1024]{1,0:T(8,128)(2,1)} %param.11) | copy-start | bytes 786436
  0.6 8.7 %copy-start.5 = (bf16[128,256]{1,0:T(8,128)(2,1)S(1)}, bf16[128,256]{1,0:T(8,128)(2,1)}, u32[]{:S(2)}) copy-start(bf16[128,256]{1,0:T(8,128)(2,1)} %param.15) | copy-start | bytes 196612
  0.7 8.9 %copy-start.6 = (bf16[128,256]{1,0:T(8,128)(2,1)S(1)}, bf16[128,256]{1,0:T(8,128)(2,1)}, u32[]{:S(2)}) copy-start(bf16[128,256]{1,0:T(8,128)(2,1)} %param.16) | copy-start | bytes 196612
  4.6 0.6 copy-start.7
  6.7 37.3 %copy-start.3 = (bf16[128,2048]{1,0:T(8,128)(2,1)S(1)}, bf16[128,2048]{1,0:T(8,128)(2,1)}, u32[]{:S(2)}) copy-start(bf16[128,2048]{1,0:T(8,128)(2,1)} %param.14) | copy-start | bytes 1572868
  7.6 16.6 %collective-permute-start = (f32[8,129,128]{2,0,1:T(8,128)}, f32[8,129,128]{2,0,1:T(8,128)S(1)}, u32[]{:S(2)}, u32[]{:S(2)}) collective-permute-start(f32[8,129,128]{2,0,1:T(8,128)} %copy.59), channel_id=1, source_target_pairs={{0,4},{8,12},{16,20},{24,28},{32,36},{40,44},{48,52},{56,60},{64,6... | collective-permute-start | bytes 1585160 | tf_op jit(solution)/shard_map/ppermute | solution.py:38
  9.7 14.6 %collective-permute-start.1 = (bf16[2,128,256]{1,2,0:T(8,128)(2,1)S(1)}, bf16[2,128,256]{1,2,0:T(8,128)(2,1)S(1)}, u32[]{:S(2)}, u32[]{:S(2)}) collective-permute-start(bf16[2,128,256]{1,2,0:T(8,128)(2,1)S(1)} %get-tuple-element.56), channel_id=1, source_target_pairs={{0,8},{4,12},{8,16},{12,20},{16,24},{20,28},{24,32},{28,36},{32,40... | collective-permute-start | bytes 393224 | tf_op jit(solution)/shard_map/ppermute | solution.py:32
  24.9 11.1 %collective-permute-start.2 = (bf16[8,130,128]{2,1,0:T(8,128)(2,1)S(1)}, bf16[8,130,128]{2,1,0:T(8,128)(2,1)S(1)}, u32[]{:S(2)}, u32[]{:S(2)}) collective-permute-start(bf16[8,130,128]{2,1,0:T(8,128)(2,1)S(1)} %pad_maximum_fusion.2), channel_id=1, source_target_pairs={{4,12},{12,20},{20,28},{28,36},{36,44},{44,52},{52,60},{60,68},{68... | collective-permute-start | bytes 798728 | tf_op jit(solution)/shard_map/ppermute | solution.py:53
  25.5 10.4 %collective-permute-start.3 = (bf16[2,128,256]{1,2,0:T(8,128)(2,1)S(1)}, bf16[2,128,256]{1,2,0:T(8,128)(2,1)S(1)}, u32[]{:S(2)}, u32[]{:S(2)}) collective-permute-start(bf16[2,128,256]{1,2,0:T(8,128)(2,1)S(1)} %collective-permute-done.1), channel_id=1, source_target_pairs={{0,8},{4,12},{8,16},{12,20},{16,24},{20,28},{24,32},{28,36},{32,40... | collective-permute-start | bytes 393224 | tf_op jit(solution)/shard_map/ppermute | solution.py:32
  35.9 9.5 %collective-permute-start.5 = (bf16[2,128,256]{1,2,0:T(8,128)(2,1)S(1)}, bf16[2,128,256]{1,2,0:T(8,128)(2,1)S(1)}, u32[]{:S(2)}, u32[]{:S(2)}) collective-permute-start(bf16[2,128,256]{1,2,0:T(8,128)(2,1)S(1)} %collective-permute-done.3), channel_id=1, source_target_pairs={{0,8},{4,12},{8,16},{12,20},{16,24},{20,28},{24,32},{28,36},{32,40... | collective-permute-start | bytes 393224 | tf_op jit(solution)/shard_map/ppermute | solution.py:32
  38.8 6.6 %collective-permute-start.4 = (bf16[8,128,128]{2,1,0:T(8,128)(2,1)}, bf16[8,128,128]{2,1,0:T(8,128)(2,1)}, u32[]{:S(2)}, u32[]{:S(2)}) collective-permute-start(bf16[8,128,128]{2,1,0:T(8,128)(2,1)} %fusion.53), channel_id=1, source_target_pairs={{4,20},{12,28},{20,36},{28,44},{36,52},{44,60},{52,68},{60,76},{68... | collective-permute-start | bytes 786440 | tf_op jit(solution)/shard_map/ppermute | solution.py:59
  45.4 17.9 %collective-permute-start.7 = (bf16[2,128,256]{1,2,0:T(8,128)(2,1)S(1)}, bf16[2,128,256]{1,2,0:T(8,128)(2,1)}, u32[]{:S(2)}, u32[]{:S(2)}) collective-permute-start(bf16[2,128,256]{1,2,0:T(8,128)(2,1)S(1)} %collective-permute-done.5), channel_id=1, source_target_pairs={{4,12},{12,20},{20,28},{28,36},{36,44},{44,52},{52,60},{60,68},{68... | collective-permute-start | bytes 393224 | tf_op jit(solution)/shard_map/ppermute | solution.py:32
  48.6 16.4 %collective-permute-start.6 = (bf16[8,128,128]{2,1,0:T(8,128)(2,1)}, bf16[8,128,128]{2,1,0:T(8,128)(2,1)S(1)}, u32[]{:S(2)}, u32[]{:S(2)}) collective-permute-start(bf16[8,128,128]{2,1,0:T(8,128)(2,1)} %add_convert_fusion.1), channel_id=1, source_target_pairs={{4,8},{12,16},{20,24},{28,32},{36,40},{44,48},{52,56},{60,64},{68,... | collective-permute-start | bytes 786440 | tf_op jit(solution)/shard_map/ppermute | solution.py:65
  50.8 14.2 %collective-permute-start.8 = (bf16[3,2,128,256]{2,3,1,0:T(8,128)(2,1)}, bf16[3,2,128,256]{2,3,1,0:T(8,128)(2,1)S(1)}, u32[]{:S(2)}, u32[]{:S(2)}) collective-permute-start(bf16[3,2,128,256]{2,3,1,0:T(8,128)(2,1)} %maximum_select_fusion), channel_id=1, source_target_pairs={{0,4},{4,0},{8,12},{12,8},{16,20},{20,16},{24,28},{28,24},{32,36},... | collective-permute-start | bytes 1179656 | tf_op jit(solution)/shard_map/ppermute | solution.py:67
  65.8 12.9 %collective-permute-start.10 = (bf16[2,128,256]{1,2,0:T(8,128)(2,1)S(1)}, bf16[2,128,256]{1,2,0:T(8,128)(2,1)}, u32[]{:S(2)}, u32[]{:S(2)}) collective-permute-start(bf16[2,128,256]{1,2,0:T(8,128)(2,1)S(1)} %broadcast_select_fusion), channel_id=1, source_target_pairs={{0,4},{4,0},{8,12},{12,8},{16,20},{20,16},{24,28},{28,24},{32,36},... | collective-permute-start | bytes 393224 | tf_op jit(solution)/shard_map/ppermute | solution.py:77
  67.8 10.9 %collective-permute-start.9 = (bf16[8,128,128]{2,1,0:T(8,128)(2,1)}, bf16[8,128,128]{2,1,0:T(8,128)(2,1)S(1)}, u32[]{:S(2)}, u32[]{:S(2)}) collective-permute-start(bf16[8,128,128]{2,1,0:T(8,128)(2,1)} %add_convert_fusion), channel_id=1, source_target_pairs={{0,4},{8,12},{16,20},{24,28},{32,36},{40,44},{48,52},{56,60},{64,6... | collective-permute-start | bytes 786440 | tf_op jit(solution)/shard_map/ppermute | solution.py:76
  71.5 3.9 %copy-start.1 = (f32[2,512,128,8]{2,1,3,0:T(8,128)S(1)}, f32[2,512,128,8]{2,1,3,0:T(8,128)}, u32[]{:S(2)}) copy-start(f32[2,512,128,8]{2,1,3,0:T(8,128)} %get-tuple-element.72) | copy-start | bytes 12582916
  76.7 2.1 %copy-start.4 = (bf16[128,1024]{1,0:T(8,128)(2,1)S(1)}, bf16[128,1024]{1,0:T(8,128)(2,1)}, u32[]{:S(2)}) copy-start(bf16[128,1024]{1,0:T(8,128)(2,1)} %param.9) | copy-start | bytes 786436
  76.7 2.4 %copy-start.8 = (f32[8,128]{1,0:T(8,128)S(1)}, f32[8,128]{1,0:T(8,128)}, u32[]{:S(2)}) copy-start(f32[8,128]{1,0:T(8,128)} %copy-done.7) | copy-start | bytes 12292
  79.1 13.7 %copy-start.2 = (f32[128,2,8,128]{0,3,2,1:T(8,128)S(1)}, f32[128,2,8,128]{0,3,2,1:T(8,128)}, u32[]{:S(2)}) copy-start(f32[128,2,8,128]{0,3,2,1:T(8,128)} %fusion.21) | copy-start | bytes 3145732
  92.8 1.4 %copy-start.9 = (f32[1024]{0:T(1024)S(1)}, f32[1024]{0:T(1024)}, u32[]{:S(2)}) copy-start(f32[1024]{0:T(1024)} %param.13) | copy-start | bytes 12292

commit v10 on v6

v10 whole, which is shorter than its diff:
```python
import jax
import jax.numpy as jnp
from jax import lax
from jax.sharding import PartitionSpec as P


LIGHTNING_HEADS = 32
HEAD_DIM = 128
BLOCK = 128


NEG_FLOOR = -10000.0
MASK_FILL = -1e30


def shift_pairs(count, by, parity=None):
    return [
        (i, i + by)
        for i in range(count)
        if 0 <= i + by < count and (parity is None or i % 2 == parity)
    ]


def exchange(element, kv_pair, axis, core, take, running):
    count = lax.axis_size(axis)
    swap = [(i, i ^ 1) for i in range(count)]
    ring = [kv_pair]

    def ring_step():
        return lax.ppermute(ring[-1], axis, shift_pairs(count, 2))

    gain, state = element
    rows = state.shape[1]
    row_of = lambda v: jnp.broadcast_to(v[:, None, None], state[:, :1].shape)
    packed = jnp.concatenate([state, row_of(gain)], 1)
    kv_next = ring_step()
    partner = lax.ppermute(packed, axis, shift_pairs(count, 1, 0))
    partner, kv_next = lax.optimization_barrier((partner, kv_next))
    ring.append(kv_next)
    partner_state, partner_gain = partner[:, :rows], partner[:, rows, 0]
    wide_state = partner_state * gain[:, None, None] + state
    wide_gain = partner_gain * gain
    high = wide_gain.astype(jnp.bfloat16)
    low = (wide_gain - high.astype(jnp.float32)).astype(jnp.bfloat16)
    packed = jnp.concatenate([wide_state.astype(jnp.bfloat16), row_of(high), row_of(low)], 1)
    got, kv_next = lax.optimization_barrier(
        (lax.ppermute(packed, axis, shift_pairs(count, 2, 1)), ring_step())
    )
    ring.append(kv_next)
    got_gain = got[:, rows, 0].astype(jnp.float32) + got[:, rows + 1, 0].astype(jnp.float32)
    wide_state = got[:, :rows].astype(jnp.float32) * wide_gain[:, None, None] + wide_state
    wide_gain = got_gain * wide_gain
    sent = jnp.where(core == 1, jnp.stack(ring[1:3]), jnp.stack(ring[0:2]))
    running = take(running, [0, 2], jnp.stack(ring[0:2]))
    got, kv_next, theirs, running = lax.optimization_barrier(
        (
            lax.ppermute(wide_state.astype(jnp.bfloat16), axis, shift_pairs(count, 4, 1)),
            ring_step(),
            lax.ppermute(sent, axis, swap),
            running,
        )
    )
    ring.append(kv_next)
    outgoing = (got.astype(jnp.float32) * wide_gain[:, None, None] + wide_state).astype(jnp.bfloat16)
    split = outgoing.size // HEAD_DIM
    cross = jnp.concatenate([outgoing.reshape(-1, HEAD_DIM), ring[3].reshape(-1, HEAD_DIM)])
    sent = jnp.where(core == 1, jnp.stack([ring[3], ring[3]]), jnp.stack(ring[2:4]))
    running = take(running, [4, 6, 1, 3], jnp.concatenate([jnp.stack(ring[2:4]), theirs]))
    cross, ahead, theirs, running = lax.optimization_barrier(
        (
            lax.ppermute(cross, axis, shift_pairs(count, 1, 1)),
            lax.ppermute(outgoing, axis, shift_pairs(count, 2, 1)),
            lax.ppermute(sent, axis, swap),
            running,
        )
    )
    behind = cross[:split].reshape(outgoing.shape)
    after = ahead.astype(jnp.float32) * partner_gain[:, None, None] + partner_state
    last = jnp.where(
        core == 0, jnp.stack([theirs[0], cross[split:].reshape(kv_pair.shape)]), theirs
    )
    running = take(running, [5, 7], last)
    return jnp.where(core == 0, behind, after.astype(jnp.bfloat16)), running


def lightning_local(light_q, light_k, light_v, log_decay, joined):
    tok_rows, feat_width = light_q.shape
    head_count = feat_width // HEAD_DIM
    queries = light_q.reshape(tok_rows, head_count, HEAD_DIM)
    key_rows = light_k.reshape(tok_rows, head_count, HEAD_DIM)
    value_rows = light_v.reshape(tok_rows, head_count, HEAD_DIM)
    levels = jnp.cumsum(log_decay, axis=1)
    offsets = jnp.arange(tok_rows, dtype=jnp.int32)
    allowed = offsets[:, None] >= offsets[None, :]
    decays = jnp.exp(jnp.where(allowed[None], levels[:, :, None] - levels[:, None, :], NEG_FLOOR))
    scores = jnp.einsum("thd,shd->hts", queries, key_rows, preferred_element_type=jnp.float32)
    weights = (scores * decays).astype(jnp.bfloat16)
    intra_part = jnp.einsum("hts,shd->thd", weights, value_rows, preferred_element_type=jnp.float32)
    tail_gain = jnp.exp(levels[:, tok_rows - 1 : tok_rows] - levels)
    keyed = (key_rows * tail_gain.T[:, :, None]).astype(jnp.bfloat16)
    local_state = jnp.einsum("shd,she->hde", keyed, value_rows, preferred_element_type=jnp.float32)
    carry_gain = jnp.where(joined, jnp.exp(levels[:, tok_rows - 1]), 0.0)
    reach_gain = jnp.where(joined, jnp.exp(levels), 0.0)
    return (intra_part, (carry_gain, local_state), reach_gain, queries)


def absorb(running, queries, key_rows, value_rows, allowed):
    row_max, row_mass, weighted = running
    scores = jnp.einsum(
        "tkgd,skd->tkgs", queries, key_rows, preferred_element_type=jnp.float32
    ) * HEAD_DIM ** (-0.5)
    scores = jnp.where(allowed[:, None, None, :], scores, MASK_FILL)
    new_max = jnp.maximum(row_max, jnp.max(scores, axis=-1))
    exponent = jnp.exp(scores - new_max[..., None])
    shrink = jnp.exp(row_max - new_max)
    row_mass = row_mass * shrink + jnp.sum(exponent, axis=-1)
    update = jnp.einsum(
        "tkgs,skd->tkgd",
        exponent.astype(jnp.bfloat16),
        value_rows,
        preferred_element_type=jnp.float32,
    )
    weighted = weighted * shrink[..., None] + update
    return (new_max, row_mass, weighted)


def body(light_q, light_k, light_v, log_decay, light_gain, soft_q, soft_k, soft_v, segment_ids):
    tok_rows = light_q.shape[0]
    assert tok_rows == BLOCK
    position = lax.axis_index(("grp", "seq"))
    here_seg = segment_ids[position]
    joined = (position > 0) & (segment_ids[jnp.maximum(position - 1, 0)] == here_seg)
    intra_part, element, reach_gain, queries = lightning_local(
        light_q, light_k, light_v, log_decay, joined
    )
    core = position % 2
    kv_heads = soft_k.shape[1] // HEAD_DIM
    group_size = soft_q.shape[1] // soft_k.shape[1]
    soft_queries = soft_q.reshape(tok_rows, kv_heads, group_size, HEAD_DIM)

    causal = jnp.arange(tok_rows)[:, None] >= jnp.arange(tok_rows)[None, :]

    def take(running, slot_list, chosen):
        key_rows = chosen[:, 0].reshape(-1, kv_heads, HEAD_DIM)
        value_rows = chosen[:, 1].reshape(-1, kv_heads, HEAD_DIM)
        allowed = jnp.concatenate(
            [
                causal
                if source == 0
                else jnp.broadcast_to(
                    (position >= source)
                    & (segment_ids[jnp.maximum(position - source, 0)] == here_seg),
                    causal.shape,
                )
                for source in slot_list
            ],
            axis=1,
        )
        return absorb(running, soft_queries, key_rows, value_rows, allowed)

    running = (
        jnp.full((tok_rows, kv_heads, group_size), MASK_FILL, jnp.float32),
        jnp.zeros((tok_rows, kv_heads, group_size), jnp.float32),
        jnp.zeros((tok_rows, kv_heads, group_size, HEAD_DIM), jnp.float32),
    )
    state_rounded, running = exchange(
        element, jnp.stack([soft_k, soft_v]), ("grp", "seq"), core, take, running
    )
    inter_part = (
        jnp.einsum("thd,hde->the", queries, state_rounded, preferred_element_type=jnp.float32)
        * reach_gain.T[:, :, None]
    )
    mixed = (intra_part + inter_part).reshape(tok_rows, -1)
    square_sum = lax.psum(jnp.sum(mixed * mixed, axis=1), "head")
    inv_norm = lax.rsqrt(square_sum / (LIGHTNING_HEADS * HEAD_DIM) + 1e-06)
    light_out = (mixed * inv_norm[:, None] * light_gain).astype(jnp.bfloat16)
    _, row_mass, weighted = running
    soft_out = (weighted / row_mass[..., None]).reshape(tok_rows, -1).astype(jnp.bfloat16)
    return (light_out, soft_out)


def solution(mesh):
    placed = (
        P(("grp", "seq"), "head"),
        P(("grp", "seq"), "head"),
        P(("grp", "seq"), "head"),
        P("head", ("grp", "seq")),
        P("head"),
        P(("grp", "seq"), "head"),
        P(("grp", "seq"), "head"),
        P(("grp", "seq"), "head"),
        P(),
    )

    return jax.shard_map(
        body,
        mesh=mesh,
        in_specs=placed,
        out_specs=(P(("grp", "seq"), "head"), P(("grp", "seq"), "head")),
        check_vma=False,
    )
```

time: 103 us -> 99.7 us (0.968)
  between operations: 2.73 us -> 9.77 us
  other arithmetic: 22.2 us -> 18 us
  matrix products: 13.8 us -> 10 us
  local copies, waits for them, and re-layouts: 19.1 us -> 15.3 us
  starting transfers between devices: 22.9 us -> 25.7 us
    ppermute x3, waiting for transfers between devices: 10 us -> 1.56 us  [ring_step(): return lax.ppermute(ring[-1], axis, shift_pairs(count, 2))]
    ppermute x1, waiting for transfers between devices: 0.01 us -> 7.79 us  [exchange(): lax.ppermute(cross, axis, shift_pairs(count, 1, 1))]
    reshape x7 -> x0, local copies, waits for them, and re-layouts: 4.32 us -> none  [token_segments(): return jnp.repeat(blocks, BLOCK)]
    ppermute x3, starting transfers between devices: 7.64 us -> 9.92 us  [ring_step(): return lax.ppermute(ring[-1], axis, shift_pairs(count, 2))]
    and x2 -> x0, other arithmetic: 1.92 us -> none  [take(): (key_pos[None, :] <= query_pos[:, None]) & (key_pos >= 0)[None, :]]
    eq x2 -> x0, other arithmetic: 1.91 us -> none  [take(): key_seg[None, :] == seg_tok[:, None]]
    concatenate x1, other arithmetic: 1.72 us -> 0.03 us  [exchange(): jnp.concatenate([outgoing.reshape(-1, HEAD_DIM), ring[3].reshape(-1, HEAD...]
    unnamed x40 -> x53, local copies, waits for them, and re-layouts: 2.25 us -> 3.91 us
  transfers between devices with their start and end apart: 10 -> 10, of which waited for: 2 -> 2; matrix products, arithmetic and copies ran while one was open for 36% -> 23% of each run, Pallas kernels for 0% -> 0%
where the time goes in v10:
time: 99.7 us; the launch traced here: 98.6 us
  starting transfers between devices  25.7 us (26%)
  other arithmetic  18 us (18%)
  local copies, waits for them, and re-layouts  15.3 us (15%)
  blocking collectives  10.5 us (11%)
  matrix products  10 us (10%)
  between operations  9.77 us (10%)
  waiting for transfers between devices  9.37 us (9%)
    psum x1, blocking collectives, body(): square_sum = lax.psum(jnp.sum(mixed * mixed, axis=1), 'head')  10.5 us
    ppermute x2, starting transfers between devices, exchange(): lax.ppermute(sent, axis, swap)  9.97 us
    ppermute x3, starting transfers between devices, ring_step(): return lax.ppermute(ring[-1], axis, shift_pairs(count, 2))  9.92 us
    ppermute x1, waiting for transfers between devices, exchange(): lax.ppermute(cross, axis, shift_pairs(count, 1, 1))  7.79 us
    dot_general x3, matrix products, absorb(): jnp.einsum('tkgs,skd->tkgd', exponent.astype(jnp.bfloat16), value_rows, p...  5.21 us
    unnamed x53, local copies, waits for them, and re-layouts  3.91 us
    dot_general x3, matrix products, absorb(): jnp.einsum('tkgd,skd->tkgs', queries, key_rows, preferred_element_type=jn...  2.67 us
    another operation x3, local copies, waits for them, and re-layouts, take(): value_rows = chosen[:, 1].reshape(-1, kv_heads, HEAD_DIM)  2.4 us
  transfers between devices with their start and end apart: 10, of which 2 were waited for; matrix products, arithmetic and copies ran while one was open for 23% of the time, Pallas kernels for 0%

profile of v10, /device:TPU:24, one launch (start us, length us, event | category | flops | bytes accessed | tf_op | source)
XLA Modules:
  0.0 98.6 jit_solution(16827126092265467630)
XLA Ops:
  0.7 1.6 %fusion.84 = (s32[1]{0:T(128)}, s32[1]{0:T(128)}, s32[1]{0:T(128)}, s32[1]{0:T(128)}, s32[1]{0:T(128)}, /*index=5*/s32[1]{0:T(128)}, s32[1]{0:T(128)}, s32[1]{0:T(128)}) fusion(s32[128]{0:T(128)} %param.17, s32[]{:T(128)S(6)} %max.35, s32[]{:T(128)S(6)} %max.32, s32[]{:T(128)S(6)} %max.31, s32[]{:T(128)S(6)} %max.30, s32[]{:T(128)S(6)} %max.29, ...), kind=kLoop, calls=%fused_computation.123 | loop fusion | bytes 96 | tf_op jit(solution)/shard_map/dynamic_slice | solution.py:152
  3.5 1.0 reduce_window_sum.11
  5.3 1.2 %copy.102 = bf16[128,1024]{0,1:T(8,128)(2,1)S(1)} copy(bf16[128,1024]{1,0:T(8,128)(2,1)} %param.10) | data formatting | bytes 524288 | tf_op jit(solution)/shard_map/reshape | solution.py:90
  7.0 1.8 %collective-permute-start = (f32[8,129,128]{2,0,1:T(8,128)S(1)}, f32[8,129,128]{2,0,1:T(8,128)S(1)}, u32[]{:S(2)}, u32[]{:S(2)}) collective-permute-start(f32[8,129,128]{2,0,1:T(8,128)S(1)} %copy.55), channel_id=1, source_target_pairs={{0,4},{8,12},{16,20},{24,28},{32,36},{40,44},{48,52},{56,60},{64,6... | collective-permute-start | bytes 1585160 | tf_op jit(solution)/shard_map/ppermute | solution.py:37
  8.8 3.8 %collective-permute-start.1 = (bf16[2,128,256]{2,1,0:T(8,128)(2,1)S(1)}, bf16[2,128,256]{2,1,0:T(8,128)(2,1)}, u32[]{:S(2)}, u32[]{:S(2)}) collective-permute-start(bf16[2,128,256]{2,1,0:T(8,128)(2,1)S(1)} %get-tuple-element.60), channel_id=1, source_target_pairs={{0,8},{4,12},{8,16},{12,20},{16,24},{20,28},{24,32},{28,36},{32,40... | collective-permute-start | bytes 393224 | tf_op jit(solution)/shard_map/ppermute | solution.py:30
  21.9 1.6 %collective-permute-done.1 = bf16[2,128,256]{2,1,0:T(8,128)(2,1)} collective-permute-done((bf16[2,128,256]{2,1,0:T(8,128)(2,1)S(1)}, bf16[2,128,256]{2,1,0:T(8,128)(2,1)}, u32[]{:S(2)}, u32[]{:S(2)}) %collective-permute-start.1) | collective-permute-done | bytes 131104 | tf_op jit(solution)/shard_map/ppermute | solution.py:30
  23.6 2.3 %collective-permute-start.3 = (bf16[2,128,256]{2,1,0:T(8,128)(2,1)}, bf16[2,128,256]{2,1,0:T(8,128)(2,1)}, u32[]{:S(2)}, u32[]{:S(2)}) collective-permute-start(bf16[2,128,256]{2,1,0:T(8,128)(2,1)} %collective-permute-done.1), channel_id=1, source_target_pairs={{0,8},{4,12},{8,16},{12,20},{16,24},{20,28},{24,32},{28,36},{32,40... | collective-permute-start | bytes 393224 | tf_op jit(solution)/shard_map/ppermute | solution.py:30
  26.7 1.6 %fusion.68 = (bf16[2,1,128,256]{3,2,1,0:T(8,128)(2,1)}, bf16[2,1,128,256]{3,2,1,0:T(8,128)(2,1)S(1)}) fusion(bf16[1,2,128,256]{3,2,1,0:T(8,128)(2,1)S(1)} %get-tuple-element.59, bf16[1,2,128,256]{3,2,1,0:T(8,128)(2,1)} %bitcast.6), kind=kLoop, calls=%fused_computation.87 | loop fusion | flops 131072 | bytes 524288 | tf_op jit(solution)/shard_map/stack | solution.py:53
  29.8 1.4 %collective-permute-start.2 = (bf16[8,130,128]{2,1,0:T(8,128)(2,1)}, bf16[8,130,128]{2,1,0:T(8,128)(2,1)}, u32[]{:S(2)}, u32[]{:S(2)}) collective-permute-start(bf16[8,130,128]{2,1,0:T(8,128)(2,1)} %pad_maximum_fusion.6), channel_id=1, source_target_pairs={{4,12},{12,20},{20,28},{28,36},{36,44},{44,52},{52,60},{60,68},{68... | collective-permute-start | bytes 798728 | tf_op jit(solution)/shard_map/ppermute | solution.py:47
  31.2 1.4 %fusion.85 = (f32[128,2,8]{0,2,1:T(8,128)S(1)}, f32[128,2,8,256]{0,3,2,1:T(8,128)S(1)}) fusion(bf16[128,2,8,128]{3,2,1,0:T(8,128)(2,1)S(1)} %bitcast.123, bf16[256,2,128,1]{2,1,0,3:T(2,128)(2,1)} %bitcast.133, pred[128,256]{0,1:T(8,128)(4,1)} %concatenate.23.clone), kind=kOutput, calls=%fused_computation.124 | convolution fusion | flops 135788544 | bytes 2793472 | tf_op jit(solution)/shard_map/tkgd,skd->tkgs/dot_general | solution.py:109
  33.4 1.6 %reshape.110 = bf16[256,2,128]{2,1,0:T(2,128)(2,1)} reshape(bf16[2,1,128,256]{3,2,1,0:T(8,128)(2,1)} %get-tuple-element.57) | data formatting | bytes 262144 | tf_op jit(solution)/shard_map/reshape;squeeze | solution.py:145
  35.0 1.3 %exponential_multiply_fusion = (f32[128,2,8]{0,2,1:T(8,128)S(1)}, f32[128,2,8]{0,2,1:T(8,128)}) fusion(f32[128,2,8]{0,2,1:T(8,128)S(1)} %get-tuple-element.74, f32[128,2,8]{0,2,1:T(8,128)} %fusion.11), kind=kLoop, calls=%fused_computation.98 | loop fusion | flops 8192 | bytes 32768 | tf_op jit(solution)/shard_map/mul;broadcast_in_dim | solution.py:116
  36.3 3.8 %collective-permute-start.5 = (bf16[2,128,256]{2,1,0:T(8,128)(2,1)}, bf16[2,128,256]{2,1,0:T(8,128)(2,1)}, u32[]{:S(2)}, u32[]{:S(2)}) collective-permute-start(bf16[2,128,256]{2,1,0:T(8,128)(2,1)} %collective-permute-done.3), channel_id=1, source_target_pairs={{0,8},{4,12},{8,16},{12,20},{16,24},{20,28},{24,32},{28,36},{32,40... | collective-permute-start | bytes 393224 | tf_op jit(solution)/shard_map/ppermute | solution.py:30
  40.2 0.9 multiply_reduce_fusion.1
  41.1 1.1 %fusion.38 = bf16[8,128,128]{2,1,0:T(8,128)(2,1)S(1)} fusion(f32[8,128,128]{2,1,0:T(8,128)S(1)} %get-tuple-element.49, f32[8]{0:T(128)S(1)} %get-tuple-element.41, bf16[8,130,128]{2,1,0:T(8,128)(2,1)} %collective-permute-done.2), kind=kLoop, calls=%fused_computation.55 | loop fusion | flops 524288 | bytes 1048608 | tf_op jit(solution)/shard_map/convert_element_type | solution.py:57
  42.9 1.1 %fusion.40 = bf16[2,2,128,256]{3,2,1,0:T(8,128)(2,1)S(1)} fusion(bf16[1,2,128,256]{3,2,1,0:T(8,128)(2,1)} %bitcast.6, bf16[1,2,128,256]{3,2,1,0:T(8,128)(2,1)S(1)} %get-tuple-element.59, bf16[1,2,128,256]{3,2,1,0:T(8,128)(2,1)} %bitcast.7, pred[]{:T(512)S(6)} %eq.56), kind=kLoop, calls=%fused_computation.65 | loop fusion | flops 393216 | bytes 655361 | tf_op jit(solution)/shard_map/jit(_where)/select_n | solution.py:53
  44.0 8.0 %collective-permute-start.6 = (bf16[2,2,128,256]{3,2,1,0:T(8,128)(2,1)S(1)}, bf16[2,2,128,256]{3,2,1,0:T(8,128)(2,1)S(1)}, u32[]{:S(2)}, u32[]{:S(2)}) collective-permute-start(bf16[2,2,128,256]{3,2,1,0:T(8,128)(2,1)S(1)} %fusion.40), channel_id=1, source_target_pairs={{0,4},{4,0},{8,12},{12,8},{16,20},{20,16},{24,28},{28,24},{32,36},... | collective-permute-start | bytes 786440 | tf_op jit(solution)/shard_map/ppermute | solution.py:59
  52.0 2.4 %fusion.17 = f32[128,2,8,128]{0,3,2,1:T(8,128)} fusion(f32[128,2,8,256]{0,3,2,1:T(8,128)S(1)} %get-tuple-element.75, f32[128,2,8]{0,2,1:T(8,128)S(1)} %broadcast_maximum_fusion, f32[128,2,8]{0,2,1:T(8,128)S(1)} %get-tuple-element.61, bf16[256,2,128,1]{2,1,0,3:T(2,128)(2,1)} %bitcast.132), kind=kOutput, calls=%fused_computation.23 | convolution fusion | flops 135528448 | bytes 3293184 | tf_op jit(solution)/shard_map/tkgs,skd->tkgd/dot_general | solution.py:117
  56.7 1.0 %reshape.101 = bf16[512,128]{1,0:T(8,128)(2,1)S(1)} reshape(bf16[2,128,256]{2,1,0:T(8,128)(2,1)} %collective-permute-done.5) | data formatting | bytes 262144 | tf_op jit(solution)/shard_map/reshape | solution.py:66
  57.7 1.8 %fusion.39 = bf16[2,2,128,256]{3,2,1,0:T(8,128)(2,1)} fusion(bf16[1,2,128,256]{3,2,1,0:T(8,128)(2,1)} %bitcast.15, bf16[1,2,128,256]{3,2,1,0:T(8,128)(2,1)} %bitcast.7, pred[]{:T(512)S(6)} %eq.56), kind=kLoop, calls=%fused_computation.64 | loop fusion | flops 393216 | bytes 524289 | tf_op jit(solution)/shard_map/jit(_where)/select_n | solution.py:67
  59.5 1.1 %pad_maximum_fusion.1 = bf16[4,2,128,256]{3,2,1,0:T(8,128)(2,1)S(1)} fusion(bf16[2,2,128,256]{3,2,1,0:T(8,128)(2,1)} %copy-done.13, bf16[1,2,128,256]{3,2,1,0:T(8,128)(2,1)} %bitcast.15, bf16[1,2,128,256]{3,2,1,0:T(8,128)(2,1)} %bitcast.7), kind=kLoop, calls=%fused_computation.38 | loop fusion | flops 524288 | bytes 1048576 | tf_op jit(solution)/shard_map/concatenate | solution.py:68
  61.5 1.9 %collective-permute-start.9 = (bf16[2,2,128,256]{3,2,1,0:T(8,128)(2,1)}, bf16[2,2,128,256]{3,2,1,0:T(8,128)(2,1)}, u32[]{:S(2)}, u32[]{:S(2)}) collective-permute-start(bf16[2,2,128,256]{3,2,1,0:T(8,128)(2,1)} %fusion.39), channel_id=1, source_target_pairs={{0,4},{4,0},{8,12},{12,8},{16,20},{20,16},{24,28},{28,24},{32,36},... | collective-permute-start | bytes 786440 | tf_op jit(solution)/shard_map/ppermute | solution.py:73
  63.4 1.1 %add_convert_fusion.1 = bf16[8,128,128]{2,1,0:T(8,128)(2,1)S(1)} fusion(bf16[8,128,128]{2,1,0:T(8,128)(2,1)S(1)} %copy-done.12, f32[8,128,128]{2,1,0:T(8,128)S(1)} %get-tuple-element.49, f32[8]{0:T(128)S(1)} %get-tuple-element.40, f32[8]{0:T(128)S(1)} %get-tuple-element.41, bf16[8,130,128]{2,1,0:T(8,128)(2,1)} %collective-permute-done.2), kind=kLoop, calls=%fused_computation.42 | loop fusion | flops 917504 | bytes 1310784 | tf_op jit(solution)/shard_map/convert_element_type | solution.py:64
  65.3 1.3 %collective-permute-start.7 = (bf16[1536,128]{1,0:T(8,128)(2,1)S(1)}, bf16[1536,128]{1,0:T(8,128)(2,1)S(1)}, u32[]{:S(2)}, u32[]{:S(2)}) collective-permute-start(bf16[1536,128]{1,0:T(8,128)(2,1)S(1)} %pad_maximum_fusion.2), channel_id=1, source_target_pairs={{4,8},{12,16},{20,24},{28,32},{36,40},{44,48},{52,56},{60,64},{68,... | collective-permute-start | bytes 1179656 | tf_op jit(solution)/shard_map/ppermute | solution.py:71
  67.5 0.9 fusion.1
  68.7 2.1 %multiply_add_fusion = f32[128,2,8,128]{0,3,2,1:T(8,128)} fusion(f32[128,2,8,128]{0,3,2,1:T(8,128)S(1)} %copy-done.3, f32[128,2,8]{0,2,1:T(8,128)S(1)} %get-tuple-element.47, f32[2,512,128,8]{2,1,3,0:T(8,128)S(1)} %get-tuple-element.77, f32[128,2,8]{0,2,1:T(8,128)S(1)} %max.33, pred[512]{0:T(512)(128)(4,1)S(1)} %copy-done.22, ...), kind=kOutput, calls=%fused_computation.33 | convolution fusion | flops 273154048 | bytes 6570496 | tf_op jit(solution)/shard_map/tkgs,skd->tkgd/dot_general | solution.py:117
  70.9 7.8 %collective-permute-done.7 = bf16[1536,128]{1,0:T(8,128)(2,1)S(1)} collective-permute-done((bf16[1536,128]{1,0:T(8,128)(2,1)S(1)}, bf16[1536,128]{1,0:T(8,128)(2,1)S(1)}, u32[]{:S(2)}, u32[]{:S(2)}) %collective-permute-start.7) | collective-permute-done | bytes 393248 | tf_op jit(solution)/shard_map/ppermute | solution.py:71
  79.9 1.5 %multiply_reduce_fusion = (f32[128]{0:T(128)S(1)}, f32[128,8,128]{0,2,1:T(8,128)S(1)}) fusion(f32[128,8,128]{0,2,1:T(8,128)S(1)} %fusion.19, bf16[128,8,128]{0,2,1:T(8,128)(2,1)S(1)} %bitcast.130, f32[8,128]{1,0:T(8,128)S(1)} %copy-done.19, pred[128,128]{1,0:T(8,128)(4,1)S(1)} %copy-done.15, bf16[128,1024]{1,0:T(8,128)(2,1)S(1)} %copy-done, ...), kind=kOutput, calls=%fused_computation.40 | convolution fusion | flops 68026240 | bytes 1856000 | tf_op jit(solution)/shard_map/hts,shd->thd/dot_general | solution.py:98
  81.4 10.5 %psum.7 = f32[128]{0:T(128)S(1)} all-reduce(f32[128]{0:T(128)S(1)} %get-tuple-element.78), channel_id=1, replica_groups=mesh['grp'=4,'seq'=32,'head'=4] {'head'}, use_global_device_ids=true, to_apply=%region_6.7 | all-reduce | flops 128 | bytes 1024 | tf_op jit(solution)/shard_map/psum | solution.py:174
  92.2 1.6 %slice.57 = bf16[1,2,128,256]{3,2,1,0:T(8,128)(2,1)} slice(bf16[2,2,128,256]{3,2,1,0:T(8,128)(2,1)} %collective-permute-done.9), slice={[0:1], [0:2], [0:128], [0:256]} | slice | bytes 262144 | tf_op jit(solution)/shard_map/slice | solution.py:80
  93.8 0.9 maximum_select_fusion
  96.7 1.0 %copy.75 = bf16[128,2048]{1,0:T(8,128)(2,1)} copy(bf16[128,2048]{0,1:T(8,128)(2,1)S(1)} %bitcast.137) | data formatting | bytes 1048576
  (112 shorter events, 16.5 us)
Async XLA Ops:
  0.6 5.9 %copy-start = (bf16[128,1024]{1,0:T(8,128)(2,1)S(1)}, bf16[128,1024]{1,0:T(8,128)(2,1)}, u32[]{:S(2)}) copy-start(bf16[128,1024]{1,0:T(8,128)(2,1)} %param.11) | copy-start | bytes 786436
  0.6 8.1 %copy-start.16 = (bf16[128,256]{1,0:T(8,128)(2,1)S(1)}, bf16[128,256]{1,0:T(8,128)(2,1)}, u32[]{:S(2)}) copy-start(bf16[128,256]{1,0:T(8,128)(2,1)} %param.16) | copy-start | bytes 196612
  0.7 8.1 %copy-start.17 = (bf16[128,256]{1,0:T(8,128)(2,1)S(1)}, bf16[128,256]{1,0:T(8,128)(2,1)}, u32[]{:S(2)}) copy-start(bf16[128,256]{1,0:T(8,128)(2,1)} %param.15) | copy-start | bytes 196612
  4.5 2.0 %copy-start.18 = (f32[8,128]{1,0:T(8,128)}, f32[8,128]{1,0:T(8,128)S(1)}, u32[]{:S(2)}) copy-start(f32[8,128]{1,0:T(8,128)S(1)} %reduce_window_sum.11) | copy-start | bytes 12292
  5.3 14.8 %copy-start.8 = (bf16[128,2048]{1,0:T(8,128)(2,1)S(1)}, bf16[128,2048]{1,0:T(8,128)(2,1)}, u32[]{:S(2)}) copy-start(bf16[128,2048]{1,0:T(8,128)(2,1)} %param.14) | copy-start | bytes 1572868
  6.5 13.7 %copy-start.4 = (bf16[128,1024]{0,1:T(8,128)(2,1)}, bf16[128,1024]{0,1:T(8,128)(2,1)S(1)}, u32[]{:S(2)}) copy-start(bf16[128,1024]{0,1:T(8,128)(2,1)S(1)} %copy.102) | copy-start | bytes 786436
  7.0 16.5 %collective-permute-start = (f32[8,129,128]{2,0,1:T(8,128)S(1)}, f32[8,129,128]{2,0,1:T(8,128)S(1)}, u32[]{:S(2)}, u32[]{:S(2)}) collective-permute-start(f32[8,129,128]{2,0,1:T(8,128)S(1)} %copy.55), channel_id=1, source_target_pairs={{0,4},{8,12},{16,20},{24,28},{32,36},{40,44},{48,52},{56,60},{64,6... | collective-permute-start | bytes 1585160 | tf_op jit(solution)/shard_map/ppermute | solution.py:37
  8.8 14.7 %collective-permute-start.1 = (bf16[2,128,256]{2,1,0:T(8,128)(2,1)S(1)}, bf16[2,128,256]{2,1,0:T(8,128)(2,1)}, u32[]{:S(2)}, u32[]{:S(2)}) collective-permute-start(bf16[2,128,256]{2,1,0:T(8,128)(2,1)S(1)} %get-tuple-element.60), channel_id=1, source_target_pairs={{0,8},{4,12},{8,16},{12,20},{16,24},{20,28},{24,32},{28,36},{32,40... | collective-permute-start | bytes 393224 | tf_op jit(solution)/shard_map/ppermute | solution.py:30
  12.7 15.5 %copy-start.14 = (pred[128,128]{1,0:T(8,128)(4,1)}, pred[128,128]{1,0:T(8,128)(4,1)S(1)}, u32[]{:S(2)}) copy-start(pred[128,128]{1,0:T(8,128)(4,1)S(1)} %iota_compare_fusion) | copy-start | bytes 49156
  23.6 7.5 %copy-start.1 = (f32[8,129,128]{2,1,0:T(8,128)}, f32[8,129,128]{2,1,0:T(8,128)S(1)}, u32[]{:S(2)}) copy-start(f32[8,129,128]{2,1,0:T(8,128)S(1)} %copy.56) | copy-start | bytes 1585156
  23.6 12.7 %collective-permute-start.3 = (bf16[2,128,256]{2,1,0:T(8,128)(2,1)}, bf16[2,128,256]{2,1,0:T(8,128)(2,1)}, u32[]{:S(2)}, u32[]{:S(2)}) collective-permute-start(bf16[2,128,256]{2,1,0:T(8,128)(2,1)} %collective-permute-done.1), channel_id=1, source_target_pairs={{0,8},{4,12},{8,16},{12,20},{16,24},{20,28},{24,32},{28,36},{32,40... | collective-permute-start | bytes 393224 | tf_op jit(solution)/shard_map/ppermute | solution.py:30
  29.8 6.6 %collective-permute-start.2 = (bf16[8,130,128]{2,1,0:T(8,128)(2,1)}, bf16[8,130,128]{2,1,0:T(8,128)(2,1)}, u32[]{:S(2)}, u32[]{:S(2)}) collective-permute-start(bf16[8,130,128]{2,1,0:T(8,128)(2,1)} %pad_maximum_fusion.6), channel_id=1, source_target_pairs={{4,12},{12,20},{20,28},{28,36},{36,44},{44,52},{52,60},{60,68},{68... | collective-permute-start | bytes 798728 | tf_op jit(solution)/shard_map/ppermute | solution.py:47
  36.3 19.0 %collective-permute-start.5 = (bf16[2,128,256]{2,1,0:T(8,128)(2,1)}, bf16[2,128,256]{2,1,0:T(8,128)(2,1)}, u32[]{:S(2)}, u32[]{:S(2)}) collective-permute-start(bf16[2,128,256]{2,1,0:T(8,128)(2,1)} %collective-permute-done.3), channel_id=1, source_target_pairs={{0,8},{4,12},{8,16},{12,20},{16,24},{20,28},{24,32},{28,36},{32,40... | collective-permute-start | bytes 393224 | tf_op jit(solution)/shard_map/ppermute | solution.py:30
  42.2 13.1 %collective-permute-start.4 = (bf16[8,128,128]{2,1,0:T(8,128)(2,1)S(1)}, bf16[8,128,128]{2,1,0:T(8,128)(2,1)S(1)}, u32[]{:S(2)}, u32[]{:S(2)}) collective-permute-start(bf16[8,128,128]{2,1,0:T(8,128)(2,1)S(1)} %fusion.38), channel_id=1, source_target_pairs={{4,20},{12,28},{20,36},{28,44},{36,52},{44,60},{52,68},{60,76},{68... | collective-permute-start | bytes 786440 | tf_op jit(solution)/shard_map/ppermute | solution.py:57
  44.0 11.3 %collective-permute-start.6 = (bf16[2,2,128,256]{3,2,1,0:T(8,128)(2,1)S(1)}, bf16[2,2,128,256]{3,2,1,0:T(8,128)(2,1)S(1)}, u32[]{:S(2)}, u32[]{:S(2)}) collective-permute-start(bf16[2,2,128,256]{3,2,1,0:T(8,128)(2,1)S(1)} %fusion.40), channel_id=1, source_target_pairs={{0,4},{4,0},{8,12},{12,8},{16,20},{20,16},{24,28},{28,24},{32,36},... | collective-permute-start | bytes 786440 | tf_op jit(solution)/shard_map/ppermute | solution.py:59
  56.7 6.7 %copy-start.12 = (bf16[8,128,128]{2,1,0:T(8,128)(2,1)S(1)}, bf16[8,128,128]{2,1,0:T(8,128)(2,1)}, u32[]{:S(2)}) copy-start(bf16[8,128,128]{2,1,0:T(8,128)(2,1)} %copy-done.11) | copy-start | bytes 786436
  60.6 6.0 %copy-start.22 = (pred[512]{0:T(512)(128)(4,1)S(1)}, pred[512]{0:T(512)(128)(4,1)}, u32[]{:S(2)}) copy-start(pred[512]{0:T(512)(128)(4,1)} %add_add_fusion) | copy-start | bytes 1540
  61.5 9.4 %collective-permute-start.9 = (bf16[2,2,128,256]{3,2,1,0:T(8,128)(2,1)}, bf16[2,2,128,256]{3,2,1,0:T(8,128)(2,1)}, u32[]{:S(2)}, u32[]{:S(2)}) collective-permute-start(bf16[2,2,128,256]{3,2,1,0:T(8,128)(2,1)} %fusion.39), channel_id=1, source_target_pairs={{0,4},{4,0},{8,12},{12,8},{16,20},{20,16},{24,28},{28,24},{32,36},... | collective-permute-start | bytes 786440 | tf_op jit(solution)/shard_map/ppermute | solution.py:73
  64.6 6.3 %collective-permute-start.8 = (bf16[8,128,128]{2,1,0:T(8,128)(2,1)S(1)}, bf16[8,128,128]{2,1,0:T(8,128)(2,1)S(1)}, u32[]{:S(2)}, u32[]{:S(2)}) collective-permute-start(bf16[8,128,128]{2,1,0:T(8,128)(2,1)S(1)} %add_convert_fusion.1), channel_id=1, source_target_pairs={{4,12},{12,20},{20,28},{28,36},{36,44},{44,52},{52,60},{60,68},{68... | collective-permute-start | bytes 786440 | tf_op jit(solution)/shard_map/ppermute | solution.py:72
  65.3 13.4 %collective-permute-start.7 = (bf16[1536,128]{1,0:T(8,128)(2,1)S(1)}, bf16[1536,128]{1,0:T(8,128)(2,1)S(1)}, u32[]{:S(2)}, u32[]{:S(2)}) collective-permute-start(bf16[1536,128]{1,0:T(8,128)(2,1)S(1)} %pad_maximum_fusion.2), channel_id=1, source_target_pairs={{4,8},{12,16},{20,24},{28,32},{36,40},{44,48},{52,56},{60,64},{68,... | collective-permute-start | bytes 1179656 | tf_op jit(solution)/shard_map/ppermute | solution.py:71
  67.4 1.2 %copy-start.3 = (f32[128,2,8,128]{0,3,2,1:T(8,128)S(1)}, f32[128,2,8,128]{0,3,2,1:T(8,128)}, u32[]{:S(2)}) copy-start(f32[128,2,8,128]{0,3,2,1:T(8,128)} %fusion.17) | copy-start | bytes 3145732
  67.4 1.3 %copy-start.7 = (bf16[512,2,128]{2,1,0:T(2,128)(2,1)S(1)}, bf16[512,2,128]{2,1,0:T(2,128)(2,1)}, u32[]{:S(2)}) copy-start(bf16[512,2,128]{2,1,0:T(2,128)(2,1)} %reshape.111) | copy-start | bytes 786436
  68.7 10.7 %copy-start.2 = (f32[8,129,128]{2,1,0:T(8,128)S(1)}, f32[8,129,128]{2,1,0:T(8,128)}, u32[]{:S(2)}) copy-start(f32[8,129,128]{2,1,0:T(8,128)} %copy-done.1) | copy-start | bytes 1585156
  68.7 10.7 %copy-start.10 = (bf16[128,1024]{1,0:T(8,128)(2,1)S(1)}, bf16[128,1024]{1,0:T(8,128)(2,1)}, u32[]{:S(2)}) copy-start(bf16[128,1024]{1,0:T(8,128)(2,1)} %param.9) | copy-start | bytes 786436
  68.7 10.7 %copy-start.21 = (f32[128,8]{0,1:T(8,128)S(1)}, f32[128,8]{0,1:T(8,128)}, u32[]{:S(2)}) copy-start(f32[128,8]{0,1:T(8,128)} %get-tuple-element.63) | copy-start | bytes 12292
  70.9 9.0 %copy-start.5 = (bf16[128,1024]{0,1:T(8,128)(2,1)S(1)}, bf16[128,1024]{0,1:T(8,128)(2,1)}, u32[]{:S(2)}) copy-start(bf16[128,1024]{0,1:T(8,128)(2,1)} %copy-done.4) | copy-start | bytes 786436
  70.9 9.0 %copy-start.15 = (pred[128,128]{1,0:T(8,128)(4,1)S(1)}, pred[128,128]{1,0:T(8,128)(4,1)}, u32[]{:S(2)}) copy-start(pred[128,128]{1,0:T(8,128)(4,1)} %copy-done.14) | copy-start | bytes 49156
  70.9 9.0 %copy-start.19 = (f32[8,128]{1,0:T(8,128)S(1)}, f32[8,128]{1,0:T(8,128)}, u32[]{:S(2)}) copy-start(f32[8,128]{1,0:T(8,128)} %copy-done.18) | copy-start | bytes 12292
  79.9 12.2 %slice-start = ((bf16[1536,128]{1,0:T(8,128)(2,1)}), bf16[512,128]{1,0:T(8,128)(2,1)S(1)}, s32[]{:S(2)}) async-start(bf16[1536,128]{1,0:T(8,128)(2,1)} %copy-done.9), calls=%async_computation | async-start | bytes 262144 | tf_op jit(solution)/shard_map/slice | solution.py:80
  81.4 13.4 %copy-start.24 = (pred[256]{0:T(512)(128)(4,1)S(1)}, pred[256]{0:T(512)(128)(4,1)}, u32[]{:S(2)}) copy-start(pred[256]{0:T(512)(128)(4,1)} %concatenate.27) | copy-start | bytes 772
  94.8 1.2 %copy-start.6 = (f32[128,2,8,128]{0,3,2,1:T(8,128)S(1)}, f32[128,2,8,128]{0,3,2,1:T(8,128)}, u32[]{:S(2)}) copy-start(f32[128,2,8,128]{0,3,2,1:T(8,128)} %multiply_add_fusion) | copy-start | bytes 3145732
  96.0 1.7 %copy-start.23 = (f32[1024]{0:T(1024)S(1)}, f32[1024]{0:T(1024)}, u32[]{:S(2)}) copy-start(f32[1024]{0:T(1024)} %param.13) | copy-start | bytes 12292
  (4 other events, 3.1 us)

commit v11 on v9

--- a/solution.py
+++ b/solution.py
@@ -71,13 +71,11 @@
     running = take(running, range(0, width, 2), mine)
     running = take(running, range(1, width - 2, 2), theirs)
     after = (before.astype(jnp.float32) * gain[:, None, None] + state).astype(jnp.bfloat16)
-    after, last, running = lax.optimization_barrier(
-        (
-            lax.ppermute(after, axis, shift_pairs(count, 1, 0)),
-            lax.ppermute(last, axis, swap),
-            running,
-        )
-    )
+    split = after.size // HEAD_DIM
+    both = jnp.concatenate([after.reshape(-1, HEAD_DIM), last.reshape(-1, HEAD_DIM)])
+    both, running = lax.optimization_barrier((lax.ppermute(both, axis, swap), running))
+    after = both[:split].reshape(after.shape)
+    last = both[split:].reshape(last.shape)
     running = take(running, [width - 1], last[None])
     return jnp.where(core == 0, before, after), running
 

time: 95.7 us -> 97.2 us (1.016)
  matrix products: 9.4 us -> 12.8 us
  local copies, waits for them, and re-layouts: 8.23 us -> 11.1 us
  other arithmetic: 11.2 us -> 8.93 us
  starting transfers between devices: 27.7 us -> 25.5 us
    reduce_sum x3, other arithmetic: 4.07 us -> 1.73 us  [absorb(): row_mass = row_mass * shrink + jnp.sum(exponent, axis=-1)]
    ppermute x2 -> x1, starting transfers between devices: 4.34 us -> 2.04 us  [exchange(): lax.ppermute(both, axis, swap)]
    dot_general x3, matrix products: 3.54 us -> 5.78 us  [absorb(): jnp.einsum('tkgs,skd->tkgd', exponent.astype(jnp.bfloat16), value_rows, p...]
    another operation x3 -> x2, local copies, waits for them, and re-layouts: 0.45 us -> 2.42 us  [take(): value_rows = chosen[:, 1].reshape(-1, kv_heads, HEAD_DIM)]
    slice x0 -> x2, local copies, waits for them, and re-layouts: none -> 1.94 us  [the longest x1 0.97 us: exchange(): last = both[split:].reshape(last.shape)]
    dot_general x3, matrix products: 3.75 us -> 4.87 us  [absorb(): jnp.einsum('tkgd,skd->tkgs', queries, key_rows, preferred_element_type=jn...]
  transfers between devices with their start and end apart: 11 -> 10, of which waited for: 4 -> 4; matrix products, arithmetic and copies ran while one was open for 17% -> 19% of each run, Pallas kernels for 0% -> 0%
where the time goes in v11:
time: 97.2 us; the launch traced here: 96.5 us
  starting transfers between devices  25.5 us (26%)
  waiting for transfers between devices  17.7 us (18%)
  matrix products  12.8 us (13%)
  local copies, waits for them, and re-layouts  11.1 us (11%)
  blocking collectives  10.5 us (11%)
  between operations  9.98 us (10%)
  other arithmetic  8.93 us (9%)
    ppermute x4, waiting for transfers between devices, ring_step(): return lax.ppermute(ring[-1], axis, shift_pairs(count, 2, parity))  16.4 us
    psum x1, blocking collectives, body(): square_sum = lax.psum(jnp.sum(mixed * mixed, axis=1), 'head')  10.5 us
    ppermute x1, starting transfers between devices, exchange(): lax.ppermute(sent, axis, swap)  9.96 us
    ppermute x4, starting transfers between devices, ring_step(): return lax.ppermute(ring[-1], axis, shift_pairs(count, 2, parity))  8.32 us
    dot_general x3, matrix products, absorb(): jnp.einsum('tkgs,skd->tkgd', exponent.astype(jnp.bfloat16), value_rows, p...  5.78 us
    dot_general x3, matrix products, absorb(): jnp.einsum('tkgd,skd->tkgs', queries, key_rows, preferred_element_type=jn...  4.87 us
    convert_element_type x3, other arithmetic, exchange(): wide_state.astype(jnp.bfloat16)  2.83 us
    another operation x2, local copies, waits for them, and re-layouts, take(): value_rows = chosen[:, 1].reshape(-1, kv_heads, HEAD_DIM)  2.42 us
  transfers between devices with their start and end apart: 10, of which 4 were waited for; matrix products, arithmetic and copies ran while one was open for 19% of the time, Pallas kernels for 0%

profile of v11, /device:TPU:24, one launch (start us, length us, event | category | flops | bytes accessed | tf_op | source)
XLA Modules:
  0.0 96.5 jit_solution(15397741078880039098)
XLA Ops:
  0.7 1.6 %fusion.89 = (s32[1]{0:T(128)}, s32[1]{0:T(128)}, s32[1]{0:T(128)}, s32[1]{0:T(128)}, s32[1]{0:T(128)}, /*index=5*/s32[1]{0:T(128)}, s32[1]{0:T(128)}, s32[1]{0:T(128)}) fusion(s32[128]{0:T(128)} %param.17, s32[]{:T(128)S(6)} %max.42, s32[]{:T(128)S(6)} %max.39, s32[]{:T(128)S(6)} %max.38, s32[]{:T(128)S(6)} %max.37, s32[]{:T(128)S(6)} %max.36, ...), kind=kLoop, calls=%fused_computation.114 | loop fusion | bytes 96 | tf_op jit(solution)/shard_map/dynamic_slice | solution.py:150
  3.6 1.0 %reduce_window_sum.11 = f32[8,128]{1,0:T(8,128)S(1)} reduce-window(f32[8,128]{1,0:T(8,128)} %param.12, f32[]{:T(128)} %constant.56.clone.1), window={size=1x128 pad=0_0x127_0}, to_apply=%region_0.0 | reduce-window | flops 130048 | bytes 8196 | tf_op jit(solution)/shard_map/jit(cumsum)/reduce_window_sum | solution.py:89
  4.8 1.1 %copy.121 = bf16[128,1024]{0,1:T(8,128)(2,1)S(1)} copy(bf16[128,1024]{1,0:T(8,128)(2,1)} %param.10) | data formatting | bytes 524288 | tf_op jit(solution)/shard_map/reshape | solution.py:87
  6.5 1.9 %collective-permute-start = (f32[8,129,128]{2,0,1:T(8,128)S(1)}, f32[8,129,128]{2,0,1:T(8,128)S(1)}, u32[]{:S(2)}, u32[]{:S(2)}) collective-permute-start(f32[8,129,128]{2,0,1:T(8,128)S(1)} %copy.78), channel_id=1, source_target_pairs={{0,4},{8,12},{16,20},{24,28},{32,36},{40,44},{48,52},{56,60},{64,6... | collective-permute-start | bytes 1585160 | tf_op jit(solution)/shard_map/ppermute | solution.py:38
  8.4 3.8 %collective-permute-start.1 = (bf16[2,128,256]{2,1,0:T(8,128)(2,1)S(1)}, bf16[2,128,256]{2,1,0:T(8,128)(2,1)S(1)}, u32[]{:S(2)}, u32[]{:S(2)}) collective-permute-start(bf16[2,128,256]{2,1,0:T(8,128)(2,1)S(1)} %get-tuple-element.56), channel_id=1, source_target_pairs={{0,8},{4,12},{8,16},{12,20},{16,24},{20,28},{24,32},{28,36},{32,40... | collective-permute-start | bytes 393224 | tf_op jit(solution)/shard_map/ppermute | solution.py:32
  12.3 10.7 %collective-permute-done.1 = bf16[2,128,256]{2,1,0:T(8,128)(2,1)S(1)} collective-permute-done((bf16[2,128,256]{2,1,0:T(8,128)(2,1)S(1)}, bf16[2,128,256]{2,1,0:T(8,128)(2,1)S(1)}, u32[]{:S(2)}, u32[]{:S(2)}) %collective-permute-start.1) | collective-permute-done | bytes 131104 | tf_op jit(solution)/shard_map/ppermute | solution.py:32
  24.3 1.9 %collective-permute-start.3 = (bf16[2,128,256]{2,1,0:T(8,128)(2,1)S(1)}, bf16[2,128,256]{2,1,0:T(8,128)(2,1)S(1)}, u32[]{:S(2)}, u32[]{:S(2)}) collective-permute-start(bf16[2,128,256]{2,1,0:T(8,128)(2,1)S(1)} %collective-permute-done.1), channel_id=1, source_target_pairs={{0,8},{4,12},{8,16},{12,20},{16,24},{20,28},{24,32},{28,36},{32,40... | collective-permute-start | bytes 393224 | tf_op jit(solution)/shard_map/ppermute | solution.py:32
  30.1 4.6 %collective-permute-done.3 = bf16[2,128,256]{2,1,0:T(8,128)(2,1)S(1)} collective-permute-done((bf16[2,128,256]{2,1,0:T(8,128)(2,1)S(1)}, bf16[2,128,256]{2,1,0:T(8,128)(2,1)S(1)}, u32[]{:S(2)}, u32[]{:S(2)}) %collective-permute-start.3) | collective-permute-done | bytes 131104 | tf_op jit(solution)/shard_map/ppermute | solution.py:32
  34.7 1.9 %collective-permute-start.5 = (bf16[2,128,256]{2,1,0:T(8,128)(2,1)S(1)}, bf16[2,128,256]{2,1,0:T(8,128)(2,1)S(1)}, u32[]{:S(2)}, u32[]{:S(2)}) collective-permute-start(bf16[2,128,256]{2,1,0:T(8,128)(2,1)S(1)} %collective-permute-done.3), channel_id=1, source_target_pairs={{0,8},{4,12},{8,16},{12,20},{16,24},{20,28},{24,32},{28,36},{32,40... | collective-permute-start | bytes 393224 | tf_op jit(solution)/shard_map/ppermute | solution.py:32
  36.7 0.8 fusion.53
  37.6 1.3 %collective-permute-start.4 = (bf16[8,128,128]{2,1,0:T(8,128)(2,1)}, bf16[8,128,128]{2,1,0:T(8,128)(2,1)}, u32[]{:S(2)}, u32[]{:S(2)}) collective-permute-start(bf16[8,128,128]{2,1,0:T(8,128)(2,1)} %fusion.53), channel_id=1, source_target_pairs={{4,20},{12,28},{20,36},{28,44},{36,52},{44,60},{52,68},{60,76},{68... | collective-permute-start | bytes 786440 | tf_op jit(solution)/shard_map/ppermute | solution.py:59
  43.1 1.1 %collective-permute-done.5 = bf16[2,128,256]{2,1,0:T(8,128)(2,1)S(1)} collective-permute-done((bf16[2,128,256]{2,1,0:T(8,128)(2,1)S(1)}, bf16[2,128,256]{2,1,0:T(8,128)(2,1)S(1)}, u32[]{:S(2)}, u32[]{:S(2)}) %collective-permute-start.5) | collective-permute-done | bytes 131104 | tf_op jit(solution)/shard_map/ppermute | solution.py:32
  44.8 1.8 %add_convert_fusion.1 = bf16[8,128,128]{2,1,0:T(8,128)(2,1)} fusion(bf16[8,128,128]{2,1,0:T(8,128)(2,1)} %collective-permute-done.4, f32[8,128,128]{2,1,0:T(8,128)S(1)} %get-tuple-element.45, f32[8]{0:T(128)S(1)} %get-tuple-element.36, f32[8]{0:T(128)S(1)} %get-tuple-element.37, bf16[8,130,128]{2,1,0:T(8,128)(2,1)S(1)} %collective-permute-done.2), kind=kLoop, calls=%fused_computation.47 | loop fusion | flops 917504 | bytes 1310784 | tf_op jit(solution)/shard_map/convert_element_type | solution.py:65
  46.7 1.3 %collective-permute-start.6 = (bf16[8,128,128]{2,1,0:T(8,128)(2,1)}, bf16[8,128,128]{2,1,0:T(8,128)(2,1)S(1)}, u32[]{:S(2)}, u32[]{:S(2)}) collective-permute-start(bf16[8,128,128]{2,1,0:T(8,128)(2,1)} %add_convert_fusion.1), channel_id=1, source_target_pairs={{4,8},{12,16},{20,24},{28,32},{36,40},{44,48},{52,56},{60,64},{68,... | collective-permute-start | bytes 786440 | tf_op jit(solution)/shard_map/ppermute | solution.py:65
  48.1 0.8 maximum_select_fusion
  48.9 10.0 %collective-permute-start.8 = (bf16[3,2,128,256]{3,2,1,0:T(8,128)(2,1)}, bf16[3,2,128,256]{3,2,1,0:T(8,128)(2,1)S(1)}, u32[]{:S(2)}, u32[]{:S(2)}) collective-permute-start(bf16[3,2,128,256]{3,2,1,0:T(8,128)(2,1)} %maximum_select_fusion), channel_id=1, source_target_pairs={{0,4},{4,0},{8,12},{12,8},{16,20},{20,16},{24,28},{28,24},{32,36},... | collective-permute-start | bytes 1179656 | tf_op jit(solution)/shard_map/ppermute | solution.py:67
  59.0 2.7 %fusion.2 = (f32[128,2,8]{0,2,1:T(8,128)S(1)}, f32[2,512,128,8]{2,1,3,0:T(8,128)}) fusion(pred[128,512]{0,1:T(8,128)(4,1)S(1)} %copy.82, bf16[128,2,8,128]{3,2,1,0:T(8,128)(2,1)S(1)} %bitcast.135, bf16[512,2,128,1]{2,1,0,3:T(2,128)(2,1)S(1)} %bitcast.141), kind=kOutput, calls=%fused_computation.4 | convolution fusion | flops 271579136 | bytes 5054464 | tf_op jit(solution)/shard_map/tkgd,skd->tkgs/dot_general | solution.py:106
  61.7 0.8 reshape.119
  62.4 1.3 %collective-permute-done.6 = bf16[8,128,128]{2,1,0:T(8,128)(2,1)S(1)} collective-permute-done((bf16[8,128,128]{2,1,0:T(8,128)(2,1)}, bf16[8,128,128]{2,1,0:T(8,128)(2,1)S(1)}, u32[]{:S(2)}, u32[]{:S(2)}) %collective-permute-start.6) | collective-permute-done | bytes 262176 | tf_op jit(solution)/shard_map/ppermute | solution.py:65
  65.4 0.8 pad_maximum_fusion.2
  66.2 2.0 %collective-permute-start.9 = (bf16[1536,128]{1,0:T(8,128)(2,1)}, bf16[1536,128]{1,0:T(8,128)(2,1)}, u32[]{:S(2)}, u32[]{:S(2)}) collective-permute-start(bf16[1536,128]{1,0:T(8,128)(2,1)} %pad_maximum_fusion.2), channel_id=1, source_target_pairs={{0,4},{4,0},{8,12},{12,8},{16,20},{20,16},{24,28},{28,24},{32,36},... | collective-permute-start | bytes 1179656 | tf_op jit(solution)/shard_map/ppermute | solution.py:76
  68.2 1.8 %fusion.5 = (f32[128,2,8]{0,2,1:T(8,128)S(1)}, f32[2,384,128,8]{2,1,3,0:T(8,128)S(1)}) fusion(pred[384]{0:T(512)(128)(4,1)S(1)} %add_add_fusion.1, bf16[128,2,8,128]{3,2,1,0:T(8,128)(2,1)} %bitcast.136, bf16[384,2,128,1]{2,1,0,3:T(2,128)(2,1)} %bitcast.145), kind=kOutput, calls=%fused_computation.9 | convolution fusion | flops 203683840 | bytes 3875200 | tf_op jit(solution)/shard_map/tkgd,skd->tkgs/dot_general | solution.py:106
  70.1 0.9 fusion.1
  71.7 2.1 %fusion.32 = f32[128,2,8,128]{0,3,2,1:T(8,128)} fusion(f32[2,512,128,8]{2,1,3,0:T(8,128)S(1)} %copy-done.1, f32[128,2,8]{0,2,1:T(8,128)S(1)} %get-tuple-element.59, pred[128,512]{0,1:T(8,128)(4,1)S(1)} %copy.82, f32[128,2,8]{0,2,1:T(8,128)S(1)} %get-tuple-element.43, f32[128,2,8]{0,2,1:T(8,128)S(1)} %get-tuple-element.57, ...), kind=kOutput, calls=%fused_computation.28 | convolution fusion | flops 273154048 | bytes 5595136 | tf_op jit(solution)/shard_map/tkgs,skd->tkgd/dot_general | solution.py:114
  73.8 1.6 %reshape_squeeze.21 = bf16[384,2,128]{2,1,0:T(2,128)(2,1)} reshape(bf16[3,1,128,256]{3,2,1,0:T(8,128)(2,1)} %get-tuple-element.51) | data formatting | bytes 393216 | tf_op jit(solution)/shard_map/reshape;squeeze | solution.py:143
  75.5 3.3 %fusion.21 = f32[128,2,8,128]{0,3,2,1:T(8,128)} fusion(f32[128,2,8,128]{0,3,2,1:T(8,128)} %fusion.32, f32[2,384,128,8]{2,1,3,0:T(8,128)S(1)} %get-tuple-element.74, f32[128,2,8]{0,2,1:T(8,128)S(1)} %get-tuple-element.26, pred[384]{0:T(512)(128)(4,1)S(1)} %add_add_fusion.1, bf16[384,2,128,1]{2,1,0,3:T(2,128)(2,1)} %bitcast.146), kind=kOutput, calls=%fused_computation.22 | convolution fusion | flops 204734464 | bytes 5448064 | tf_op jit(solution)/shard_map/tkgs,skd->tkgd/dot_general | solution.py:114
  78.8 1.0 %slice.54 = bf16[512,128]{1,0:T(8,128)(2,1)S(1)} slice(bf16[1536,128]{1,0:T(8,128)(2,1)} %collective-permute-done.9), slice={[1024:1536], [0:128]} | slice | bytes 262144 | tf_op jit(solution)/shard_map/slice | solution.py:78
  79.8 1.0 %slice.53 = bf16[1024,128]{1,0:T(8,128)(2,1)S(1)} slice(bf16[1536,128]{1,0:T(8,128)(2,1)} %collective-permute-done.9), slice={[0:1024], [0:128]} | slice | bytes 524288 | tf_op jit(solution)/shard_map/slice | solution.py:77
  81.1 1.6 %multiply_reduce_fusion = (f32[128]{0:T(128)S(1)}, f32[128,8,128]{0,2,1:T(8,128)S(1)}) fusion(f32[128,8,128]{0,2,1:T(8,128)S(1)} %fusion.36, bf16[128,8,128]{0,2,1:T(8,128)(2,1)} %bitcast.144, f32[8,128]{1,0:T(8,128)S(1)} %reduce_window_sum.11, pred[128,128]{1,0:T(8,128)(4,1)S(1)} %iota_compare_fusion, bf16[128,1024]{1,0:T(8,128)(2,1)S(1)} %copy-done, ...), kind=kOutput, calls=%fused_computation.45 | convolution fusion | flops 68026240 | bytes 1856000 | tf_op jit(solution)/shard_map/hts,shd->thd/dot_general | solution.py:95
  82.7 10.5 %psum.7 = f32[128]{0:T(128)S(1)} all-reduce(f32[128]{0:T(128)S(1)} %get-tuple-element.75), channel_id=1, replica_groups=mesh['grp'=4,'seq'=32,'head'=4] {'head'}, use_global_device_ids=true, to_apply=%region_6.7 | all-reduce | flops 128 | bytes 1024 | tf_op jit(solution)/shard_map/psum | solution.py:172
  94.7 1.0 %copy.99 = bf16[128,2048]{1,0:T(8,128)(2,1)} copy(bf16[128,2048]{0,1:T(8,128)(2,1)S(1)} %bitcast.149) | data formatting | bytes 1048576
  95.7 0.8 multiply_convert_fusion
  (89 shorter events, 7.5 us)
Async XLA Ops:
  0.6 5.3 %copy-start = (bf16[128,1024]{1,0:T(8,128)(2,1)S(1)}, bf16[128,1024]{1,0:T(8,128)(2,1)}, u32[]{:S(2)}) copy-start(bf16[128,1024]{1,0:T(8,128)(2,1)} %param.11) | copy-start | bytes 786436
  0.6 7.7 %copy-start.11 = (bf16[128,256]{1,0:T(8,128)(2,1)S(1)}, bf16[128,256]{1,0:T(8,128)(2,1)}, u32[]{:S(2)}) copy-start(bf16[128,256]{1,0:T(8,128)(2,1)} %param.16) | copy-start | bytes 196612
  0.7 7.7 %copy-start.12 = (bf16[128,256]{1,0:T(8,128)(2,1)S(1)}, bf16[128,256]{1,0:T(8,128)(2,1)}, u32[]{:S(2)}) copy-start(bf16[128,256]{1,0:T(8,128)(2,1)} %param.15) | copy-start | bytes 196612
  6.0 2.4 %copy-start.6 = (bf16[128,1024]{0,1:T(8,128)(2,1)}, bf16[128,1024]{0,1:T(8,128)(2,1)S(1)}, u32[]{:S(2)}) copy-start(bf16[128,1024]{0,1:T(8,128)(2,1)S(1)} %copy.121) | copy-start | bytes 786436
  6.3 36.5 %copy-start.8 = (bf16[128,2048]{1,0:T(8,128)(2,1)S(1)}, bf16[128,2048]{1,0:T(8,128)(2,1)}, u32[]{:S(2)}) copy-start(bf16[128,2048]{1,0:T(8,128)(2,1)} %param.14) | copy-start | bytes 1572868
  6.5 16.6 %collective-permute-start = (f32[8,129,128]{2,0,1:T(8,128)S(1)}, f32[8,129,128]{2,0,1:T(8,128)S(1)}, u32[]{:S(2)}, u32[]{:S(2)}) collective-permute-start(f32[8,129,128]{2,0,1:T(8,128)S(1)} %copy.78), channel_id=1, source_target_pairs={{0,4},{8,12},{16,20},{24,28},{32,36},{40,44},{48,52},{56,60},{64,6... | collective-permute-start | bytes 1585160 | tf_op jit(solution)/shard_map/ppermute | solution.py:38
  8.4 14.6 %collective-permute-start.1 = (bf16[2,128,256]{2,1,0:T(8,128)(2,1)S(1)}, bf16[2,128,256]{2,1,0:T(8,128)(2,1)S(1)}, u32[]{:S(2)}, u32[]{:S(2)}) collective-permute-start(bf16[2,128,256]{2,1,0:T(8,128)(2,1)S(1)} %get-tuple-element.56), channel_id=1, source_target_pairs={{0,8},{4,12},{8,16},{12,20},{16,24},{20,28},{24,32},{28,36},{32,40... | collective-permute-start | bytes 393224 | tf_op jit(solution)/shard_map/ppermute | solution.py:32
  23.6 11.1 %collective-permute-start.2 = (bf16[8,130,128]{2,1,0:T(8,128)(2,1)S(1)}, bf16[8,130,128]{2,1,0:T(8,128)(2,1)S(1)}, u32[]{:S(2)}, u32[]{:S(2)}) collective-permute-start(bf16[8,130,128]{2,1,0:T(8,128)(2,1)S(1)} %pad_maximum_fusion.3), channel_id=1, source_target_pairs={{4,12},{12,20},{20,28},{28,36},{36,44},{44,52},{52,60},{60,68},{68... | collective-permute-start | bytes 798728 | tf_op jit(solution)/shard_map/ppermute | solution.py:53
  24.3 10.4 %collective-permute-start.3 = (bf16[2,128,256]{2,1,0:T(8,128)(2,1)S(1)}, bf16[2,128,256]{2,1,0:T(8,128)(2,1)S(1)}, u32[]{:S(2)}, u32[]{:S(2)}) collective-permute-start(bf16[2,128,256]{2,1,0:T(8,128)(2,1)S(1)} %collective-permute-done.1), channel_id=1, source_target_pairs={{0,8},{4,12},{8,16},{12,20},{16,24},{20,28},{24,32},{28,36},{32,40... | collective-permute-start | bytes 393224 | tf_op jit(solution)/shard_map/ppermute | solution.py:32
  34.7 9.5 %collective-permute-start.5 = (bf16[2,128,256]{2,1,0:T(8,128)(2,1)S(1)}, bf16[2,128,256]{2,1,0:T(8,128)(2,1)S(1)}, u32[]{:S(2)}, u32[]{:S(2)}) collective-permute-start(bf16[2,128,256]{2,1,0:T(8,128)(2,1)S(1)} %collective-permute-done.3), channel_id=1, source_target_pairs={{0,8},{4,12},{8,16},{12,20},{16,24},{20,28},{24,32},{28,36},{32,40... | collective-permute-start | bytes 393224 | tf_op jit(solution)/shard_map/ppermute | solution.py:32
  37.6 6.6 %collective-permute-start.4 = (bf16[8,128,128]{2,1,0:T(8,128)(2,1)}, bf16[8,128,128]{2,1,0:T(8,128)(2,1)}, u32[]{:S(2)}, u32[]{:S(2)}) collective-permute-start(bf16[8,128,128]{2,1,0:T(8,128)(2,1)} %fusion.53), channel_id=1, source_target_pairs={{4,20},{12,28},{20,36},{28,44},{36,52},{44,60},{52,68},{60,76},{68... | collective-permute-start | bytes 786440 | tf_op jit(solution)/shard_map/ppermute | solution.py:59
  43.0 18.7 %copy-start.2 = (bf16[16,8,16,128]{3,2,1,0:T(8,128)(2,1)}, bf16[16,8,16,128]{3,2,1,0:T(8,128)(2,1)S(1)}, u32[]{:S(2)}) copy-start(bf16[16,8,16,128]{3,2,1,0:T(8,128)(2,1)S(1)} %copy.124) | copy-start | bytes 1572868
  44.2 18.3 %collective-permute-start.7 = (bf16[2,128,256]{2,1,0:T(8,128)(2,1)S(1)}, bf16[2,128,256]{2,1,0:T(8,128)(2,1)S(1)}, u32[]{:S(2)}, u32[]{:S(2)}) collective-permute-start(bf16[2,128,256]{2,1,0:T(8,128)(2,1)S(1)} %collective-permute-done.5), channel_id=1, source_target_pairs={{4,12},{12,20},{20,28},{28,36},{36,44},{44,52},{52,60},{60,68},{68... | collective-permute-start | bytes 393224 | tf_op jit(solution)/shard_map/ppermute | solution.py:32
  46.7 17.0 %collective-permute-start.6 = (bf16[8,128,128]{2,1,0:T(8,128)(2,1)}, bf16[8,128,128]{2,1,0:T(8,128)(2,1)S(1)}, u32[]{:S(2)}, u32[]{:S(2)}) collective-permute-start(bf16[8,128,128]{2,1,0:T(8,128)(2,1)} %add_convert_fusion.1), channel_id=1, source_target_pairs={{4,8},{12,16},{20,24},{28,32},{36,40},{44,48},{52,56},{60,64},{68,... | collective-permute-start | bytes 786440 | tf_op jit(solution)/shard_map/ppermute | solution.py:65
  48.9 14.8 %collective-permute-start.8 = (bf16[3,2,128,256]{3,2,1,0:T(8,128)(2,1)}, bf16[3,2,128,256]{3,2,1,0:T(8,128)(2,1)S(1)}, u32[]{:S(2)}, u32[]{:S(2)}) collective-permute-start(bf16[3,2,128,256]{3,2,1,0:T(8,128)(2,1)} %maximum_select_fusion), channel_id=1, source_target_pairs={{0,4},{4,0},{8,12},{12,8},{16,20},{20,16},{24,28},{28,24},{32,36},... | collective-permute-start | bytes 1179656 | tf_op jit(solution)/shard_map/ppermute | solution.py:67
  63.7 4.5 %copy-start.4 = (bf16[8,128,128]{2,1,0:T(8,128)(2,1)}, bf16[8,128,128]{2,1,0:T(8,128)(2,1)S(1)}, u32[]{:S(2)}) copy-start(bf16[8,128,128]{2,1,0:T(8,128)(2,1)S(1)} %collective-permute-done.6) | copy-start | bytes 786436
  65.4 4.7 %copy-start.1 = (f32[2,512,128,8]{2,1,3,0:T(8,128)S(1)}, f32[2,512,128,8]{2,1,3,0:T(8,128)}, u32[]{:S(2)}) copy-start(f32[2,512,128,8]{2,1,3,0:T(8,128)} %get-tuple-element.72) | copy-start | bytes 12582916
  66.2 12.6 %collective-permute-start.9 = (bf16[1536,128]{1,0:T(8,128)(2,1)}, bf16[1536,128]{1,0:T(8,128)(2,1)}, u32[]{:S(2)}, u32[]{:S(2)}) collective-permute-start(bf16[1536,128]{1,0:T(8,128)(2,1)} %pad_maximum_fusion.2), channel_id=1, source_target_pairs={{0,4},{4,0},{8,12},{12,8},{16,20},{20,16},{24,28},{28,24},{32,36},... | collective-permute-start | bytes 1179656 | tf_op jit(solution)/shard_map/ppermute | solution.py:76
  70.1 1.6 %copy-start.10 = (bf16[512,2,128]{2,1,0:T(2,128)(2,1)S(1)}, bf16[512,2,128]{2,1,0:T(2,128)(2,1)}, u32[]{:S(2)}) copy-start(bf16[512,2,128]{2,1,0:T(2,128)(2,1)} %reshape.119) | copy-start | bytes 786436
  75.5 5.3 %copy-start.5 = (bf16[8,128,128]{2,1,0:T(8,128)(2,1)S(1)}, bf16[8,128,128]{2,1,0:T(8,128)(2,1)}, u32[]{:S(2)}) copy-start(bf16[8,128,128]{2,1,0:T(8,128)(2,1)} %copy-done.4) | copy-start | bytes 786436
  75.5 5.3 %copy-start.9 = (bf16[128,1024]{1,0:T(8,128)(2,1)S(1)}, bf16[128,1024]{1,0:T(8,128)(2,1)}, u32[]{:S(2)}) copy-start(bf16[128,1024]{1,0:T(8,128)(2,1)} %param.9) | copy-start | bytes 786436
  78.8 15.0 %copy-start.3 = (bf16[16,8,16,128]{3,2,1,0:T(8,128)(2,1)S(1)}, bf16[16,8,16,128]{3,2,1,0:T(8,128)(2,1)}, u32[]{:S(2)}) copy-start(bf16[16,8,16,128]{3,2,1,0:T(8,128)(2,1)} %copy-done.2) | copy-start | bytes 1572868
  81.1 13.3 %copy-start.7 = (f32[128,2,8,128]{0,3,2,1:T(8,128)S(1)}, f32[128,2,8,128]{0,3,2,1:T(8,128)}, u32[]{:S(2)}) copy-start(f32[128,2,8,128]{0,3,2,1:T(8,128)} %fusion.21) | copy-start | bytes 3145732
  94.3 1.4 %copy-start.13 = (f32[1024]{0:T(1024)S(1)}, f32[1024]{0:T(1024)}, u32[]{:S(2)}) copy-start(f32[1024]{0:T(1024)} %param.13) | copy-start | bytes 12292

commit v12 on v9

--- a/solution.py
+++ b/solution.py
@@ -80,6 +80,15 @@
     )
     running = take(running, [width - 1], last[None])
     return jnp.where(core == 0, before, after), running
+
+
+def butterfly_sum(x, axis):
+    count = lax.axis_size(axis)
+    step = 1
+    while step < count:
+        x = x + lax.ppermute(x, axis, [(i, i ^ step) for i in range(count)])
+        step *= 2
+    return x
 
 
 def lightning_local(light_q, light_k, light_v, log_decay, joined):
@@ -171,7 +180,7 @@
         * reach_gain.T[:, :, None]
     )
     mixed = (intra_part + inter_part).reshape(tok_rows, -1)
-    square_sum = lax.psum(jnp.sum(mixed * mixed, axis=1), "head")
+    square_sum = butterfly_sum(jnp.sum(mixed * mixed, axis=1), "head")
     inv_norm = lax.rsqrt(square_sum / (LIGHTNING_HEADS * HEAD_DIM) + 1e-06)
     light_out = (mixed * inv_norm[:, None] * light_gain).astype(jnp.bfloat16)
     _, row_mass, weighted = running

time: 95.7 us -> 94.6 us (0.989)
  blocking collectives: 10.5 us -> 0 us
  starting transfers between devices: 27.7 us -> 36 us
  waiting for transfers between devices: 18.2 us -> 19.2 us
    psum x1 -> x0, blocking collectives: 10.5 us -> none  [body(): square_sum = lax.psum(jnp.sum(mixed * mixed, axis=1), 'head')]
    ppermute x0 -> x2, starting transfers between devices: none -> 8.31 us  [butterfly_sum(): x = x + lax.ppermute(x, axis, [(i, i ^ step) for i in range(count)])]
    ppermute x0 -> x2, waiting for transfers between devices: none -> 1.05 us  [butterfly_sum(): x = x + lax.ppermute(x, axis, [(i, i ^ step) for i in range(count)])]
  transfers between devices with their start and end apart: 11 -> 13, of which waited for: 4 -> 6; matrix products, arithmetic and copies ran while one was open for 17% -> 20% of each run, Pallas kernels for 0% -> 0%
where the time goes in v12:
time: 94.6 us; the launch traced here: 93.9 us
  starting transfers between devices  36 us (38%)
  waiting for transfers between devices  19.2 us (20%)
  other arithmetic  11.2 us (12%)
  between operations  9.82 us (10%)
  matrix products  9.41 us (10%)
  local copies, waits for them, and re-layouts  8.23 us (9%)
    ppermute x4, waiting for transfers between devices, ring_step(): return lax.ppermute(ring[-1], axis, shift_pairs(count, 2, parity))  16.6 us
    ppermute x1, starting transfers between devices, exchange(): lax.ppermute(sent, axis, swap)  9.33 us
    ppermute x4, starting transfers between devices, ring_step(): return lax.ppermute(ring[-1], axis, shift_pairs(count, 2, parity))  8.96 us
    ppermute x2, starting transfers between devices, butterfly_sum(): x = x + lax.ppermute(x, axis, [(i, i ^ step) for i in range(count)])  8.31 us
    reduce_sum x3, other arithmetic, absorb(): row_mass = row_mass * shrink + jnp.sum(exponent, axis=-1)  4.07 us
    dot_general x3, matrix products, absorb(): jnp.einsum('tkgd,skd->tkgs', queries, key_rows, preferred_element_type=jn...  3.75 us
    dot_general x3, matrix products, absorb(): jnp.einsum('tkgs,skd->tkgd', exponent.astype(jnp.bfloat16), value_rows, p...  3.55 us
    convert_element_type x3, other arithmetic, exchange(): wide_state.astype(jnp.bfloat16)  2.82 us
  transfers between devices with their start and end apart: 13, of which 6 were waited for; matrix products, arithmetic and copies ran while one was open for 20% of the time, Pallas kernels for 0%

profile of v12, /device:TPU:24, one launch (start us, length us, event | category | flops | bytes accessed | tf_op | source)
XLA Modules:
  0.0 93.9 jit_solution(12509656562607740743)
XLA Ops:
  0.7 1.7 %fusion.89 = (s32[1]{0:T(128)}, s32[1]{0:T(128)}, s32[1]{0:T(128)}, s32[1]{0:T(128)}, s32[1]{0:T(128)}, /*index=5*/s32[1]{0:T(128)}, s32[1]{0:T(128)}, s32[1]{0:T(128)}) fusion(s32[128]{0:T(128)} %param.17, s32[]{:T(128)S(6)} %max.42, s32[]{:T(128)S(6)} %max.39, s32[]{:T(128)S(6)} %max.38, s32[]{:T(128)S(6)} %max.37, s32[]{:T(128)S(6)} %max.36, ...), kind=kLoop, calls=%fused_computation.113 | loop fusion | bytes 96 | tf_op jit(solution)/shard_map/dynamic_slice | solution.py:161
  3.6 1.0 %reduce_window_sum.11 = f32[8,128]{1,0:T(8,128)S(1)} reduce-window(f32[8,128]{1,0:T(8,128)} %param.12, f32[]{:T(128)} %constant.56.clone.1), window={size=1x128 pad=0_0x127_0}, to_apply=%region_0.0 | reduce-window | flops 130048 | bytes 8196 | tf_op jit(solution)/shard_map/jit(cumsum)/reduce_window_sum | solution.py:100
  5.2 1.1 %copy.102 = bf16[128,1024]{0,1:T(8,128)(2,1)S(1)} copy(bf16[128,1024]{1,0:T(8,128)(2,1)} %param.10) | data formatting | bytes 524288 | tf_op jit(solution)/shard_map/reshape | solution.py:98
  6.7 0.9 copy.59
  7.6 1.8 %collective-permute-start = (f32[8,129,128]{2,0,1:T(8,128)}, f32[8,129,128]{2,0,1:T(8,128)S(1)}, u32[]{:S(2)}, u32[]{:S(2)}) collective-permute-start(f32[8,129,128]{2,0,1:T(8,128)} %copy.59), channel_id=1, source_target_pairs={{0,4},{8,12},{16,20},{24,28},{32,36},{40,44},{48,52},{56,60},{64,6... | collective-permute-start | bytes 1585160 | tf_op jit(solution)/shard_map/ppermute | solution.py:38
  9.7 3.8 %collective-permute-start.1 = (bf16[2,128,256]{1,2,0:T(8,128)(2,1)S(1)}, bf16[2,128,256]{1,2,0:T(8,128)(2,1)S(1)}, u32[]{:S(2)}, u32[]{:S(2)}) collective-permute-start(bf16[2,128,256]{1,2,0:T(8,128)(2,1)S(1)} %get-tuple-element.56), channel_id=1, source_target_pairs={{0,8},{4,12},{8,16},{12,20},{16,24},{20,28},{24,32},{28,36},{32,40... | collective-permute-start | bytes 393224 | tf_op jit(solution)/shard_map/ppermute | solution.py:32
  13.5 10.7 %collective-permute-done.1 = bf16[2,128,256]{1,2,0:T(8,128)(2,1)S(1)} collective-permute-done((bf16[2,128,256]{1,2,0:T(8,128)(2,1)S(1)}, bf16[2,128,256]{1,2,0:T(8,128)(2,1)S(1)}, u32[]{:S(2)}, u32[]{:S(2)}) %collective-permute-start.1) | collective-permute-done | bytes 131104 | tf_op jit(solution)/shard_map/ppermute | solution.py:32
  25.5 1.9 %collective-permute-start.3 = (bf16[2,128,256]{1,2,0:T(8,128)(2,1)S(1)}, bf16[2,128,256]{1,2,0:T(8,128)(2,1)S(1)}, u32[]{:S(2)}, u32[]{:S(2)}) collective-permute-start(bf16[2,128,256]{1,2,0:T(8,128)(2,1)S(1)} %collective-permute-done.1), channel_id=1, source_target_pairs={{0,8},{4,12},{8,16},{12,20},{16,24},{20,28},{24,32},{28,36},{32,40... | collective-permute-start | bytes 393224 | tf_op jit(solution)/shard_map/ppermute | solution.py:32
  31.3 4.6 %collective-permute-done.3 = bf16[2,128,256]{1,2,0:T(8,128)(2,1)S(1)} collective-permute-done((bf16[2,128,256]{1,2,0:T(8,128)(2,1)S(1)}, bf16[2,128,256]{1,2,0:T(8,128)(2,1)S(1)}, u32[]{:S(2)}, u32[]{:S(2)}) %collective-permute-start.3) | collective-permute-done | bytes 131104 | tf_op jit(solution)/shard_map/ppermute | solution.py:32
  35.9 1.9 %collective-permute-start.5 = (bf16[2,128,256]{1,2,0:T(8,128)(2,1)S(1)}, bf16[2,128,256]{1,2,0:T(8,128)(2,1)S(1)}, u32[]{:S(2)}, u32[]{:S(2)}) collective-permute-start(bf16[2,128,256]{1,2,0:T(8,128)(2,1)S(1)} %collective-permute-done.3), channel_id=1, source_target_pairs={{0,8},{4,12},{8,16},{12,20},{16,24},{20,28},{24,32},{28,36},{32,40... | collective-permute-start | bytes 393224 | tf_op jit(solution)/shard_map/ppermute | solution.py:32
  38.0 0.8 fusion.53
  38.8 1.3 %collective-permute-start.4 = (bf16[8,128,128]{2,1,0:T(8,128)(2,1)}, bf16[8,128,128]{2,1,0:T(8,128)(2,1)}, u32[]{:S(2)}, u32[]{:S(2)}) collective-permute-start(bf16[8,128,128]{2,1,0:T(8,128)(2,1)} %fusion.53), channel_id=1, source_target_pairs={{4,20},{12,28},{20,36},{28,44},{36,52},{44,60},{52,68},{60,76},{68... | collective-permute-start | bytes 786440 | tf_op jit(solution)/shard_map/ppermute | solution.py:59
  44.2 1.2 %collective-permute-done.5 = bf16[2,128,256]{1,2,0:T(8,128)(2,1)S(1)} collective-permute-done((bf16[2,128,256]{1,2,0:T(8,128)(2,1)S(1)}, bf16[2,128,256]{1,2,0:T(8,128)(2,1)S(1)}, u32[]{:S(2)}, u32[]{:S(2)}) %collective-permute-start.5) | collective-permute-done | bytes 131104 | tf_op jit(solution)/shard_map/ppermute | solution.py:32
  45.4 1.3 %collective-permute-start.7 = (bf16[2,128,256]{1,2,0:T(8,128)(2,1)S(1)}, bf16[2,128,256]{1,2,0:T(8,128)(2,1)}, u32[]{:S(2)}, u32[]{:S(2)}) collective-permute-start(bf16[2,128,256]{1,2,0:T(8,128)(2,1)S(1)} %collective-permute-done.5), channel_id=1, source_target_pairs={{4,12},{12,20},{20,28},{28,36},{36,44},{44,52},{52,60},{60,68},{68... | collective-permute-start | bytes 393224 | tf_op jit(solution)/shard_map/ppermute | solution.py:32
  46.7 1.8 %add_convert_fusion.1 = bf16[8,128,128]{2,1,0:T(8,128)(2,1)} fusion(bf16[8,128,128]{2,1,0:T(8,128)(2,1)} %collective-permute-done.4, f32[8,128,128]{2,1,0:T(8,128)S(1)} %get-tuple-element.45, f32[8]{0:T(128)S(1)} %get-tuple-element.36, f32[8]{0:T(128)S(1)} %get-tuple-element.37, bf16[8,130,128]{2,1,0:T(8,128)(2,1)S(1)} %collective-permute-done.2), kind=kLoop, calls=%fused_computation.47 | loop fusion | flops 917504 | bytes 1310784 | tf_op jit(solution)/shard_map/convert_element_type | solution.py:65
  48.6 1.3 %collective-permute-start.6 = (bf16[8,128,128]{2,1,0:T(8,128)(2,1)}, bf16[8,128,128]{2,1,0:T(8,128)(2,1)S(1)}, u32[]{:S(2)}, u32[]{:S(2)}) collective-permute-start(bf16[8,128,128]{2,1,0:T(8,128)(2,1)} %add_convert_fusion.1), channel_id=1, source_target_pairs={{4,8},{12,16},{20,24},{28,32},{36,40},{44,48},{52,56},{60,64},{68,... | collective-permute-start | bytes 786440 | tf_op jit(solution)/shard_map/ppermute | solution.py:65
  49.9 0.8 maximum_select_fusion
  50.8 9.3 %collective-permute-start.8 = (bf16[3,2,128,256]{2,3,1,0:T(8,128)(2,1)}, bf16[3,2,128,256]{2,3,1,0:T(8,128)(2,1)S(1)}, u32[]{:S(2)}, u32[]{:S(2)}) collective-permute-start(bf16[3,2,128,256]{2,3,1,0:T(8,128)(2,1)} %maximum_select_fusion), channel_id=1, source_target_pairs={{0,4},{4,0},{8,12},{12,8},{16,20},{20,16},{24,28},{28,24},{32,36},... | collective-permute-start | bytes 1179656 | tf_op jit(solution)/shard_map/ppermute | solution.py:67
  60.4 2.7 %fusion.2 = (f32[128,2,8]{0,2,1:T(8,128)S(1)}, f32[2,512,128,8]{2,1,3,0:T(8,128)}) fusion(pred[128,512]{0,1:T(8,128)(4,1)S(1)} %copy.65, bf16[128,2,8,128]{3,2,1,0:T(8,128)(2,1)S(1)} %bitcast.142, bf16[512,2,128,1]{2,1,0,3:T(2,128)(2,1)S(1)} %bitcast.147), kind=kOutput, calls=%fused_computation.4 | convolution fusion | flops 271579136 | bytes 5054464 | tf_op jit(solution)/shard_map/tkgd,skd->tkgs/dot_general | solution.py:117
  63.4 1.6 %collective-permute-done.6 = bf16[8,128,128]{2,1,0:T(8,128)(2,1)S(1)} collective-permute-done((bf16[8,128,128]{2,1,0:T(8,128)(2,1)}, bf16[8,128,128]{2,1,0:T(8,128)(2,1)S(1)}, u32[]{:S(2)}, u32[]{:S(2)}) %collective-permute-start.6) | collective-permute-done | bytes 262176 | tf_op jit(solution)/shard_map/ppermute | solution.py:65
  65.0 0.8 add_convert_fusion
  65.8 1.9 %collective-permute-start.10 = (bf16[2,128,256]{1,2,0:T(8,128)(2,1)S(1)}, bf16[2,128,256]{1,2,0:T(8,128)(2,1)}, u32[]{:S(2)}, u32[]{:S(2)}) collective-permute-start(bf16[2,128,256]{1,2,0:T(8,128)(2,1)S(1)} %broadcast_select_fusion), channel_id=1, source_target_pairs={{0,4},{4,0},{8,12},{12,8},{16,20},{20,16},{24,28},{28,24},{32,36},... | collective-permute-start | bytes 393224 | tf_op jit(solution)/shard_map/ppermute | solution.py:77
  67.8 2.4 %collective-permute-start.9 = (bf16[8,128,128]{2,1,0:T(8,128)(2,1)}, bf16[8,128,128]{2,1,0:T(8,128)(2,1)S(1)}, u32[]{:S(2)}, u32[]{:S(2)}) collective-permute-start(bf16[8,128,128]{2,1,0:T(8,128)(2,1)} %add_convert_fusion), channel_id=1, source_target_pairs={{0,4},{8,12},{16,20},{24,28},{32,36},{40,44},{48,52},{56,60},{64,6... | collective-permute-start | bytes 786440 | tf_op jit(solution)/shard_map/ppermute | solution.py:76
  71.5 3.2 %fusion.1 = f32[128,2,8]{0,2,1:T(8,128)S(1)} fusion(f32[2,512,128,8]{2,1,3,0:T(8,128)} %get-tuple-element.72, f32[128,2,8]{0,2,1:T(8,128)S(1)} %get-tuple-element.59, pred[128,512]{0,1:T(8,128)(4,1)S(1)} %copy.65), kind=kLoop, calls=%fused_computation.3 | loop fusion | flops 4192256 | bytes 4276224 | tf_op jit(solution)/shard_map/reduce_sum | solution.py:124
  75.5 1.2 %fusion.32 = f32[128,2,8,128]{0,3,2,1:T(8,128)S(1)} fusion(f32[2,512,128,8]{2,1,3,0:T(8,128)S(1)} %copy-done.1, f32[128,2,8]{0,2,1:T(8,128)S(1)} %get-tuple-element.59, pred[128,512]{0,1:T(8,128)(4,1)S(1)} %copy.65, f32[128,2,8]{0,2,1:T(8,128)S(1)} %get-tuple-element.43, f32[128,2,8]{0,2,1:T(8,128)S(1)} %get-tuple-element.57, ...), kind=kOutput, calls=%fused_computation.28 | convolution fusion | flops 273154048 | bytes 5595136 | tf_op jit(solution)/shard_map/tkgs,skd->tkgd/dot_general | solution.py:125
  76.7 2.0 %fusion.21 = f32[128,2,8,128]{0,3,2,1:T(8,128)} fusion(f32[128,2,8,128]{0,3,2,1:T(8,128)S(1)} %fusion.32, f32[2,384,128,8]{2,1,3,0:T(8,128)S(1)} %get-tuple-element.74, f32[128,2,8]{0,2,1:T(8,128)S(1)} %get-tuple-element.27, pred[384]{0:T(512)(128)(4,1)S(1)} %add_add_fusion.1, bf16[384,2,128,1]{0,2,1,3:T(8,128)(2,1)S(1)} %reshape.104), kind=kOutput, calls=%fused_computation.22 | convolution fusion | flops 204734464 | bytes 5448064 | tf_op jit(solution)/shard_map/tkgs,skd->tkgd/dot_general | solution.py:125
  79.1 1.6 %multiply_reduce_fusion = (f32[128]{0:T(128)S(1)}, f32[128,8,128]{0,2,1:T(8,128)S(1)}) fusion(f32[128,8,128]{0,2,1:T(8,128)S(1)} %fusion.36, bf16[128,8,128]{0,2,1:T(8,128)(2,1)S(1)} %bitcast.149, f32[8,128]{1,0:T(8,128)S(1)} %copy-done.8, pred[128,128]{1,0:T(8,128)(4,1)S(1)} %iota_compare_fusion, bf16[128,1024]{1,0:T(8,128)(2,1)S(1)} %copy-done, ...), kind=kOutput, calls=%fused_computation.45 | convolution fusion | flops 68026240 | bytes 1856000 | tf_op jit(solution)/shard_map/hts,shd->thd/dot_general | solution.py:106
  80.6 3.4 %collective-permute-start.11 = (f32[128]{0:T(128)S(1)}, f32[128]{0:T(128)S(1)}, u32[]{:S(2)}, u32[]{:S(2)}) collective-permute-start(f32[128]{0:T(128)S(1)} %get-tuple-element.75), channel_id=1, source_target_pairs={{0,1},{1,0},{2,3},{3,2},{4,5},{5,4},{6,7},{7,6},{8,9},{9,8},{10,11... | collective-permute-start | bytes 1544 | tf_op jit(solution)/shard_map/ppermute | solution.py:89
  84.0 0.9 fusion.88
  86.1 4.9 %collective-permute-start.12 = (f32[128]{0:T(128)S(1)}, f32[128]{0:T(128)S(1)}, u32[]{:S(2)}, u32[]{:S(2)}) collective-permute-start(f32[128]{0:T(128)S(1)} %add.87), channel_id=1, source_target_pairs={{0,2},{1,3},{2,0},{3,1},{4,6},{5,7},{6,4},{7,5},{8,10},{9,11},{10,... | collective-permute-start | bytes 1544 | tf_op jit(solution)/shard_map/ppermute | solution.py:89
  91.6 1.0 %copy.83 = bf16[128,2048]{1,0:T(8,128)(2,1)} copy(bf16[128,2048]{0,1:T(8,128)(2,1)S(1)} %bitcast.153) | data formatting | bytes 1048576
  93.1 0.8 multiply_convert_fusion
  (86 shorter events, 8.2 us)
Async XLA Ops:
  0.6 5.7 %copy-start = (bf16[128,1024]{1,0:T(8,128)(2,1)S(1)}, bf16[128,1024]{1,0:T(8,128)(2,1)}, u32[]{:S(2)}) copy-start(bf16[128,1024]{1,0:T(8,128)(2,1)} %param.11) | copy-start | bytes 786436
  0.6 8.7 %copy-start.5 = (bf16[128,256]{1,0:T(8,128)(2,1)S(1)}, bf16[128,256]{1,0:T(8,128)(2,1)}, u32[]{:S(2)}) copy-start(bf16[128,256]{1,0:T(8,128)(2,1)} %param.15) | copy-start | bytes 196612
  0.7 8.9 %copy-start.6 = (bf16[128,256]{1,0:T(8,128)(2,1)S(1)}, bf16[128,256]{1,0:T(8,128)(2,1)}, u32[]{:S(2)}) copy-start(bf16[128,256]{1,0:T(8,128)(2,1)} %param.16) | copy-start | bytes 196612
  4.6 0.6 copy-start.7
  6.7 37.3 %copy-start.3 = (bf16[128,2048]{1,0:T(8,128)(2,1)S(1)}, bf16[128,2048]{1,0:T(8,128)(2,1)}, u32[]{:S(2)}) copy-start(bf16[128,2048]{1,0:T(8,128)(2,1)} %param.14) | copy-start | bytes 1572868
  7.6 16.6 %collective-permute-start = (f32[8,129,128]{2,0,1:T(8,128)}, f32[8,129,128]{2,0,1:T(8,128)S(1)}, u32[]{:S(2)}, u32[]{:S(2)}) collective-permute-start(f32[8,129,128]{2,0,1:T(8,128)} %copy.59), channel_id=1, source_target_pairs={{0,4},{8,12},{16,20},{24,28},{32,36},{40,44},{48,52},{56,60},{64,6... | collective-permute-start | bytes 1585160 | tf_op jit(solution)/shard_map/ppermute | solution.py:38
  9.7 14.6 %collective-permute-start.1 = (bf16[2,128,256]{1,2,0:T(8,128)(2,1)S(1)}, bf16[2,128,256]{1,2,0:T(8,128)(2,1)S(1)}, u32[]{:S(2)}, u32[]{:S(2)}) collective-permute-start(bf16[2,128,256]{1,2,0:T(8,128)(2,1)S(1)} %get-tuple-element.56), channel_id=1, source_target_pairs={{0,8},{4,12},{8,16},{12,20},{16,24},{20,28},{24,32},{28,36},{32,40... | collective-permute-start | bytes 393224 | tf_op jit(solution)/shard_map/ppermute | solution.py:32
  24.9 11.1 %collective-permute-start.2 = (bf16[8,130,128]{2,1,0:T(8,128)(2,1)S(1)}, bf16[8,130,128]{2,1,0:T(8,128)(2,1)S(1)}, u32[]{:S(2)}, u32[]{:S(2)}) collective-permute-start(bf16[8,130,128]{2,1,0:T(8,128)(2,1)S(1)} %pad_maximum_fusion.2), channel_id=1, source_target_pairs={{4,12},{12,20},{20,28},{28,36},{36,44},{44,52},{52,60},{60,68},{68... | collective-permute-start | bytes 798728 | tf_op jit(solution)/shard_map/ppermute | solution.py:53
  25.5 10.4 %collective-permute-start.3 = (bf16[2,128,256]{1,2,0:T(8,128)(2,1)S(1)}, bf16[2,128,256]{1,2,0:T(8,128)(2,1)S(1)}, u32[]{:S(2)}, u32[]{:S(2)}) collective-permute-start(bf16[2,128,256]{1,2,0:T(8,128)(2,1)S(1)} %collective-permute-done.1), channel_id=1, source_target_pairs={{0,8},{4,12},{8,16},{12,20},{16,24},{20,28},{24,32},{28,36},{32,40... | collective-permute-start | bytes 393224 | tf_op jit(solution)/shard_map/ppermute | solution.py:32
  35.9 9.5 %collective-permute-start.5 = (bf16[2,128,256]{1,2,0:T(8,128)(2,1)S(1)}, bf16[2,128,256]{1,2,0:T(8,128)(2,1)S(1)}, u32[]{:S(2)}, u32[]{:S(2)}) collective-permute-start(bf16[2,128,256]{1,2,0:T(8,128)(2,1)S(1)} %collective-permute-done.3), channel_id=1, source_target_pairs={{0,8},{4,12},{8,16},{12,20},{16,24},{20,28},{24,32},{28,36},{32,40... | collective-permute-start | bytes 393224 | tf_op jit(solution)/shard_map/ppermute | solution.py:32
  38.8 6.6 %collective-permute-start.4 = (bf16[8,128,128]{2,1,0:T(8,128)(2,1)}, bf16[8,128,128]{2,1,0:T(8,128)(2,1)}, u32[]{:S(2)}, u32[]{:S(2)}) collective-permute-start(bf16[8,128,128]{2,1,0:T(8,128)(2,1)} %fusion.53), channel_id=1, source_target_pairs={{4,20},{12,28},{20,36},{28,44},{36,52},{44,60},{52,68},{60,76},{68... | collective-permute-start | bytes 786440 | tf_op jit(solution)/shard_map/ppermute | solution.py:59
  45.4 17.9 %collective-permute-start.7 = (bf16[2,128,256]{1,2,0:T(8,128)(2,1)S(1)}, bf16[2,128,256]{1,2,0:T(8,128)(2,1)}, u32[]{:S(2)}, u32[]{:S(2)}) collective-permute-start(bf16[2,128,256]{1,2,0:T(8,128)(2,1)S(1)} %collective-permute-done.5), channel_id=1, source_target_pairs={{4,12},{12,20},{20,28},{28,36},{36,44},{44,52},{52,60},{60,68},{68... | collective-permute-start | bytes 393224 | tf_op jit(solution)/shard_map/ppermute | solution.py:32
  48.6 16.4 %collective-permute-start.6 = (bf16[8,128,128]{2,1,0:T(8,128)(2,1)}, bf16[8,128,128]{2,1,0:T(8,128)(2,1)S(1)}, u32[]{:S(2)}, u32[]{:S(2)}) collective-permute-start(bf16[8,128,128]{2,1,0:T(8,128)(2,1)} %add_convert_fusion.1), channel_id=1, source_target_pairs={{4,8},{12,16},{20,24},{28,32},{36,40},{44,48},{52,56},{60,64},{68,... | collective-permute-start | bytes 786440 | tf_op jit(solution)/shard_map/ppermute | solution.py:65
  50.8 14.2 %collective-permute-start.8 = (bf16[3,2,128,256]{2,3,1,0:T(8,128)(2,1)}, bf16[3,2,128,256]{2,3,1,0:T(8,128)(2,1)S(1)}, u32[]{:S(2)}, u32[]{:S(2)}) collective-permute-start(bf16[3,2,128,256]{2,3,1,0:T(8,128)(2,1)} %maximum_select_fusion), channel_id=1, source_target_pairs={{0,4},{4,0},{8,12},{12,8},{16,20},{20,16},{24,28},{28,24},{32,36},... | collective-permute-start | bytes 1179656 | tf_op jit(solution)/shard_map/ppermute | solution.py:67
  65.8 12.9 %collective-permute-start.10 = (bf16[2,128,256]{1,2,0:T(8,128)(2,1)S(1)}, bf16[2,128,256]{1,2,0:T(8,128)(2,1)}, u32[]{:S(2)}, u32[]{:S(2)}) collective-permute-start(bf16[2,128,256]{1,2,0:T(8,128)(2,1)S(1)} %broadcast_select_fusion), channel_id=1, source_target_pairs={{0,4},{4,0},{8,12},{12,8},{16,20},{20,16},{24,28},{28,24},{32,36},... | collective-permute-start | bytes 393224 | tf_op jit(solution)/shard_map/ppermute | solution.py:77
  67.8 10.9 %collective-permute-start.9 = (bf16[8,128,128]{2,1,0:T(8,128)(2,1)}, bf16[8,128,128]{2,1,0:T(8,128)(2,1)S(1)}, u32[]{:S(2)}, u32[]{:S(2)}) collective-permute-start(bf16[8,128,128]{2,1,0:T(8,128)(2,1)} %add_convert_fusion), channel_id=1, source_target_pairs={{0,4},{8,12},{16,20},{24,28},{32,36},{40,44},{48,52},{56,60},{64,6... | collective-permute-start | bytes 786440 | tf_op jit(solution)/shard_map/ppermute | solution.py:76
  71.5 3.9 %copy-start.1 = (f32[2,512,128,8]{2,1,3,0:T(8,128)S(1)}, f32[2,512,128,8]{2,1,3,0:T(8,128)}, u32[]{:S(2)}) copy-start(f32[2,512,128,8]{2,1,3,0:T(8,128)} %get-tuple-element.72) | copy-start | bytes 12582916
  76.7 2.1 %copy-start.4 = (bf16[128,1024]{1,0:T(8,128)(2,1)S(1)}, bf16[128,1024]{1,0:T(8,128)(2,1)}, u32[]{:S(2)}) copy-start(bf16[128,1024]{1,0:T(8,128)(2,1)} %param.9) | copy-start | bytes 786436
  76.7 2.4 %copy-start.8 = (f32[8,128]{1,0:T(8,128)S(1)}, f32[8,128]{1,0:T(8,128)}, u32[]{:S(2)}) copy-start(f32[8,128]{1,0:T(8,128)} %copy-done.7) | copy-start | bytes 12292
  79.1 12.0 %copy-start.2 = (f32[128,2,8,128]{0,3,2,1:T(8,128)S(1)}, f32[128,2,8,128]{0,3,2,1:T(8,128)}, u32[]{:S(2)}) copy-start(f32[128,2,8,128]{0,3,2,1:T(8,128)} %fusion.21) | copy-start | bytes 3145732
  80.6 5.5 %collective-permute-start.11 = (f32[128]{0:T(128)S(1)}, f32[128]{0:T(128)S(1)}, u32[]{:S(2)}, u32[]{:S(2)}) collective-permute-start(f32[128]{0:T(128)S(1)} %get-tuple-element.75), channel_id=1, source_target_pairs={{0,1},{1,0},{2,3},{3,2},{4,5},{5,4},{6,7},{7,6},{8,9},{9,8},{10,11... | collective-permute-start | bytes 1544 | tf_op jit(solution)/shard_map/ppermute | solution.py:89
  86.1 7.0 %collective-permute-start.12 = (f32[128]{0:T(128)S(1)}, f32[128]{0:T(128)S(1)}, u32[]{:S(2)}, u32[]{:S(2)}) collective-permute-start(f32[128]{0:T(128)S(1)} %add.87), channel_id=1, source_target_pairs={{0,2},{1,3},{2,0},{3,1},{4,6},{5,7},{6,4},{7,5},{8,10},{9,11},{10,... | collective-permute-start | bytes 1544 | tf_op jit(solution)/shard_map/ppermute | solution.py:89
  91.0 2.0 %copy-start.9 = (f32[1024]{0:T(1024)S(1)}, f32[1024]{0:T(1024)}, u32[]{:S(2)}) copy-start(f32[1024]{0:T(1024)} %param.13) | copy-start | bytes 12292

commit v13 on v12

--- a/solution.py
+++ b/solution.py
@@ -57,27 +57,24 @@
     wide_state = got[:, :rows].astype(jnp.float32) * wide_gain[:, None, None] + wide_state
     wide_gain = got_gain * wide_gain
     got = lax.ppermute(wide_state.astype(jnp.bfloat16), axis, shift_pairs(count, 4, 1))
-    got, kv_next = lax.optimization_barrier((got, ring_step()))
+    kv_next = ring_step()
+    got, kv_next = lax.optimization_barrier((got, kv_next))
     ring.append(kv_next)
     wide_state = got.astype(jnp.float32) * wide_gain[:, None, None] + wide_state
     mine = jnp.stack(ring[:half])
     sent = jnp.where(core == 1, jnp.stack(ring[1:half]), jnp.stack(ring[: half - 1]))
     before = lax.ppermute(wide_state.astype(jnp.bfloat16), axis, shift_pairs(count, 1, 1))
-    before, kv_next, theirs = lax.optimization_barrier(
-        (before, ring_step(1), lax.ppermute(sent, axis, swap))
-    )
+    kv_next = ring_step(1)
+    theirs = lax.ppermute(sent, axis, swap)
+    running = take(running, range(0, width, 2), mine)
+    before, kv_next, theirs, running = lax.optimization_barrier((before, kv_next, theirs, running))
     ring.append(kv_next)
     last = jnp.where(core == 1, ring[half], ring[half - 1])
-    running = take(running, range(0, width, 2), mine)
     running = take(running, range(1, width - 2, 2), theirs)
     after = (before.astype(jnp.float32) * gain[:, None, None] + state).astype(jnp.bfloat16)
-    after, last, running = lax.optimization_barrier(
-        (
-            lax.ppermute(after, axis, shift_pairs(count, 1, 0)),
-            lax.ppermute(last, axis, swap),
-            running,
-        )
-    )
+    after = lax.ppermute(after, axis, shift_pairs(count, 1, 0))
+    last = lax.ppermute(last, axis, swap)
+    after, last, running = lax.optimization_barrier((after, last, running))
     running = take(running, [width - 1], last[None])
     return jnp.where(core == 0, before, after), running
 

time: 94.6 us -> 96.1 us (1.016)
  waiting for transfers between devices: 19.2 us -> 17 us
  starting transfers between devices: 36 us -> 37.1 us
  matrix products: 9.41 us -> 10.4 us
    dot_general x3, matrix products: 3.55 us -> 6.62 us  [absorb(): jnp.einsum('tkgs,skd->tkgd', exponent.astype(jnp.bfloat16), value_rows, p...]
    reduce_sum x3, other arithmetic: 4.07 us -> 1.77 us  [absorb(): row_mass = row_mass * shrink + jnp.sum(exponent, axis=-1)]
    dot_general x3, matrix products: 3.75 us -> 1.84 us  [absorb(): jnp.einsum('tkgd,skd->tkgs', queries, key_rows, preferred_element_type=jn...]
    ppermute x1, waiting for transfers between devices: 1.58 us -> 0.01 us  [exchange(): lax.ppermute(wide_state.astype(jnp.bfloat16), axis, shift_pairs(count, 1,...]
    unnamed x24 -> x36, local copies, waits for them, and re-layouts: 1.79 us -> 3.33 us
    add x2, other arithmetic: 0.02 us -> 1.32 us  [absorb(): row_mass = row_mass * shrink + jnp.sum(exponent, axis=-1)]
    ppermute x3, starting transfers between devices: 13.7 us -> 14.8 us  [the longest x1 9.33 us: exchange(): theirs = lax.ppermute(sent, axis, swap)]
  transfers between devices with their start and end apart: 13 -> 13, of which waited for: 6 -> 5; matrix products, arithmetic and copies ran while one was open for 20% -> 20% of each run, Pallas kernels for 0% -> 0%
where the time goes in v13:
time: 96.1 us; the launch traced here: 95.4 us
  starting transfers between devices  37.1 us (39%)
  waiting for transfers between devices  17 us (18%)
  other arithmetic  11.9 us (12%)
  matrix products  10.4 us (11%)
  between operations  10.1 us (11%)
  local copies, waits for them, and re-layouts  8.86 us (9%)
    ppermute x4, waiting for transfers between devices, ring_step(): return lax.ppermute(ring[-1], axis, shift_pairs(count, 2, parity))  15.7 us
    ppermute x1, starting transfers between devices, exchange(): theirs = lax.ppermute(sent, axis, swap)  9.33 us
    ppermute x4, starting transfers between devices, ring_step(): return lax.ppermute(ring[-1], axis, shift_pairs(count, 2, parity))  8.96 us
    ppermute x2, starting transfers between devices, butterfly_sum(): x = x + lax.ppermute(x, axis, [(i, i ^ step) for i in range(count)])  8.31 us
    dot_general x3, matrix products, absorb(): jnp.einsum('tkgs,skd->tkgd', exponent.astype(jnp.bfloat16), value_rows, p...  6.62 us
    unnamed x36, local copies, waits for them, and re-layouts  3.33 us
    convert_element_type x3, other arithmetic, exchange(): wide_state.astype(jnp.bfloat16)  2.82 us
    ppermute x1, starting transfers between devices, exchange(): last = lax.ppermute(last, axis, swap)  2.82 us
  transfers between devices with their start and end apart: 13, of which 5 were waited for; matrix products, arithmetic and copies ran while one was open for 20% of the time, Pallas kernels for 0%

profile of v13, /device:TPU:24, one launch (start us, length us, event | category | flops | bytes accessed | tf_op | source)
XLA Modules:
  0.0 95.4 jit_solution(3036650955996275771)
XLA Ops:
  0.7 1.6 %fusion.87 = (s32[1]{0:T(128)}, s32[1]{0:T(128)}, s32[1]{0:T(128)}, s32[1]{0:T(128)}, s32[1]{0:T(128)}, /*index=5*/s32[1]{0:T(128)}, s32[1]{0:T(128)}, s32[1]{0:T(128)}) fusion(s32[128]{0:T(128)} %param.17, s32[]{:T(128)S(6)} %max.35, s32[]{:T(128)S(6)} %max.32, s32[]{:T(128)S(6)} %max.31, s32[]{:T(128)S(6)} %max.30, s32[]{:T(128)S(6)} %max.29, ...), kind=kLoop, calls=%fused_computation.112 | loop fusion | bytes 96 | tf_op jit(solution)/shard_map/dynamic_slice | solution.py:158
  3.6 1.0 %reduce_window_sum.11 = f32[8,128]{1,0:T(8,128)S(1)} reduce-window(f32[8,128]{1,0:T(8,128)} %param.12, f32[]{:T(128)} %constant.56.clone.1), window={size=1x128 pad=0_0x127_0}, to_apply=%region_0.0 | reduce-window | flops 130048 | bytes 8196 | tf_op jit(solution)/shard_map/jit(cumsum)/reduce_window_sum | solution.py:97
  5.3 1.1 %copy.102 = bf16[128,1024]{0,1:T(8,128)(2,1)S(1)} copy(bf16[128,1024]{1,0:T(8,128)(2,1)} %param.10) | data formatting | bytes 524288 | tf_op jit(solution)/shard_map/reshape | solution.py:95
  6.8 0.9 copy.59
  7.7 1.8 %collective-permute-start = (f32[8,129,128]{2,0,1:T(8,128)}, f32[8,129,128]{2,0,1:T(8,128)S(1)}, u32[]{:S(2)}, u32[]{:S(2)}) collective-permute-start(f32[8,129,128]{2,0,1:T(8,128)} %copy.59), channel_id=1, source_target_pairs={{0,4},{8,12},{16,20},{24,28},{32,36},{40,44},{48,52},{56,60},{64,6... | collective-permute-start | bytes 1585160 | tf_op jit(solution)/shard_map/ppermute | solution.py:38
  9.8 3.8 %collective-permute-start.1 = (bf16[2,128,256]{1,2,0:T(8,128)(2,1)S(1)}, bf16[2,128,256]{1,2,0:T(8,128)(2,1)S(1)}, u32[]{:S(2)}, u32[]{:S(2)}) collective-permute-start(bf16[2,128,256]{1,2,0:T(8,128)(2,1)S(1)} %get-tuple-element.62), channel_id=1, source_target_pairs={{0,8},{4,12},{8,16},{12,20},{16,24},{20,28},{24,32},{28,36},{32,40... | collective-permute-start | bytes 393224 | tf_op jit(solution)/shard_map/ppermute | solution.py:32
  13.6 10.7 %collective-permute-done.1 = bf16[2,128,256]{1,2,0:T(8,128)(2,1)S(1)} collective-permute-done((bf16[2,128,256]{1,2,0:T(8,128)(2,1)S(1)}, bf16[2,128,256]{1,2,0:T(8,128)(2,1)S(1)}, u32[]{:S(2)}, u32[]{:S(2)}) %collective-permute-start.1) | collective-permute-done | bytes 131104 | tf_op jit(solution)/shard_map/ppermute | solution.py:32
  25.7 1.9 %collective-permute-start.3 = (bf16[2,128,256]{1,2,0:T(8,128)(2,1)S(1)}, bf16[2,128,256]{1,2,0:T(8,128)(2,1)S(1)}, u32[]{:S(2)}, u32[]{:S(2)}) collective-permute-start(bf16[2,128,256]{1,2,0:T(8,128)(2,1)S(1)} %collective-permute-done.1), channel_id=1, source_target_pairs={{0,8},{4,12},{8,16},{12,20},{16,24},{20,28},{24,32},{28,36},{32,40... | collective-permute-start | bytes 393224 | tf_op jit(solution)/shard_map/ppermute | solution.py:32
  31.5 4.5 %collective-permute-done.3 = bf16[2,128,256]{1,2,0:T(8,128)(2,1)S(1)} collective-permute-done((bf16[2,128,256]{1,2,0:T(8,128)(2,1)S(1)}, bf16[2,128,256]{1,2,0:T(8,128)(2,1)S(1)}, u32[]{:S(2)}, u32[]{:S(2)}) %collective-permute-start.3) | collective-permute-done | bytes 131104 | tf_op jit(solution)/shard_map/ppermute | solution.py:32
  36.0 1.9 %collective-permute-start.5 = (bf16[2,128,256]{1,2,0:T(8,128)(2,1)S(1)}, bf16[2,128,256]{1,2,0:T(8,128)(2,1)S(1)}, u32[]{:S(2)}, u32[]{:S(2)}) collective-permute-start(bf16[2,128,256]{1,2,0:T(8,128)(2,1)S(1)} %collective-permute-done.3), channel_id=1, source_target_pairs={{0,8},{4,12},{8,16},{12,20},{16,24},{20,28},{24,32},{28,36},{32,40... | collective-permute-start | bytes 393224 | tf_op jit(solution)/shard_map/ppermute | solution.py:32
  38.1 0.8 fusion.47
  38.9 1.3 %collective-permute-start.4 = (bf16[8,128,128]{2,1,0:T(8,128)(2,1)}, bf16[8,128,128]{2,1,0:T(8,128)(2,1)}, u32[]{:S(2)}, u32[]{:S(2)}) collective-permute-start(bf16[8,128,128]{2,1,0:T(8,128)(2,1)} %fusion.47), channel_id=1, source_target_pairs={{4,20},{12,28},{20,36},{28,44},{36,52},{44,60},{52,68},{60,76},{68... | collective-permute-start | bytes 786440 | tf_op jit(solution)/shard_map/ppermute | solution.py:59
  45.5 1.3 %collective-permute-start.7 = (bf16[2,128,256]{1,2,0:T(8,128)(2,1)S(1)}, bf16[2,128,256]{1,2,0:T(8,128)(2,1)}, u32[]{:S(2)}, u32[]{:S(2)}) collective-permute-start(bf16[2,128,256]{1,2,0:T(8,128)(2,1)S(1)} %collective-permute-done.5), channel_id=1, source_target_pairs={{4,12},{12,20},{20,28},{28,36},{36,44},{44,52},{52,60},{60,68},{68... | collective-permute-start | bytes 393224 | tf_op jit(solution)/shard_map/ppermute | solution.py:32
  46.9 1.8 %add_convert_fusion.1 = bf16[8,128,128]{2,1,0:T(8,128)(2,1)} fusion(bf16[8,128,128]{2,1,0:T(8,128)(2,1)} %collective-permute-done.4, f32[8,128,128]{2,1,0:T(8,128)S(1)} %get-tuple-element.51, f32[8]{0:T(128)S(1)} %get-tuple-element.42, f32[8]{0:T(128)S(1)} %get-tuple-element.43, bf16[8,130,128]{2,1,0:T(8,128)(2,1)S(1)} %collective-permute-done.2), kind=kLoop, calls=%fused_computation.46 | loop fusion | flops 917504 | bytes 1310784 | tf_op jit(solution)/shard_map/convert_element_type | solution.py:66
  48.7 1.3 %collective-permute-start.6 = (bf16[8,128,128]{2,1,0:T(8,128)(2,1)}, bf16[8,128,128]{2,1,0:T(8,128)(2,1)S(1)}, u32[]{:S(2)}, u32[]{:S(2)}) collective-permute-start(bf16[8,128,128]{2,1,0:T(8,128)(2,1)} %add_convert_fusion.1), channel_id=1, source_target_pairs={{4,8},{12,16},{20,24},{28,32},{36,40},{44,48},{52,56},{60,64},{68,... | collective-permute-start | bytes 786440 | tf_op jit(solution)/shard_map/ppermute | solution.py:66
  50.1 0.8 maximum_select_fusion
  51.1 9.3 %collective-permute-start.8 = (bf16[3,2,128,256]{2,3,1,0:T(8,128)(2,1)}, bf16[3,2,128,256]{2,3,1,0:T(8,128)(2,1)S(1)}, u32[]{:S(2)}, u32[]{:S(2)}) collective-permute-start(bf16[3,2,128,256]{2,3,1,0:T(8,128)(2,1)} %maximum_select_fusion), channel_id=1, source_target_pairs={{0,4},{4,0},{8,12},{12,8},{16,20},{20,16},{24,28},{28,24},{32,36},... | collective-permute-start | bytes 1179656 | tf_op jit(solution)/shard_map/ppermute | solution.py:68
  60.5 0.8 fusion.2
  61.3 1.9 %copy-done.1 = f32[2,512,128,8]{2,1,3,0:T(8,128)} copy-done((f32[2,512,128,8]{2,1,3,0:T(8,128)}, f32[2,512,128,8]{2,1,3,0:T(8,128)S(1)}, u32[]{:S(2)}) %copy-start.1) | copy-done | bytes 4194328
  63.2 0.9 fusion.1
  65.0 4.3 %fusion.26 = f32[128,2,8,128]{0,3,2,1:T(8,128)} fusion(f32[2,512,128,8]{2,1,3,0:T(8,128)} %copy-done.1, f32[128,2,8]{0,2,1:T(8,128)S(1)} %broadcast_maximum_fusion, pred[128,512]{0,1:T(8,128)(4,1)S(1)} %copy.65, f32[128,2,8]{0,2,1:T(8,128)S(1)} %get-tuple-element.63, bf16[512,2,128,1]{0,2,1,3:T(8,128)(2,1)S(1)} %reshape.93), kind=kOutput, calls=%fused_computation.26 | convolution fusion | flops 272891904 | bytes 5586944 | tf_op jit(solution)/shard_map/tkgs,skd->tkgd/dot_general | solution.py:122
  69.4 0.8 add_convert_fusion
  70.2 2.8 %collective-permute-start.10 = (bf16[2,128,256]{1,2,0:T(8,128)(2,1)S(1)}, bf16[2,128,256]{1,2,0:T(8,128)(2,1)S(1)}, u32[]{:S(2)}, u32[]{:S(2)}) collective-permute-start(bf16[2,128,256]{1,2,0:T(8,128)(2,1)S(1)} %broadcast_select_fusion), channel_id=1, source_target_pairs={{0,4},{4,0},{8,12},{12,8},{16,20},{20,16},{24,28},{28,24},{32,36},... | collective-permute-start | bytes 393224 | tf_op jit(solution)/shard_map/ppermute | solution.py:76
  73.1 2.6 %collective-permute-start.9 = (bf16[8,128,128]{2,1,0:T(8,128)(2,1)}, bf16[8,128,128]{2,1,0:T(8,128)(2,1)}, u32[]{:S(2)}, u32[]{:S(2)}) collective-permute-start(bf16[8,128,128]{2,1,0:T(8,128)(2,1)} %add_convert_fusion), channel_id=1, source_target_pairs={{0,4},{8,12},{16,20},{24,28},{32,36},{40,44},{48,52},{56,60},{64,6... | collective-permute-start | bytes 786440 | tf_op jit(solution)/shard_map/ppermute | solution.py:75
  77.0 0.7 fusion.4
  78.4 2.0 %multiply_add_fusion = f32[128,2,8,128]{0,3,2,1:T(8,128)} fusion(f32[128,2,8,128]{0,3,2,1:T(8,128)S(1)} %copy-done.3, f32[128,2,8]{0,2,1:T(8,128)S(1)} %get-tuple-element.49, f32[2,384,128,8]{2,1,3,0:T(8,128)S(1)} %get-tuple-element.79, f32[128,2,8]{0,2,1:T(8,128)S(1)} %max.34, pred[384]{0:T(512)(128)(4,1)S(1)} %copy-done.14, ...), kind=kOutput, calls=%fused_computation.35 | convolution fusion | flops 204996608 | bytes 5456256 | tf_op jit(solution)/shard_map/tkgs,skd->tkgd/dot_general | solution.py:122
  80.8 1.3 %multiply_reduce_fusion = (f32[128]{0:T(128)S(1)}, f32[128,8,128]{0,2,1:T(8,128)S(1)}) fusion(f32[128,8,128]{0,2,1:T(8,128)S(1)} %fusion.30, bf16[128,8,128]{0,2,1:T(8,128)(2,1)S(1)} %bitcast.147, f32[8,128]{1,0:T(8,128)S(1)} %copy-done.10, pred[128,128]{1,0:T(8,128)(4,1)} %copy-done.8, bf16[128,1024]{1,0:T(8,128)(2,1)S(1)} %copy-done, ...), kind=kOutput, calls=%fused_computation.44 | convolution fusion | flops 68026240 | bytes 1856000 | tf_op jit(solution)/shard_map/hts,shd->thd/dot_general | solution.py:103
  82.1 3.4 %collective-permute-start.11 = (f32[128]{0:T(128)S(1)}, f32[128]{0:T(128)S(1)}, u32[]{:S(2)}, u32[]{:S(2)}) collective-permute-start(f32[128]{0:T(128)S(1)} %get-tuple-element.80), channel_id=1, source_target_pairs={{0,1},{1,0},{2,3},{3,2},{4,5},{5,4},{6,7},{7,6},{8,9},{9,8},{10,11... | collective-permute-start | bytes 1544 | tf_op jit(solution)/shard_map/ppermute | solution.py:86
  86.8 0.8 collective-permute-done.11
  87.6 4.9 %collective-permute-start.12 = (f32[128]{0:T(128)S(1)}, f32[128]{0:T(128)S(1)}, u32[]{:S(2)}, u32[]{:S(2)}) collective-permute-start(f32[128]{0:T(128)S(1)} %add.87), channel_id=1, source_target_pairs={{0,2},{1,3},{2,0},{3,1},{4,6},{5,7},{6,4},{7,5},{8,10},{9,11},{10,... | collective-permute-start | bytes 1544 | tf_op jit(solution)/shard_map/ppermute | solution.py:86
  93.1 1.0 %copy.83 = bf16[128,2048]{1,0:T(8,128)(2,1)} copy(bf16[128,2048]{0,1:T(8,128)(2,1)S(1)} %bitcast.151) | data formatting | bytes 1048576
  94.5 0.8 multiply_convert_fusion
  (100 shorter events, 10.0 us)
Async XLA Ops:
  0.6 5.8 %copy-start = (bf16[128,1024]{1,0:T(8,128)(2,1)S(1)}, bf16[128,1024]{1,0:T(8,128)(2,1)}, u32[]{:S(2)}) copy-start(bf16[128,1024]{1,0:T(8,128)(2,1)} %param.11) | copy-start | bytes 786436
  0.6 8.9 %copy-start.6 = (bf16[128,256]{1,0:T(8,128)(2,1)S(1)}, bf16[128,256]{1,0:T(8,128)(2,1)}, u32[]{:S(2)}) copy-start(bf16[128,256]{1,0:T(8,128)(2,1)} %param.15) | copy-start | bytes 196612
  0.7 9.0 %copy-start.7 = (bf16[128,256]{1,0:T(8,128)(2,1)S(1)}, bf16[128,256]{1,0:T(8,128)(2,1)}, u32[]{:S(2)}) copy-start(bf16[128,256]{1,0:T(8,128)(2,1)} %param.16) | copy-start | bytes 196612
  4.5 5.2 %copy-start.9 = (f32[8,128]{1,0:T(8,128)}, f32[8,128]{1,0:T(8,128)S(1)}, u32[]{:S(2)}) copy-start(f32[8,128]{1,0:T(8,128)S(1)} %reduce_window_sum.11) | copy-start | bytes 12292
  6.8 37.5 %copy-start.4 = (bf16[128,2048]{1,0:T(8,128)(2,1)S(1)}, bf16[128,2048]{1,0:T(8,128)(2,1)}, u32[]{:S(2)}) copy-start(bf16[128,2048]{1,0:T(8,128)(2,1)} %param.14) | copy-start | bytes 1572868
  7.7 16.7 %collective-permute-start = (f32[8,129,128]{2,0,1:T(8,128)}, f32[8,129,128]{2,0,1:T(8,128)S(1)}, u32[]{:S(2)}, u32[]{:S(2)}) collective-permute-start(f32[8,129,128]{2,0,1:T(8,128)} %copy.59), channel_id=1, source_target_pairs={{0,4},{8,12},{16,20},{24,28},{32,36},{40,44},{48,52},{56,60},{64,6... | collective-permute-start | bytes 1585160 | tf_op jit(solution)/shard_map/ppermute | solution.py:38
  9.8 14.6 %collective-permute-start.1 = (bf16[2,128,256]{1,2,0:T(8,128)(2,1)S(1)}, bf16[2,128,256]{1,2,0:T(8,128)(2,1)S(1)}, u32[]{:S(2)}, u32[]{:S(2)}) collective-permute-start(bf16[2,128,256]{1,2,0:T(8,128)(2,1)S(1)} %get-tuple-element.62), channel_id=1, source_target_pairs={{0,8},{4,12},{8,16},{12,20},{16,24},{20,28},{24,32},{28,36},{32,40... | collective-permute-start | bytes 393224 | tf_op jit(solution)/shard_map/ppermute | solution.py:32
  25.0 11.1 %collective-permute-start.2 = (bf16[8,130,128]{2,1,0:T(8,128)(2,1)S(1)}, bf16[8,130,128]{2,1,0:T(8,128)(2,1)S(1)}, u32[]{:S(2)}, u32[]{:S(2)}) collective-permute-start(bf16[8,130,128]{2,1,0:T(8,128)(2,1)S(1)} %pad_maximum_fusion.2), channel_id=1, source_target_pairs={{4,12},{12,20},{20,28},{28,36},{36,44},{44,52},{52,60},{60,68},{68... | collective-permute-start | bytes 798728 | tf_op jit(solution)/shard_map/ppermute | solution.py:53
  25.7 10.4 %collective-permute-start.3 = (bf16[2,128,256]{1,2,0:T(8,128)(2,1)S(1)}, bf16[2,128,256]{1,2,0:T(8,128)(2,1)S(1)}, u32[]{:S(2)}, u32[]{:S(2)}) collective-permute-start(bf16[2,128,256]{1,2,0:T(8,128)(2,1)S(1)} %collective-permute-done.1), channel_id=1, source_target_pairs={{0,8},{4,12},{8,16},{12,20},{16,24},{20,28},{24,32},{28,36},{32,40... | collective-permute-start | bytes 393224 | tf_op jit(solution)/shard_map/ppermute | solution.py:32
  31.5 12.8 %copy-start.8 = (pred[128,128]{1,0:T(8,128)(4,1)}, pred[128,128]{1,0:T(8,128)(4,1)S(1)}, u32[]{:S(2)}) copy-start(pred[128,128]{1,0:T(8,128)(4,1)S(1)} %iota_compare_fusion) | copy-start | bytes 49156
  36.0 9.5 %collective-permute-start.5 = (bf16[2,128,256]{1,2,0:T(8,128)(2,1)S(1)}, bf16[2,128,256]{1,2,0:T(8,128)(2,1)S(1)}, u32[]{:S(2)}, u32[]{:S(2)}) collective-permute-start(bf16[2,128,256]{1,2,0:T(8,128)(2,1)S(1)} %collective-permute-done.3), channel_id=1, source_target_pairs={{0,8},{4,12},{8,16},{12,20},{16,24},{20,28},{24,32},{28,36},{32,40... | collective-permute-start | bytes 393224 | tf_op jit(solution)/shard_map/ppermute | solution.py:32
  38.9 6.6 %collective-permute-start.4 = (bf16[8,128,128]{2,1,0:T(8,128)(2,1)}, bf16[8,128,128]{2,1,0:T(8,128)(2,1)}, u32[]{:S(2)}, u32[]{:S(2)}) collective-permute-start(bf16[8,128,128]{2,1,0:T(8,128)(2,1)} %fusion.47), channel_id=1, source_target_pairs={{4,20},{12,28},{20,36},{28,44},{36,52},{44,60},{52,68},{60,76},{68... | collective-permute-start | bytes 786440 | tf_op jit(solution)/shard_map/ppermute | solution.py:59
  45.5 23.8 %collective-permute-start.7 = (bf16[2,128,256]{1,2,0:T(8,128)(2,1)S(1)}, bf16[2,128,256]{1,2,0:T(8,128)(2,1)}, u32[]{:S(2)}, u32[]{:S(2)}) collective-permute-start(bf16[2,128,256]{1,2,0:T(8,128)(2,1)S(1)} %collective-permute-done.5), channel_id=1, source_target_pairs={{4,12},{12,20},{20,28},{28,36},{36,44},{44,52},{52,60},{60,68},{68... | collective-permute-start | bytes 393224 | tf_op jit(solution)/shard_map/ppermute | solution.py:32
  48.7 20.7 %collective-permute-start.6 = (bf16[8,128,128]{2,1,0:T(8,128)(2,1)}, bf16[8,128,128]{2,1,0:T(8,128)(2,1)S(1)}, u32[]{:S(2)}, u32[]{:S(2)}) collective-permute-start(bf16[8,128,128]{2,1,0:T(8,128)(2,1)} %add_convert_fusion.1), channel_id=1, source_target_pairs={{4,8},{12,16},{20,24},{28,32},{36,40},{44,48},{52,56},{60,64},{68,... | collective-permute-start | bytes 786440 | tf_op jit(solution)/shard_map/ppermute | solution.py:66
  51.1 18.2 %collective-permute-start.8 = (bf16[3,2,128,256]{2,3,1,0:T(8,128)(2,1)}, bf16[3,2,128,256]{2,3,1,0:T(8,128)(2,1)S(1)}, u32[]{:S(2)}, u32[]{:S(2)}) collective-permute-start(bf16[3,2,128,256]{2,3,1,0:T(8,128)(2,1)} %maximum_select_fusion), channel_id=1, source_target_pairs={{0,4},{4,0},{8,12},{12,8},{16,20},{20,16},{24,28},{28,24},{32,36},... | collective-permute-start | bytes 1179656 | tf_op jit(solution)/shard_map/ppermute | solution.py:68
  61.3 1.9 %copy-start.1 = (f32[2,512,128,8]{2,1,3,0:T(8,128)}, f32[2,512,128,8]{2,1,3,0:T(8,128)S(1)}, u32[]{:S(2)}) copy-start(f32[2,512,128,8]{2,1,3,0:T(8,128)S(1)} %get-tuple-element.77) | copy-start | bytes 12582916
  69.3 6.9 %copy-start.13 = (pred[384]{0:T(512)(128)(4,1)S(1)}, pred[384]{0:T(512)(128)(4,1)}, u32[]{:S(2)}) copy-start(pred[384]{0:T(512)(128)(4,1)} %add_add_fusion.1) | copy-start | bytes 1156
  70.2 10.2 %collective-permute-start.10 = (bf16[2,128,256]{1,2,0:T(8,128)(2,1)S(1)}, bf16[2,128,256]{1,2,0:T(8,128)(2,1)S(1)}, u32[]{:S(2)}, u32[]{:S(2)}) collective-permute-start(bf16[2,128,256]{1,2,0:T(8,128)(2,1)S(1)} %broadcast_select_fusion), channel_id=1, source_target_pairs={{0,4},{4,0},{8,12},{12,8},{16,20},{20,16},{24,28},{28,24},{32,36},... | collective-permute-start | bytes 393224 | tf_op jit(solution)/shard_map/ppermute | solution.py:76
  73.1 7.3 %collective-permute-start.9 = (bf16[8,128,128]{2,1,0:T(8,128)(2,1)}, bf16[8,128,128]{2,1,0:T(8,128)(2,1)}, u32[]{:S(2)}, u32[]{:S(2)}) collective-permute-start(bf16[8,128,128]{2,1,0:T(8,128)(2,1)} %add_convert_fusion), channel_id=1, source_target_pairs={{0,4},{8,12},{16,20},{24,28},{32,36},{40,44},{48,52},{56,60},{64,6... | collective-permute-start | bytes 786440 | tf_op jit(solution)/shard_map/ppermute | solution.py:75
  76.3 1.5 %copy-start.11 = (f32[128,2,8]{0,2,1:T(8,128)S(1)}, f32[128,2,8]{0,2,1:T(8,128)}, u32[]{:S(2)}) copy-start(f32[128,2,8]{0,2,1:T(8,128)} %get-tuple-element.29) | copy-start | bytes 24580
  76.3 2.1 %copy-start.3 = (f32[128,2,8,128]{0,3,2,1:T(8,128)S(1)}, f32[128,2,8,128]{0,3,2,1:T(8,128)}, u32[]{:S(2)}) copy-start(f32[128,2,8,128]{0,3,2,1:T(8,128)} %fusion.26) | copy-start | bytes 3145732
  76.3 2.1 %copy-start.14 = (pred[384]{0:T(512)(128)(4,1)S(1)}, pred[384]{0:T(512)(128)(4,1)}, u32[]{:S(2)}) copy-start(pred[384]{0:T(512)(128)(4,1)} %add_add_fusion.1) | copy-start | bytes 1156
  77.8 2.6 %copy-start.5 = (bf16[128,1024]{1,0:T(8,128)(2,1)S(1)}, bf16[128,1024]{1,0:T(8,128)(2,1)}, u32[]{:S(2)}) copy-start(bf16[128,1024]{1,0:T(8,128)(2,1)} %param.9) | copy-start | bytes 786436
  77.8 2.6 %copy-start.12 = (f32[128,8]{0,1:T(8,128)S(1)}, f32[128,8]{0,1:T(8,128)}, u32[]{:S(2)}) copy-start(f32[128,8]{0,1:T(8,128)} %get-tuple-element.67) | copy-start | bytes 12292
  78.4 2.4 %copy-start.10 = (f32[8,128]{1,0:T(8,128)S(1)}, f32[8,128]{1,0:T(8,128)}, u32[]{:S(2)}) copy-start(f32[8,128]{1,0:T(8,128)} %copy-done.9) | copy-start | bytes 12292
  80.8 11.7 %copy-start.2 = (f32[128,2,8,128]{0,3,2,1:T(8,128)S(1)}, f32[128,2,8,128]{0,3,2,1:T(8,128)}, u32[]{:S(2)}) copy-start(f32[128,2,8,128]{0,3,2,1:T(8,128)} %multiply_add_fusion) | copy-start | bytes 3145732
  82.1 5.5 %collective-permute-start.11 = (f32[128]{0:T(128)S(1)}, f32[128]{0:T(128)S(1)}, u32[]{:S(2)}, u32[]{:S(2)}) collective-permute-start(f32[128]{0:T(128)S(1)} %get-tuple-element.80), channel_id=1, source_target_pairs={{0,1},{1,0},{2,3},{3,2},{4,5},{5,4},{6,7},{7,6},{8,9},{9,8},{10,11... | collective-permute-start | bytes 1544 | tf_op jit(solution)/shard_map/ppermute | solution.py:86
  87.6 7.0 %collective-permute-start.12 = (f32[128]{0:T(128)S(1)}, f32[128]{0:T(128)S(1)}, u32[]{:S(2)}, u32[]{:S(2)}) collective-permute-start(f32[128]{0:T(128)S(1)} %add.87), channel_id=1, source_target_pairs={{0,2},{1,3},{2,0},{3,1},{4,6},{5,7},{6,4},{7,5},{8,10},{9,11},{10,... | collective-permute-start | bytes 1544 | tf_op jit(solution)/shard_map/ppermute | solution.py:86
  92.5 2.0 %copy-start.15 = (f32[1024]{0:T(1024)S(1)}, f32[1024]{0:T(1024)}, u32[]{:S(2)}) copy-start(f32[1024]{0:T(1024)} %param.13) | copy-start | bytes 12292

commit v14 on v13

--- a/solution.py
+++ b/solution.py
@@ -66,15 +66,18 @@
     before = lax.ppermute(wide_state.astype(jnp.bfloat16), axis, shift_pairs(count, 1, 1))
     kv_next = ring_step(1)
     theirs = lax.ppermute(sent, axis, swap)
+    before, kv_next, theirs = lax.optimization_barrier((before, kv_next, theirs))
+    ring.append(kv_next)
+    last = jnp.where(core == 1, ring[half], ring[half - 1])
     running = take(running, range(0, width, 2), mine)
-    before, kv_next, theirs, running = lax.optimization_barrier((before, kv_next, theirs, running))
-    ring.append(kv_next)
-    last = jnp.where(core == 1, ring[half], ring[half - 1])
     running = take(running, range(1, width - 2, 2), theirs)
     after = (before.astype(jnp.float32) * gain[:, None, None] + state).astype(jnp.bfloat16)
-    after = lax.ppermute(after, axis, shift_pairs(count, 1, 0))
-    last = lax.ppermute(last, axis, swap)
-    after, last, running = lax.optimization_barrier((after, last, running))
+    split = after.size // HEAD_DIM
+    both = jnp.concatenate([after.reshape(-1, HEAD_DIM), last.reshape(-1, HEAD_DIM)])
+    both = lax.ppermute(both, axis, swap)
+    both, running = lax.optimization_barrier((both, running))
+    after = both[:split].reshape(after.shape)
+    last = both[split:].reshape(last.shape)
     running = take(running, [width - 1], last[None])
     return jnp.where(core == 0, before, after), running
 

time: 96.1 us -> 98.5 us (1.025)
  matrix products: 10.4 us -> 14 us
  starting transfers between devices: 37.1 us -> 33.9 us
  local copies, waits for them, and re-layouts: 8.86 us -> 11.7 us
  other arithmetic: 11.9 us -> 9.59 us
  waiting for transfers between devices: 17 us -> 18.1 us
    ppermute x2 -> x1, starting transfers between devices: 5.45 us -> 2.04 us  [exchange(): both = lax.ppermute(both, axis, swap)]
    dot_general x3, matrix products: 1.84 us -> 4.89 us  [absorb(): jnp.einsum('tkgd,skd->tkgs', queries, key_rows, preferred_element_type=jn...]
    unnamed x36 -> x34, local copies, waits for them, and re-layouts: 3.33 us -> 1.2 us
    another operation x3 -> x2, local copies, waits for them, and re-layouts: 0.45 us -> 2.4 us  [take(): value_rows = chosen[:, 1].reshape(-1, kv_heads, HEAD_DIM)]
    slice x0 -> x2, local copies, waits for them, and re-layouts: none -> 1.94 us  [the longest x1 0.97 us: exchange(): last = both[split:].reshape(last.shape)]
    add x2, other arithmetic: 1.32 us -> 0.02 us  [absorb(): row_mass = row_mass * shrink + jnp.sum(exponent, axis=-1)]
    ppermute x1, waiting for transfers between devices: 0.01 us -> 1.28 us  [exchange(): lax.ppermute(wide_state.astype(jnp.bfloat16), axis, shift_pairs(count, 1,...]
    slice x4, local copies, waits for them, and re-layouts: 0.28 us -> 1.5 us  [take(): value_rows = chosen[:, 1].reshape(-1, kv_heads, HEAD_DIM)]
  transfers between devices with their start and end apart: 13 -> 12, of which waited for: 5 -> 5; matrix products, arithmetic and copies ran while one was open for 20% -> 22% of each run, Pallas kernels for 0% -> 0%
where the time goes in v14:
time: 98.5 us; the launch traced here: 97.6 us
  starting transfers between devices  33.9 us (34%)
  waiting for transfers between devices  18.1 us (18%)
  matrix products  14 us (14%)
  local copies, waits for them, and re-layouts  11.7 us (12%)
  between operations  10.4 us (11%)
  other arithmetic  9.59 us (10%)
    ppermute x4, waiting for transfers between devices, ring_step(): return lax.ppermute(ring[-1], axis, shift_pairs(count, 2, parity))  16 us
    ppermute x1, starting transfers between devices, exchange(): theirs = lax.ppermute(sent, axis, swap)  9.96 us
    ppermute x2, starting transfers between devices, butterfly_sum(): x = x + lax.ppermute(x, axis, [(i, i ^ step) for i in range(count)])  8.35 us
    ppermute x4, starting transfers between devices, ring_step(): return lax.ppermute(ring[-1], axis, shift_pairs(count, 2, parity))  8.31 us
    dot_general x3, matrix products, absorb(): jnp.einsum('tkgs,skd->tkgd', exponent.astype(jnp.bfloat16), value_rows, p...  6.56 us
    dot_general x3, matrix products, absorb(): jnp.einsum('tkgd,skd->tkgs', queries, key_rows, preferred_element_type=jn...  4.89 us
    convert_element_type x3, other arithmetic, exchange(): wide_state.astype(jnp.bfloat16)  2.83 us
    another operation x2, local copies, waits for them, and re-layouts, take(): value_rows = chosen[:, 1].reshape(-1, kv_heads, HEAD_DIM)  2.4 us
  transfers between devices with their start and end apart: 12, of which 5 were waited for; matrix products, arithmetic and copies ran while one was open for 22% of the time, Pallas kernels for 0%

profile of v14, /device:TPU:24, one launch (start us, length us, event | category | flops | bytes accessed | tf_op | source)
XLA Modules:
  0.0 97.6 jit_solution(13278483087633700648)
XLA Ops:
  0.7 1.6 %fusion.89 = (s32[1]{0:T(128)}, s32[1]{0:T(128)}, s32[1]{0:T(128)}, s32[1]{0:T(128)}, s32[1]{0:T(128)}, /*index=5*/s32[1]{0:T(128)}, s32[1]{0:T(128)}, s32[1]{0:T(128)}) fusion(s32[128]{0:T(128)} %param.17, s32[]{:T(128)S(6)} %max.42, s32[]{:T(128)S(6)} %max.39, s32[]{:T(128)S(6)} %max.38, s32[]{:T(128)S(6)} %max.37, s32[]{:T(128)S(6)} %max.36, ...), kind=kLoop, calls=%fused_computation.114 | loop fusion | bytes 96 | tf_op jit(solution)/shard_map/dynamic_slice | solution.py:161
  3.6 1.0 reduce_window_sum.11
  4.8 1.1 %copy.121 = bf16[128,1024]{0,1:T(8,128)(2,1)S(1)} copy(bf16[128,1024]{1,0:T(8,128)(2,1)} %param.10) | data formatting | bytes 524288 | tf_op jit(solution)/shard_map/reshape | solution.py:98
  6.4 1.9 %collective-permute-start = (f32[8,129,128]{2,0,1:T(8,128)S(1)}, f32[8,129,128]{2,0,1:T(8,128)S(1)}, u32[]{:S(2)}, u32[]{:S(2)}) collective-permute-start(f32[8,129,128]{2,0,1:T(8,128)S(1)} %copy.78), channel_id=1, source_target_pairs={{0,4},{8,12},{16,20},{24,28},{32,36},{40,44},{48,52},{56,60},{64,6... | collective-permute-start | bytes 1585160 | tf_op jit(solution)/shard_map/ppermute | solution.py:38
  8.4 3.8 %collective-permute-start.1 = (bf16[2,128,256]{2,1,0:T(8,128)(2,1)S(1)}, bf16[2,128,256]{2,1,0:T(8,128)(2,1)S(1)}, u32[]{:S(2)}, u32[]{:S(2)}) collective-permute-start(bf16[2,128,256]{2,1,0:T(8,128)(2,1)S(1)} %get-tuple-element.56), channel_id=1, source_target_pairs={{0,8},{4,12},{8,16},{12,20},{16,24},{20,28},{24,32},{28,36},{32,40... | collective-permute-start | bytes 393224 | tf_op jit(solution)/shard_map/ppermute | solution.py:32
  12.3 10.7 %collective-permute-done.1 = bf16[2,128,256]{2,1,0:T(8,128)(2,1)S(1)} collective-permute-done((bf16[2,128,256]{2,1,0:T(8,128)(2,1)S(1)}, bf16[2,128,256]{2,1,0:T(8,128)(2,1)S(1)}, u32[]{:S(2)}, u32[]{:S(2)}) %collective-permute-start.1) | collective-permute-done | bytes 131104 | tf_op jit(solution)/shard_map/ppermute | solution.py:32
  24.3 1.9 %collective-permute-start.3 = (bf16[2,128,256]{2,1,0:T(8,128)(2,1)S(1)}, bf16[2,128,256]{2,1,0:T(8,128)(2,1)S(1)}, u32[]{:S(2)}, u32[]{:S(2)}) collective-permute-start(bf16[2,128,256]{2,1,0:T(8,128)(2,1)S(1)} %collective-permute-done.1), channel_id=1, source_target_pairs={{0,8},{4,12},{8,16},{12,20},{16,24},{20,28},{24,32},{28,36},{32,40... | collective-permute-start | bytes 393224 | tf_op jit(solution)/shard_map/ppermute | solution.py:32
  30.3 4.4 %collective-permute-done.3 = bf16[2,128,256]{2,1,0:T(8,128)(2,1)S(1)} collective-permute-done((bf16[2,128,256]{2,1,0:T(8,128)(2,1)S(1)}, bf16[2,128,256]{2,1,0:T(8,128)(2,1)S(1)}, u32[]{:S(2)}, u32[]{:S(2)}) %collective-permute-start.3) | collective-permute-done | bytes 131104 | tf_op jit(solution)/shard_map/ppermute | solution.py:32
  34.7 1.9 %collective-permute-start.5 = (bf16[2,128,256]{2,1,0:T(8,128)(2,1)S(1)}, bf16[2,128,256]{2,1,0:T(8,128)(2,1)S(1)}, u32[]{:S(2)}, u32[]{:S(2)}) collective-permute-start(bf16[2,128,256]{2,1,0:T(8,128)(2,1)S(1)} %collective-permute-done.3), channel_id=1, source_target_pairs={{0,8},{4,12},{8,16},{12,20},{16,24},{20,28},{24,32},{28,36},{32,40... | collective-permute-start | bytes 393224 | tf_op jit(solution)/shard_map/ppermute | solution.py:32
  36.7 0.8 fusion.53
  37.6 1.3 %collective-permute-start.4 = (bf16[8,128,128]{2,1,0:T(8,128)(2,1)}, bf16[8,128,128]{2,1,0:T(8,128)(2,1)}, u32[]{:S(2)}, u32[]{:S(2)}) collective-permute-start(bf16[8,128,128]{2,1,0:T(8,128)(2,1)} %fusion.53), channel_id=1, source_target_pairs={{4,20},{12,28},{20,36},{28,44},{36,52},{44,60},{52,68},{60,76},{68... | collective-permute-start | bytes 786440 | tf_op jit(solution)/shard_map/ppermute | solution.py:59
  43.3 0.9 collective-permute-done.5
  44.8 1.8 %add_convert_fusion.1 = bf16[8,128,128]{2,1,0:T(8,128)(2,1)} fusion(bf16[8,128,128]{2,1,0:T(8,128)(2,1)} %collective-permute-done.4, f32[8,128,128]{2,1,0:T(8,128)S(1)} %get-tuple-element.45, f32[8]{0:T(128)S(1)} %get-tuple-element.36, f32[8]{0:T(128)S(1)} %get-tuple-element.37, bf16[8,130,128]{2,1,0:T(8,128)(2,1)S(1)} %collective-permute-done.2), kind=kLoop, calls=%fused_computation.47 | loop fusion | flops 917504 | bytes 1310784 | tf_op jit(solution)/shard_map/convert_element_type | solution.py:66
  46.7 1.3 %collective-permute-start.6 = (bf16[8,128,128]{2,1,0:T(8,128)(2,1)}, bf16[8,128,128]{2,1,0:T(8,128)(2,1)S(1)}, u32[]{:S(2)}, u32[]{:S(2)}) collective-permute-start(bf16[8,128,128]{2,1,0:T(8,128)(2,1)} %add_convert_fusion.1), channel_id=1, source_target_pairs={{4,8},{12,16},{20,24},{28,32},{36,40},{44,48},{52,56},{60,64},{68,... | collective-permute-start | bytes 786440 | tf_op jit(solution)/shard_map/ppermute | solution.py:66
  48.0 0.8 maximum_select_fusion
  48.9 10.0 %collective-permute-start.8 = (bf16[3,2,128,256]{3,2,1,0:T(8,128)(2,1)}, bf16[3,2,128,256]{3,2,1,0:T(8,128)(2,1)S(1)}, u32[]{:S(2)}, u32[]{:S(2)}) collective-permute-start(bf16[3,2,128,256]{3,2,1,0:T(8,128)(2,1)} %maximum_select_fusion), channel_id=1, source_target_pairs={{0,4},{4,0},{8,12},{12,8},{16,20},{20,16},{24,28},{28,24},{32,36},... | collective-permute-start | bytes 1179656 | tf_op jit(solution)/shard_map/ppermute | solution.py:68
  58.9 2.7 %fusion.2 = (f32[128,2,8]{0,2,1:T(8,128)S(1)}, f32[2,512,128,8]{2,1,3,0:T(8,128)}) fusion(pred[128,512]{0,1:T(8,128)(4,1)S(1)} %copy.82, bf16[128,2,8,128]{3,2,1,0:T(8,128)(2,1)S(1)} %bitcast.135, bf16[512,2,128,1]{2,1,0,3:T(2,128)(2,1)S(1)} %bitcast.141), kind=kOutput, calls=%fused_computation.4 | convolution fusion | flops 271579136 | bytes 5054464 | tf_op jit(solution)/shard_map/tkgd,skd->tkgs/dot_general | solution.py:117
  62.4 1.3 %collective-permute-done.6 = bf16[8,128,128]{2,1,0:T(8,128)(2,1)S(1)} collective-permute-done((bf16[8,128,128]{2,1,0:T(8,128)(2,1)}, bf16[8,128,128]{2,1,0:T(8,128)(2,1)S(1)}, u32[]{:S(2)}, u32[]{:S(2)}) %collective-permute-start.6) | collective-permute-done | bytes 262176 | tf_op jit(solution)/shard_map/ppermute | solution.py:66
  66.2 2.0 %collective-permute-start.9 = (bf16[1536,128]{1,0:T(8,128)(2,1)}, bf16[1536,128]{1,0:T(8,128)(2,1)}, u32[]{:S(2)}, u32[]{:S(2)}) collective-permute-start(bf16[1536,128]{1,0:T(8,128)(2,1)} %pad_maximum_fusion.2), channel_id=1, source_target_pairs={{0,4},{4,0},{8,12},{12,8},{16,20},{20,16},{24,28},{28,24},{32,36},... | collective-permute-start | bytes 1179656 | tf_op jit(solution)/shard_map/ppermute | solution.py:77
  68.2 1.8 %fusion.5 = (f32[128,2,8]{0,2,1:T(8,128)S(1)}, f32[2,384,128,8]{2,1,3,0:T(8,128)S(1)}) fusion(pred[384]{0:T(512)(128)(4,1)S(1)} %add_add_fusion.1, bf16[128,2,8,128]{3,2,1,0:T(8,128)(2,1)} %bitcast.136, bf16[384,2,128,1]{2,1,0,3:T(2,128)(2,1)} %bitcast.145), kind=kOutput, calls=%fused_computation.9 | convolution fusion | flops 203683840 | bytes 3875200 | tf_op jit(solution)/shard_map/tkgd,skd->tkgs/dot_general | solution.py:117
  70.1 0.9 fusion.1
  71.7 2.1 %fusion.32 = f32[128,2,8,128]{0,3,2,1:T(8,128)} fusion(f32[2,512,128,8]{2,1,3,0:T(8,128)S(1)} %copy-done.1, f32[128,2,8]{0,2,1:T(8,128)S(1)} %get-tuple-element.59, pred[128,512]{0,1:T(8,128)(4,1)S(1)} %copy.82, f32[128,2,8]{0,2,1:T(8,128)S(1)} %get-tuple-element.43, f32[128,2,8]{0,2,1:T(8,128)S(1)} %get-tuple-element.57, ...), kind=kOutput, calls=%fused_computation.28 | convolution fusion | flops 273154048 | bytes 5595136 | tf_op jit(solution)/shard_map/tkgs,skd->tkgd/dot_general | solution.py:125
  73.8 1.6 %reshape_squeeze.21 = bf16[384,2,128]{2,1,0:T(2,128)(2,1)} reshape(bf16[3,1,128,256]{3,2,1,0:T(8,128)(2,1)} %get-tuple-element.51) | data formatting | bytes 393216 | tf_op jit(solution)/shard_map/reshape;squeeze | solution.py:154
  75.4 3.3 %fusion.21 = f32[128,2,8,128]{0,3,2,1:T(8,128)} fusion(f32[128,2,8,128]{0,3,2,1:T(8,128)} %fusion.32, f32[2,384,128,8]{2,1,3,0:T(8,128)S(1)} %get-tuple-element.74, f32[128,2,8]{0,2,1:T(8,128)S(1)} %get-tuple-element.26, pred[384]{0:T(512)(128)(4,1)S(1)} %copy-done.14, bf16[384,2,128,1]{2,1,0,3:T(2,128)(2,1)} %bitcast.146), kind=kOutput, calls=%fused_computation.22 | convolution fusion | flops 204734464 | bytes 5448064 | tf_op jit(solution)/shard_map/tkgs,skd->tkgd/dot_general | solution.py:125
  78.7 1.0 slice.54
  79.7 1.0 slice.53
  81.1 2.0 %multiply_reduce_fusion = (f32[128]{0:T(128)}, f32[128,8,128]{0,2,1:T(8,128)S(1)}) fusion(f32[128,8,128]{0,2,1:T(8,128)S(1)} %fusion.36, bf16[128,8,128]{0,2,1:T(8,128)(2,1)} %bitcast.144, f32[8,128]{1,0:T(8,128)S(1)} %reduce_window_sum.11, pred[128,128]{1,0:T(8,128)(4,1)S(1)} %iota_compare_fusion, bf16[128,1024]{1,0:T(8,128)(2,1)S(1)} %copy-done, ...), kind=kOutput, calls=%fused_computation.45 | convolution fusion | flops 68026240 | bytes 1856000 | tf_op jit(solution)/shard_map/hts,shd->thd/dot_general | solution.py:106
  83.2 3.4 %collective-permute-start.10 = (f32[128]{0:T(128)}, f32[128]{0:T(128)}, u32[]{:S(2)}, u32[]{:S(2)}) collective-permute-start(f32[128]{0:T(128)} %get-tuple-element.75), channel_id=1, source_target_pairs={{0,1},{1,0},{2,3},{3,2},{4,5},{5,4},{6,7},{7,6},{8,9},{9,8},{10,11... | collective-permute-start | bytes 1544 | tf_op jit(solution)/shard_map/ppermute | solution.py:89
  89.5 4.9 %collective-permute-start.11 = (f32[128]{0:T(128)S(1)}, f32[128]{0:T(128)S(1)}, u32[]{:S(2)}, u32[]{:S(2)}) collective-permute-start(f32[128]{0:T(128)S(1)} %add.87), channel_id=1, source_target_pairs={{0,2},{1,3},{2,0},{3,1},{4,6},{5,7},{6,4},{7,5},{8,10},{9,11},{10,... | collective-permute-start | bytes 1544 | tf_op jit(solution)/shard_map/ppermute | solution.py:89
  94.4 1.2 %divide_convert_fusion = bf16[128,2,8,128]{0,3,2,1:T(8,128)(2,1)S(1)} fusion(f32[128,2,8,128]{0,3,2,1:T(8,128)S(1)} %copy-done.7, f32[128,2,8]{0,2,1:T(8,128)S(1)} %get-tuple-element.40, bf16[128,2,128,1]{0,2,3,1:T(8,128)(2,1)} %bitcast.156, f32[128,2,8,128]{0,3,2,1:T(8,128)S(1)} %get-tuple-element.78, f32[128,2,8]{0,2,1:T(8,128)S(1)} %max.43, ...), kind=kOutput, calls=%fused_computation.35 | convolution fusion | flops 68681728 | bytes 2711552 | tf_op jit(solution)/shard_map/tkgs,skd->tkgd/dot_general | solution.py:125
  95.8 1.0 %copy.99 = bf16[128,2048]{1,0:T(8,128)(2,1)} copy(bf16[128,2048]{0,1:T(8,128)(2,1)S(1)} %bitcast.149) | data formatting | bytes 1048576
  96.8 0.8 multiply_convert_fusion
  (97 shorter events, 10.8 us)
Async XLA Ops:
  0.6 5.3 %copy-start = (bf16[128,1024]{1,0:T(8,128)(2,1)S(1)}, bf16[128,1024]{1,0:T(8,128)(2,1)}, u32[]{:S(2)}) copy-start(bf16[128,1024]{1,0:T(8,128)(2,1)} %param.11) | copy-start | bytes 786436
  0.6 7.7 %copy-start.11 = (bf16[128,256]{1,0:T(8,128)(2,1)S(1)}, bf16[128,256]{1,0:T(8,128)(2,1)}, u32[]{:S(2)}) copy-start(bf16[128,256]{1,0:T(8,128)(2,1)} %param.16) | copy-start | bytes 196612
  0.7 7.7 %copy-start.12 = (bf16[128,256]{1,0:T(8,128)(2,1)S(1)}, bf16[128,256]{1,0:T(8,128)(2,1)}, u32[]{:S(2)}) copy-start(bf16[128,256]{1,0:T(8,128)(2,1)} %param.15) | copy-start | bytes 196612
  5.9 2.4 %copy-start.6 = (bf16[128,1024]{0,1:T(8,128)(2,1)}, bf16[128,1024]{0,1:T(8,128)(2,1)S(1)}, u32[]{:S(2)}) copy-start(bf16[128,1024]{0,1:T(8,128)(2,1)S(1)} %copy.121) | copy-start | bytes 786436
  6.3 36.7 %copy-start.8 = (bf16[128,2048]{1,0:T(8,128)(2,1)S(1)}, bf16[128,2048]{1,0:T(8,128)(2,1)}, u32[]{:S(2)}) copy-start(bf16[128,2048]{1,0:T(8,128)(2,1)} %param.14) | copy-start | bytes 1572868
  6.4 16.6 %collective-permute-start = (f32[8,129,128]{2,0,1:T(8,128)S(1)}, f32[8,129,128]{2,0,1:T(8,128)S(1)}, u32[]{:S(2)}, u32[]{:S(2)}) collective-permute-start(f32[8,129,128]{2,0,1:T(8,128)S(1)} %copy.78), channel_id=1, source_target_pairs={{0,4},{8,12},{16,20},{24,28},{32,36},{40,44},{48,52},{56,60},{64,6... | collective-permute-start | bytes 1585160 | tf_op jit(solution)/shard_map/ppermute | solution.py:38
  8.4 14.6 %collective-permute-start.1 = (bf16[2,128,256]{2,1,0:T(8,128)(2,1)S(1)}, bf16[2,128,256]{2,1,0:T(8,128)(2,1)S(1)}, u32[]{:S(2)}, u32[]{:S(2)}) collective-permute-start(bf16[2,128,256]{2,1,0:T(8,128)(2,1)S(1)} %get-tuple-element.56), channel_id=1, source_target_pairs={{0,8},{4,12},{8,16},{12,20},{16,24},{20,28},{24,32},{28,36},{32,40... | collective-permute-start | bytes 393224 | tf_op jit(solution)/shard_map/ppermute | solution.py:32
  23.6 11.1 %collective-permute-start.2 = (bf16[8,130,128]{2,1,0:T(8,128)(2,1)S(1)}, bf16[8,130,128]{2,1,0:T(8,128)(2,1)S(1)}, u32[]{:S(2)}, u32[]{:S(2)}) collective-permute-start(bf16[8,130,128]{2,1,0:T(8,128)(2,1)S(1)} %pad_maximum_fusion.3), channel_id=1, source_target_pairs={{4,12},{12,20},{20,28},{28,36},{36,44},{44,52},{52,60},{60,68},{68... | collective-permute-start | bytes 798728 | tf_op jit(solution)/shard_map/ppermute | solution.py:53
  24.3 10.4 %collective-permute-start.3 = (bf16[2,128,256]{2,1,0:T(8,128)(2,1)S(1)}, bf16[2,128,256]{2,1,0:T(8,128)(2,1)S(1)}, u32[]{:S(2)}, u32[]{:S(2)}) collective-permute-start(bf16[2,128,256]{2,1,0:T(8,128)(2,1)S(1)} %collective-permute-done.1), channel_id=1, source_target_pairs={{0,8},{4,12},{8,16},{12,20},{16,24},{20,28},{24,32},{28,36},{32,40... | collective-permute-start | bytes 393224 | tf_op jit(solution)/shard_map/ppermute | solution.py:32
  34.7 9.5 %collective-permute-start.5 = (bf16[2,128,256]{2,1,0:T(8,128)(2,1)S(1)}, bf16[2,128,256]{2,1,0:T(8,128)(2,1)S(1)}, u32[]{:S(2)}, u32[]{:S(2)}) collective-permute-start(bf16[2,128,256]{2,1,0:T(8,128)(2,1)S(1)} %collective-permute-done.3), channel_id=1, source_target_pairs={{0,8},{4,12},{8,16},{12,20},{16,24},{20,28},{24,32},{28,36},{32,40... | collective-permute-start | bytes 393224 | tf_op jit(solution)/shard_map/ppermute | solution.py:32
  37.6 6.6 %collective-permute-start.4 = (bf16[8,128,128]{2,1,0:T(8,128)(2,1)}, bf16[8,128,128]{2,1,0:T(8,128)(2,1)}, u32[]{:S(2)}, u32[]{:S(2)}) collective-permute-start(bf16[8,128,128]{2,1,0:T(8,128)(2,1)} %fusion.53), channel_id=1, source_target_pairs={{4,20},{12,28},{20,36},{28,44},{36,52},{44,60},{52,68},{60,76},{68... | collective-permute-start | bytes 786440 | tf_op jit(solution)/shard_map/ppermute | solution.py:59
  43.2 18.5 %copy-start.2 = (bf16[16,8,16,128]{3,2,1,0:T(8,128)(2,1)}, bf16[16,8,16,128]{3,2,1,0:T(8,128)(2,1)S(1)}, u32[]{:S(2)}) copy-start(bf16[16,8,16,128]{3,2,1,0:T(8,128)(2,1)S(1)} %copy.124) | copy-start | bytes 1572868
  43.3 27.7 %copy-start.13 = (pred[384]{0:T(512)(128)(4,1)}, pred[384]{0:T(512)(128)(4,1)S(1)}, u32[]{:S(2)}) copy-start(pred[384]{0:T(512)(128)(4,1)S(1)} %add_add_fusion.1) | copy-start | bytes 1156
  44.2 18.3 %collective-permute-start.7 = (bf16[2,128,256]{2,1,0:T(8,128)(2,1)S(1)}, bf16[2,128,256]{2,1,0:T(8,128)(2,1)S(1)}, u32[]{:S(2)}, u32[]{:S(2)}) collective-permute-start(bf16[2,128,256]{2,1,0:T(8,128)(2,1)S(1)} %collective-permute-done.5), channel_id=1, source_target_pairs={{4,12},{12,20},{20,28},{28,36},{36,44},{44,52},{52,60},{60,68},{68... | collective-permute-start | bytes 393224 | tf_op jit(solution)/shard_map/ppermute | solution.py:32
  46.7 17.0 %collective-permute-start.6 = (bf16[8,128,128]{2,1,0:T(8,128)(2,1)}, bf16[8,128,128]{2,1,0:T(8,128)(2,1)S(1)}, u32[]{:S(2)}, u32[]{:S(2)}) collective-permute-start(bf16[8,128,128]{2,1,0:T(8,128)(2,1)} %add_convert_fusion.1), channel_id=1, source_target_pairs={{4,8},{12,16},{20,24},{28,32},{36,40},{44,48},{52,56},{60,64},{68,... | collective-permute-start | bytes 786440 | tf_op jit(solution)/shard_map/ppermute | solution.py:66
  48.9 14.8 %collective-permute-start.8 = (bf16[3,2,128,256]{3,2,1,0:T(8,128)(2,1)}, bf16[3,2,128,256]{3,2,1,0:T(8,128)(2,1)S(1)}, u32[]{:S(2)}, u32[]{:S(2)}) collective-permute-start(bf16[3,2,128,256]{3,2,1,0:T(8,128)(2,1)} %maximum_select_fusion), channel_id=1, source_target_pairs={{0,4},{4,0},{8,12},{12,8},{16,20},{20,16},{24,28},{28,24},{32,36},... | collective-permute-start | bytes 1179656 | tf_op jit(solution)/shard_map/ppermute | solution.py:68
  63.7 4.5 %copy-start.4 = (bf16[8,128,128]{2,1,0:T(8,128)(2,1)}, bf16[8,128,128]{2,1,0:T(8,128)(2,1)S(1)}, u32[]{:S(2)}) copy-start(bf16[8,128,128]{2,1,0:T(8,128)(2,1)S(1)} %collective-permute-done.6) | copy-start | bytes 786436
  65.4 4.7 %copy-start.1 = (f32[2,512,128,8]{2,1,3,0:T(8,128)S(1)}, f32[2,512,128,8]{2,1,3,0:T(8,128)}, u32[]{:S(2)}) copy-start(f32[2,512,128,8]{2,1,3,0:T(8,128)} %get-tuple-element.72) | copy-start | bytes 12582916
  66.2 12.6 %collective-permute-start.9 = (bf16[1536,128]{1,0:T(8,128)(2,1)}, bf16[1536,128]{1,0:T(8,128)(2,1)}, u32[]{:S(2)}, u32[]{:S(2)}) collective-permute-start(bf16[1536,128]{1,0:T(8,128)(2,1)} %pad_maximum_fusion.2), channel_id=1, source_target_pairs={{0,4},{4,0},{8,12},{12,8},{16,20},{20,16},{24,28},{28,24},{32,36},... | collective-permute-start | bytes 1179656 | tf_op jit(solution)/shard_map/ppermute | solution.py:77
  70.1 1.6 %copy-start.10 = (bf16[512,2,128]{2,1,0:T(2,128)(2,1)S(1)}, bf16[512,2,128]{2,1,0:T(2,128)(2,1)}, u32[]{:S(2)}) copy-start(bf16[512,2,128]{2,1,0:T(2,128)(2,1)} %reshape.119) | copy-start | bytes 786436
  71.7 3.8 %copy-start.14 = (pred[384]{0:T(512)(128)(4,1)S(1)}, pred[384]{0:T(512)(128)(4,1)}, u32[]{:S(2)}) copy-start(pred[384]{0:T(512)(128)(4,1)} %copy-done.13) | copy-start | bytes 1156
  75.4 5.3 %copy-start.5 = (bf16[8,128,128]{2,1,0:T(8,128)(2,1)S(1)}, bf16[8,128,128]{2,1,0:T(8,128)(2,1)}, u32[]{:S(2)}) copy-start(bf16[8,128,128]{2,1,0:T(8,128)(2,1)} %copy-done.4) | copy-start | bytes 786436
  75.4 5.3 %copy-start.9 = (bf16[128,1024]{1,0:T(8,128)(2,1)S(1)}, bf16[128,1024]{1,0:T(8,128)(2,1)}, u32[]{:S(2)}) copy-start(bf16[128,1024]{1,0:T(8,128)(2,1)} %param.9) | copy-start | bytes 786436
  78.7 8.0 %copy-start.3 = (bf16[16,8,16,128]{3,2,1,0:T(8,128)(2,1)S(1)}, bf16[16,8,16,128]{3,2,1,0:T(8,128)(2,1)}, u32[]{:S(2)}) copy-start(bf16[16,8,16,128]{3,2,1,0:T(8,128)(2,1)} %copy-done.2) | copy-start | bytes 1572868
  80.7 13.7 %copy-start.7 = (f32[128,2,8,128]{0,3,2,1:T(8,128)S(1)}, f32[128,2,8,128]{0,3,2,1:T(8,128)}, u32[]{:S(2)}) copy-start(f32[128,2,8,128]{0,3,2,1:T(8,128)} %fusion.21) | copy-start | bytes 3145732
  83.2 5.6 %collective-permute-start.10 = (f32[128]{0:T(128)}, f32[128]{0:T(128)}, u32[]{:S(2)}, u32[]{:S(2)}) collective-permute-start(f32[128]{0:T(128)} %get-tuple-element.75), channel_id=1, source_target_pairs={{0,1},{1,0},{2,3},{3,2},{4,5},{5,4},{6,7},{7,6},{8,9},{9,8},{10,11... | collective-permute-start | bytes 1544 | tf_op jit(solution)/shard_map/ppermute | solution.py:89
  89.5 7.3 %collective-permute-start.11 = (f32[128]{0:T(128)S(1)}, f32[128]{0:T(128)S(1)}, u32[]{:S(2)}, u32[]{:S(2)}) collective-permute-start(f32[128]{0:T(128)S(1)} %add.87), channel_id=1, source_target_pairs={{0,2},{1,3},{2,0},{3,1},{4,6},{5,7},{6,4},{7,5},{8,10},{9,11},{10,... | collective-permute-start | bytes 1544 | tf_op jit(solution)/shard_map/ppermute | solution.py:89
  94.4 2.4 %copy-start.15 = (f32[1024]{0:T(1024)S(1)}, f32[1024]{0:T(1024)}, u32[]{:S(2)}) copy-start(f32[1024]{0:T(1024)} %param.13) | copy-start | bytes 12292

commit v15 on v13

--- a/solution.py
+++ b/solution.py
@@ -66,10 +66,10 @@
     before = lax.ppermute(wide_state.astype(jnp.bfloat16), axis, shift_pairs(count, 1, 1))
     kv_next = ring_step(1)
     theirs = lax.ppermute(sent, axis, swap)
-    running = take(running, range(0, width, 2), mine)
-    before, kv_next, theirs, running = lax.optimization_barrier((before, kv_next, theirs, running))
+    before, kv_next, theirs = lax.optimization_barrier((before, kv_next, theirs))
     ring.append(kv_next)
     last = jnp.where(core == 1, ring[half], ring[half - 1])
+    running = take(running, range(0, width, 2), mine)
     running = take(running, range(1, width - 2, 2), theirs)
     after = (before.astype(jnp.float32) * gain[:, None, None] + state).astype(jnp.bfloat16)
     after = lax.ppermute(after, axis, shift_pairs(count, 1, 0))
@@ -77,15 +77,6 @@
     after, last, running = lax.optimization_barrier((after, last, running))
     running = take(running, [width - 1], last[None])
     return jnp.where(core == 0, before, after), running
-
-
-def butterfly_sum(x, axis):
-    count = lax.axis_size(axis)
-    step = 1
-    while step < count:
-        x = x + lax.ppermute(x, axis, [(i, i ^ step) for i in range(count)])
-        step *= 2
-    return x
 
 
 def lightning_local(light_q, light_k, light_v, log_decay, joined):
@@ -177,7 +168,7 @@
         * reach_gain.T[:, :, None]
     )
     mixed = (intra_part + inter_part).reshape(tok_rows, -1)
-    square_sum = butterfly_sum(jnp.sum(mixed * mixed, axis=1), "head")
+    square_sum = lax.psum(jnp.sum(mixed * mixed, axis=1), "head")
     inv_norm = lax.rsqrt(square_sum / (LIGHTNING_HEADS * HEAD_DIM) + 1e-06)
     light_out = (mixed * inv_norm[:, None] * light_gain).astype(jnp.bfloat16)
     _, row_mass, weighted = running

time: 96.1 us -> 95.7 us (level)
  blocking collectives: 0 us -> 10.5 us
  starting transfers between devices: 37.1 us -> 27.7 us
  waiting for transfers between devices: 17 us -> 18.2 us
  matrix products: 10.4 us -> 9.4 us
    psum x0 -> x1, blocking collectives: none -> 10.5 us  [body(): square_sum = lax.psum(jnp.sum(mixed * mixed, axis=1), 'head')]
    ppermute x2 -> x0, starting transfers between devices: 8.31 us -> none  [butterfly_sum(): x = x + lax.ppermute(x, axis, [(i, i ^ step) for i in range(count)])]
    dot_general x3, matrix products: 6.62 us -> 3.54 us  [absorb(): jnp.einsum('tkgs,skd->tkgd', exponent.astype(jnp.bfloat16), value_rows, p...]
    reduce_sum x3, other arithmetic: 1.77 us -> 4.07 us  [absorb(): row_mass = row_mass * shrink + jnp.sum(exponent, axis=-1)]
    dot_general x3, matrix products: 1.84 us -> 3.75 us  [absorb(): jnp.einsum('tkgd,skd->tkgs', queries, key_rows, preferred_element_type=jn...]
    ppermute x1, waiting for transfers between devices: 0.01 us -> 1.58 us  [exchange(): lax.ppermute(wide_state.astype(jnp.bfloat16), axis, shift_pairs(count, 1,...]
    unnamed x36 -> x24, local copies, waits for them, and re-layouts: 3.33 us -> 1.79 us
    add x2, other arithmetic: 1.32 us -> 0.02 us  [absorb(): row_mass = row_mass * shrink + jnp.sum(exponent, axis=-1)]
  transfers between devices with their start and end apart: 13 -> 11, of which waited for: 5 -> 4; matrix products, arithmetic and copies ran while one was open for 20% -> 17% of each run, Pallas kernels for 0% -> 0%
where the time goes in v15:
time: 95.7 us; the launch traced here: 95 us
  starting transfers between devices  27.7 us (29%)
  waiting for transfers between devices  18.2 us (19%)
  other arithmetic  11.2 us (12%)
  blocking collectives  10.5 us (11%)
  between operations  9.8 us (10%)
  matrix products  9.4 us (10%)
  local copies, waits for them, and re-layouts  8.23 us (9%)
    ppermute x4, waiting for transfers between devices, ring_step(): return lax.ppermute(ring[-1], axis, shift_pairs(count, 2, parity))  16.6 us
    psum x1, blocking collectives, body(): square_sum = lax.psum(jnp.sum(mixed * mixed, axis=1), 'head')  10.5 us
    ppermute x1, starting transfers between devices, exchange(): theirs = lax.ppermute(sent, axis, swap)  9.33 us
    ppermute x4, starting transfers between devices, ring_step(): return lax.ppermute(ring[-1], axis, shift_pairs(count, 2, parity))  8.96 us
    reduce_sum x3, other arithmetic, absorb(): row_mass = row_mass * shrink + jnp.sum(exponent, axis=-1)  4.07 us
    dot_general x3, matrix products, absorb(): jnp.einsum('tkgd,skd->tkgs', queries, key_rows, preferred_element_type=jn...  3.75 us
    dot_general x3, matrix products, absorb(): jnp.einsum('tkgs,skd->tkgd', exponent.astype(jnp.bfloat16), value_rows, p...  3.54 us
    convert_element_type x3, other arithmetic, exchange(): wide_state.astype(jnp.bfloat16)  2.82 us
  transfers between devices with their start and end apart: 11, of which 4 were waited for; matrix products, arithmetic and copies ran while one was open for 17% of the time, Pallas kernels for 0%

profile of v15, /device:TPU:24, one launch (start us, length us, event | category | flops | bytes accessed | tf_op | source)
XLA Modules:
  0.0 95.0 jit_solution(16894926588817561190)
XLA Ops:
  0.7 1.7 %fusion.89 = (s32[1]{0:T(128)}, s32[1]{0:T(128)}, s32[1]{0:T(128)}, s32[1]{0:T(128)}, s32[1]{0:T(128)}, /*index=5*/s32[1]{0:T(128)}, s32[1]{0:T(128)}, s32[1]{0:T(128)}) fusion(s32[128]{0:T(128)} %param.17, s32[]{:T(128)S(6)} %max.42, s32[]{:T(128)S(6)} %max.39, s32[]{:T(128)S(6)} %max.38, s32[]{:T(128)S(6)} %max.37, s32[]{:T(128)S(6)} %max.36, ...), kind=kLoop, calls=%fused_computation.113 | loop fusion | bytes 96 | tf_op jit(solution)/shard_map/dynamic_slice | solution.py:149
  3.6 1.0 %reduce_window_sum.11 = f32[8,128]{1,0:T(8,128)S(1)} reduce-window(f32[8,128]{1,0:T(8,128)} %param.12, f32[]{:T(128)} %constant.56.clone.1), window={size=1x128 pad=0_0x127_0}, to_apply=%region_0.0 | reduce-window | flops 130048 | bytes 8196 | tf_op jit(solution)/shard_map/jit(cumsum)/reduce_window_sum | solution.py:88
  5.2 1.1 %copy.102 = bf16[128,1024]{0,1:T(8,128)(2,1)S(1)} copy(bf16[128,1024]{1,0:T(8,128)(2,1)} %param.10) | data formatting | bytes 524288 | tf_op jit(solution)/shard_map/reshape | solution.py:86
  6.7 0.9 copy.59
  7.6 1.8 %collective-permute-start = (f32[8,129,128]{2,0,1:T(8,128)}, f32[8,129,128]{2,0,1:T(8,128)S(1)}, u32[]{:S(2)}, u32[]{:S(2)}) collective-permute-start(f32[8,129,128]{2,0,1:T(8,128)} %copy.59), channel_id=1, source_target_pairs={{0,4},{8,12},{16,20},{24,28},{32,36},{40,44},{48,52},{56,60},{64,6... | collective-permute-start | bytes 1585160 | tf_op jit(solution)/shard_map/ppermute | solution.py:38
  9.7 3.8 %collective-permute-start.1 = (bf16[2,128,256]{1,2,0:T(8,128)(2,1)S(1)}, bf16[2,128,256]{1,2,0:T(8,128)(2,1)S(1)}, u32[]{:S(2)}, u32[]{:S(2)}) collective-permute-start(bf16[2,128,256]{1,2,0:T(8,128)(2,1)S(1)} %get-tuple-element.56), channel_id=1, source_target_pairs={{0,8},{4,12},{8,16},{12,20},{16,24},{20,28},{24,32},{28,36},{32,40... | collective-permute-start | bytes 393224 | tf_op jit(solution)/shard_map/ppermute | solution.py:32
  13.5 10.7 %collective-permute-done.1 = bf16[2,128,256]{1,2,0:T(8,128)(2,1)S(1)} collective-permute-done((bf16[2,128,256]{1,2,0:T(8,128)(2,1)S(1)}, bf16[2,128,256]{1,2,0:T(8,128)(2,1)S(1)}, u32[]{:S(2)}, u32[]{:S(2)}) %collective-permute-start.1) | collective-permute-done | bytes 131104 | tf_op jit(solution)/shard_map/ppermute | solution.py:32
  25.5 1.9 %collective-permute-start.3 = (bf16[2,128,256]{1,2,0:T(8,128)(2,1)S(1)}, bf16[2,128,256]{1,2,0:T(8,128)(2,1)S(1)}, u32[]{:S(2)}, u32[]{:S(2)}) collective-permute-start(bf16[2,128,256]{1,2,0:T(8,128)(2,1)S(1)} %collective-permute-done.1), channel_id=1, source_target_pairs={{0,8},{4,12},{8,16},{12,20},{16,24},{20,28},{24,32},{28,36},{32,40... | collective-permute-start | bytes 393224 | tf_op jit(solution)/shard_map/ppermute | solution.py:32
  31.3 4.6 %collective-permute-done.3 = bf16[2,128,256]{1,2,0:T(8,128)(2,1)S(1)} collective-permute-done((bf16[2,128,256]{1,2,0:T(8,128)(2,1)S(1)}, bf16[2,128,256]{1,2,0:T(8,128)(2,1)S(1)}, u32[]{:S(2)}, u32[]{:S(2)}) %collective-permute-start.3) | collective-permute-done | bytes 131104 | tf_op jit(solution)/shard_map/ppermute | solution.py:32
  35.9 1.9 %collective-permute-start.5 = (bf16[2,128,256]{1,2,0:T(8,128)(2,1)S(1)}, bf16[2,128,256]{1,2,0:T(8,128)(2,1)S(1)}, u32[]{:S(2)}, u32[]{:S(2)}) collective-permute-start(bf16[2,128,256]{1,2,0:T(8,128)(2,1)S(1)} %collective-permute-done.3), channel_id=1, source_target_pairs={{0,8},{4,12},{8,16},{12,20},{16,24},{20,28},{24,32},{28,36},{32,40... | collective-permute-start | bytes 393224 | tf_op jit(solution)/shard_map/ppermute | solution.py:32
  38.0 0.8 fusion.53
  38.8 1.3 %collective-permute-start.4 = (bf16[8,128,128]{2,1,0:T(8,128)(2,1)}, bf16[8,128,128]{2,1,0:T(8,128)(2,1)}, u32[]{:S(2)}, u32[]{:S(2)}) collective-permute-start(bf16[8,128,128]{2,1,0:T(8,128)(2,1)} %fusion.53), channel_id=1, source_target_pairs={{4,20},{12,28},{20,36},{28,44},{36,52},{44,60},{52,68},{60,76},{68... | collective-permute-start | bytes 786440 | tf_op jit(solution)/shard_map/ppermute | solution.py:59
  44.2 1.2 %collective-permute-done.5 = bf16[2,128,256]{1,2,0:T(8,128)(2,1)S(1)} collective-permute-done((bf16[2,128,256]{1,2,0:T(8,128)(2,1)S(1)}, bf16[2,128,256]{1,2,0:T(8,128)(2,1)S(1)}, u32[]{:S(2)}, u32[]{:S(2)}) %collective-permute-start.5) | collective-permute-done | bytes 131104 | tf_op jit(solution)/shard_map/ppermute | solution.py:32
  45.4 1.3 %collective-permute-start.7 = (bf16[2,128,256]{1,2,0:T(8,128)(2,1)S(1)}, bf16[2,128,256]{1,2,0:T(8,128)(2,1)}, u32[]{:S(2)}, u32[]{:S(2)}) collective-permute-start(bf16[2,128,256]{1,2,0:T(8,128)(2,1)S(1)} %collective-permute-done.5), channel_id=1, source_target_pairs={{4,12},{12,20},{20,28},{28,36},{36,44},{44,52},{52,60},{60,68},{68... | collective-permute-start | bytes 393224 | tf_op jit(solution)/shard_map/ppermute | solution.py:32
  46.7 1.8 %add_convert_fusion.1 = bf16[8,128,128]{2,1,0:T(8,128)(2,1)} fusion(bf16[8,128,128]{2,1,0:T(8,128)(2,1)} %collective-permute-done.4, f32[8,128,128]{2,1,0:T(8,128)S(1)} %get-tuple-element.45, f32[8]{0:T(128)S(1)} %get-tuple-element.36, f32[8]{0:T(128)S(1)} %get-tuple-element.37, bf16[8,130,128]{2,1,0:T(8,128)(2,1)S(1)} %collective-permute-done.2), kind=kLoop, calls=%fused_computation.47 | loop fusion | flops 917504 | bytes 1310784 | tf_op jit(solution)/shard_map/convert_element_type | solution.py:66
  48.6 1.3 %collective-permute-start.6 = (bf16[8,128,128]{2,1,0:T(8,128)(2,1)}, bf16[8,128,128]{2,1,0:T(8,128)(2,1)S(1)}, u32[]{:S(2)}, u32[]{:S(2)}) collective-permute-start(bf16[8,128,128]{2,1,0:T(8,128)(2,1)} %add_convert_fusion.1), channel_id=1, source_target_pairs={{4,8},{12,16},{20,24},{28,32},{36,40},{44,48},{52,56},{60,64},{68,... | collective-permute-start | bytes 786440 | tf_op jit(solution)/shard_map/ppermute | solution.py:66
  49.9 0.8 maximum_select_fusion
  50.8 9.3 %collective-permute-start.8 = (bf16[3,2,128,256]{2,3,1,0:T(8,128)(2,1)}, bf16[3,2,128,256]{2,3,1,0:T(8,128)(2,1)S(1)}, u32[]{:S(2)}, u32[]{:S(2)}) collective-permute-start(bf16[3,2,128,256]{2,3,1,0:T(8,128)(2,1)} %maximum_select_fusion), channel_id=1, source_target_pairs={{0,4},{4,0},{8,12},{12,8},{16,20},{20,16},{24,28},{28,24},{32,36},... | collective-permute-start | bytes 1179656 | tf_op jit(solution)/shard_map/ppermute | solution.py:68
  60.4 2.7 %fusion.2 = (f32[128,2,8]{0,2,1:T(8,128)S(1)}, f32[2,512,128,8]{2,1,3,0:T(8,128)}) fusion(pred[128,512]{0,1:T(8,128)(4,1)S(1)} %copy.65, bf16[128,2,8,128]{3,2,1,0:T(8,128)(2,1)S(1)} %bitcast.142, bf16[512,2,128,1]{2,1,0,3:T(2,128)(2,1)S(1)} %bitcast.147), kind=kOutput, calls=%fused_computation.4 | convolution fusion | flops 271579136 | bytes 5054464 | tf_op jit(solution)/shard_map/tkgd,skd->tkgs/dot_general | solution.py:105
  63.4 1.6 %collective-permute-done.6 = bf16[8,128,128]{2,1,0:T(8,128)(2,1)S(1)} collective-permute-done((bf16[8,128,128]{2,1,0:T(8,128)(2,1)}, bf16[8,128,128]{2,1,0:T(8,128)(2,1)S(1)}, u32[]{:S(2)}, u32[]{:S(2)}) %collective-permute-start.6) | collective-permute-done | bytes 262176 | tf_op jit(solution)/shard_map/ppermute | solution.py:66
  65.0 0.8 add_convert_fusion
  65.8 1.9 %collective-permute-start.10 = (bf16[2,128,256]{1,2,0:T(8,128)(2,1)S(1)}, bf16[2,128,256]{1,2,0:T(8,128)(2,1)}, u32[]{:S(2)}, u32[]{:S(2)}) collective-permute-start(bf16[2,128,256]{1,2,0:T(8,128)(2,1)S(1)} %broadcast_select_fusion), channel_id=1, source_target_pairs={{0,4},{4,0},{8,12},{12,8},{16,20},{20,16},{24,28},{28,24},{32,36},... | collective-permute-start | bytes 393224 | tf_op jit(solution)/shard_map/ppermute | solution.py:76
  67.8 2.4 %collective-permute-start.9 = (bf16[8,128,128]{2,1,0:T(8,128)(2,1)}, bf16[8,128,128]{2,1,0:T(8,128)(2,1)S(1)}, u32[]{:S(2)}, u32[]{:S(2)}) collective-permute-start(bf16[8,128,128]{2,1,0:T(8,128)(2,1)} %add_convert_fusion), channel_id=1, source_target_pairs={{0,4},{8,12},{16,20},{24,28},{32,36},{40,44},{48,52},{56,60},{64,6... | collective-permute-start | bytes 786440 | tf_op jit(solution)/shard_map/ppermute | solution.py:75
  71.5 3.2 %fusion.1 = f32[128,2,8]{0,2,1:T(8,128)S(1)} fusion(f32[2,512,128,8]{2,1,3,0:T(8,128)} %get-tuple-element.72, f32[128,2,8]{0,2,1:T(8,128)S(1)} %get-tuple-element.59, pred[128,512]{0,1:T(8,128)(4,1)S(1)} %copy.65), kind=kLoop, calls=%fused_computation.3 | loop fusion | flops 4192256 | bytes 4276224 | tf_op jit(solution)/shard_map/reduce_sum | solution.py:112
  74.7 0.7 fusion.4
  75.5 1.2 %fusion.32 = f32[128,2,8,128]{0,3,2,1:T(8,128)S(1)} fusion(f32[2,512,128,8]{2,1,3,0:T(8,128)S(1)} %copy-done.1, f32[128,2,8]{0,2,1:T(8,128)S(1)} %get-tuple-element.59, pred[128,512]{0,1:T(8,128)(4,1)S(1)} %copy.65, f32[128,2,8]{0,2,1:T(8,128)S(1)} %get-tuple-element.43, f32[128,2,8]{0,2,1:T(8,128)S(1)} %get-tuple-element.57, ...), kind=kOutput, calls=%fused_computation.28 | convolution fusion | flops 273154048 | bytes 5595136 | tf_op jit(solution)/shard_map/tkgs,skd->tkgd/dot_general | solution.py:113
  76.7 2.0 %fusion.21 = f32[128,2,8,128]{0,3,2,1:T(8,128)} fusion(f32[128,2,8,128]{0,3,2,1:T(8,128)S(1)} %fusion.32, f32[2,384,128,8]{2,1,3,0:T(8,128)S(1)} %get-tuple-element.74, f32[128,2,8]{0,2,1:T(8,128)S(1)} %get-tuple-element.27, pred[384]{0:T(512)(128)(4,1)S(1)} %add_add_fusion.1, bf16[384,2,128,1]{0,2,1,3:T(8,128)(2,1)S(1)} %reshape.104), kind=kOutput, calls=%fused_computation.22 | convolution fusion | flops 204734464 | bytes 5448064 | tf_op jit(solution)/shard_map/tkgs,skd->tkgd/dot_general | solution.py:113
  79.1 1.6 %multiply_reduce_fusion = (f32[128]{0:T(128)S(1)}, f32[128,8,128]{0,2,1:T(8,128)S(1)}) fusion(f32[128,8,128]{0,2,1:T(8,128)S(1)} %fusion.36, bf16[128,8,128]{0,2,1:T(8,128)(2,1)S(1)} %bitcast.149, f32[8,128]{1,0:T(8,128)S(1)} %copy-done.8, pred[128,128]{1,0:T(8,128)(4,1)S(1)} %iota_compare_fusion, bf16[128,1024]{1,0:T(8,128)(2,1)S(1)} %copy-done, ...), kind=kOutput, calls=%fused_computation.45 | convolution fusion | flops 68026240 | bytes 1856000 | tf_op jit(solution)/shard_map/hts,shd->thd/dot_general | solution.py:94
  80.6 10.5 %psum.7 = f32[128]{0:T(128)S(1)} all-reduce(f32[128]{0:T(128)S(1)} %get-tuple-element.75), channel_id=1, replica_groups=mesh['grp'=4,'seq'=32,'head'=4] {'head'}, use_global_device_ids=true, to_apply=%region_6.7 | all-reduce | flops 128 | bytes 1024 | tf_op jit(solution)/shard_map/psum | solution.py:171
  91.3 0.9 fusion.88
  93.1 1.0 %copy.83 = bf16[128,2048]{1,0:T(8,128)(2,1)} copy(bf16[128,2048]{0,1:T(8,128)(2,1)S(1)} %bitcast.153) | data formatting | bytes 1048576
  94.2 0.8 multiply_convert_fusion
  (82 shorter events, 6.4 us)
Async XLA Ops:
  0.6 5.7 %copy-start = (bf16[128,1024]{1,0:T(8,128)(2,1)S(1)}, bf16[128,1024]{1,0:T(8,128)(2,1)}, u32[]{:S(2)}) copy-start(bf16[128,1024]{1,0:T(8,128)(2,1)} %param.11) | copy-start | bytes 786436
  0.6 8.7 %copy-start.5 = (bf16[128,256]{1,0:T(8,128)(2,1)S(1)}, bf16[128,256]{1,0:T(8,128)(2,1)}, u32[]{:S(2)}) copy-start(bf16[128,256]{1,0:T(8,128)(2,1)} %param.15) | copy-start | bytes 196612
  0.7 8.9 %copy-start.6 = (bf16[128,256]{1,0:T(8,128)(2,1)S(1)}, bf16[128,256]{1,0:T(8,128)(2,1)}, u32[]{:S(2)}) copy-start(bf16[128,256]{1,0:T(8,128)(2,1)} %param.16) | copy-start | bytes 196612
  4.6 0.6 copy-start.7
  6.7 37.3 %copy-start.3 = (bf16[128,2048]{1,0:T(8,128)(2,1)S(1)}, bf16[128,2048]{1,0:T(8,128)(2,1)}, u32[]{:S(2)}) copy-start(bf16[128,2048]{1,0:T(8,128)(2,1)} %param.14) | copy-start | bytes 1572868
  7.6 16.6 %collective-permute-start = (f32[8,129,128]{2,0,1:T(8,128)}, f32[8,129,128]{2,0,1:T(8,128)S(1)}, u32[]{:S(2)}, u32[]{:S(2)}) collective-permute-start(f32[8,129,128]{2,0,1:T(8,128)} %copy.59), channel_id=1, source_target_pairs={{0,4},{8,12},{16,20},{24,28},{32,36},{40,44},{48,52},{56,60},{64,6... | collective-permute-start | bytes 1585160 | tf_op jit(solution)/shard_map/ppermute | solution.py:38
  9.7 14.6 %collective-permute-start.1 = (bf16[2,128,256]{1,2,0:T(8,128)(2,1)S(1)}, bf16[2,128,256]{1,2,0:T(8,128)(2,1)S(1)}, u32[]{:S(2)}, u32[]{:S(2)}) collective-permute-start(bf16[2,128,256]{1,2,0:T(8,128)(2,1)S(1)} %get-tuple-element.56), channel_id=1, source_target_pairs={{0,8},{4,12},{8,16},{12,20},{16,24},{20,28},{24,32},{28,36},{32,40... | collective-permute-start | bytes 393224 | tf_op jit(solution)/shard_map/ppermute | solution.py:32
  24.9 11.1 %collective-permute-start.2 = (bf16[8,130,128]{2,1,0:T(8,128)(2,1)S(1)}, bf16[8,130,128]{2,1,0:T(8,128)(2,1)S(1)}, u32[]{:S(2)}, u32[]{:S(2)}) collective-permute-start(bf16[8,130,128]{2,1,0:T(8,128)(2,1)S(1)} %pad_maximum_fusion.2), channel_id=1, source_target_pairs={{4,12},{12,20},{20,28},{28,36},{36,44},{44,52},{52,60},{60,68},{68... | collective-permute-start | bytes 798728 | tf_op jit(solution)/shard_map/ppermute | solution.py:53
  25.5 10.4 %collective-permute-start.3 = (bf16[2,128,256]{1,2,0:T(8,128)(2,1)S(1)}, bf16[2,128,256]{1,2,0:T(8,128)(2,1)S(1)}, u32[]{:S(2)}, u32[]{:S(2)}) collective-permute-start(bf16[2,128,256]{1,2,0:T(8,128)(2,1)S(1)} %collective-permute-done.1), channel_id=1, source_target_pairs={{0,8},{4,12},{8,16},{12,20},{16,24},{20,28},{24,32},{28,36},{32,40... | collective-permute-start | bytes 393224 | tf_op jit(solution)/shard_map/ppermute | solution.py:32
  35.9 9.5 %collective-permute-start.5 = (bf16[2,128,256]{1,2,0:T(8,128)(2,1)S(1)}, bf16[2,128,256]{1,2,0:T(8,128)(2,1)S(1)}, u32[]{:S(2)}, u32[]{:S(2)}) collective-permute-start(bf16[2,128,256]{1,2,0:T(8,128)(2,1)S(1)} %collective-permute-done.3), channel_id=1, source_target_pairs={{0,8},{4,12},{8,16},{12,20},{16,24},{20,28},{24,32},{28,36},{32,40... | collective-permute-start | bytes 393224 | tf_op jit(solution)/shard_map/ppermute | solution.py:32
  38.8 6.6 %collective-permute-start.4 = (bf16[8,128,128]{2,1,0:T(8,128)(2,1)}, bf16[8,128,128]{2,1,0:T(8,128)(2,1)}, u32[]{:S(2)}, u32[]{:S(2)}) collective-permute-start(bf16[8,128,128]{2,1,0:T(8,128)(2,1)} %fusion.53), channel_id=1, source_target_pairs={{4,20},{12,28},{20,36},{28,44},{36,52},{44,60},{52,68},{60,76},{68... | collective-permute-start | bytes 786440 | tf_op jit(solution)/shard_map/ppermute | solution.py:59
  45.4 17.9 %collective-permute-start.7 = (bf16[2,128,256]{1,2,0:T(8,128)(2,1)S(1)}, bf16[2,128,256]{1,2,0:T(8,128)(2,1)}, u32[]{:S(2)}, u32[]{:S(2)}) collective-permute-start(bf16[2,128,256]{1,2,0:T(8,128)(2,1)S(1)} %collective-permute-done.5), channel_id=1, source_target_pairs={{4,12},{12,20},{20,28},{28,36},{36,44},{44,52},{52,60},{60,68},{68... | collective-permute-start | bytes 393224 | tf_op jit(solution)/shard_map/ppermute | solution.py:32
  48.6 16.4 %collective-permute-start.6 = (bf16[8,128,128]{2,1,0:T(8,128)(2,1)}, bf16[8,128,128]{2,1,0:T(8,128)(2,1)S(1)}, u32[]{:S(2)}, u32[]{:S(2)}) collective-permute-start(bf16[8,128,128]{2,1,0:T(8,128)(2,1)} %add_convert_fusion.1), channel_id=1, source_target_pairs={{4,8},{12,16},{20,24},{28,32},{36,40},{44,48},{52,56},{60,64},{68,... | collective-permute-start | bytes 786440 | tf_op jit(solution)/shard_map/ppermute | solution.py:66
  50.8 14.2 %collective-permute-start.8 = (bf16[3,2,128,256]{2,3,1,0:T(8,128)(2,1)}, bf16[3,2,128,256]{2,3,1,0:T(8,128)(2,1)S(1)}, u32[]{:S(2)}, u32[]{:S(2)}) collective-permute-start(bf16[3,2,128,256]{2,3,1,0:T(8,128)(2,1)} %maximum_select_fusion), channel_id=1, source_target_pairs={{0,4},{4,0},{8,12},{12,8},{16,20},{20,16},{24,28},{28,24},{32,36},... | collective-permute-start | bytes 1179656 | tf_op jit(solution)/shard_map/ppermute | solution.py:68
  65.8 12.9 %collective-permute-start.10 = (bf16[2,128,256]{1,2,0:T(8,128)(2,1)S(1)}, bf16[2,128,256]{1,2,0:T(8,128)(2,1)}, u32[]{:S(2)}, u32[]{:S(2)}) collective-permute-start(bf16[2,128,256]{1,2,0:T(8,128)(2,1)S(1)} %broadcast_select_fusion), channel_id=1, source_target_pairs={{0,4},{4,0},{8,12},{12,8},{16,20},{20,16},{24,28},{28,24},{32,36},... | collective-permute-start | bytes 393224 | tf_op jit(solution)/shard_map/ppermute | solution.py:76
  67.8 10.9 %collective-permute-start.9 = (bf16[8,128,128]{2,1,0:T(8,128)(2,1)}, bf16[8,128,128]{2,1,0:T(8,128)(2,1)S(1)}, u32[]{:S(2)}, u32[]{:S(2)}) collective-permute-start(bf16[8,128,128]{2,1,0:T(8,128)(2,1)} %add_convert_fusion), channel_id=1, source_target_pairs={{0,4},{8,12},{16,20},{24,28},{32,36},{40,44},{48,52},{56,60},{64,6... | collective-permute-start | bytes 786440 | tf_op jit(solution)/shard_map/ppermute | solution.py:75
  71.5 3.9 %copy-start.1 = (f32[2,512,128,8]{2,1,3,0:T(8,128)S(1)}, f32[2,512,128,8]{2,1,3,0:T(8,128)}, u32[]{:S(2)}) copy-start(f32[2,512,128,8]{2,1,3,0:T(8,128)} %get-tuple-element.72) | copy-start | bytes 12582916
  76.7 2.1 %copy-start.4 = (bf16[128,1024]{1,0:T(8,128)(2,1)S(1)}, bf16[128,1024]{1,0:T(8,128)(2,1)}, u32[]{:S(2)}) copy-start(bf16[128,1024]{1,0:T(8,128)(2,1)} %param.9) | copy-start | bytes 786436
  76.7 2.4 %copy-start.8 = (f32[8,128]{1,0:T(8,128)S(1)}, f32[8,128]{1,0:T(8,128)}, u32[]{:S(2)}) copy-start(f32[8,128]{1,0:T(8,128)} %copy-done.7) | copy-start | bytes 12292
  79.1 13.7 %copy-start.2 = (f32[128,2,8,128]{0,3,2,1:T(8,128)S(1)}, f32[128,2,8,128]{0,3,2,1:T(8,128)}, u32[]{:S(2)}) copy-start(f32[128,2,8,128]{0,3,2,1:T(8,128)} %fusion.21) | copy-start | bytes 3145732
  92.8 1.4 %copy-start.9 = (f32[1024]{0:T(1024)S(1)}, f32[1024]{0:T(1024)}, u32[]{:S(2)}) copy-start(f32[1024]{0:T(1024)} %param.13) | copy-start | bytes 12292
